TPU v7x, 256 devices: a whole 4x4x8 slice. The times are simulated.
256 devices in a mesh: rad: 16 (over x, y_hi, core), azi: 16 (over z, y_lo).
Axes of the slice: x: 4, y: 4 (y_hi: 2, y_lo: 2; y = y_hi * 2 + y_lo), z: 8, core: 2. Of those that a mesh axis runs over, the one named last changes fastest.
Arguments:
- fields: float32 [5, 512, 256, 128], P(None, 'rad', 'azi'), may hold values from -6 to 6
- kappa: float32 [512, 256, 128], P('rad', 'azi'), may hold values from 0.01 to 0.1
- radial_speed: float32 [5, 512], P(None, 'rad'), may hold values from -0.5 to 0.5
- azimuth_speed: float32 [5, 512], P(None, 'rad'), may hold values from -0.5 to 0.5
- shifts: int32 [512], P('rad'), may hold values from 0 to 255
Outputs:
- advanced: float32 [5, 512, 256, 128], P(None, 'rad', 'azi')
All inputs are finite; a program needn't handle non-finite values.
Results may differ from a plain program's by a relative error of at most 0.00002.
Values sent between devices are 32-bit elements; how exact they have to be, the bound alone decides.
No kernel may reach another device: no remote copies, remote signals or barrier semaphores. Data moves between devices by JAX's collectives and lax.ppermute only.
A program may use at most 64 MiB of HBM per device.

v0:
```python
import jax
import jax.numpy as jnp
from jax import lax
from jax.sharding import PartitionSpec as P


def with_halo(cells, sides, width, closed):
    for axis, dim in sides:
        count = lax.axis_size(axis)
        ends = count if closed else count - 1
        head = lax.slice_in_dim(cells, 0, width, axis=dim)
        tail = lax.slice_in_dim(cells, cells.shape[dim] - width, cells.shape[dim], axis=dim)
        cells = jnp.concatenate(
            [
                lax.ppermute(tail, axis, [(i, (i + 1) % count) for i in range(ends)]),
                cells,
                lax.ppermute(head, axis, [((i + 1) % count, i) for i in range(ends)]),
            ],
            axis=dim,
        )
    return cells


def from_behind(array, axis, by):
    peers = lax.axis_size(axis)
    return lax.ppermute(array, axis, [(i, (i + by) % peers) for i in range(peers)])


def stencil(padded, kap, speed_r, speed_p):
    n_r = padded.shape[1] - 4
    n_p = padded.shape[2] - 4

    def tap(a, b):
        return padded[:, 2 + a : 2 + a + n_r, 2 + b : 2 + b + n_p, :]

    centre = tap(0, 0)
    height = centre.shape[3]
    zpad = jnp.pad(centre, ((0, 0), (0, 0), (0, 0), (2, 2)))

    def ztap(a):
        return zpad[:, :, :, 2 + a : 2 + a + height]

    first_r = (tap(-2, 0) - 8.0 * tap(-1, 0) + 8.0 * tap(1, 0) - tap(2, 0)) / 12.0
    first_p = (tap(0, -2) - 8.0 * tap(0, -1) + 8.0 * tap(0, 1) - tap(0, 2)) / 12.0
    second_r = (
        -tap(-2, 0) + 16.0 * tap(-1, 0) - 30.0 * centre + 16.0 * tap(1, 0) - tap(2, 0)
    ) / 12.0
    second_p = (
        -tap(0, -2) + 16.0 * tap(0, -1) - 30.0 * centre + 16.0 * tap(0, 1) - tap(0, 2)
    ) / 12.0
    second_z = (-ztap(-2) + 16.0 * ztap(-1) - 30.0 * centre + 16.0 * ztap(1) - ztap(2)) / 12.0
    return (
        -speed_r[:, :, None, None] * first_r
        - speed_p[:, :, None, None] * first_p
        + kap[None] * (second_r + second_p + second_z)
    )


def extend(field, width):
    beside_all = with_halo(field, (("azi", 2),), width, True)
    return with_halo(beside_all, (("rad", 1),), width, False)


def heun_sections(field, kappa, speed_r, speed_p):
    first = field + stencil(extend(field, 2), kappa, speed_r, speed_p)
    return 0.5 * (field + first + stencil(extend(first, 2), kappa, speed_r, speed_p))


def rotate_rows(joined, offset, length):
    current = joined
    for level in range((length - 1).bit_length()):
        step_size = 1 << level
        pushed = jnp.concatenate(
            [jnp.zeros_like(current[:, :, :step_size]), current[:, :, :-step_size]], axis=2
        )
        chosen = offset // step_size % 2 == 1
        current = jnp.where(chosen[None, :, None, None], pushed, current)
    return current[:, :, length : 2 * length]


def shift_rows(half, shifts):
    fcount, rows, sector, height = half.shape
    whole = shifts // sector
    remain = shifts % sector
    moved = half
    for level in range((lax.axis_size("azi") - 1).bit_length()):
        other = from_behind(moved, "azi", 1 << level)
        taken = whole // (1 << level) % 2 == 1
        moved = jnp.where(taken[None, :, None, None], other, moved)
    before = from_behind(moved, "azi", 1)
    joined = jnp.concatenate([before, moved], axis=2)
    return rotate_rows(joined, remain, sector)


def shards(fields, kappa, radial_speed, azimuth_speed, shifts):
    half = heun_sections(fields, kappa, radial_speed, azimuth_speed)
    moved = shift_rows(half, shifts)
    return heun_sections(moved, kappa, radial_speed, azimuth_speed)


def solution(mesh):
    placed = (
        P(None, "rad", "azi", None),
        P("rad", "azi", None),
        P(None, "rad"),
        P(None, "rad"),
        P("rad"),
    )
    return jax.shard_map(
        shards, mesh=mesh, in_specs=placed, out_specs=P(None, "rad", "azi", None), check_vma=False
    )
```

profile of v0, /device:TPU:53, one launch (start us, length us, event | category | flops | bytes accessed | tf_op | source)
XLA Modules:
  0.0 377.5 jit_solution(17053951647244507343)
XLA Ops:
  4.3 3.6 collective-permute-done
  8.5 4.0 %collective-permute-done.1 = f32[5,32,2,128]{3,1,2,0:T(8,128)S(1)} collective-permute-done((f32[5,32,2,128]{3,1,2,0:T(8,128)S(1)}, f32[5,32,2,128]{3,1,2,0:T(8,128)S(1)}, u32[]{:S(2)}, u32[]{:S(2)}) %collective-permute-start.1) | collective-permute-done | bytes 163872 | tf_op jit(solution)/shard_map/ppermute | solution.py:17
  12.5 3.0 collective-permute-start.2
  15.5 1.9 collective-permute-start.3
  17.6 6.3 %collective-permute-done.3 = f32[5,2,20,128]{3,1,2,0:T(2,128)S(1)} collective-permute-done((f32[5,2,20,128]{3,1,2,0:T(2,128)S(1)}, f32[5,2,20,128]{3,1,2,0:T(2,128)S(1)}, u32[]{:S(2)}, u32[]{:S(2)}) %collective-permute-start.3) | collective-permute-done | bytes 102432 | tf_op jit(solution)/shard_map/ppermute | solution.py:17
  23.9 3.3 fusion.18
  29.6 5.0 %collective-permute-done.4 = f32[5,32,2,128]{3,1,2,0:T(8,128)S(1)} collective-permute-done((f32[5,32,2,128]{3,1,2,0:T(8,128)S(1)}, f32[5,32,2,128]{3,1,2,0:T(8,128)S(1)}, u32[]{:S(2)}, u32[]{:S(2)}) %collective-permute-start.4) | collective-permute-done | bytes 163872 | tf_op jit(solution)/shard_map/ppermute | solution.py:15
  34.6 2.1 collective-permute-done.5
  36.8 3.8 %collective-permute-start.6 = (f32[5,2,20,128]{3,1,2,0:T(2,128)S(1)}, f32[5,2,20,128]{3,1,2,0:T(2,128)S(1)}, u32[]{:S(2)}, u32[]{:S(2)}) collective-permute-start(f32[5,2,20,128]{3,1,2,0:T(2,128)S(1)} %get-tuple-element.21), channel_id=1, source_target_pairs={{0,16},{16,32},{32,48},{48,64},{64,80},{80,96},{96,112},{112,128},... | collective-permute-start | bytes 307208 | tf_op jit(solution)/shard_map/ppermute | solution.py:15
  40.6 1.9 collective-permute-start.7
  42.5 6.4 %collective-permute-done.7 = f32[5,2,20,128]{3,1,2,0:T(2,128)S(1)} collective-permute-done((f32[5,2,20,128]{3,1,2,0:T(2,128)S(1)}, f32[5,2,20,128]{3,1,2,0:T(2,128)S(1)}, u32[]{:S(2)}, u32[]{:S(2)}) %collective-permute-start.7) | collective-permute-done | bytes 102432 | tf_op jit(solution)/shard_map/ppermute | solution.py:17
  49.3 2.6 fusion.30
  52.1 29.3 %collective-permute-done.8 = f32[5,32,16,128]{3,1,2,0:T(8,128)S(1)} collective-permute-done((f32[5,32,16,128]{3,1,2,0:T(8,128)S(1)}, f32[5,32,16,128]{3,1,2,0:T(8,128)S(1)}, u32[]{:S(2)}, u32[]{:S(2)}) %collective-permute-start.8) | collective-permute-done | bytes 1310752 | tf_op jit(solution)/shard_map/ppermute | solution.py:26
  83.4 27.9 %collective-permute-done.9 = f32[5,32,16,128]{3,1,2,0:T(8,128)S(1)} collective-permute-done((f32[5,32,16,128]{3,1,2,0:T(8,128)S(1)}, f32[5,32,16,128]{3,1,2,0:T(8,128)S(1)}, u32[]{:S(2)}, u32[]{:S(2)}) %collective-permute-start.9) | collective-permute-done | bytes 1310752 | tf_op jit(solution)/shard_map/ppermute | solution.py:26
  111.8 3.1 collective-permute-start.10
  114.8 59.3 %collective-permute-done.10 = f32[5,32,16,128]{3,1,2,0:T(8,128)S(1)} collective-permute-done((f32[5,32,16,128]{3,1,2,0:T(8,128)S(1)}, f32[5,32,16,128]{3,1,2,0:T(8,128)S(1)}, u32[]{:S(2)}, u32[]{:S(2)}) %collective-permute-start.10) | collective-permute-done | bytes 1310752 | tf_op jit(solution)/shard_map/ppermute | solution.py:26
  174.4 3.9 %collective-permute-start.11 = (f32[5,32,16,128]{3,1,2,0:T(8,128)S(1)}, f32[5,32,16,128]{3,1,2,0:T(8,128)S(1)}, u32[]{:S(2)}, u32[]{:S(2)}) collective-permute-start(f32[5,32,16,128]{3,1,2,0:T(8,128)S(1)} %broadcast_select_fusion.2), channel_id=1, source_target_pairs={{0,8},{1,9},{2,10},{3,11},{4,12},{5,13},{6,14},{7,15},{8,0},{9,1},... | collective-permute-start | bytes 3932168 | tf_op jit(solution)/shard_map/ppermute | solution.py:26
  178.3 58.8 %collective-permute-done.11 = f32[5,32,16,128]{3,1,2,0:T(8,128)S(1)} collective-permute-done((f32[5,32,16,128]{3,1,2,0:T(8,128)S(1)}, f32[5,32,16,128]{3,1,2,0:T(8,128)S(1)}, u32[]{:S(2)}, u32[]{:S(2)}) %collective-permute-start.11) | collective-permute-done | bytes 1310752 | tf_op jit(solution)/shard_map/ppermute | solution.py:26
  237.7 30.5 %collective-permute-done.12 = f32[5,32,16,128]{3,1,2,0:T(8,128)S(1)} collective-permute-done((f32[5,32,16,128]{3,1,2,0:T(8,128)S(1)}, f32[5,32,16,128]{3,1,2,0:T(8,128)S(1)}, u32[]{:S(2)}, u32[]{:S(2)}) %collective-permute-start.12) | collective-permute-done | bytes 1310752 | tf_op jit(solution)/shard_map/ppermute | solution.py:26
  272.3 2.4 collective-permute-start.14
  274.8 4.5 %collective-permute-done.13 = f32[5,32,2,128]{3,1,2,0:T(8,128)S(1)} collective-permute-done((f32[5,32,2,128]{3,1,2,0:T(8,128)S(1)}, f32[5,32,2,128]{3,1,2,0:T(8,128)S(1)}, u32[]{:S(2)}, u32[]{:S(2)}) %collective-permute-start.13) | collective-permute-done | bytes 163872 | tf_op jit(solution)/shard_map/ppermute | solution.py:15
  279.3 1.9 collective-permute-done.14
  281.3 60.4 %collective-permute-start.15 = (f32[5,2,20,128]{3,1,2,0:T(2,128)S(1)}, f32[5,2,20,128]{3,1,2,0:T(2,128)S(1)}, u32[]{:S(2)}, u32[]{:S(2)}) collective-permute-start(f32[5,2,20,128]{3,1,2,0:T(2,128)S(1)} %get-tuple-element.17), channel_id=1, source_target_pairs={{0,16},{16,32},{32,48},{48,64},{64,80},{80,96},{96,112},{112,128},... | collective-permute-start | bytes 307208 | tf_op jit(solution)/shard_map/ppermute | solution.py:15
  341.6 1.9 collective-permute-start.16
  343.6 6.4 %collective-permute-done.16 = f32[5,2,20,128]{3,1,2,0:T(2,128)S(1)} collective-permute-done((f32[5,2,20,128]{3,1,2,0:T(2,128)S(1)}, f32[5,2,20,128]{3,1,2,0:T(2,128)S(1)}, u32[]{:S(2)}, u32[]{:S(2)}) %collective-permute-start.16) | collective-permute-done | bytes 102432 | tf_op jit(solution)/shard_map/ppermute | solution.py:17
  350.4 2.3 fusion.41
  352.8 1.8 collective-permute-start.17
  355.2 3.4 collective-permute-done.17
  359.8 4.7 %collective-permute-start.19 = (f32[5,2,20,128]{3,1,2,0:T(2,128)S(1)}, f32[5,2,20,128]{3,1,2,0:T(2,128)S(1)}, u32[]{:S(2)}, u32[]{:S(2)}) collective-permute-start(f32[5,2,20,128]{3,1,2,0:T(2,128)S(1)} %get-tuple-element.13), channel_id=1, source_target_pairs={{0,16},{16,32},{32,48},{48,64},{64,80},{80,96},{96,112},{112,128},... | collective-permute-start | bytes 307208 | tf_op jit(solution)/shard_map/ppermute | solution.py:15
  364.5 1.9 collective-permute-start.20
  366.4 6.4 %collective-permute-done.20 = f32[5,2,20,128]{3,1,2,0:T(2,128)S(1)} collective-permute-done((f32[5,2,20,128]{3,1,2,0:T(2,128)S(1)}, f32[5,2,20,128]{3,1,2,0:T(2,128)S(1)}, u32[]{:S(2)}, u32[]{:S(2)}) %collective-permute-start.20) | collective-permute-done | bytes 102432 | tf_op jit(solution)/shard_map/ppermute | solution.py:17
  373.3 2.4 fusion.53
  (59 shorter events, 19.9 us)
Async XLA Ops:
  0.0 4.3 %copy-start.1 = (f32[32,16,128]{2,1,0:T(8,128)S(1)}, f32[32,16,128]{2,1,0:T(8,128)}, u32[]{:S(2)}) copy-start(f32[32,16,128]{2,1,0:T(8,128)} %param.6) | copy-start | bytes 786436
  1.8 6.2 %copy-start = (f32[5,32,16,128]{3,2,1,0:T(8,128)S(1)}, f32[5,32,16,128]{3,2,1,0:T(8,128)}, u32[]{:S(2)}) copy-start(f32[5,32,16,128]{3,2,1,0:T(8,128)} %param.5) | copy-start | bytes 3932164
  1.8 6.1 %collective-permute-start = (f32[5,32,2,128]{3,1,2,0:T(8,128)S(1)}, f32[5,32,2,128]{3,1,2,0:T(8,128)S(1)}, u32[]{:S(2)}, u32[]{:S(2)}) collective-permute-start(f32[5,32,2,128]{3,1,2,0:T(8,128)S(1)} %get-tuple-element.32), channel_id=1, source_target_pairs={{0,1},{1,2},{2,3},{3,4},{4,5},{5,6},{6,7},{7,8},{8,9},{9,10},{10,1... | collective-permute-start | bytes 491528 | tf_op jit(solution)/shard_map/ppermute | solution.py:15
  2.9 9.5 %collective-permute-start.1 = (f32[5,32,2,128]{3,1,2,0:T(8,128)S(1)}, f32[5,32,2,128]{3,1,2,0:T(8,128)S(1)}, u32[]{:S(2)}, u32[]{:S(2)}) collective-permute-start(f32[5,32,2,128]{3,1,2,0:T(8,128)S(1)} %get-tuple-element.33), channel_id=1, source_target_pairs={{1,0},{2,1},{3,2},{4,3},{5,4},{6,5},{7,6},{8,7},{9,8},{10,9},{11,1... | collective-permute-start | bytes 491528 | tf_op jit(solution)/shard_map/ppermute | solution.py:17
  7.9 9.5 %copy-start.2 = (f32[5,32]{1,0:T(8,128)S(1)}, f32[5,32]{1,0:T(8,128)}, u32[]{:S(2)}) copy-start(f32[5,32]{1,0:T(8,128)} %param.7) | copy-start | bytes 1924
  8.0 9.5 %copy-start.3 = (f32[5,32]{1,0:T(8,128)S(1)}, f32[5,32]{1,0:T(8,128)}, u32[]{:S(2)}) copy-start(f32[5,32]{1,0:T(8,128)} %param.8) | copy-start | bytes 1924
  12.5 5.0 %collective-permute-start.2 = (f32[5,2,20,128]{3,1,2,0:T(2,128)S(1)}, f32[5,2,20,128]{3,1,2,0:T(2,128)S(1)}, u32[]{:S(2)}, u32[]{:S(2)}) collective-permute-start(f32[5,2,20,128]{3,1,2,0:T(2,128)S(1)} %get-tuple-element.23), channel_id=1, source_target_pairs={{0,16},{16,32},{32,48},{48,64},{64,80},{80,96},{96,112},{112,128},... | collective-permute-start | bytes 307208 | tf_op jit(solution)/shard_map/ppermute | solution.py:15
  15.5 8.4 %collective-permute-start.3 = (f32[5,2,20,128]{3,1,2,0:T(2,128)S(1)}, f32[5,2,20,128]{3,1,2,0:T(2,128)S(1)}, u32[]{:S(2)}, u32[]{:S(2)}) collective-permute-start(f32[5,2,20,128]{3,1,2,0:T(2,128)S(1)} %get-tuple-element.24), channel_id=1, source_target_pairs={{16,0},{32,16},{48,32},{64,48},{80,64},{96,80},{112,96},{128,112},... | collective-permute-start | bytes 307208 | tf_op jit(solution)/shard_map/ppermute | solution.py:17
  27.2 7.4 %collective-permute-start.4 = (f32[5,32,2,128]{3,1,2,0:T(8,128)S(1)}, f32[5,32,2,128]{3,1,2,0:T(8,128)S(1)}, u32[]{:S(2)}, u32[]{:S(2)}) collective-permute-start(f32[5,32,2,128]{3,1,2,0:T(8,128)S(1)} %get-tuple-element.27), channel_id=1, source_target_pairs={{0,1},{1,2},{2,3},{3,4},{4,5},{5,6},{6,7},{7,8},{8,9},{9,10},{10,1... | collective-permute-start | bytes 491528 | tf_op jit(solution)/shard_map/ppermute | solution.py:15
  28.9 7.8 %collective-permute-start.5 = (f32[5,32,2,128]{3,1,2,0:T(8,128)S(1)}, f32[5,32,2,128]{3,1,2,0:T(8,128)S(1)}, u32[]{:S(2)}, u32[]{:S(2)}) collective-permute-start(f32[5,32,2,128]{3,1,2,0:T(8,128)S(1)} %get-tuple-element.28), channel_id=1, source_target_pairs={{1,0},{2,1},{3,2},{4,3},{5,4},{6,5},{7,6},{8,7},{9,8},{10,9},{11,1... | collective-permute-start | bytes 491528 | tf_op jit(solution)/shard_map/ppermute | solution.py:17
  36.8 5.7 %collective-permute-start.6 = (f32[5,2,20,128]{3,1,2,0:T(2,128)S(1)}, f32[5,2,20,128]{3,1,2,0:T(2,128)S(1)}, u32[]{:S(2)}, u32[]{:S(2)}) collective-permute-start(f32[5,2,20,128]{3,1,2,0:T(2,128)S(1)} %get-tuple-element.21), channel_id=1, source_target_pairs={{0,16},{16,32},{32,48},{48,64},{64,80},{80,96},{96,112},{112,128},... | collective-permute-start | bytes 307208 | tf_op jit(solution)/shard_map/ppermute | solution.py:15
  40.6 8.4 %collective-permute-start.7 = (f32[5,2,20,128]{3,1,2,0:T(2,128)S(1)}, f32[5,2,20,128]{3,1,2,0:T(2,128)S(1)}, u32[]{:S(2)}, u32[]{:S(2)}) collective-permute-start(f32[5,2,20,128]{3,1,2,0:T(2,128)S(1)} %get-tuple-element.22), channel_id=1, source_target_pairs={{16,0},{32,16},{48,32},{64,48},{80,64},{96,80},{112,96},{128,112},... | collective-permute-start | bytes 307208 | tf_op jit(solution)/shard_map/ppermute | solution.py:17
  49.3 2.7 copy-start.4
  51.9 29.5 %collective-permute-start.8 = (f32[5,32,16,128]{3,1,2,0:T(8,128)S(1)}, f32[5,32,16,128]{3,1,2,0:T(8,128)S(1)}, u32[]{:S(2)}, u32[]{:S(2)}) collective-permute-start(f32[5,32,16,128]{3,1,2,0:T(8,128)S(1)} %fusion.30), channel_id=1, source_target_pairs={{0,1},{1,2},{2,3},{3,4},{4,5},{5,6},{6,7},{7,8},{8,9},{9,10},{10,1... | collective-permute-start | bytes 3932168 | tf_op jit(solution)/shard_map/ppermute | solution.py:26
  81.7 29.7 %collective-permute-start.9 = (f32[5,32,16,128]{3,1,2,0:T(8,128)S(1)}, f32[5,32,16,128]{3,1,2,0:T(8,128)S(1)}, u32[]{:S(2)}, u32[]{:S(2)}) collective-permute-start(f32[5,32,16,128]{3,1,2,0:T(8,128)S(1)} %broadcast_select_fusion), channel_id=1, source_target_pairs={{0,2},{1,3},{2,4},{3,5},{4,6},{5,7},{6,8},{7,9},{8,10},{9,11},{10,... | collective-permute-start | bytes 3932168 | tf_op jit(solution)/shard_map/ppermute | solution.py:26
  111.8 62.3 %collective-permute-start.10 = (f32[5,32,16,128]{3,1,2,0:T(8,128)S(1)}, f32[5,32,16,128]{3,1,2,0:T(8,128)S(1)}, u32[]{:S(2)}, u32[]{:S(2)}) collective-permute-start(f32[5,32,16,128]{3,1,2,0:T(8,128)S(1)} %broadcast_select_fusion.1), channel_id=1, source_target_pairs={{0,4},{1,5},{2,6},{3,7},{4,8},{5,9},{6,10},{7,11},{8,12},{9,13},{1... | collective-permute-start | bytes 3932168 | tf_op jit(solution)/shard_map/ppermute | solution.py:26
  174.4 62.8 %collective-permute-start.11 = (f32[5,32,16,128]{3,1,2,0:T(8,128)S(1)}, f32[5,32,16,128]{3,1,2,0:T(8,128)S(1)}, u32[]{:S(2)}, u32[]{:S(2)}) collective-permute-start(f32[5,32,16,128]{3,1,2,0:T(8,128)S(1)} %broadcast_select_fusion.2), channel_id=1, source_target_pairs={{0,8},{1,9},{2,10},{3,11},{4,12},{5,13},{6,14},{7,15},{8,0},{9,1},... | collective-permute-start | bytes 3932168 | tf_op jit(solution)/shard_map/ppermute | solution.py:26
  237.5 30.6 %collective-permute-start.12 = (f32[5,32,16,128]{3,1,2,0:T(8,128)S(1)}, f32[5,32,16,128]{3,1,2,0:T(8,128)S(1)}, u32[]{:S(2)}, u32[]{:S(2)}) collective-permute-start(f32[5,32,16,128]{3,1,2,0:T(8,128)S(1)} %broadcast_select_fusion.3), channel_id=1, source_target_pairs={{0,1},{1,2},{2,3},{3,4},{4,5},{5,6},{6,7},{7,8},{8,9},{9,10},{10,1... | collective-permute-start | bytes 3932168 | tf_op jit(solution)/shard_map/ppermute | solution.py:26
  272.3 7.0 %collective-permute-start.13 = (f32[5,32,2,128]{3,1,2,0:T(8,128)S(1)}, f32[5,32,2,128]{3,1,2,0:T(8,128)S(1)}, u32[]{:S(2)}, u32[]{:S(2)}) collective-permute-start(f32[5,32,2,128]{3,1,2,0:T(8,128)S(1)} %get-tuple-element.9), channel_id=1, source_target_pairs={{0,1},{1,2},{2,3},{3,4},{4,5},{5,6},{6,7},{7,8},{8,9},{9,10},{10,1... | collective-permute-start | bytes 491528 | tf_op jit(solution)/shard_map/ppermute | solution.py:15
  272.3 8.8 %collective-permute-start.14 = (f32[5,32,2,128]{3,1,2,0:T(8,128)S(1)}, f32[5,32,2,128]{3,1,2,0:T(8,128)S(1)}, u32[]{:S(2)}, u32[]{:S(2)}) collective-permute-start(f32[5,32,2,128]{3,1,2,0:T(8,128)S(1)} %get-tuple-element.10), channel_id=1, source_target_pairs={{1,0},{2,1},{3,2},{4,3},{5,4},{6,5},{7,6},{8,7},{9,8},{10,9},{11,1... | collective-permute-start | bytes 491528 | tf_op jit(solution)/shard_map/ppermute | solution.py:17
  281.3 62.3 %collective-permute-start.15 = (f32[5,2,20,128]{3,1,2,0:T(2,128)S(1)}, f32[5,2,20,128]{3,1,2,0:T(2,128)S(1)}, u32[]{:S(2)}, u32[]{:S(2)}) collective-permute-start(f32[5,2,20,128]{3,1,2,0:T(2,128)S(1)} %get-tuple-element.17), channel_id=1, source_target_pairs={{0,16},{16,32},{32,48},{48,64},{64,80},{80,96},{96,112},{112,128},... | collective-permute-start | bytes 307208 | tf_op jit(solution)/shard_map/ppermute | solution.py:15
  341.6 8.4 %collective-permute-start.16 = (f32[5,2,20,128]{3,1,2,0:T(2,128)S(1)}, f32[5,2,20,128]{3,1,2,0:T(2,128)S(1)}, u32[]{:S(2)}, u32[]{:S(2)}) collective-permute-start(f32[5,2,20,128]{3,1,2,0:T(2,128)S(1)} %get-tuple-element.18), channel_id=1, source_target_pairs={{16,0},{32,16},{48,32},{64,48},{80,64},{96,80},{112,96},{128,112},... | collective-permute-start | bytes 307208 | tf_op jit(solution)/shard_map/ppermute | solution.py:17
  352.8 5.8 %collective-permute-start.17 = (f32[5,32,2,128]{3,1,2,0:T(8,128)S(1)}, f32[5,32,2,128]{3,1,2,0:T(8,128)S(1)}, u32[]{:S(2)}, u32[]{:S(2)}) collective-permute-start(f32[5,32,2,128]{3,1,2,0:T(8,128)S(1)} %get-tuple-element.25), channel_id=1, source_target_pairs={{0,1},{1,2},{2,3},{3,4},{4,5},{5,6},{6,7},{7,8},{8,9},{9,10},{10,1... | collective-permute-start | bytes 491528 | tf_op jit(solution)/shard_map/ppermute | solution.py:15
  354.6 5.1 %collective-permute-start.18 = (f32[5,32,2,128]{3,1,2,0:T(8,128)S(1)}, f32[5,32,2,128]{3,1,2,0:T(8,128)S(1)}, u32[]{:S(2)}, u32[]{:S(2)}) collective-permute-start(f32[5,32,2,128]{3,1,2,0:T(8,128)S(1)} %get-tuple-element.26), channel_id=1, source_target_pairs={{1,0},{2,1},{3,2},{4,3},{5,4},{6,5},{7,6},{8,7},{9,8},{10,9},{11,1... | collective-permute-start | bytes 491528 | tf_op jit(solution)/shard_map/ppermute | solution.py:17
  359.8 6.7 %collective-permute-start.19 = (f32[5,2,20,128]{3,1,2,0:T(2,128)S(1)}, f32[5,2,20,128]{3,1,2,0:T(2,128)S(1)}, u32[]{:S(2)}, u32[]{:S(2)}) collective-permute-start(f32[5,2,20,128]{3,1,2,0:T(2,128)S(1)} %get-tuple-element.13), channel_id=1, source_target_pairs={{0,16},{16,32},{32,48},{48,64},{64,80},{80,96},{96,112},{112,128},... | collective-permute-start | bytes 307208 | tf_op jit(solution)/shard_map/ppermute | solution.py:15
  364.5 8.4 %collective-permute-start.20 = (f32[5,2,20,128]{3,1,2,0:T(2,128)S(1)}, f32[5,2,20,128]{3,1,2,0:T(2,128)S(1)}, u32[]{:S(2)}, u32[]{:S(2)}) collective-permute-start(f32[5,2,20,128]{3,1,2,0:T(2,128)S(1)} %get-tuple-element.14), channel_id=1, source_target_pairs={{16,0},{32,16},{48,32},{64,48},{80,64},{96,80},{112,96},{128,112},... | collective-permute-start | bytes 307208 | tf_op jit(solution)/shard_map/ppermute | solution.py:17
where the time goes:
time: 378 us
  waiting for transfers between devices  257 us (68%)
  starting transfers between devices  98.2 us (26%)
  other arithmetic  16.5 us (4%)
  local copies, waits for them, and re-layouts  5.4 us (1%)
    ppermute x5, waiting for transfers between devices, from_behind(): lax.ppermute(array, axis, [(i, (i + by) % peers) for i in range(peers)])  206 us
    ppermute x8, starting transfers between devices, with_halo(): lax.ppermute(tail, axis, [(i, (i + 1) % count) for i in range(ends)])  76.5 us
    ppermute x8, waiting for transfers between devices, with_halo(): lax.ppermute(head, axis, [((i + 1) % count, i) for i in range(ends)])  34.6 us
    ppermute x8, waiting for transfers between devices, with_halo(): lax.ppermute(tail, axis, [(i, (i + 1) % count) for i in range(ends)])  16.5 us
    ppermute x8, starting transfers between devices, with_halo(): lax.ppermute(head, axis, [((i + 1) % count, i) for i in range(ends)])  12.8 us
    ppermute x5, starting transfers between devices, from_behind(): lax.ppermute(array, axis, [(i, (i + by) % peers) for i in range(peers)])  8.87 us
  transfers between devices with their start and end apart: 21, of which 17 were waited for; matrix products, arithmetic and copies ran while one was open for 0% of the time, Pallas kernels for 0%

commit v1 on v0

--- a/solution.py
+++ b/solution.py
@@ -19,11 +19,6 @@
             axis=dim,
         )
     return cells
-
-
-def from_behind(array, axis, by):
-    peers = lax.axis_size(axis)
-    return lax.ppermute(array, axis, [(i, (i + by) % peers) for i in range(peers)])
 
 
 def stencil(padded, kap, speed_r, speed_p):
@@ -66,30 +61,21 @@
     return 0.5 * (field + first + stencil(extend(first, 2), kappa, speed_r, speed_p))
 
 
-def rotate_rows(joined, offset, length):
-    current = joined
-    for level in range((length - 1).bit_length()):
-        step_size = 1 << level
-        pushed = jnp.concatenate(
-            [jnp.zeros_like(current[:, :, :step_size]), current[:, :, :-step_size]], axis=2
-        )
-        chosen = offset // step_size % 2 == 1
-        current = jnp.where(chosen[None, :, None, None], pushed, current)
-    return current[:, :, length : 2 * length]
-
-
 def shift_rows(half, shifts):
-    fcount, rows, sector, height = half.shape
-    whole = shifts // sector
-    remain = shifts % sector
-    moved = half
-    for level in range((lax.axis_size("azi") - 1).bit_length()):
-        other = from_behind(moved, "azi", 1 << level)
-        taken = whole // (1 << level) % 2 == 1
-        moved = jnp.where(taken[None, :, None, None], other, moved)
-    before = from_behind(moved, "azi", 1)
-    joined = jnp.concatenate([before, moved], axis=2)
-    return rotate_rows(joined, remain, sector)
+    peers = lax.axis_size("azi")
+    rows = half.shape[1]
+    per = rows // peers
+    full = lax.all_to_all(half, "azi", 1, 2, tiled=True)
+    length = full.shape[2]
+    first = lax.axis_index("azi") * per
+    mine = lax.dynamic_slice_in_dim(shifts, first, per)
+    doubled = jnp.concatenate([full, full], axis=2)
+    rolled = []
+    for row in range(per):
+        start = (length - mine[row] % length) % length
+        rolled.append(lax.dynamic_slice_in_dim(doubled[:, row], start, length, axis=1))
+    moved = jnp.stack(rolled, axis=1)
+    return lax.all_to_all(moved, "azi", 2, 1, tiled=True)
 
 
 def shards(fields, kappa, radial_speed, azimuth_speed, shifts):

time: 378 us -> 188 us (0.50)
  the two profiles are of different devices: /device:TPU:53 before, /device:TPU:1 now
where the time goes in v1:
time: 188 us; the launch traced here: 185 us
  waiting for transfers between devices  58.8 us (31%)
  starting transfers between devices  58.4 us (31%)
  blocking collectives  37.5 us (20%)
  other arithmetic  19.4 us (10%)
  local copies, waits for them, and re-layouts  6.69 us (4%)
  between operations  3.89 us (2%)
    all_to_all x1, blocking collectives, shift_rows(): return lax.all_to_all(moved, 'azi', 2, 1, tiled=True)  37.5 us
    all_to_all x1, waiting for transfers between devices, shift_rows(): full = lax.all_to_all(half, 'azi', 1, 2, tiled=True)  25.7 us
    ppermute x8, starting transfers between devices, with_halo(): lax.ppermute(head, axis, [((i + 1) % count, i) for i in range(ends)])  24.8 us
    ppermute x8, starting transfers between devices, with_halo(): lax.ppermute(tail, axis, [(i, (i + 1) % count) for i in range(ends)])  24.3 us
    ppermute x8, waiting for transfers between devices, with_halo(): lax.ppermute(head, axis, [((i + 1) % count, i) for i in range(ends)])  24.2 us
    all_to_all x1, starting transfers between devices, shift_rows(): full = lax.all_to_all(half, 'azi', 1, 2, tiled=True)  9.32 us
    ppermute x8, waiting for transfers between devices, with_halo(): lax.ppermute(tail, axis, [(i, (i + 1) % count) for i in range(ends)])  8.88 us
    mul x2, other arithmetic, heun_sections(): 0.5 * (field + first + stencil(extend(first, 2), kappa, speed_r, speed_p))  8.39 us
  transfers between devices with their start and end apart: 17, of which 10 were waited for; matrix products, arithmetic and copies ran while one was open for 2% of the time, Pallas kernels for 0%

profile of v1, /device:TPU:1, one launch (start us, length us, event | category | flops | bytes accessed | tf_op | source)
XLA Modules:
  0.0 184.7 jit_solution(8919407360870830838)
XLA Ops:
  0.0 1.4 fusion.61
  1.4 2.2 %collective-permute-start = (f32[5,32,2,128]{3,2,1,0:T(2,128)S(1)}, f32[5,32,2,128]{3,2,1,0:T(2,128)S(1)}, u32[]{:S(2)}, u32[]{:S(2)}) collective-permute-start(f32[5,32,2,128]{3,2,1,0:T(2,128)S(1)} %get-tuple-element.29), channel_id=1, source_target_pairs={{0,1},{1,2},{2,3},{3,4},{4,5},{5,6},{6,7},{7,8},{8,9},{9,10},{10,1... | collective-permute-start | bytes 491528 | tf_op jit(solution)/shard_map/ppermute | solution.py:15
  3.6 5.4 %collective-permute-start.1 = (f32[5,32,2,128]{3,2,1,0:T(2,128)S(1)}, f32[5,32,2,128]{3,2,1,0:T(2,128)S(1)}, u32[]{:S(2)}, u32[]{:S(2)}) collective-permute-start(f32[5,32,2,128]{3,2,1,0:T(2,128)S(1)} %get-tuple-element.30), channel_id=1, source_target_pairs={{1,0},{2,1},{3,2},{4,3},{5,4},{6,5},{7,6},{8,7},{9,8},{10,9},{11,1... | collective-permute-start | bytes 491528 | tf_op jit(solution)/shard_map/ppermute | solution.py:17
  9.0 1.0 broadcast_multiply_fusion
  10.7 1.5 constant_dynamic-update-slice_fusion.1
  12.9 5.7 %collective-permute-start.2 = (f32[5,2,20,128]{3,2,1,0:T(8,128)S(1)}, f32[5,2,20,128]{3,2,1,0:T(8,128)S(1)}, u32[]{:S(2)}, u32[]{:S(2)}) collective-permute-start(f32[5,2,20,128]{3,2,1,0:T(8,128)S(1)} %get-tuple-element.19), channel_id=1, source_target_pairs={{0,16},{16,32},{32,48},{48,64},{64,80},{80,96},{96,112},{112,128},... | collective-permute-start | bytes 307208 | tf_op jit(solution)/shard_map/ppermute | solution.py:15
  18.6 1.9 %collective-permute-start.3 = (f32[5,2,20,128]{3,2,1,0:T(8,128)S(1)}, f32[5,2,20,128]{3,2,1,0:T(8,128)S(1)}, u32[]{:S(2)}, u32[]{:S(2)}) collective-permute-start(f32[5,2,20,128]{3,2,1,0:T(8,128)S(1)} %get-tuple-element.20), channel_id=1, source_target_pairs={{16,0},{32,16},{48,32},{64,48},{80,64},{96,80},{112,96},{128,112},... | collective-permute-start | bytes 307208 | tf_op jit(solution)/shard_map/ppermute | solution.py:17
  20.6 5.7 %collective-permute-done.3 = f32[5,2,20,128]{3,2,1,0:T(8,128)S(1)} collective-permute-done((f32[5,2,20,128]{3,2,1,0:T(8,128)S(1)}, f32[5,2,20,128]{3,2,1,0:T(8,128)S(1)}, u32[]{:S(2)}, u32[]{:S(2)}) %collective-permute-start.3) | collective-permute-done | bytes 102432 | tf_op jit(solution)/shard_map/ppermute | solution.py:17
  26.6 3.6 %fusion.15 = f32[5,32,16,128]{3,2,1,0:T(8,128)S(1)} fusion(f32[5,32,16,128]{3,2,1,0:T(8,128)S(1)} %copy-done, f32[5,32,18,128]{3,2,1,0:T(8,128)S(1)} %constant_dynamic-update-slice_fusion, f32[5,32,2,128]{3,2,1,0:T(2,128)S(1)} %collective-permute-done, f32[5,34,20,128]{3,2,1,0:T(8,128)S(1)} %get-tuple-element.18, ...), kind=kLoop, calls=%fused_computation.55 | loop fusion | flops 13762560 | bytes 10913024 | tf_op jit(solution)/shard_map/add | solution.py:60
  30.5 4.4 %collective-permute-start.5 = (f32[5,32,2,128]{3,2,1,0:T(2,128)S(1)}, f32[5,32,2,128]{3,2,1,0:T(2,128)S(1)}, u32[]{:S(2)}, u32[]{:S(2)}) collective-permute-start(f32[5,32,2,128]{3,2,1,0:T(2,128)S(1)} %get-tuple-element.28), channel_id=1, source_target_pairs={{1,0},{2,1},{3,2},{4,3},{5,4},{6,5},{7,6},{8,7},{9,8},{10,9},{11,1... | collective-permute-start | bytes 491528 | tf_op jit(solution)/shard_map/ppermute | solution.py:17
  34.9 2.6 %collective-permute-done.4 = f32[5,32,2,128]{3,2,1,0:T(2,128)S(1)} collective-permute-done((f32[5,32,2,128]{3,2,1,0:T(2,128)S(1)}, f32[5,32,2,128]{3,2,1,0:T(2,128)S(1)}, u32[]{:S(2)}, u32[]{:S(2)}) %collective-permute-start.4) | collective-permute-done | bytes 163872 | tf_op jit(solution)/shard_map/ppermute | solution.py:15
  37.6 3.4 %collective-permute-start.6 = (f32[5,2,20,128]{3,2,1,0:T(8,128)S(1)}, f32[5,2,20,128]{3,2,1,0:T(8,128)S(1)}, u32[]{:S(2)}, u32[]{:S(2)}) collective-permute-start(f32[5,2,20,128]{3,2,1,0:T(8,128)S(1)} %get-tuple-element.15), channel_id=1, source_target_pairs={{0,16},{16,32},{32,48},{48,64},{64,80},{80,96},{96,112},{112,128},... | collective-permute-start | bytes 307208 | tf_op jit(solution)/shard_map/ppermute | solution.py:15
  41.0 1.9 %collective-permute-start.7 = (f32[5,2,20,128]{3,2,1,0:T(8,128)S(1)}, f32[5,2,20,128]{3,2,1,0:T(8,128)S(1)}, u32[]{:S(2)}, u32[]{:S(2)}) collective-permute-start(f32[5,2,20,128]{3,2,1,0:T(8,128)S(1)} %get-tuple-element.16), channel_id=1, source_target_pairs={{16,0},{32,16},{48,32},{64,48},{80,64},{96,80},{112,96},{128,112},... | collective-permute-start | bytes 307208 | tf_op jit(solution)/shard_map/ppermute | solution.py:17
  42.9 5.8 %collective-permute-done.7 = f32[5,2,20,128]{3,2,1,0:T(8,128)S(1)} collective-permute-done((f32[5,2,20,128]{3,2,1,0:T(8,128)S(1)}, f32[5,2,20,128]{3,2,1,0:T(8,128)S(1)}, u32[]{:S(2)}, u32[]{:S(2)}) %collective-permute-start.7) | collective-permute-done | bytes 102432 | tf_op jit(solution)/shard_map/ppermute | solution.py:17
  49.0 3.8 %fusion.27 = f32[5,32,16,128]{3,2,1,0:T(8,128)S(1)} fusion(f32[5,32,16,128]{3,2,1,0:T(8,128)S(1)} %fusion.15, f32[5,32,2,128]{3,2,1,0:T(2,128)S(1)} %collective-permute-done.5, f32[5,32,2,128]{3,2,1,0:T(2,128)S(1)} %collective-permute-done.4, f32[5,34,20,128]{3,2,1,0:T(8,128)S(1)} %get-tuple-element.14, f32[5,34,20,128]{3,2,1,0:T(8,128)S(1)} %get-tuple-element.13, ...), kind=kLoop, calls=%fused_computation.67 | loop fusion | flops 15073280 | bytes 9766144 | tf_op jit(solution)/shard_map/mul | solution.py:61
  52.9 1.1 copy.8
  54.0 9.3 %all-to-all-start = ((f32[5,32,16,128]{3,2,0,1:T(8,128)}), f32[5,32,16,128]{3,2,0,1:T(8,128)S(1)}, u32[]{:S(2)}, u32[]{:S(2)}) async-start(f32[5,32,16,128]{3,2,0,1:T(8,128)} %copy.8), calls=%async_computation | async-start | bytes 2621440 | tf_op jit(solution)/shard_map/all_to_all | solution.py:68
  67.6 25.7 %all-to-all-done = f32[5,32,16,128]{3,2,0,1:T(8,128)S(1)} async-done(((f32[5,32,16,128]{3,2,0,1:T(8,128)}), f32[5,32,16,128]{3,2,0,1:T(8,128)S(1)}, u32[]{:S(2)}, u32[]{:S(2)}) %all-to-all-start) | async-done | bytes 1310752 | tf_op jit(solution)/shard_map/all_to_all | solution.py:68
  94.0 1.0 copy.11
  95.0 37.5 %all_to_all.36 = f32[5,2,256,128]{3,1,0,2:T(2,128)S(1)} all-to-all(f32[5,2,256,128]{3,1,0,2:T(2,128)S(1)} %copy.11), channel_id=1, replica_groups=mesh['rad'=16,'azi'=16] {'azi'}, dimensions={2} | all-to-all | bytes 2621440 | tf_op jit(solution)/shard_map/all_to_all | solution.py:78
  133.0 3.6 %collective-permute-start.9 = (f32[5,32,2,128]{3,2,1,0:T(2,128)S(1)}, f32[5,32,2,128]{3,2,1,0:T(2,128)S(1)}, u32[]{:S(2)}, u32[]{:S(2)}) collective-permute-start(f32[5,32,2,128]{3,2,1,0:T(2,128)S(1)} %get-tuple-element.24), channel_id=1, source_target_pairs={{1,0},{2,1},{3,2},{4,3},{5,4},{6,5},{7,6},{8,7},{9,8},{10,9},{11,1... | collective-permute-start | bytes 491528 | tf_op jit(solution)/shard_map/ppermute | solution.py:17
  136.6 2.8 %collective-permute-done.8 = f32[5,32,2,128]{3,2,1,0:T(2,128)S(1)} collective-permute-done((f32[5,32,2,128]{3,2,1,0:T(2,128)S(1)}, f32[5,32,2,128]{3,2,1,0:T(2,128)S(1)}, u32[]{:S(2)}, u32[]{:S(2)}) %collective-permute-start.8) | collective-permute-done | bytes 163872 | tf_op jit(solution)/shard_map/ppermute | solution.py:15
  139.4 9.9 %collective-permute-start.10 = (f32[5,2,20,128]{3,2,1,0:T(8,128)S(1)}, f32[5,2,20,128]{3,2,1,0:T(8,128)S(1)}, u32[]{:S(2)}, u32[]{:S(2)}) collective-permute-start(f32[5,2,20,128]{3,2,1,0:T(8,128)S(1)} %get-tuple-element.11), channel_id=1, source_target_pairs={{0,16},{16,32},{32,48},{48,64},{64,80},{80,96},{96,112},{112,128},... | collective-permute-start | bytes 307208 | tf_op jit(solution)/shard_map/ppermute | solution.py:15
  149.3 2.1 %collective-permute-start.11 = (f32[5,2,20,128]{3,2,1,0:T(8,128)S(1)}, f32[5,2,20,128]{3,2,1,0:T(8,128)S(1)}, u32[]{:S(2)}, u32[]{:S(2)}) collective-permute-start(f32[5,2,20,128]{3,2,1,0:T(8,128)S(1)} %get-tuple-element.12), channel_id=1, source_target_pairs={{16,0},{32,16},{48,32},{64,48},{80,64},{96,80},{112,96},{128,112},... | collective-permute-start | bytes 307208 | tf_op jit(solution)/shard_map/ppermute | solution.py:17
  151.4 5.6 %collective-permute-done.11 = f32[5,2,20,128]{3,2,1,0:T(8,128)S(1)} collective-permute-done((f32[5,2,20,128]{3,2,1,0:T(8,128)S(1)}, f32[5,2,20,128]{3,2,1,0:T(8,128)S(1)}, u32[]{:S(2)}, u32[]{:S(2)}) %collective-permute-start.11) | collective-permute-done | bytes 102432 | tf_op jit(solution)/shard_map/ppermute | solution.py:17
  157.4 3.7 %fusion.38 = f32[5,32,16,128]{3,2,1,0:T(8,128)S(1)} fusion(f32[5,32,16,128]{3,2,1,0:T(8,128)S(1)} %bitcast.13, f32[5,32,2,128]{3,2,1,0:T(2,128)S(1)} %collective-permute-done.9, f32[5,32,2,128]{3,2,1,0:T(2,128)S(1)} %collective-permute-done.8, f32[5,34,20,128]{3,2,1,0:T(8,128)S(1)} %get-tuple-element.10, f32[5,34,20,128]{3,2,1,0:T(8,128)S(1)} %get-tuple-element.9, ...), kind=kLoop, calls=%fused_computation.78 | loop fusion | flops 14417920 | bytes 8455424 | tf_op jit(solution)/shard_map/add | solution.py:60
  161.3 3.6 %collective-permute-start.13 = (f32[5,32,2,128]{3,2,1,0:T(2,128)S(1)}, f32[5,32,2,128]{3,2,1,0:T(2,128)S(1)}, u32[]{:S(2)}, u32[]{:S(2)}) collective-permute-start(f32[5,32,2,128]{3,2,1,0:T(2,128)S(1)} %get-tuple-element.22), channel_id=1, source_target_pairs={{1,0},{2,1},{3,2},{4,3},{5,4},{6,5},{7,6},{8,7},{9,8},{10,9},{11,1... | collective-permute-start | bytes 491528 | tf_op jit(solution)/shard_map/ppermute | solution.py:17
  164.9 2.8 %collective-permute-done.12 = f32[5,32,2,128]{3,2,1,0:T(2,128)S(1)} collective-permute-done((f32[5,32,2,128]{3,2,1,0:T(2,128)S(1)}, f32[5,32,2,128]{3,2,1,0:T(2,128)S(1)}, u32[]{:S(2)}, u32[]{:S(2)}) %collective-permute-start.12) | collective-permute-done | bytes 163872 | tf_op jit(solution)/shard_map/ppermute | solution.py:15
  168.1 2.9 %collective-permute-start.14 = (f32[5,2,20,128]{3,2,1,0:T(8,128)S(1)}, f32[5,2,20,128]{3,2,1,0:T(8,128)S(1)}, u32[]{:S(2)}, u32[]{:S(2)}) collective-permute-start(f32[5,2,20,128]{3,2,1,0:T(8,128)S(1)} %get-tuple-element.7), channel_id=1, source_target_pairs={{0,16},{16,32},{32,48},{48,64},{64,80},{80,96},{96,112},{112,128},... | collective-permute-start | bytes 307208 | tf_op jit(solution)/shard_map/ppermute | solution.py:15
  171.0 1.9 %collective-permute-start.15 = (f32[5,2,20,128]{3,2,1,0:T(8,128)S(1)}, f32[5,2,20,128]{3,2,1,0:T(8,128)S(1)}, u32[]{:S(2)}, u32[]{:S(2)}) collective-permute-start(f32[5,2,20,128]{3,2,1,0:T(8,128)S(1)} %get-tuple-element.8), channel_id=1, source_target_pairs={{16,0},{32,16},{48,32},{64,48},{80,64},{96,80},{112,96},{128,112},... | collective-permute-start | bytes 307208 | tf_op jit(solution)/shard_map/ppermute | solution.py:17
  173.0 6.8 %collective-permute-done.15 = f32[5,2,20,128]{3,2,1,0:T(8,128)S(1)} collective-permute-done((f32[5,2,20,128]{3,2,1,0:T(8,128)S(1)}, f32[5,2,20,128]{3,2,1,0:T(8,128)S(1)}, u32[]{:S(2)}, u32[]{:S(2)}) %collective-permute-start.15) | collective-permute-done | bytes 102432 | tf_op jit(solution)/shard_map/ppermute | solution.py:17
  180.1 4.6 %fusion.50 = f32[5,32,16,128]{3,2,1,0:T(8,128)} fusion(f32[5,32,16,128]{3,2,1,0:T(8,128)S(1)} %fusion.38, f32[5,32,2,128]{3,2,1,0:T(2,128)S(1)} %collective-permute-done.13, f32[5,32,2,128]{3,2,1,0:T(2,128)S(1)} %collective-permute-done.12, f32[5,34,20,128]{3,2,1,0:T(8,128)S(1)} %get-tuple-element.6, f32[5,34,20,128]{3,2,1,0:T(8,128)S(1)} %get-tuple-element.5, ...), kind=kLoop, calls=%fused_computation.90 | loop fusion | flops 15073280 | bytes 9766144 | tf_op jit(solution)/shard_map/mul | solution.py:61
  (38 shorter events, 5.6 us)
Async XLA Ops:
  1.4 11.4 %collective-permute-start = (f32[5,32,2,128]{3,2,1,0:T(2,128)S(1)}, f32[5,32,2,128]{3,2,1,0:T(2,128)S(1)}, u32[]{:S(2)}, u32[]{:S(2)}) collective-permute-start(f32[5,32,2,128]{3,2,1,0:T(2,128)S(1)} %get-tuple-element.29), channel_id=1, source_target_pairs={{0,1},{1,2},{2,3},{3,4},{4,5},{5,6},{6,7},{7,8},{8,9},{9,10},{10,1... | collective-permute-start | bytes 491528 | tf_op jit(solution)/shard_map/ppermute | solution.py:15
  3.6 9.2 %collective-permute-start.1 = (f32[5,32,2,128]{3,2,1,0:T(2,128)S(1)}, f32[5,32,2,128]{3,2,1,0:T(2,128)S(1)}, u32[]{:S(2)}, u32[]{:S(2)}) collective-permute-start(f32[5,32,2,128]{3,2,1,0:T(2,128)S(1)} %get-tuple-element.30), channel_id=1, source_target_pairs={{1,0},{2,1},{3,2},{4,3},{5,4},{6,5},{7,6},{8,7},{9,8},{10,9},{11,1... | collective-permute-start | bytes 491528 | tf_op jit(solution)/shard_map/ppermute | solution.py:17
  10.7 2.2 %copy-start = (f32[5,32,16,128]{3,2,1,0:T(8,128)S(1)}, f32[5,32,16,128]{3,2,1,0:T(8,128)}, u32[]{:S(2)}) copy-start(f32[5,32,16,128]{3,2,1,0:T(8,128)} %param.5) | copy-start | bytes 3932164
  12.9 7.7 %collective-permute-start.2 = (f32[5,2,20,128]{3,2,1,0:T(8,128)S(1)}, f32[5,2,20,128]{3,2,1,0:T(8,128)S(1)}, u32[]{:S(2)}, u32[]{:S(2)}) collective-permute-start(f32[5,2,20,128]{3,2,1,0:T(8,128)S(1)} %get-tuple-element.19), channel_id=1, source_target_pairs={{0,16},{16,32},{32,48},{48,64},{64,80},{80,96},{96,112},{112,128},... | collective-permute-start | bytes 307208 | tf_op jit(solution)/shard_map/ppermute | solution.py:15
  18.6 7.7 %collective-permute-start.3 = (f32[5,2,20,128]{3,2,1,0:T(8,128)S(1)}, f32[5,2,20,128]{3,2,1,0:T(8,128)S(1)}, u32[]{:S(2)}, u32[]{:S(2)}) collective-permute-start(f32[5,2,20,128]{3,2,1,0:T(8,128)S(1)} %get-tuple-element.20), channel_id=1, source_target_pairs={{16,0},{32,16},{48,32},{64,48},{80,64},{96,80},{112,96},{128,112},... | collective-permute-start | bytes 307208 | tf_op jit(solution)/shard_map/ppermute | solution.py:17
  30.4 7.1 %collective-permute-start.4 = (f32[5,32,2,128]{3,2,1,0:T(2,128)S(1)}, f32[5,32,2,128]{3,2,1,0:T(2,128)S(1)}, u32[]{:S(2)}, u32[]{:S(2)}) collective-permute-start(f32[5,32,2,128]{3,2,1,0:T(2,128)S(1)} %get-tuple-element.27), channel_id=1, source_target_pairs={{0,1},{1,2},{2,3},{3,4},{4,5},{5,6},{6,7},{7,8},{8,9},{9,10},{10,1... | collective-permute-start | bytes 491528 | tf_op jit(solution)/shard_map/ppermute | solution.py:15
  30.5 7.0 %collective-permute-start.5 = (f32[5,32,2,128]{3,2,1,0:T(2,128)S(1)}, f32[5,32,2,128]{3,2,1,0:T(2,128)S(1)}, u32[]{:S(2)}, u32[]{:S(2)}) collective-permute-start(f32[5,32,2,128]{3,2,1,0:T(2,128)S(1)} %get-tuple-element.28), channel_id=1, source_target_pairs={{1,0},{2,1},{3,2},{4,3},{5,4},{6,5},{7,6},{8,7},{9,8},{10,9},{11,1... | collective-permute-start | bytes 491528 | tf_op jit(solution)/shard_map/ppermute | solution.py:17
  37.6 5.3 %collective-permute-start.6 = (f32[5,2,20,128]{3,2,1,0:T(8,128)S(1)}, f32[5,2,20,128]{3,2,1,0:T(8,128)S(1)}, u32[]{:S(2)}, u32[]{:S(2)}) collective-permute-start(f32[5,2,20,128]{3,2,1,0:T(8,128)S(1)} %get-tuple-element.15), channel_id=1, source_target_pairs={{0,16},{16,32},{32,48},{48,64},{64,80},{80,96},{96,112},{112,128},... | collective-permute-start | bytes 307208 | tf_op jit(solution)/shard_map/ppermute | solution.py:15
  41.0 7.7 %collective-permute-start.7 = (f32[5,2,20,128]{3,2,1,0:T(8,128)S(1)}, f32[5,2,20,128]{3,2,1,0:T(8,128)S(1)}, u32[]{:S(2)}, u32[]{:S(2)}) collective-permute-start(f32[5,2,20,128]{3,2,1,0:T(8,128)S(1)} %get-tuple-element.16), channel_id=1, source_target_pairs={{16,0},{32,16},{48,32},{64,48},{80,64},{96,80},{112,96},{128,112},... | collective-permute-start | bytes 307208 | tf_op jit(solution)/shard_map/ppermute | solution.py:17
  54.0 9.3 %copy-start.1 = (s32[32]{0:T(128)S(1)}, s32[32]{0:T(128)}, u32[]{:S(2)}) copy-start(s32[32]{0:T(128)} %param.9) | copy-start | bytes 388
  54.0 39.3 %all-to-all-start = ((f32[5,32,16,128]{3,2,0,1:T(8,128)}), f32[5,32,16,128]{3,2,0,1:T(8,128)S(1)}, u32[]{:S(2)}, u32[]{:S(2)}) async-start(f32[5,32,16,128]{3,2,0,1:T(8,128)} %copy.8), calls=%async_computation | async-start | bytes 2621440 | tf_op jit(solution)/shard_map/all_to_all | solution.py:68
  132.9 6.5 %collective-permute-start.8 = (f32[5,32,2,128]{3,2,1,0:T(2,128)S(1)}, f32[5,32,2,128]{3,2,1,0:T(2,128)S(1)}, u32[]{:S(2)}, u32[]{:S(2)}) collective-permute-start(f32[5,32,2,128]{3,2,1,0:T(2,128)S(1)} %get-tuple-element.23), channel_id=1, source_target_pairs={{0,1},{1,2},{2,3},{3,4},{4,5},{5,6},{6,7},{7,8},{8,9},{9,10},{10,1... | collective-permute-start | bytes 491528 | tf_op jit(solution)/shard_map/ppermute | solution.py:15
  133.0 6.4 %collective-permute-start.9 = (f32[5,32,2,128]{3,2,1,0:T(2,128)S(1)}, f32[5,32,2,128]{3,2,1,0:T(2,128)S(1)}, u32[]{:S(2)}, u32[]{:S(2)}) collective-permute-start(f32[5,32,2,128]{3,2,1,0:T(2,128)S(1)} %get-tuple-element.24), channel_id=1, source_target_pairs={{1,0},{2,1},{3,2},{4,3},{5,4},{6,5},{7,6},{8,7},{9,8},{10,9},{11,1... | collective-permute-start | bytes 491528 | tf_op jit(solution)/shard_map/ppermute | solution.py:17
  139.4 12.0 %collective-permute-start.10 = (f32[5,2,20,128]{3,2,1,0:T(8,128)S(1)}, f32[5,2,20,128]{3,2,1,0:T(8,128)S(1)}, u32[]{:S(2)}, u32[]{:S(2)}) collective-permute-start(f32[5,2,20,128]{3,2,1,0:T(8,128)S(1)} %get-tuple-element.11), channel_id=1, source_target_pairs={{0,16},{16,32},{32,48},{48,64},{64,80},{80,96},{96,112},{112,128},... | collective-permute-start | bytes 307208 | tf_op jit(solution)/shard_map/ppermute | solution.py:15
  149.3 7.7 %collective-permute-start.11 = (f32[5,2,20,128]{3,2,1,0:T(8,128)S(1)}, f32[5,2,20,128]{3,2,1,0:T(8,128)S(1)}, u32[]{:S(2)}, u32[]{:S(2)}) collective-permute-start(f32[5,2,20,128]{3,2,1,0:T(8,128)S(1)} %get-tuple-element.12), channel_id=1, source_target_pairs={{16,0},{32,16},{48,32},{64,48},{80,64},{96,80},{112,96},{128,112},... | collective-permute-start | bytes 307208 | tf_op jit(solution)/shard_map/ppermute | solution.py:17
  161.2 6.5 %collective-permute-start.12 = (f32[5,32,2,128]{3,2,1,0:T(2,128)S(1)}, f32[5,32,2,128]{3,2,1,0:T(2,128)S(1)}, u32[]{:S(2)}, u32[]{:S(2)}) collective-permute-start(f32[5,32,2,128]{3,2,1,0:T(2,128)S(1)} %get-tuple-element.21), channel_id=1, source_target_pairs={{0,1},{1,2},{2,3},{3,4},{4,5},{5,6},{6,7},{7,8},{8,9},{9,10},{10,1... | collective-permute-start | bytes 491528 | tf_op jit(solution)/shard_map/ppermute | solution.py:15
  161.3 6.7 %collective-permute-start.13 = (f32[5,32,2,128]{3,2,1,0:T(2,128)S(1)}, f32[5,32,2,128]{3,2,1,0:T(2,128)S(1)}, u32[]{:S(2)}, u32[]{:S(2)}) collective-permute-start(f32[5,32,2,128]{3,2,1,0:T(2,128)S(1)} %get-tuple-element.22), channel_id=1, source_target_pairs={{1,0},{2,1},{3,2},{4,3},{5,4},{6,5},{7,6},{8,7},{9,8},{10,9},{11,1... | collective-permute-start | bytes 491528 | tf_op jit(solution)/shard_map/ppermute | solution.py:17
  168.1 4.9 %collective-permute-start.14 = (f32[5,2,20,128]{3,2,1,0:T(8,128)S(1)}, f32[5,2,20,128]{3,2,1,0:T(8,128)S(1)}, u32[]{:S(2)}, u32[]{:S(2)}) collective-permute-start(f32[5,2,20,128]{3,2,1,0:T(8,128)S(1)} %get-tuple-element.7), channel_id=1, source_target_pairs={{0,16},{16,32},{32,48},{48,64},{64,80},{80,96},{96,112},{112,128},... | collective-permute-start | bytes 307208 | tf_op jit(solution)/shard_map/ppermute | solution.py:15
  171.0 8.7 %collective-permute-start.15 = (f32[5,2,20,128]{3,2,1,0:T(8,128)S(1)}, f32[5,2,20,128]{3,2,1,0:T(8,128)S(1)}, u32[]{:S(2)}, u32[]{:S(2)}) collective-permute-start(f32[5,2,20,128]{3,2,1,0:T(8,128)S(1)} %get-tuple-element.8), channel_id=1, source_target_pairs={{16,0},{32,16},{48,32},{64,48},{80,64},{96,80},{112,96},{128,112},... | collective-permute-start | bytes 307208 | tf_op jit(solution)/shard_map/ppermute | solution.py:17

commit v2 on v1

--- a/solution.py
+++ b/solution.py
@@ -2,23 +2,6 @@
 import jax.numpy as jnp
 from jax import lax
 from jax.sharding import PartitionSpec as P
-
-
-def with_halo(cells, sides, width, closed):
-    for axis, dim in sides:
-        count = lax.axis_size(axis)
-        ends = count if closed else count - 1
-        head = lax.slice_in_dim(cells, 0, width, axis=dim)
-        tail = lax.slice_in_dim(cells, cells.shape[dim] - width, cells.shape[dim], axis=dim)
-        cells = jnp.concatenate(
-            [
-                lax.ppermute(tail, axis, [(i, (i + 1) % count) for i in range(ends)]),
-                cells,
-                lax.ppermute(head, axis, [((i + 1) % count, i) for i in range(ends)]),
-            ],
-            axis=dim,
-        )
-    return cells
 
 
 def stencil(padded, kap, speed_r, speed_p):
@@ -51,14 +34,43 @@
     )
 
 
-def extend(field, width):
-    beside_all = with_halo(field, (("azi", 2),), width, True)
-    return with_halo(beside_all, (("rad", 1),), width, False)
+def extend(cells, width):
+    rings, sectors = lax.axis_size("rad"), lax.axis_size("azi")
+    rows, cols = cells.shape[-3], cells.shape[-2]
+    spans = {-1: (rows - width, rows), 0: (0, rows), 1: (0, width)}
+    cuts = {-1: (cols - width, cols), 0: (0, cols), 1: (0, width)}
+
+    def piece(di, dj):
+        block = cells[..., slice(*spans[di]), slice(*cuts[dj]), :]
+        pairs = [
+            (a * sectors + b, (a - di) * sectors + (b - dj) % sectors)
+            for a in range(rings)
+            for b in range(sectors)
+            if 0 <= a - di < rings
+        ]
+        return lax.ppermute(block, ("rad", "azi"), pairs)
+
+    bands = []
+    for di in (-1, 0, 1):
+        parts = [cells if di == dj == 0 else piece(di, dj) for dj in (-1, 0, 1)]
+        bands.append(jnp.concatenate(parts, axis=-2))
+    return jnp.concatenate(bands, axis=-3)
 
 
-def heun_sections(field, kappa, speed_r, speed_p):
-    first = field + stencil(extend(field, 2), kappa, speed_r, speed_p)
-    return 0.5 * (field + first + stencil(extend(first, 2), kappa, speed_r, speed_p))
+def radial_halo(values, width):
+    rings = lax.axis_size("rad")
+    rows = values.shape[-1]
+    above = lax.ppermute(values[..., rows - width :], "rad", [(i, i + 1) for i in range(rings - 1)])
+    below = lax.ppermute(values[..., :width], "rad", [(i + 1, i) for i in range(rings - 1)])
+    return jnp.concatenate([above, values, below], axis=-1)
+
+
+def heun_sections(field, ext, kap_ext, speed_r, speed_p, inside):
+    first = ext[:, 2:-2, 2:-2] + stencil(ext, kap_ext, speed_r, speed_p)
+    first = jnp.where(inside[None, :, None, None], first, 0.0)
+    kap = kap_ext[2:-2, 2:-2]
+    inner = stencil(first, kap, speed_r[:, 2:-2], speed_p[:, 2:-2])
+    return 0.5 * (field + first[:, 2:-2, 2:-2] + inner)
 
 
 def shift_rows(half, shifts):
@@ -79,9 +91,17 @@
 
 
 def shards(fields, kappa, radial_speed, azimuth_speed, shifts):
-    half = heun_sections(fields, kappa, radial_speed, azimuth_speed)
+    fcount, rows = fields.shape[0], fields.shape[1]
+    joined = extend(jnp.concatenate([fields, kappa[None]], axis=0), 4)
+    ext, kap_ext = joined[:fcount], joined[fcount, 2:-2, 2:-2]
+    speeds = radial_halo(jnp.stack([radial_speed, azimuth_speed]), 2)
+    speed_r, speed_p = speeds[0], speeds[1]
+    start = lax.axis_index("rad") * rows - 2
+    places = start + jnp.arange(rows + 4)
+    inside = (places >= 0) & (places < lax.axis_size("rad") * rows)
+    half = heun_sections(fields, ext, kap_ext, speed_r, speed_p, inside)
     moved = shift_rows(half, shifts)
-    return heun_sections(moved, kappa, radial_speed, azimuth_speed)
+    return heun_sections(moved, extend(moved, 4), kap_ext, speed_r, speed_p, inside)
 
 
 def solution(mesh):

time: 188 us -> 194 us (1.032)
  the two profiles are of different devices: /device:TPU:1 before, /device:TPU:2 now
where the time goes in v2:
time: 194 us
  starting transfers between devices  63.8 us (33%)
  waiting for transfers between devices  50.6 us (26%)
  blocking collectives  41.3 us (21%)
  other arithmetic  28.9 us (15%)
  between operations  4.58 us (2%)
  local copies, waits for them, and re-layouts  4.35 us (2%)
    ppermute x16, starting transfers between devices, piece(): return lax.ppermute(block, ('rad', 'azi'), pairs)  47.6 us
    all_to_all x1, blocking collectives, shift_rows(): return lax.all_to_all(moved, 'azi', 2, 1, tiled=True)  41.3 us
    all_to_all x1, waiting for transfers between devices, shift_rows(): full = lax.all_to_all(half, 'azi', 1, 2, tiled=True)  26.9 us
    ppermute x16, waiting for transfers between devices, piece(): return lax.ppermute(block, ('rad', 'azi'), pairs)  23.7 us
    select_n x2, other arithmetic, heun_sections(): first = jnp.where(inside[None, :, None, None], first, 0.0)  15.1 us
    all_to_all x1, starting transfers between devices, shift_rows(): full = lax.all_to_all(half, 'azi', 1, 2, tiled=True)  8.18 us
    mul x2, other arithmetic, heun_sections(): return 0.5 * (field + first[:, 2:-2, 2:-2] + inner)  7.49 us
    ppermute x1, starting transfers between devices, radial_halo(): lax.ppermute(values[..., :width], 'rad', [(i + 1, i) for i in range(rings...  6.05 us
  transfers between devices with their start and end apart: 19, of which 7 were waited for; matrix products, arithmetic and copies ran while one was open for 2% of the time, Pallas kernels for 0%

profile of v2, /device:TPU:2, one launch (start us, length us, event | category | flops | bytes accessed | tf_op | source)
XLA Modules:
  0.0 193.5 jit_solution(1320013572903492001)
XLA Ops:
  0.9 1.9 collective-permute-start.8
  2.9 6.0 %collective-permute-start.9 = (f32[2,5,2]{2,1,0:T(8,128)S(1)}, f32[2,5,2]{2,1,0:T(8,128)S(1)}, u32[]{:S(2)}, u32[]{:S(2)}) collective-permute-start(f32[2,5,2]{2,1,0:T(8,128)S(1)} %get-tuple-element.28), channel_id=1, source_target_pairs={{16,0},{32,16},{48,32},{64,48},{80,64},{96,80},{112,96},{128,112},... | collective-permute-start | bytes 248 | tf_op jit(solution)/shard_map/ppermute | solution.py:64
  8.9 1.1 pad_maximum_fusion.22
  10.1 1.9 collective-permute-start
  12.0 7.1 %collective-permute-start.5 = (f32[6,4,4,128]{3,2,1,0:T(4,128)S(1)}, f32[6,4,4,128]{3,2,1,0:T(4,128)S(1)}, u32[]{:S(2)}, u32[]{:S(2)}) collective-permute-start(f32[6,4,4,128]{3,2,1,0:T(4,128)S(1)} %get-tuple-element.6), channel_id=1, source_target_pairs={{16,1},{17,2},{18,3},{19,4},{20,5},{21,6},{22,7},{23,8},{24,9},{25... | collective-permute-start | bytes 147464 | tf_op jit(solution)/shard_map/ppermute | solution.py:51
  19.1 2.7 %collective-permute-start.7 = (f32[6,4,4,128]{3,2,1,0:T(4,128)S(1)}, f32[6,4,4,128]{3,2,1,0:T(4,128)S(1)}, u32[]{:S(2)}, u32[]{:S(2)}) collective-permute-start(f32[6,4,4,128]{3,2,1,0:T(4,128)S(1)} %get-tuple-element.7), channel_id=1, source_target_pairs={{16,15},{17,0},{18,1},{19,2},{20,3},{21,4},{22,5},{23,6},{24,7},{2... | collective-permute-start | bytes 147464 | tf_op jit(solution)/shard_map/ppermute | solution.py:51
  23.0 4.1 %collective-permute-start.4 = (f32[6,32,4,128]{3,2,1,0:T(4,128)S(1)}, f32[6,32,4,128]{3,2,1,0:T(4,128)S(1)}, u32[]{:S(2)}, u32[]{:S(2)}) collective-permute-start(f32[6,32,4,128]{3,2,1,0:T(4,128)S(1)} %get-tuple-element.12), channel_id=1, source_target_pairs={{0,15},{1,0},{2,1},{3,2},{4,3},{5,4},{6,5},{7,6},{8,7},{9,8},{10,9... | collective-permute-start | bytes 1179656 | tf_op jit(solution)/shard_map/ppermute | solution.py:51
  27.3 3.7 %collective-permute-start.2 = (f32[6,4,4,128]{3,2,1,0:T(4,128)S(1)}, f32[6,4,4,128]{3,2,1,0:T(4,128)S(1)}, u32[]{:S(2)}, u32[]{:S(2)}) collective-permute-start(f32[6,4,4,128]{3,2,1,0:T(4,128)S(1)} %get-tuple-element.8), channel_id=1, source_target_pairs={{0,31},{1,16},{2,17},{3,18},{4,19},{5,20},{6,21},{7,22},{8,23},{9,... | collective-permute-start | bytes 147464 | tf_op jit(solution)/shard_map/ppermute | solution.py:51
  31.0 2.5 %collective-permute-start.1 = (f32[6,4,16,128]{3,2,1,0:T(8,128)S(1)}, f32[6,4,16,128]{3,2,1,0:T(8,128)S(1)}, u32[]{:S(2)}, u32[]{:S(2)}) collective-permute-start(f32[6,4,16,128]{3,2,1,0:T(8,128)S(1)} %get-tuple-element.9), channel_id=1, source_target_pairs={{0,16},{1,17},{2,18},{3,19},{4,20},{5,21},{6,22},{7,23},{8,24},{9,... | collective-permute-start | bytes 589832 | tf_op jit(solution)/shard_map/ppermute | solution.py:51
  33.4 5.5 %collective-permute-start.6 = (f32[6,4,16,128]{3,2,1,0:T(8,128)S(1)}, f32[6,4,16,128]{3,2,1,0:T(8,128)S(1)}, u32[]{:S(2)}, u32[]{:S(2)}) collective-permute-start(f32[6,4,16,128]{3,2,1,0:T(8,128)S(1)} %get-tuple-element.10), channel_id=1, source_target_pairs={{16,0},{17,1},{18,2},{19,3},{20,4},{21,5},{22,6},{23,7},{24,8},{25... | collective-permute-start | bytes 589832 | tf_op jit(solution)/shard_map/ppermute | solution.py:51
  39.0 1.5 collective-permute-done.1
  40.5 1.7 collective-permute-done.6
  42.1 3.8 %collective-permute-done.4 = f32[6,32,4,128]{3,2,1,0:T(4,128)S(1)} collective-permute-done((f32[6,32,4,128]{3,2,1,0:T(4,128)S(1)}, f32[6,32,4,128]{3,2,1,0:T(4,128)S(1)}, u32[]{:S(2)}, u32[]{:S(2)}) %collective-permute-start.4) | collective-permute-done | bytes 393248 | tf_op jit(solution)/shard_map/ppermute | solution.py:51
  45.9 2.3 %maximum_maximum_fusion = f32[6,40,24,128]{3,2,1,0:T(8,128)S(1)} fusion(f32[6,4,4,128]{3,2,1,0:T(4,128)S(1)} %collective-permute-done.7, f32[6,4,16,128]{3,2,1,0:T(8,128)S(1)} %collective-permute-done.6, f32[6,4,4,128]{3,2,1,0:T(4,128)S(1)} %collective-permute-done.5, f32[6,32,4,128]{3,2,1,0:T(4,128)S(1)} %collective-permute-done.4, ...), kind=kLoop, calls=%fused_computation.20 | loop fusion | flops 6635520 | bytes 5898240 | tf_op jit(solution)/shard_map/concatenate | solution.py:57
  48.6 7.8 %fusion.9 = f32[5,36,20,128]{3,2,1,0:T(8,128)S(1)} fusion(f32[5,36,20,128]{3,2,1,0:T(8,128)S(1)} %slice.381, f32[6,40,24,128]{3,2,1,0:T(8,128)S(1)} %maximum_maximum_fusion, f32[6,4,4,128]{3,2,1,0:T(4,128)S(1)} %collective-permute-done.7, f32[6,4,16,128]{3,2,1,0:T(8,128)S(1)} %collective-permute-done.6, f32[6,4,4,128]{3,2,1,0:T(4,128)S(1)} %collective-permute-done.5, ...), kind=kLoop, calls=%fused_computation.33 | loop fusion | flops 24422400 | bytes 18064836 | tf_op jit(solution)/shard_map/jit(_where)/select_n | solution.py:70
  56.5 3.4 %fusion.41 = f32[5,32,16,128]{3,2,1,0:T(8,128)S(1)} fusion(f32[5,32,16,128]{3,2,1,0:T(8,128)S(1)} %slice.393, f32[5,36,20,128]{3,2,1,0:T(8,128)S(1)} %fusion.9, f32[5,32,16,128]{3,2,1,0:T(8,128)S(1)} %copy-done, f32[32,16,128]{2,1,0:T(8,128)S(1)} %slice_multiply_fusion, f32[5,32]{1,0:T(8,128)S(1)} %get-tuple-element.31, f32[5,32]{1,0:T(8,128)S(1)} %get-tuple-element.32), kind=kLoop, calls=%fused_computation.89 | loop fusion | flops 13762560 | bytes 14681344 | tf_op jit(solution)/shard_map/mul | solution.py:73
  59.9 1.1 copy.8
  61.1 8.2 %all-to-all-start = ((f32[5,32,16,128]{3,2,0,1:T(8,128)}), f32[5,32,16,128]{3,2,0,1:T(8,128)S(1)}, u32[]{:S(2)}, u32[]{:S(2)}) async-start(f32[5,32,16,128]{3,2,0,1:T(8,128)} %copy.8), calls=%async_computation | async-start | bytes 2621440 | tf_op jit(solution)/shard_map/all_to_all | solution.py:80
  74.1 26.9 %all-to-all-done = f32[5,32,16,128]{3,2,0,1:T(8,128)S(1)} async-done(((f32[5,32,16,128]{3,2,0,1:T(8,128)}), f32[5,32,16,128]{3,2,0,1:T(8,128)S(1)}, u32[]{:S(2)}, u32[]{:S(2)}) %all-to-all-start) | async-done | bytes 1310752 | tf_op jit(solution)/shard_map/all_to_all | solution.py:80
  102.8 41.3 %all_to_all.36 = f32[5,2,256,128]{3,1,0,2:T(2,128)S(1)} all-to-all(f32[5,2,256,128]{3,1,0,2:T(2,128)S(1)} %copy.11), channel_id=1, replica_groups=mesh['rad'=16,'azi'=16] {'azi'}, dimensions={2} | all-to-all | bytes 2621440 | tf_op jit(solution)/shard_map/all_to_all | solution.py:90
  144.5 1.9 collective-permute-start.10
  147.1 3.5 %collective-permute-start.14 = (f32[5,32,4,128]{3,2,1,0:T(4,128)S(1)}, f32[5,32,4,128]{3,2,1,0:T(4,128)S(1)}, u32[]{:S(2)}, u32[]{:S(2)}) collective-permute-start(f32[5,32,4,128]{3,2,1,0:T(4,128)S(1)} %get-tuple-element.20), channel_id=1, source_target_pairs={{0,15},{1,0},{2,1},{3,2},{4,3},{5,4},{6,5},{7,6},{8,7},{9,8},{10,9... | collective-permute-start | bytes 983048 | tf_op jit(solution)/shard_map/ppermute | solution.py:51
  150.7 1.9 collective-permute-start.11
  152.6 6.0 %collective-permute-start.16 = (f32[5,4,16,128]{3,2,1,0:T(8,128)S(1)}, f32[5,4,16,128]{3,2,1,0:T(8,128)S(1)}, u32[]{:S(2)}, u32[]{:S(2)}) collective-permute-start(f32[5,4,16,128]{3,2,1,0:T(8,128)S(1)} %get-tuple-element.18), channel_id=1, source_target_pairs={{16,0},{17,1},{18,2},{19,3},{20,4},{21,5},{22,6},{23,7},{24,8},{25... | collective-permute-start | bytes 491528 | tf_op jit(solution)/shard_map/ppermute | solution.py:51
  158.7 1.9 collective-permute-start.17
  160.6 5.9 %collective-permute-done.17 = f32[5,4,4,128]{3,2,1,0:T(4,128)S(1)} collective-permute-done((f32[5,4,4,128]{3,2,1,0:T(4,128)S(1)}, f32[5,4,4,128]{3,2,1,0:T(4,128)S(1)}, u32[]{:S(2)}, u32[]{:S(2)}) %collective-permute-start.17) | collective-permute-done | bytes 40992 | tf_op jit(solution)/shard_map/ppermute | solution.py:51
  166.5 1.9 collective-permute-start.15
  168.4 5.5 %collective-permute-done.15 = f32[5,4,4,128]{3,2,1,0:T(4,128)S(1)} collective-permute-done((f32[5,4,4,128]{3,2,1,0:T(4,128)S(1)}, f32[5,4,4,128]{3,2,1,0:T(4,128)S(1)}, u32[]{:S(2)}, u32[]{:S(2)}) %collective-permute-start.15) | collective-permute-done | bytes 40992 | tf_op jit(solution)/shard_map/ppermute | solution.py:51
  173.9 2.1 %collective-permute-start.12 = (f32[5,4,4,128]{3,2,1,0:T(4,128)S(1)}, f32[5,4,4,128]{3,2,1,0:T(4,128)S(1)}, u32[]{:S(2)}, u32[]{:S(2)}) collective-permute-start(f32[5,4,4,128]{3,2,1,0:T(4,128)S(1)} %get-tuple-element.16), channel_id=1, source_target_pairs={{0,31},{1,16},{2,17},{3,18},{4,19},{5,20},{6,21},{7,22},{8,23},{9,... | collective-permute-start | bytes 122888 | tf_op jit(solution)/shard_map/ppermute | solution.py:51
  176.0 5.3 %collective-permute-done.12 = f32[5,4,4,128]{3,2,1,0:T(4,128)S(1)} collective-permute-done((f32[5,4,4,128]{3,2,1,0:T(4,128)S(1)}, f32[5,4,4,128]{3,2,1,0:T(4,128)S(1)}, u32[]{:S(2)}, u32[]{:S(2)}) %collective-permute-start.12) | collective-permute-done | bytes 40992 | tf_op jit(solution)/shard_map/ppermute | solution.py:51
  182.0 7.4 %fusion.21 = f32[5,36,20,128]{3,2,1,0:T(8,128)S(1)} fusion(f32[5,36,20,128]{3,2,1,0:T(8,128)S(1)} %slice.413, f32[5,40,24,128]{3,2,1,0:T(8,128)S(1)} %maximum_maximum_fusion.1, f32[5,4,4,128]{3,2,1,0:T(4,128)S(1)} %collective-permute-done.17, f32[5,4,16,128]{3,2,1,0:T(8,128)S(1)} %collective-permute-done.16, ...), kind=kLoop, calls=%fused_computation.45 | loop fusion | flops 23500800 | bytes 17573316 | tf_op jit(solution)/shard_map/jit(_where)/select_n | solution.py:70
  189.5 4.0 %fusion.53 = f32[5,32,16,128]{3,2,1,0:T(8,128)} fusion(f32[5,32,16,128]{3,2,1,0:T(8,128)S(1)} %slice.420, f32[5,36,20,128]{3,2,1,0:T(8,128)S(1)} %fusion.21, f32[5,32,16,128]{3,2,1,0:T(8,128)S(1)} %bitcast.30, f32[32,16,128]{2,1,0:T(8,128)S(1)} %slice_multiply_fusion, f32[5,32]{1,0:T(8,128)S(1)} %get-tuple-element.31, f32[5,32]{1,0:T(8,128)S(1)} %get-tuple-element.32), kind=kLoop, calls=%fused_computation.101 | loop fusion | flops 13762560 | bytes 14681344 | tf_op jit(solution)/shard_map/mul | solution.py:73
  (53 shorter events, 6.9 us)
Async XLA Ops:
  0.0 21.9 %copy-start = (f32[5,32,16,128]{3,2,1,0:T(8,128)S(1)}, f32[5,32,16,128]{3,2,1,0:T(8,128)}, u32[]{:S(2)}) copy-start(f32[5,32,16,128]{3,2,1,0:T(8,128)} %param.5) | copy-start | bytes 3932164
  0.0 22.7 %copy-start.1 = (f32[32,16,128]{2,1,0:T(8,128)S(1)}, f32[32,16,128]{2,1,0:T(8,128)}, u32[]{:S(2)}) copy-start(f32[32,16,128]{2,1,0:T(8,128)} %param.6) | copy-start | bytes 786436
  0.9 21.9 %collective-permute-start.8 = (f32[2,5,2]{2,1,0:T(8,128)S(1)}, f32[2,5,2]{2,1,0:T(8,128)S(1)}, u32[]{:S(2)}, u32[]{:S(2)}) collective-permute-start(f32[2,5,2]{2,1,0:T(8,128)S(1)} %get-tuple-element.27), channel_id=1, source_target_pairs={{0,16},{16,32},{32,48},{48,64},{64,80},{80,96},{96,112},{112,128},... | collective-permute-start | bytes 248 | tf_op jit(solution)/shard_map/ppermute | solution.py:63
  2.9 20.1 %collective-permute-start.9 = (f32[2,5,2]{2,1,0:T(8,128)S(1)}, f32[2,5,2]{2,1,0:T(8,128)S(1)}, u32[]{:S(2)}, u32[]{:S(2)}) collective-permute-start(f32[2,5,2]{2,1,0:T(8,128)S(1)} %get-tuple-element.28), channel_id=1, source_target_pairs={{16,0},{32,16},{48,32},{64,48},{80,64},{96,80},{112,96},{128,112},... | collective-permute-start | bytes 248 | tf_op jit(solution)/shard_map/ppermute | solution.py:64
  10.0 17.1 %copy-start.2 = (f32[5,32]{1,0:T(8,128)S(1)}, f32[5,32]{1,0:T(8,128)}, u32[]{:S(2)}) copy-start(f32[5,32]{1,0:T(8,128)} %param.8) | copy-start | bytes 1924
  10.0 17.1 %copy-start.3 = (f32[5,32]{1,0:T(8,128)S(1)}, f32[5,32]{1,0:T(8,128)}, u32[]{:S(2)}) copy-start(f32[5,32]{1,0:T(8,128)} %param.7) | copy-start | bytes 1924
  10.1 17.2 %collective-permute-start = (f32[6,4,4,128]{3,2,1,0:T(4,128)S(1)}, f32[6,4,4,128]{3,2,1,0:T(4,128)S(1)}, u32[]{:S(2)}, u32[]{:S(2)}) collective-permute-start(f32[6,4,4,128]{3,2,1,0:T(4,128)S(1)} %get-tuple-element.5), channel_id=1, source_target_pairs={{0,17},{1,18},{2,19},{3,20},{4,21},{5,22},{6,23},{7,24},{8,25},{9,... | collective-permute-start | bytes 147464 | tf_op jit(solution)/shard_map/ppermute | solution.py:51
  12.0 19.0 %collective-permute-start.5 = (f32[6,4,4,128]{3,2,1,0:T(4,128)S(1)}, f32[6,4,4,128]{3,2,1,0:T(4,128)S(1)}, u32[]{:S(2)}, u32[]{:S(2)}) collective-permute-start(f32[6,4,4,128]{3,2,1,0:T(4,128)S(1)} %get-tuple-element.6), channel_id=1, source_target_pairs={{16,1},{17,2},{18,3},{19,4},{20,5},{21,6},{22,7},{23,8},{24,9},{25... | collective-permute-start | bytes 147464 | tf_op jit(solution)/shard_map/ppermute | solution.py:51
  19.1 14.3 %collective-permute-start.7 = (f32[6,4,4,128]{3,2,1,0:T(4,128)S(1)}, f32[6,4,4,128]{3,2,1,0:T(4,128)S(1)}, u32[]{:S(2)}, u32[]{:S(2)}) collective-permute-start(f32[6,4,4,128]{3,2,1,0:T(4,128)S(1)} %get-tuple-element.7), channel_id=1, source_target_pairs={{16,15},{17,0},{18,1},{19,2},{20,3},{21,4},{22,5},{23,6},{24,7},{2... | collective-permute-start | bytes 147464 | tf_op jit(solution)/shard_map/ppermute | solution.py:51
  22.9 19.3 %collective-permute-start.3 = (f32[6,32,4,128]{3,2,1,0:T(4,128)S(1)}, f32[6,32,4,128]{3,2,1,0:T(4,128)S(1)}, u32[]{:S(2)}, u32[]{:S(2)}) collective-permute-start(f32[6,32,4,128]{3,2,1,0:T(4,128)S(1)} %get-tuple-element.11), channel_id=1, source_target_pairs={{0,1},{1,2},{2,3},{3,4},{4,5},{5,6},{6,7},{7,8},{8,9},{9,10},{10,1... | collective-permute-start | bytes 1179656 | tf_op jit(solution)/shard_map/ppermute | solution.py:51
  23.0 22.9 %collective-permute-start.4 = (f32[6,32,4,128]{3,2,1,0:T(4,128)S(1)}, f32[6,32,4,128]{3,2,1,0:T(4,128)S(1)}, u32[]{:S(2)}, u32[]{:S(2)}) collective-permute-start(f32[6,32,4,128]{3,2,1,0:T(4,128)S(1)} %get-tuple-element.12), channel_id=1, source_target_pairs={{0,15},{1,0},{2,1},{3,2},{4,3},{5,4},{6,5},{7,6},{8,7},{9,8},{10,9... | collective-permute-start | bytes 1179656 | tf_op jit(solution)/shard_map/ppermute | solution.py:51
  27.3 11.7 %collective-permute-start.2 = (f32[6,4,4,128]{3,2,1,0:T(4,128)S(1)}, f32[6,4,4,128]{3,2,1,0:T(4,128)S(1)}, u32[]{:S(2)}, u32[]{:S(2)}) collective-permute-start(f32[6,4,4,128]{3,2,1,0:T(4,128)S(1)} %get-tuple-element.8), channel_id=1, source_target_pairs={{0,31},{1,16},{2,17},{3,18},{4,19},{5,20},{6,21},{7,22},{8,23},{9,... | collective-permute-start | bytes 147464 | tf_op jit(solution)/shard_map/ppermute | solution.py:51
  31.0 9.5 %collective-permute-start.1 = (f32[6,4,16,128]{3,2,1,0:T(8,128)S(1)}, f32[6,4,16,128]{3,2,1,0:T(8,128)S(1)}, u32[]{:S(2)}, u32[]{:S(2)}) collective-permute-start(f32[6,4,16,128]{3,2,1,0:T(8,128)S(1)} %get-tuple-element.9), channel_id=1, source_target_pairs={{0,16},{1,17},{2,18},{3,19},{4,20},{5,21},{6,22},{7,23},{8,24},{9,... | collective-permute-start | bytes 589832 | tf_op jit(solution)/shard_map/ppermute | solution.py:51
  33.4 8.7 %collective-permute-start.6 = (f32[6,4,16,128]{3,2,1,0:T(8,128)S(1)}, f32[6,4,16,128]{3,2,1,0:T(8,128)S(1)}, u32[]{:S(2)}, u32[]{:S(2)}) collective-permute-start(f32[6,4,16,128]{3,2,1,0:T(8,128)S(1)} %get-tuple-element.10), channel_id=1, source_target_pairs={{16,0},{17,1},{18,2},{19,3},{20,4},{21,5},{22,6},{23,7},{24,8},{25... | collective-permute-start | bytes 589832 | tf_op jit(solution)/shard_map/ppermute | solution.py:51
  59.9 9.3 %copy-start.4 = (s32[32]{0:T(128)S(1)}, s32[32]{0:T(128)}, u32[]{:S(2)}) copy-start(s32[32]{0:T(128)} %param.9) | copy-start | bytes 388
  61.1 39.9 %all-to-all-start = ((f32[5,32,16,128]{3,2,0,1:T(8,128)}), f32[5,32,16,128]{3,2,0,1:T(8,128)S(1)}, u32[]{:S(2)}, u32[]{:S(2)}) async-start(f32[5,32,16,128]{3,2,0,1:T(8,128)} %copy.8), calls=%async_computation | async-start | bytes 2621440 | tf_op jit(solution)/shard_map/all_to_all | solution.py:80
  144.5 14.2 %collective-permute-start.10 = (f32[5,4,4,128]{3,2,1,0:T(4,128)S(1)}, f32[5,4,4,128]{3,2,1,0:T(4,128)S(1)}, u32[]{:S(2)}, u32[]{:S(2)}) collective-permute-start(f32[5,4,4,128]{3,2,1,0:T(4,128)S(1)} %get-tuple-element.13), channel_id=1, source_target_pairs={{0,17},{1,18},{2,19},{3,20},{4,21},{5,22},{6,23},{7,24},{8,25},{9,... | collective-permute-start | bytes 122888 | tf_op jit(solution)/shard_map/ppermute | solution.py:51
  146.4 34.9 %collective-permute-start.13 = (f32[5,32,4,128]{3,2,1,0:T(4,128)S(1)}, f32[5,32,4,128]{3,2,1,0:T(4,128)S(1)}, u32[]{:S(2)}, u32[]{:S(2)}) collective-permute-start(f32[5,32,4,128]{3,2,1,0:T(4,128)S(1)} %get-tuple-element.19), channel_id=1, source_target_pairs={{0,1},{1,2},{2,3},{3,4},{4,5},{5,6},{6,7},{7,8},{8,9},{9,10},{10,1... | collective-permute-start | bytes 983048 | tf_op jit(solution)/shard_map/ppermute | solution.py:51
  147.1 34.3 %collective-permute-start.14 = (f32[5,32,4,128]{3,2,1,0:T(4,128)S(1)}, f32[5,32,4,128]{3,2,1,0:T(4,128)S(1)}, u32[]{:S(2)}, u32[]{:S(2)}) collective-permute-start(f32[5,32,4,128]{3,2,1,0:T(4,128)S(1)} %get-tuple-element.20), channel_id=1, source_target_pairs={{0,15},{1,0},{2,1},{3,2},{4,3},{5,4},{6,5},{7,6},{8,7},{9,8},{10,9... | collective-permute-start | bytes 983048 | tf_op jit(solution)/shard_map/ppermute | solution.py:51
  150.7 30.7 %collective-permute-start.11 = (f32[5,4,16,128]{3,2,1,0:T(8,128)S(1)}, f32[5,4,16,128]{3,2,1,0:T(8,128)S(1)}, u32[]{:S(2)}, u32[]{:S(2)}) collective-permute-start(f32[5,4,16,128]{3,2,1,0:T(8,128)S(1)} %get-tuple-element.17), channel_id=1, source_target_pairs={{0,16},{1,17},{2,18},{3,19},{4,20},{5,21},{6,22},{7,23},{8,24},{9,... | collective-permute-start | bytes 491528 | tf_op jit(solution)/shard_map/ppermute | solution.py:51
  152.6 28.8 %collective-permute-start.16 = (f32[5,4,16,128]{3,2,1,0:T(8,128)S(1)}, f32[5,4,16,128]{3,2,1,0:T(8,128)S(1)}, u32[]{:S(2)}, u32[]{:S(2)}) collective-permute-start(f32[5,4,16,128]{3,2,1,0:T(8,128)S(1)} %get-tuple-element.18), channel_id=1, source_target_pairs={{16,0},{17,1},{18,2},{19,3},{20,4},{21,5},{22,6},{23,7},{24,8},{25... | collective-permute-start | bytes 491528 | tf_op jit(solution)/shard_map/ppermute | solution.py:51
  158.7 7.9 %collective-permute-start.17 = (f32[5,4,4,128]{3,2,1,0:T(4,128)S(1)}, f32[5,4,4,128]{3,2,1,0:T(4,128)S(1)}, u32[]{:S(2)}, u32[]{:S(2)}) collective-permute-start(f32[5,4,4,128]{3,2,1,0:T(4,128)S(1)} %get-tuple-element.14), channel_id=1, source_target_pairs={{16,15},{17,0},{18,1},{19,2},{20,3},{21,4},{22,5},{23,6},{24,7},{2... | collective-permute-start | bytes 122888 | tf_op jit(solution)/shard_map/ppermute | solution.py:51
  166.5 7.4 %collective-permute-start.15 = (f32[5,4,4,128]{3,2,1,0:T(4,128)S(1)}, f32[5,4,4,128]{3,2,1,0:T(4,128)S(1)}, u32[]{:S(2)}, u32[]{:S(2)}) collective-permute-start(f32[5,4,4,128]{3,2,1,0:T(4,128)S(1)} %get-tuple-element.15), channel_id=1, source_target_pairs={{16,1},{17,2},{18,3},{19,4},{20,5},{21,6},{22,7},{23,8},{24,9},{25... | collective-permute-start | bytes 122888 | tf_op jit(solution)/shard_map/ppermute | solution.py:51
  173.9 7.4 %collective-permute-start.12 = (f32[5,4,4,128]{3,2,1,0:T(4,128)S(1)}, f32[5,4,4,128]{3,2,1,0:T(4,128)S(1)}, u32[]{:S(2)}, u32[]{:S(2)}) collective-permute-start(f32[5,4,4,128]{3,2,1,0:T(4,128)S(1)} %get-tuple-element.16), channel_id=1, source_target_pairs={{0,31},{1,16},{2,17},{3,18},{4,19},{5,20},{6,21},{7,22},{8,23},{9,... | collective-permute-start | bytes 122888 | tf_op jit(solution)/shard_map/ppermute | solution.py:51

commit v3 on v2

--- a/solution.py
+++ b/solution.py
@@ -35,26 +35,14 @@
 
 
 def extend(cells, width):
-    rings, sectors = lax.axis_size("rad"), lax.axis_size("azi")
+    sectors, rings = lax.axis_size("azi"), lax.axis_size("rad")
     rows, cols = cells.shape[-3], cells.shape[-2]
-    spans = {-1: (rows - width, rows), 0: (0, rows), 1: (0, width)}
-    cuts = {-1: (cols - width, cols), 0: (0, cols), 1: (0, width)}
-
-    def piece(di, dj):
-        block = cells[..., slice(*spans[di]), slice(*cuts[dj]), :]
-        pairs = [
-            (a * sectors + b, (a - di) * sectors + (b - dj) % sectors)
-            for a in range(rings)
-            for b in range(sectors)
-            if 0 <= a - di < rings
-        ]
-        return lax.ppermute(block, ("rad", "azi"), pairs)
-
-    bands = []
-    for di in (-1, 0, 1):
-        parts = [cells if di == dj == 0 else piece(di, dj) for dj in (-1, 0, 1)]
-        bands.append(jnp.concatenate(parts, axis=-2))
-    return jnp.concatenate(bands, axis=-3)
+    left = lax.ppermute(cells[..., cols - width :, :], "azi", [(i, (i + 1) % sectors) for i in range(sectors)])
+    right = lax.ppermute(cells[..., :width, :], "azi", [((i + 1) % sectors, i) for i in range(sectors)])
+    wide = jnp.concatenate([left, cells, right], axis=-2)
+    above = lax.ppermute(wide[..., rows - width :, :, :], "rad", [(i, i + 1) for i in range(rings - 1)])
+    below = lax.ppermute(wide[..., :width, :, :], "rad", [(i + 1, i) for i in range(rings - 1)])
+    return jnp.concatenate([above, wide, below], axis=-3)
 
 
 def radial_halo(values, width):

time: 194 us -> 179 us (0.923)
  the two profiles are of different devices: /device:TPU:2 before, /device:TPU:1 now
where the time goes in v3:
time: 179 us
  waiting for transfers between devices  62.9 us (35%)
  starting transfers between devices  45.6 us (25%)
  blocking collectives  37.2 us (21%)
  other arithmetic  24.8 us (14%)
  local copies, waits for them, and re-layouts  4.29 us (2%)
  between operations  4.12 us (2%)
    all_to_all x1, blocking collectives, shift_rows(): return lax.all_to_all(moved, 'azi', 2, 1, tiled=True)  37.2 us
    all_to_all x1, waiting for transfers between devices, shift_rows(): full = lax.all_to_all(half, 'azi', 1, 2, tiled=True)  23.6 us
    ppermute x2, waiting for transfers between devices, extend(): lax.ppermute(cells[..., cols - width:, :], 'azi', [(i, (i + 1) % sectors)...  20.6 us
    ppermute x2, starting transfers between devices, extend(): lax.ppermute(wide[..., rows - width:, :, :], 'rad', [(i, i + 1) for i in...  15.6 us
    select_n x2, other arithmetic, heun_sections(): first = jnp.where(inside[None, :, None, None], first, 0.0)  13.2 us
    ppermute x2, waiting for transfers between devices, extend(): lax.ppermute(wide[..., :width, :, :], 'rad', [(i + 1, i) for i in range(r...  11.8 us
    ppermute x2, starting transfers between devices, extend(): lax.ppermute(cells[..., :width, :], 'azi', [((i + 1) % sectors, i) for i...  8.94 us
    all_to_all x1, starting transfers between devices, shift_rows(): full = lax.all_to_all(half, 'azi', 1, 2, tiled=True)  8.29 us
  transfers between devices with their start and end apart: 11, of which 9 were waited for; matrix products, arithmetic and copies ran while one was open for 1% of the time, Pallas kernels for 0%

profile of v3, /device:TPU:1, one launch (start us, length us, event | category | flops | bytes accessed | tf_op | source)
XLA Modules:
  0.0 178.9 jit_solution(6310726203397252922)
XLA Ops:
  0.0 0.9 slice_maximum_fusion
  1.0 6.2 %collective-permute-start.4 = (f32[2,5,2]{2,1,0:T(8,128)S(1)}, f32[2,5,2]{2,1,0:T(8,128)S(1)}, u32[]{:S(2)}, u32[]{:S(2)}) collective-permute-start(f32[2,5,2]{2,1,0:T(8,128)S(1)} %get-tuple-element.19), channel_id=1, source_target_pairs={{0,16},{16,32},{32,48},{48,64},{64,80},{80,96},{96,112},{112,128},... | collective-permute-start | bytes 248 | tf_op jit(solution)/shard_map/ppermute | solution.py:51
  7.2 1.9 %collective-permute-start.5 = (f32[2,5,2]{2,1,0:T(8,128)S(1)}, f32[2,5,2]{2,1,0:T(8,128)S(1)}, u32[]{:S(2)}, u32[]{:S(2)}) collective-permute-start(f32[2,5,2]{2,1,0:T(8,128)S(1)} %get-tuple-element.20), channel_id=1, source_target_pairs={{16,0},{32,16},{48,32},{64,48},{80,64},{96,80},{112,96},{128,112},... | collective-permute-start | bytes 248 | tf_op jit(solution)/shard_map/ppermute | solution.py:52
  9.1 1.6 pad_maximum_fusion.18
  10.7 0.5 collective-permute-start
  11.2 5.4 %collective-permute-start.1 = (f32[6,32,4,128]{3,2,1,0:T(4,128)S(1)}, f32[6,32,4,128]{3,2,1,0:T(4,128)S(1)}, u32[]{:S(2)}, u32[]{:S(2)}) collective-permute-start(f32[6,32,4,128]{3,2,1,0:T(4,128)S(1)} %get-tuple-element.10), channel_id=1, source_target_pairs={{1,0},{2,1},{3,2},{4,3},{5,4},{6,5},{7,6},{8,7},{9,8},{10,9},{11,1... | collective-permute-start | bytes 1179656 | tf_op jit(solution)/shard_map/ppermute | solution.py:41
  16.7 9.7 %collective-permute-done = f32[6,32,4,128]{3,2,1,0:T(4,128)S(1)} collective-permute-done((f32[6,32,4,128]{3,2,1,0:T(4,128)S(1)}, f32[6,32,4,128]{3,2,1,0:T(4,128)S(1)}, u32[]{:S(2)}, u32[]{:S(2)}) %collective-permute-start) | collective-permute-done | bytes 393248 | tf_op jit(solution)/shard_map/ppermute | solution.py:40
  26.4 2.2 %collective-permute-done.1 = f32[6,32,4,128]{3,2,1,0:T(4,128)S(1)} collective-permute-done((f32[6,32,4,128]{3,2,1,0:T(4,128)S(1)}, f32[6,32,4,128]{3,2,1,0:T(4,128)S(1)}, u32[]{:S(2)}, u32[]{:S(2)}) %collective-permute-start.1) | collective-permute-done | bytes 393248 | tf_op jit(solution)/shard_map/ppermute | solution.py:41
  28.6 6.8 %collective-permute-start.2 = (f32[6,4,24,128]{3,2,1,0:T(8,128)S(1)}, f32[6,4,24,128]{3,2,1,0:T(8,128)S(1)}, u32[]{:S(2)}, u32[]{:S(2)}) collective-permute-start(f32[6,4,24,128]{3,2,1,0:T(8,128)S(1)} %get-tuple-element.5), channel_id=1, source_target_pairs={{0,16},{16,32},{32,48},{48,64},{64,80},{80,96},{96,112},{112,128},... | collective-permute-start | bytes 884744 | tf_op jit(solution)/shard_map/ppermute | solution.py:43
  35.5 1.9 %collective-permute-start.3 = (f32[6,4,24,128]{3,2,1,0:T(8,128)S(1)}, f32[6,4,24,128]{3,2,1,0:T(8,128)S(1)}, u32[]{:S(2)}, u32[]{:S(2)}) collective-permute-start(f32[6,4,24,128]{3,2,1,0:T(8,128)S(1)} %get-tuple-element.6), channel_id=1, source_target_pairs={{16,0},{32,16},{48,32},{64,48},{80,64},{96,80},{112,96},{128,112},... | collective-permute-start | bytes 884744 | tf_op jit(solution)/shard_map/ppermute | solution.py:44
  37.5 1.6 collective-permute-done.2
  39.1 5.9 %collective-permute-done.3 = f32[6,4,24,128]{3,2,1,0:T(8,128)S(1)} collective-permute-done((f32[6,4,24,128]{3,2,1,0:T(8,128)S(1)}, f32[6,4,24,128]{3,2,1,0:T(8,128)S(1)}, u32[]{:S(2)}, u32[]{:S(2)}) %collective-permute-start.3) | collective-permute-done | bytes 294944 | tf_op jit(solution)/shard_map/ppermute | solution.py:44
  45.0 0.4 pad_maximum_fusion
  45.6 0.2 slice.341
  45.8 6.9 %fusion.9 = f32[5,36,20,128]{3,2,1,0:T(8,128)S(1)} fusion(f32[5,36,20,128]{3,2,1,0:T(8,128)S(1)} %slice.341, f32[6,40,24,128]{3,2,1,0:T(8,128)S(1)} %pad_maximum_fusion, f32[6,4,24,128]{3,2,1,0:T(8,128)S(1)} %collective-permute-done.3, f32[6,32,4,128]{3,2,1,0:T(4,128)S(1)} %collective-permute-done.1, f32[1,32,16,128]{3,2,1,0:T(8,128)S(1)} %bitcast.37, ...), kind=kLoop, calls=%fused_computation.29 | loop fusion | flops 22579200 | bytes 18064836 | tf_op jit(solution)/shard_map/jit(_where)/select_n | solution.py:58
  52.8 3.4 %fusion.37 = f32[5,32,16,128]{3,2,1,0:T(8,128)S(1)} fusion(f32[5,32,16,128]{3,2,1,0:T(8,128)S(1)} %slice.353, f32[5,36,20,128]{3,2,1,0:T(8,128)S(1)} %fusion.9, f32[5,32,16,128]{3,2,1,0:T(8,128)S(1)} %copy-done, f32[32,16,128]{2,1,0:T(8,128)S(1)} %slice_multiply_fusion, f32[5,32]{1,0:T(8,128)S(1)} %get-tuple-element.23, f32[5,32]{1,0:T(8,128)S(1)} %get-tuple-element.24), kind=kLoop, calls=%fused_computation.73 | loop fusion | flops 13762560 | bytes 14681344 | tf_op jit(solution)/shard_map/mul | solution.py:61
  56.3 1.1 copy.8
  57.4 8.3 %all-to-all-start = ((f32[5,32,16,128]{3,2,0,1:T(8,128)}), f32[5,32,16,128]{3,2,0,1:T(8,128)S(1)}, u32[]{:S(2)}, u32[]{:S(2)}) async-start(f32[5,32,16,128]{3,2,0,1:T(8,128)} %copy.8), calls=%async_computation | async-start | bytes 2621440 | tf_op jit(solution)/shard_map/all_to_all | solution.py:68
  65.8 0.6 fusion.54
  70.3 23.6 %all-to-all-done = f32[5,32,16,128]{3,2,0,1:T(8,128)S(1)} async-done(((f32[5,32,16,128]{3,2,0,1:T(8,128)}), f32[5,32,16,128]{3,2,0,1:T(8,128)S(1)}, u32[]{:S(2)}, u32[]{:S(2)}) %all-to-all-start) | async-done | bytes 1310752 | tf_op jit(solution)/shard_map/all_to_all | solution.py:68
  94.6 1.0 copy.11
  95.7 37.2 %all_to_all.36 = f32[5,2,256,128]{3,1,0,2:T(2,128)S(1)} all-to-all(f32[5,2,256,128]{3,1,0,2:T(2,128)S(1)} %copy.11), channel_id=1, replica_groups=mesh['rad'=16,'azi'=16] {'azi'}, dimensions={2} | all-to-all | bytes 2621440 | tf_op jit(solution)/shard_map/all_to_all | solution.py:78
  133.3 3.6 %collective-permute-start.7 = (f32[5,32,4,128]{3,2,1,0:T(4,128)S(1)}, f32[5,32,4,128]{3,2,1,0:T(4,128)S(1)}, u32[]{:S(2)}, u32[]{:S(2)}) collective-permute-start(f32[5,32,4,128]{3,2,1,0:T(4,128)S(1)} %get-tuple-element.12), channel_id=1, source_target_pairs={{1,0},{2,1},{3,2},{4,3},{5,4},{6,5},{7,6},{8,7},{9,8},{10,9},{11,1... | collective-permute-start | bytes 983048 | tf_op jit(solution)/shard_map/ppermute | solution.py:41
  136.9 10.9 %collective-permute-done.6 = f32[5,32,4,128]{3,2,1,0:T(4,128)S(1)} collective-permute-done((f32[5,32,4,128]{3,2,1,0:T(4,128)S(1)}, f32[5,32,4,128]{3,2,1,0:T(4,128)S(1)}, u32[]{:S(2)}, u32[]{:S(2)}) %collective-permute-start.6) | collective-permute-done | bytes 327712 | tf_op jit(solution)/shard_map/ppermute | solution.py:40
  147.8 2.1 %collective-permute-done.7 = f32[5,32,4,128]{3,2,1,0:T(4,128)S(1)} collective-permute-done((f32[5,32,4,128]{3,2,1,0:T(4,128)S(1)}, f32[5,32,4,128]{3,2,1,0:T(4,128)S(1)}, u32[]{:S(2)}, u32[]{:S(2)}) %collective-permute-start.7) | collective-permute-done | bytes 327712 | tf_op jit(solution)/shard_map/ppermute | solution.py:41
  149.9 8.8 %collective-permute-start.8 = (f32[5,4,24,128]{3,2,1,0:T(8,128)S(1)}, f32[5,4,24,128]{3,2,1,0:T(8,128)S(1)}, u32[]{:S(2)}, u32[]{:S(2)}) collective-permute-start(f32[5,4,24,128]{3,2,1,0:T(8,128)S(1)} %get-tuple-element.7), channel_id=1, source_target_pairs={{0,16},{16,32},{32,48},{48,64},{64,80},{80,96},{96,112},{112,128},... | collective-permute-start | bytes 737288 | tf_op jit(solution)/shard_map/ppermute | solution.py:43
  158.7 2.1 %collective-permute-start.9 = (f32[5,4,24,128]{3,2,1,0:T(8,128)S(1)}, f32[5,4,24,128]{3,2,1,0:T(8,128)S(1)}, u32[]{:S(2)}, u32[]{:S(2)}) collective-permute-start(f32[5,4,24,128]{3,2,1,0:T(8,128)S(1)} %get-tuple-element.8), channel_id=1, source_target_pairs={{16,0},{32,16},{48,32},{64,48},{80,64},{96,80},{112,96},{128,112},... | collective-permute-start | bytes 737288 | tf_op jit(solution)/shard_map/ppermute | solution.py:44
  160.9 1.0 collective-permute-done.8
  161.9 5.9 %collective-permute-done.9 = f32[5,4,24,128]{3,2,1,0:T(8,128)S(1)} collective-permute-done((f32[5,4,24,128]{3,2,1,0:T(8,128)S(1)}, f32[5,4,24,128]{3,2,1,0:T(8,128)S(1)}, u32[]{:S(2)}, u32[]{:S(2)}) %collective-permute-start.9) | collective-permute-done | bytes 245792 | tf_op jit(solution)/shard_map/ppermute | solution.py:44
  167.8 0.3 pad_maximum_fusion.1
  168.3 6.4 %fusion.21 = f32[5,36,20,128]{3,2,1,0:T(8,128)S(1)} fusion(f32[5,36,20,128]{3,2,1,0:T(8,128)S(1)} %slice.367, f32[5,40,24,128]{3,2,1,0:T(8,128)S(1)} %pad_maximum_fusion.1, f32[5,4,24,128]{3,2,1,0:T(8,128)S(1)} %collective-permute-done.9, f32[5,32,4,128]{3,2,1,0:T(4,128)S(1)} %collective-permute-done.7, f32[5,32,16,128]{3,2,1,0:T(8,128)S(1)} %bitcast.28, ...), kind=kLoop, calls=%fused_computation.41 | loop fusion | flops 21657600 | bytes 17573316 | tf_op jit(solution)/shard_map/jit(_where)/select_n | solution.py:58
  174.8 4.0 %fusion.49 = f32[5,32,16,128]{3,2,1,0:T(8,128)} fusion(f32[5,32,16,128]{3,2,1,0:T(8,128)S(1)} %slice.374, f32[5,36,20,128]{3,2,1,0:T(8,128)S(1)} %fusion.21, f32[5,32,16,128]{3,2,1,0:T(8,128)S(1)} %bitcast.29, f32[32,16,128]{2,1,0:T(8,128)S(1)} %slice_multiply_fusion, f32[5,32]{1,0:T(8,128)S(1)} %get-tuple-element.23, f32[5,32]{1,0:T(8,128)S(1)} %get-tuple-element.24), kind=kLoop, calls=%fused_computation.85 | loop fusion | flops 13762560 | bytes 14681344 | tf_op jit(solution)/shard_map/mul | solution.py:61
  (35 shorter events, 2.2 us)
Async XLA Ops:
  0.0 16.6 %copy-start.2 = (f32[5,32]{1,0:T(8,128)S(1)}, f32[5,32]{1,0:T(8,128)}, u32[]{:S(2)}) copy-start(f32[5,32]{1,0:T(8,128)} %param.8) | copy-start | bytes 1924
  0.0 16.6 %copy-start.3 = (f32[5,32]{1,0:T(8,128)S(1)}, f32[5,32]{1,0:T(8,128)}, u32[]{:S(2)}) copy-start(f32[5,32]{1,0:T(8,128)} %param.7) | copy-start | bytes 1924
  0.0 28.5 %copy-start = (f32[5,32,16,128]{3,2,1,0:T(8,128)S(1)}, f32[5,32,16,128]{3,2,1,0:T(8,128)}, u32[]{:S(2)}) copy-start(f32[5,32,16,128]{3,2,1,0:T(8,128)} %param.5) | copy-start | bytes 3932164
  0.0 28.5 %copy-start.1 = (f32[32,16,128]{2,1,0:T(8,128)S(1)}, f32[32,16,128]{2,1,0:T(8,128)}, u32[]{:S(2)}) copy-start(f32[32,16,128]{2,1,0:T(8,128)} %param.6) | copy-start | bytes 786436
  1.0 15.6 %collective-permute-start.4 = (f32[2,5,2]{2,1,0:T(8,128)S(1)}, f32[2,5,2]{2,1,0:T(8,128)S(1)}, u32[]{:S(2)}, u32[]{:S(2)}) collective-permute-start(f32[2,5,2]{2,1,0:T(8,128)S(1)} %get-tuple-element.19), channel_id=1, source_target_pairs={{0,16},{16,32},{32,48},{48,64},{64,80},{80,96},{96,112},{112,128},... | collective-permute-start | bytes 248 | tf_op jit(solution)/shard_map/ppermute | solution.py:51
  7.2 9.4 %collective-permute-start.5 = (f32[2,5,2]{2,1,0:T(8,128)S(1)}, f32[2,5,2]{2,1,0:T(8,128)S(1)}, u32[]{:S(2)}, u32[]{:S(2)}) collective-permute-start(f32[2,5,2]{2,1,0:T(8,128)S(1)} %get-tuple-element.20), channel_id=1, source_target_pairs={{16,0},{32,16},{48,32},{64,48},{80,64},{96,80},{112,96},{128,112},... | collective-permute-start | bytes 248 | tf_op jit(solution)/shard_map/ppermute | solution.py:52
  10.7 15.7 %collective-permute-start = (f32[6,32,4,128]{3,2,1,0:T(4,128)S(1)}, f32[6,32,4,128]{3,2,1,0:T(4,128)S(1)}, u32[]{:S(2)}, u32[]{:S(2)}) collective-permute-start(f32[6,32,4,128]{3,2,1,0:T(4,128)S(1)} %get-tuple-element.9), channel_id=1, source_target_pairs={{0,1},{1,2},{2,3},{3,4},{4,5},{5,6},{6,7},{7,8},{8,9},{9,10},{10,1... | collective-permute-start | bytes 1179656 | tf_op jit(solution)/shard_map/ppermute | solution.py:40
  11.2 17.4 %collective-permute-start.1 = (f32[6,32,4,128]{3,2,1,0:T(4,128)S(1)}, f32[6,32,4,128]{3,2,1,0:T(4,128)S(1)}, u32[]{:S(2)}, u32[]{:S(2)}) collective-permute-start(f32[6,32,4,128]{3,2,1,0:T(4,128)S(1)} %get-tuple-element.10), channel_id=1, source_target_pairs={{1,0},{2,1},{3,2},{4,3},{5,4},{6,5},{7,6},{8,7},{9,8},{10,9},{11,1... | collective-permute-start | bytes 1179656 | tf_op jit(solution)/shard_map/ppermute | solution.py:41
  28.6 10.5 %collective-permute-start.2 = (f32[6,4,24,128]{3,2,1,0:T(8,128)S(1)}, f32[6,4,24,128]{3,2,1,0:T(8,128)S(1)}, u32[]{:S(2)}, u32[]{:S(2)}) collective-permute-start(f32[6,4,24,128]{3,2,1,0:T(8,128)S(1)} %get-tuple-element.5), channel_id=1, source_target_pairs={{0,16},{16,32},{32,48},{48,64},{64,80},{80,96},{96,112},{112,128},... | collective-permute-start | bytes 884744 | tf_op jit(solution)/shard_map/ppermute | solution.py:43
  35.5 9.5 %collective-permute-start.3 = (f32[6,4,24,128]{3,2,1,0:T(8,128)S(1)}, f32[6,4,24,128]{3,2,1,0:T(8,128)S(1)}, u32[]{:S(2)}, u32[]{:S(2)}) collective-permute-start(f32[6,4,24,128]{3,2,1,0:T(8,128)S(1)} %get-tuple-element.6), channel_id=1, source_target_pairs={{16,0},{32,16},{48,32},{64,48},{80,64},{96,80},{112,96},{128,112},... | collective-permute-start | bytes 884744 | tf_op jit(solution)/shard_map/ppermute | solution.py:44
  56.3 9.5 %copy-start.4 = (s32[32]{0:T(128)S(1)}, s32[32]{0:T(128)}, u32[]{:S(2)}) copy-start(s32[32]{0:T(128)} %param.9) | copy-start | bytes 388
  57.4 36.5 %all-to-all-start = ((f32[5,32,16,128]{3,2,0,1:T(8,128)}), f32[5,32,16,128]{3,2,0,1:T(8,128)S(1)}, u32[]{:S(2)}, u32[]{:S(2)}) async-start(f32[5,32,16,128]{3,2,0,1:T(8,128)} %copy.8), calls=%async_computation | async-start | bytes 2621440 | tf_op jit(solution)/shard_map/all_to_all | solution.py:68
  133.3 14.5 %collective-permute-start.6 = (f32[5,32,4,128]{3,2,1,0:T(4,128)S(1)}, f32[5,32,4,128]{3,2,1,0:T(4,128)S(1)}, u32[]{:S(2)}, u32[]{:S(2)}) collective-permute-start(f32[5,32,4,128]{3,2,1,0:T(4,128)S(1)} %get-tuple-element.11), channel_id=1, source_target_pairs={{0,1},{1,2},{2,3},{3,4},{4,5},{5,6},{6,7},{7,8},{8,9},{9,10},{10,1... | collective-permute-start | bytes 983048 | tf_op jit(solution)/shard_map/ppermute | solution.py:40
  133.3 16.5 %collective-permute-start.7 = (f32[5,32,4,128]{3,2,1,0:T(4,128)S(1)}, f32[5,32,4,128]{3,2,1,0:T(4,128)S(1)}, u32[]{:S(2)}, u32[]{:S(2)}) collective-permute-start(f32[5,32,4,128]{3,2,1,0:T(4,128)S(1)} %get-tuple-element.12), channel_id=1, source_target_pairs={{1,0},{2,1},{3,2},{4,3},{5,4},{6,5},{7,6},{8,7},{9,8},{10,9},{11,1... | collective-permute-start | bytes 983048 | tf_op jit(solution)/shard_map/ppermute | solution.py:41
  149.9 11.9 %collective-permute-start.8 = (f32[5,4,24,128]{3,2,1,0:T(8,128)S(1)}, f32[5,4,24,128]{3,2,1,0:T(8,128)S(1)}, u32[]{:S(2)}, u32[]{:S(2)}) collective-permute-start(f32[5,4,24,128]{3,2,1,0:T(8,128)S(1)} %get-tuple-element.7), channel_id=1, source_target_pairs={{0,16},{16,32},{32,48},{48,64},{64,80},{80,96},{96,112},{112,128},... | collective-permute-start | bytes 737288 | tf_op jit(solution)/shard_map/ppermute | solution.py:43
  158.7 9.0 %collective-permute-start.9 = (f32[5,4,24,128]{3,2,1,0:T(8,128)S(1)}, f32[5,4,24,128]{3,2,1,0:T(8,128)S(1)}, u32[]{:S(2)}, u32[]{:S(2)}) collective-permute-start(f32[5,4,24,128]{3,2,1,0:T(8,128)S(1)} %get-tuple-element.8), channel_id=1, source_target_pairs={{16,0},{32,16},{48,32},{64,48},{80,64},{96,80},{112,96},{128,112},... | collective-permute-start | bytes 737288 | tf_op jit(solution)/shard_map/ppermute | solution.py:44

commit v4 on v1

--- a/solution.py
+++ b/solution.py
@@ -2,23 +2,6 @@
 import jax.numpy as jnp
 from jax import lax
 from jax.sharding import PartitionSpec as P
-
-
-def with_halo(cells, sides, width, closed):
-    for axis, dim in sides:
-        count = lax.axis_size(axis)
-        ends = count if closed else count - 1
-        head = lax.slice_in_dim(cells, 0, width, axis=dim)
-        tail = lax.slice_in_dim(cells, cells.shape[dim] - width, cells.shape[dim], axis=dim)
-        cells = jnp.concatenate(
-            [
-                lax.ppermute(tail, axis, [(i, (i + 1) % count) for i in range(ends)]),
-                cells,
-                lax.ppermute(head, axis, [((i + 1) % count, i) for i in range(ends)]),
-            ],
-            axis=dim,
-        )
-    return cells
 
 
 def stencil(padded, kap, speed_r, speed_p):
@@ -51,9 +34,16 @@
     )
 
 
-def extend(field, width):
-    beside_all = with_halo(field, (("azi", 2),), width, True)
-    return with_halo(beside_all, (("rad", 1),), width, False)
+def extend(cells, width):
+    sectors, rings = lax.axis_size("azi"), lax.axis_size("rad")
+    rows, cols = cells.shape[-3], cells.shape[-2]
+    left = lax.ppermute(cells[..., cols - width :, :], "azi", [(i, (i + 1) % sectors) for i in range(sectors)])
+    right = lax.ppermute(cells[..., :width, :], "azi", [((i + 1) % sectors, i) for i in range(sectors)])
+    above = lax.ppermute(cells[..., rows - width :, :, :], "rad", [(i, i + 1) for i in range(rings - 1)])
+    below = lax.ppermute(cells[..., :width, :, :], "rad", [(i + 1, i) for i in range(rings - 1)])
+    wide = jnp.concatenate([left, cells, right], axis=-2)
+    corners = [(0, 0)] * (cells.ndim - 2) + [(width, width), (0, 0)]
+    return jnp.concatenate([jnp.pad(above, corners), wide, jnp.pad(below, corners)], axis=-3)
 
 
 def heun_sections(field, kappa, speed_r, speed_p):

time: 188 us -> 169 us (0.90); the launches traced: 185 us -> 168 us
  waiting for transfers between devices: 58.8 us -> 45 us
  starting transfers between devices: 58.4 us -> 56.1 us
    ppermute x16, waiting for transfers between devices: 33.1 us -> 19.6 us  [the longest x4 17.1 us: extend(): lax.ppermute(cells[..., :width, :, :], 'rad', [(i + 1, i) for i in range(...]
    all_to_all x1, starting transfers between devices: 9.32 us -> 6.83 us  [shift_rows(): full = lax.all_to_all(half, 'azi', 1, 2, tiled=True)]
  transfers between devices with their start and end apart: 17 -> 17, of which waited for: 10 -> 5; matrix products, arithmetic and copies ran while one was open for 2% -> 2% of each run, Pallas kernels for 0% -> 0%
where the time goes in v4:
time: 169 us; the launch traced here: 168 us
  starting transfers between devices  56.1 us (33%)
  waiting for transfers between devices  45 us (27%)
  blocking collectives  37.1 us (22%)
  other arithmetic  18.6 us (11%)
  local copies, waits for them, and re-layouts  6.44 us (4%)
  between operations  4.48 us (3%)
    all_to_all x1, blocking collectives, shift_rows(): return lax.all_to_all(moved, 'azi', 2, 1, tiled=True)  37.1 us
    all_to_all x1, waiting for transfers between devices, shift_rows(): full = lax.all_to_all(half, 'azi', 1, 2, tiled=True)  25.4 us
    ppermute x4, starting transfers between devices, extend(): lax.ppermute(cells[..., rows - width:, :, :], 'rad', [(i, i + 1) for i in...  23.3 us
    ppermute x4, starting transfers between devices, extend(): lax.ppermute(cells[..., :width, :], 'azi', [((i + 1) % sectors, i) for i...  17.3 us
    ppermute x4, waiting for transfers between devices, extend(): lax.ppermute(cells[..., :width, :, :], 'rad', [(i + 1, i) for i in range(...  17.1 us
    mul x2, other arithmetic, heun_sections(): 0.5 * (field + first + stencil(extend(first, 2), kappa, speed_r, speed_p))  8.39 us
    ppermute x4, starting transfers between devices, extend(): lax.ppermute(cells[..., :width, :, :], 'rad', [(i + 1, i) for i in range(...  7.86 us
    add x2, other arithmetic, heun_sections(): first = field + stencil(extend(field, 2), kappa, speed_r, speed_p)  7.34 us
  transfers between devices with their start and end apart: 17, of which 5 were waited for; matrix products, arithmetic and copies ran while one was open for 2% of the time, Pallas kernels for 0%

profile of v4, /device:TPU:1, one launch (start us, length us, event | category | flops | bytes accessed | tf_op | source)
XLA Modules:
  0.0 167.7 jit_solution(10832597027105087473)
XLA Ops:
  0.0 1.0 fusion.64
  1.1 6.2 %collective-permute-start = (f32[5,2,16,128]{3,2,1,0:T(8,128)S(1)}, f32[5,2,16,128]{3,2,1,0:T(8,128)S(1)}, u32[]{:S(2)}, u32[]{:S(2)}) collective-permute-start(f32[5,2,16,128]{3,2,1,0:T(8,128)S(1)} %get-tuple-element.27), channel_id=1, source_target_pairs={{0,16},{16,32},{32,48},{48,64},{64,80},{80,96},{96,112},{112,128},... | collective-permute-start | bytes 245768 | tf_op jit(solution)/shard_map/ppermute | solution.py:42
  7.3 1.9 %collective-permute-start.3 = (f32[5,2,16,128]{3,2,1,0:T(8,128)S(1)}, f32[5,2,16,128]{3,2,1,0:T(8,128)S(1)}, u32[]{:S(2)}, u32[]{:S(2)}) collective-permute-start(f32[5,2,16,128]{3,2,1,0:T(8,128)S(1)} %get-tuple-element.28), channel_id=1, source_target_pairs={{16,0},{32,16},{48,32},{64,48},{80,64},{96,80},{112,96},{128,112},... | collective-permute-start | bytes 245768 | tf_op jit(solution)/shard_map/ppermute | solution.py:43
  9.2 1.4 fusion.65
  10.6 0.5 collective-permute-start.1
  11.1 5.4 %collective-permute-start.2 = (f32[5,32,2,128]{3,2,1,0:T(2,128)S(1)}, f32[5,32,2,128]{3,2,1,0:T(2,128)S(1)}, u32[]{:S(2)}, u32[]{:S(2)}) collective-permute-start(f32[5,32,2,128]{3,2,1,0:T(2,128)S(1)} %get-tuple-element.30), channel_id=1, source_target_pairs={{1,0},{2,1},{3,2},{4,3},{5,4},{6,5},{7,6},{8,7},{9,8},{10,9},{11,1... | collective-permute-start | bytes 491528 | tf_op jit(solution)/shard_map/ppermute | solution.py:41
  16.5 1.0 broadcast_multiply_fusion
  17.6 2.4 %collective-permute-done.2 = f32[5,32,2,128]{3,2,1,0:T(2,128)S(1)} collective-permute-done((f32[5,32,2,128]{3,2,1,0:T(2,128)S(1)}, f32[5,32,2,128]{3,2,1,0:T(2,128)S(1)}, u32[]{:S(2)}, u32[]{:S(2)}) %collective-permute-start.2) | collective-permute-done | bytes 163872 | tf_op jit(solution)/shard_map/ppermute | solution.py:41
  20.5 3.6 %fusion.15 = f32[5,32,16,128]{3,2,1,0:T(8,128)S(1)} fusion(f32[5,32,16,128]{3,2,1,0:T(8,128)S(1)} %copy-done, f32[5,32,18,128]{3,2,1,0:T(8,128)S(1)} %constant_dynamic-update-slice_fusion, f32[5,32,2,128]{3,2,1,0:T(2,128)S(1)} %collective-permute-done.1, f32[5,34,20,128]{3,2,1,0:T(8,128)S(1)} %get-tuple-element.12, ...), kind=kLoop, calls=%fused_computation.57 | loop fusion | flops 13762560 | bytes 10913024 | tf_op jit(solution)/shard_map/add | solution.py:50
  24.4 4.9 %collective-permute-start.6 = (f32[5,32,2,128]{3,2,1,0:T(2,128)S(1)}, f32[5,32,2,128]{3,2,1,0:T(2,128)S(1)}, u32[]{:S(2)}, u32[]{:S(2)}) collective-permute-start(f32[5,32,2,128]{3,2,1,0:T(2,128)S(1)} %get-tuple-element.26), channel_id=1, source_target_pairs={{1,0},{2,1},{3,2},{4,3},{5,4},{6,5},{7,6},{8,7},{9,8},{10,9},{11,1... | collective-permute-start | bytes 491528 | tf_op jit(solution)/shard_map/ppermute | solution.py:41
  29.2 6.3 %collective-permute-start.4 = (f32[5,2,16,128]{3,2,1,0:T(8,128)S(1)}, f32[5,2,16,128]{3,2,1,0:T(8,128)S(1)}, u32[]{:S(2)}, u32[]{:S(2)}) collective-permute-start(f32[5,2,16,128]{3,2,1,0:T(8,128)S(1)} %get-tuple-element.23), channel_id=1, source_target_pairs={{0,16},{16,32},{32,48},{48,64},{64,80},{80,96},{96,112},{112,128},... | collective-permute-start | bytes 245768 | tf_op jit(solution)/shard_map/ppermute | solution.py:42
  35.6 1.9 %collective-permute-start.7 = (f32[5,2,16,128]{3,2,1,0:T(8,128)S(1)}, f32[5,2,16,128]{3,2,1,0:T(8,128)S(1)}, u32[]{:S(2)}, u32[]{:S(2)}) collective-permute-start(f32[5,2,16,128]{3,2,1,0:T(8,128)S(1)} %get-tuple-element.24), channel_id=1, source_target_pairs={{16,0},{32,16},{48,32},{64,48},{80,64},{96,80},{112,96},{128,112},... | collective-permute-start | bytes 245768 | tf_op jit(solution)/shard_map/ppermute | solution.py:43
  37.5 5.3 %collective-permute-done.7 = f32[5,2,16,128]{3,2,1,0:T(8,128)S(1)} collective-permute-done((f32[5,2,16,128]{3,2,1,0:T(8,128)S(1)}, f32[5,2,16,128]{3,2,1,0:T(8,128)S(1)}, u32[]{:S(2)}, u32[]{:S(2)}) %collective-permute-start.7) | collective-permute-done | bytes 81952 | tf_op jit(solution)/shard_map/ppermute | solution.py:43
  42.9 0.4 select_maximum_fusion.5
  43.2 3.8 %fusion.27 = f32[5,32,16,128]{3,2,1,0:T(8,128)S(1)} fusion(f32[5,32,16,128]{3,2,1,0:T(8,128)S(1)} %fusion.15, f32[5,32,2,128]{3,2,1,0:T(2,128)S(1)} %collective-permute-done.6, f32[5,32,2,128]{3,2,1,0:T(2,128)S(1)} %collective-permute-done.5, f32[5,34,20,128]{3,2,1,0:T(8,128)S(1)} %get-tuple-element.10, f32[5,34,20,128]{3,2,1,0:T(8,128)S(1)} %get-tuple-element.9, ...), kind=kLoop, calls=%fused_computation.69 | loop fusion | flops 15073280 | bytes 9766144 | tf_op jit(solution)/shard_map/mul | solution.py:51
  47.1 1.1 copy.8
  48.2 6.8 %all-to-all-start = ((f32[5,32,16,128]{3,2,0,1:T(8,128)}), f32[5,32,16,128]{3,2,0,1:T(8,128)S(1)}, u32[]{:S(2)}, u32[]{:S(2)}) async-start(f32[5,32,16,128]{3,2,0,1:T(8,128)} %copy.8), calls=%async_computation | async-start | bytes 2621440 | tf_op jit(solution)/shard_map/all_to_all | solution.py:58
  55.1 0.7 fusion.66
  59.9 25.4 %all-to-all-done = f32[5,32,16,128]{3,2,0,1:T(8,128)S(1)} async-done(((f32[5,32,16,128]{3,2,0,1:T(8,128)}), f32[5,32,16,128]{3,2,0,1:T(8,128)S(1)}, u32[]{:S(2)}, u32[]{:S(2)}) %all-to-all-start) | async-done | bytes 1310752 | tf_op jit(solution)/shard_map/all_to_all | solution.py:58
  86.0 1.0 copy.11
  87.0 37.1 %all_to_all.36 = f32[5,2,256,128]{3,1,0,2:T(2,128)S(1)} all-to-all(f32[5,2,256,128]{3,1,0,2:T(2,128)S(1)} %copy.11), channel_id=1, replica_groups=mesh['rad'=16,'azi'=16] {'azi'}, dimensions={2} | all-to-all | bytes 2621440 | tf_op jit(solution)/shard_map/all_to_all | solution.py:68
  124.7 3.5 %collective-permute-start.10 = (f32[5,32,2,128]{3,2,1,0:T(2,128)S(1)}, f32[5,32,2,128]{3,2,1,0:T(2,128)S(1)}, u32[]{:S(2)}, u32[]{:S(2)}) collective-permute-start(f32[5,32,2,128]{3,2,1,0:T(2,128)S(1)} %get-tuple-element.20), channel_id=1, source_target_pairs={{1,0},{2,1},{3,2},{4,3},{5,4},{6,5},{7,6},{8,7},{9,8},{10,9},{11,1... | collective-permute-start | bytes 491528 | tf_op jit(solution)/shard_map/ppermute | solution.py:41
  128.3 8.3 %collective-permute-start.8 = (f32[5,2,16,128]{3,2,1,0:T(8,128)S(1)}, f32[5,2,16,128]{3,2,1,0:T(8,128)S(1)}, u32[]{:S(2)}, u32[]{:S(2)}) collective-permute-start(f32[5,2,16,128]{3,2,1,0:T(8,128)S(1)} %get-tuple-element.17), channel_id=1, source_target_pairs={{0,16},{16,32},{32,48},{48,64},{64,80},{80,96},{96,112},{112,128},... | collective-permute-start | bytes 245768 | tf_op jit(solution)/shard_map/ppermute | solution.py:42
  136.6 2.1 %collective-permute-start.11 = (f32[5,2,16,128]{3,2,1,0:T(8,128)S(1)}, f32[5,2,16,128]{3,2,1,0:T(8,128)S(1)}, u32[]{:S(2)}, u32[]{:S(2)}) collective-permute-start(f32[5,2,16,128]{3,2,1,0:T(8,128)S(1)} %get-tuple-element.18), channel_id=1, source_target_pairs={{16,0},{32,16},{48,32},{64,48},{80,64},{96,80},{112,96},{128,112},... | collective-permute-start | bytes 245768 | tf_op jit(solution)/shard_map/ppermute | solution.py:43
  138.7 5.1 %collective-permute-done.11 = f32[5,2,16,128]{3,2,1,0:T(8,128)S(1)} collective-permute-done((f32[5,2,16,128]{3,2,1,0:T(8,128)S(1)}, f32[5,2,16,128]{3,2,1,0:T(8,128)S(1)}, u32[]{:S(2)}, u32[]{:S(2)}) %collective-permute-start.11) | collective-permute-done | bytes 81952 | tf_op jit(solution)/shard_map/ppermute | solution.py:43
  144.2 3.7 %fusion.38 = f32[5,32,16,128]{3,2,1,0:T(8,128)S(1)} fusion(f32[5,32,16,128]{3,2,1,0:T(8,128)S(1)} %bitcast.13, f32[5,32,2,128]{3,2,1,0:T(2,128)S(1)} %collective-permute-done.10, f32[5,32,2,128]{3,2,1,0:T(2,128)S(1)} %collective-permute-done.9, f32[5,34,20,128]{3,2,1,0:T(8,128)S(1)} %get-tuple-element.8, f32[5,34,20,128]{3,2,1,0:T(8,128)S(1)} %get-tuple-element.7, ...), kind=kLoop, calls=%fused_computation.80 | loop fusion | flops 14417920 | bytes 8455424 | tf_op jit(solution)/shard_map/add | solution.py:50
  148.2 3.6 %collective-permute-start.14 = (f32[5,32,2,128]{3,2,1,0:T(2,128)S(1)}, f32[5,32,2,128]{3,2,1,0:T(2,128)S(1)}, u32[]{:S(2)}, u32[]{:S(2)}) collective-permute-start(f32[5,32,2,128]{3,2,1,0:T(2,128)S(1)} %get-tuple-element.16), channel_id=1, source_target_pairs={{1,0},{2,1},{3,2},{4,3},{5,4},{6,5},{7,6},{8,7},{9,8},{10,9},{11,1... | collective-permute-start | bytes 491528 | tf_op jit(solution)/shard_map/ppermute | solution.py:41
  151.7 2.4 %collective-permute-start.12 = (f32[5,2,16,128]{3,2,1,0:T(8,128)S(1)}, f32[5,2,16,128]{3,2,1,0:T(8,128)S(1)}, u32[]{:S(2)}, u32[]{:S(2)}) collective-permute-start(f32[5,2,16,128]{3,2,1,0:T(8,128)S(1)} %get-tuple-element.13), channel_id=1, source_target_pairs={{0,16},{16,32},{32,48},{48,64},{64,80},{80,96},{96,112},{112,128},... | collective-permute-start | bytes 245768 | tf_op jit(solution)/shard_map/ppermute | solution.py:42
  154.1 1.9 %collective-permute-start.15 = (f32[5,2,16,128]{3,2,1,0:T(8,128)S(1)}, f32[5,2,16,128]{3,2,1,0:T(8,128)S(1)}, u32[]{:S(2)}, u32[]{:S(2)}) collective-permute-start(f32[5,2,16,128]{3,2,1,0:T(8,128)S(1)} %get-tuple-element.14), channel_id=1, source_target_pairs={{16,0},{32,16},{48,32},{64,48},{80,64},{96,80},{112,96},{128,112},... | collective-permute-start | bytes 245768 | tf_op jit(solution)/shard_map/ppermute | solution.py:43
  156.1 6.6 %collective-permute-done.15 = f32[5,2,16,128]{3,2,1,0:T(8,128)S(1)} collective-permute-done((f32[5,2,16,128]{3,2,1,0:T(8,128)S(1)}, f32[5,2,16,128]{3,2,1,0:T(8,128)S(1)}, u32[]{:S(2)}, u32[]{:S(2)}) %collective-permute-start.15) | collective-permute-done | bytes 81952 | tf_op jit(solution)/shard_map/ppermute | solution.py:43
  162.7 0.4 select_maximum_fusion.1
  163.1 4.6 %fusion.50 = f32[5,32,16,128]{3,2,1,0:T(8,128)} fusion(f32[5,32,16,128]{3,2,1,0:T(8,128)S(1)} %fusion.38, f32[5,32,2,128]{3,2,1,0:T(2,128)S(1)} %collective-permute-done.14, f32[5,32,2,128]{3,2,1,0:T(2,128)S(1)} %collective-permute-done.13, f32[5,34,20,128]{3,2,1,0:T(8,128)S(1)} %get-tuple-element.6, f32[5,34,20,128]{3,2,1,0:T(8,128)S(1)} %get-tuple-element.5, ...), kind=kLoop, calls=%fused_computation.92 | loop fusion | flops 15073280 | bytes 9766144 | tf_op jit(solution)/shard_map/mul | solution.py:51
  (42 shorter events, 2.6 us)
Async XLA Ops:
  0.0 17.5 %copy-start = (f32[5,32,16,128]{3,2,1,0:T(8,128)S(1)}, f32[5,32,16,128]{3,2,1,0:T(8,128)}, u32[]{:S(2)}) copy-start(f32[5,32,16,128]{3,2,1,0:T(8,128)} %param.5) | copy-start | bytes 3932164
  0.0 17.5 %copy-start.2 = (f32[5,32]{1,0:T(8,128)S(1)}, f32[5,32]{1,0:T(8,128)}, u32[]{:S(2)}) copy-start(f32[5,32]{1,0:T(8,128)} %param.8) | copy-start | bytes 1924
  0.0 17.5 %copy-start.1 = (f32[5,32]{1,0:T(8,128)S(1)}, f32[5,32]{1,0:T(8,128)}, u32[]{:S(2)}) copy-start(f32[5,32]{1,0:T(8,128)} %param.7) | copy-start | bytes 1924
  1.1 19.0 %collective-permute-start = (f32[5,2,16,128]{3,2,1,0:T(8,128)S(1)}, f32[5,2,16,128]{3,2,1,0:T(8,128)S(1)}, u32[]{:S(2)}, u32[]{:S(2)}) collective-permute-start(f32[5,2,16,128]{3,2,1,0:T(8,128)S(1)} %get-tuple-element.27), channel_id=1, source_target_pairs={{0,16},{16,32},{32,48},{48,64},{64,80},{80,96},{96,112},{112,128},... | collective-permute-start | bytes 245768 | tf_op jit(solution)/shard_map/ppermute | solution.py:42
  7.3 12.8 %collective-permute-start.3 = (f32[5,2,16,128]{3,2,1,0:T(8,128)S(1)}, f32[5,2,16,128]{3,2,1,0:T(8,128)S(1)}, u32[]{:S(2)}, u32[]{:S(2)}) collective-permute-start(f32[5,2,16,128]{3,2,1,0:T(8,128)S(1)} %get-tuple-element.28), channel_id=1, source_target_pairs={{16,0},{32,16},{48,32},{64,48},{80,64},{96,80},{112,96},{128,112},... | collective-permute-start | bytes 245768 | tf_op jit(solution)/shard_map/ppermute | solution.py:43
  10.6 9.5 %collective-permute-start.1 = (f32[5,32,2,128]{3,2,1,0:T(2,128)S(1)}, f32[5,32,2,128]{3,2,1,0:T(2,128)S(1)}, u32[]{:S(2)}, u32[]{:S(2)}) collective-permute-start(f32[5,32,2,128]{3,2,1,0:T(2,128)S(1)} %get-tuple-element.29), channel_id=1, source_target_pairs={{0,1},{1,2},{2,3},{3,4},{4,5},{5,6},{6,7},{7,8},{8,9},{9,10},{10,1... | collective-permute-start | bytes 491528 | tf_op jit(solution)/shard_map/ppermute | solution.py:40
  11.1 8.9 %collective-permute-start.2 = (f32[5,32,2,128]{3,2,1,0:T(2,128)S(1)}, f32[5,32,2,128]{3,2,1,0:T(2,128)S(1)}, u32[]{:S(2)}, u32[]{:S(2)}) collective-permute-start(f32[5,32,2,128]{3,2,1,0:T(2,128)S(1)} %get-tuple-element.30), channel_id=1, source_target_pairs={{1,0},{2,1},{3,2},{4,3},{5,4},{6,5},{7,6},{8,7},{9,8},{10,9},{11,1... | collective-permute-start | bytes 491528 | tf_op jit(solution)/shard_map/ppermute | solution.py:41
  24.3 18.6 %collective-permute-start.5 = (f32[5,32,2,128]{3,2,1,0:T(2,128)S(1)}, f32[5,32,2,128]{3,2,1,0:T(2,128)S(1)}, u32[]{:S(2)}, u32[]{:S(2)}) collective-permute-start(f32[5,32,2,128]{3,2,1,0:T(2,128)S(1)} %get-tuple-element.25), channel_id=1, source_target_pairs={{0,1},{1,2},{2,3},{3,4},{4,5},{5,6},{6,7},{7,8},{8,9},{9,10},{10,1... | collective-permute-start | bytes 491528 | tf_op jit(solution)/shard_map/ppermute | solution.py:40
  24.4 18.5 %collective-permute-start.6 = (f32[5,32,2,128]{3,2,1,0:T(2,128)S(1)}, f32[5,32,2,128]{3,2,1,0:T(2,128)S(1)}, u32[]{:S(2)}, u32[]{:S(2)}) collective-permute-start(f32[5,32,2,128]{3,2,1,0:T(2,128)S(1)} %get-tuple-element.26), channel_id=1, source_target_pairs={{1,0},{2,1},{3,2},{4,3},{5,4},{6,5},{7,6},{8,7},{9,8},{10,9},{11,1... | collective-permute-start | bytes 491528 | tf_op jit(solution)/shard_map/ppermute | solution.py:41
  29.2 8.3 %collective-permute-start.4 = (f32[5,2,16,128]{3,2,1,0:T(8,128)S(1)}, f32[5,2,16,128]{3,2,1,0:T(8,128)S(1)}, u32[]{:S(2)}, u32[]{:S(2)}) collective-permute-start(f32[5,2,16,128]{3,2,1,0:T(8,128)S(1)} %get-tuple-element.23), channel_id=1, source_target_pairs={{0,16},{16,32},{32,48},{48,64},{64,80},{80,96},{96,112},{112,128},... | collective-permute-start | bytes 245768 | tf_op jit(solution)/shard_map/ppermute | solution.py:42
  35.6 7.3 %collective-permute-start.7 = (f32[5,2,16,128]{3,2,1,0:T(8,128)S(1)}, f32[5,2,16,128]{3,2,1,0:T(8,128)S(1)}, u32[]{:S(2)}, u32[]{:S(2)}) collective-permute-start(f32[5,2,16,128]{3,2,1,0:T(8,128)S(1)} %get-tuple-element.24), channel_id=1, source_target_pairs={{16,0},{32,16},{48,32},{64,48},{80,64},{96,80},{112,96},{128,112},... | collective-permute-start | bytes 245768 | tf_op jit(solution)/shard_map/ppermute | solution.py:43
  48.2 6.8 %copy-start.3 = (s32[32]{0:T(128)S(1)}, s32[32]{0:T(128)}, u32[]{:S(2)}) copy-start(s32[32]{0:T(128)} %param.9) | copy-start | bytes 388
  48.2 37.1 %all-to-all-start = ((f32[5,32,16,128]{3,2,0,1:T(8,128)}), f32[5,32,16,128]{3,2,0,1:T(8,128)S(1)}, u32[]{:S(2)}, u32[]{:S(2)}) async-start(f32[5,32,16,128]{3,2,0,1:T(8,128)} %copy.8), calls=%async_computation | async-start | bytes 2621440 | tf_op jit(solution)/shard_map/all_to_all | solution.py:58
  124.6 19.3 %collective-permute-start.9 = (f32[5,32,2,128]{3,2,1,0:T(2,128)S(1)}, f32[5,32,2,128]{3,2,1,0:T(2,128)S(1)}, u32[]{:S(2)}, u32[]{:S(2)}) collective-permute-start(f32[5,32,2,128]{3,2,1,0:T(2,128)S(1)} %get-tuple-element.19), channel_id=1, source_target_pairs={{0,1},{1,2},{2,3},{3,4},{4,5},{5,6},{6,7},{7,8},{8,9},{9,10},{10,1... | collective-permute-start | bytes 491528 | tf_op jit(solution)/shard_map/ppermute | solution.py:40
  124.7 19.2 %collective-permute-start.10 = (f32[5,32,2,128]{3,2,1,0:T(2,128)S(1)}, f32[5,32,2,128]{3,2,1,0:T(2,128)S(1)}, u32[]{:S(2)}, u32[]{:S(2)}) collective-permute-start(f32[5,32,2,128]{3,2,1,0:T(2,128)S(1)} %get-tuple-element.20), channel_id=1, source_target_pairs={{1,0},{2,1},{3,2},{4,3},{5,4},{6,5},{7,6},{8,7},{9,8},{10,9},{11,1... | collective-permute-start | bytes 491528 | tf_op jit(solution)/shard_map/ppermute | solution.py:41
  128.3 10.4 %collective-permute-start.8 = (f32[5,2,16,128]{3,2,1,0:T(8,128)S(1)}, f32[5,2,16,128]{3,2,1,0:T(8,128)S(1)}, u32[]{:S(2)}, u32[]{:S(2)}) collective-permute-start(f32[5,2,16,128]{3,2,1,0:T(8,128)S(1)} %get-tuple-element.17), channel_id=1, source_target_pairs={{0,16},{16,32},{32,48},{48,64},{64,80},{80,96},{96,112},{112,128},... | collective-permute-start | bytes 245768 | tf_op jit(solution)/shard_map/ppermute | solution.py:42
  136.6 7.3 %collective-permute-start.11 = (f32[5,2,16,128]{3,2,1,0:T(8,128)S(1)}, f32[5,2,16,128]{3,2,1,0:T(8,128)S(1)}, u32[]{:S(2)}, u32[]{:S(2)}) collective-permute-start(f32[5,2,16,128]{3,2,1,0:T(8,128)S(1)} %get-tuple-element.18), channel_id=1, source_target_pairs={{16,0},{32,16},{48,32},{64,48},{80,64},{96,80},{112,96},{128,112},... | collective-permute-start | bytes 245768 | tf_op jit(solution)/shard_map/ppermute | solution.py:43
  148.1 14.7 %collective-permute-start.13 = (f32[5,32,2,128]{3,2,1,0:T(2,128)S(1)}, f32[5,32,2,128]{3,2,1,0:T(2,128)S(1)}, u32[]{:S(2)}, u32[]{:S(2)}) collective-permute-start(f32[5,32,2,128]{3,2,1,0:T(2,128)S(1)} %get-tuple-element.15), channel_id=1, source_target_pairs={{0,1},{1,2},{2,3},{3,4},{4,5},{5,6},{6,7},{7,8},{8,9},{9,10},{10,1... | collective-permute-start | bytes 491528 | tf_op jit(solution)/shard_map/ppermute | solution.py:40
  148.2 14.6 %collective-permute-start.14 = (f32[5,32,2,128]{3,2,1,0:T(2,128)S(1)}, f32[5,32,2,128]{3,2,1,0:T(2,128)S(1)}, u32[]{:S(2)}, u32[]{:S(2)}) collective-permute-start(f32[5,32,2,128]{3,2,1,0:T(2,128)S(1)} %get-tuple-element.16), channel_id=1, source_target_pairs={{1,0},{2,1},{3,2},{4,3},{5,4},{6,5},{7,6},{8,7},{9,8},{10,9},{11,1... | collective-permute-start | bytes 491528 | tf_op jit(solution)/shard_map/ppermute | solution.py:41
  151.7 4.3 %collective-permute-start.12 = (f32[5,2,16,128]{3,2,1,0:T(8,128)S(1)}, f32[5,2,16,128]{3,2,1,0:T(8,128)S(1)}, u32[]{:S(2)}, u32[]{:S(2)}) collective-permute-start(f32[5,2,16,128]{3,2,1,0:T(8,128)S(1)} %get-tuple-element.13), channel_id=1, source_target_pairs={{0,16},{16,32},{32,48},{48,64},{64,80},{80,96},{96,112},{112,128},... | collective-permute-start | bytes 245768 | tf_op jit(solution)/shard_map/ppermute | solution.py:42
  154.1 8.6 %collective-permute-start.15 = (f32[5,2,16,128]{3,2,1,0:T(8,128)S(1)}, f32[5,2,16,128]{3,2,1,0:T(8,128)S(1)}, u32[]{:S(2)}, u32[]{:S(2)}) collective-permute-start(f32[5,2,16,128]{3,2,1,0:T(8,128)S(1)} %get-tuple-element.14), channel_id=1, source_target_pairs={{16,0},{32,16},{48,32},{64,48},{80,64},{96,80},{112,96},{128,112},... | collective-permute-start | bytes 245768 | tf_op jit(solution)/shard_map/ppermute | solution.py:43

commit v5 on v4

--- a/solution.py
+++ b/solution.py
@@ -69,9 +69,13 @@
 
 
 def shards(fields, kappa, radial_speed, azimuth_speed, shifts):
-    half = heun_sections(fields, kappa, radial_speed, azimuth_speed)
-    moved = shift_rows(half, shifts)
-    return heun_sections(moved, kappa, radial_speed, azimuth_speed)
+    fcount = fields.shape[0]
+    bounds = [0, (fcount + 1) // 2, fcount]
+    groups = [(fields[lo:hi], radial_speed[lo:hi], azimuth_speed[lo:hi]) for lo, hi in zip(bounds, bounds[1:])]
+    halves = [heun_sections(f, kappa, r, p) for f, r, p in groups]
+    moved = [shift_rows(h, shifts) for h in halves]
+    done = [heun_sections(m, kappa, r, p) for m, (_, r, p) in zip(moved, groups)]
+    return jnp.concatenate(done, axis=0)
 
 
 def solution(mesh):

time: 169 us -> 202 us (1.20)
  starting transfers between devices: 56.1 us -> 122 us
  blocking collectives: 37.1 us -> 0 us
  local copies, waits for them, and re-layouts: 6.44 us -> 10.2 us
    all_to_all x1 -> x0, blocking collectives: 37.1 us -> none  [shift_rows(): return lax.all_to_all(moved, 'azi', 2, 1, tiled=True)]
    ppermute x4 -> x8, starting transfers between devices: 23.3 us -> 56.1 us  [extend(): lax.ppermute(cells[..., rows - width:, :, :], 'rad', [(i, i + 1) for i in...]
    all_to_all x1 -> x2, waiting for transfers between devices: 25.4 us -> 11.9 us  [shift_rows(): full = lax.all_to_all(half, 'azi', 1, 2, tiled=True)]
    all_to_all x0 -> x2, waiting for transfers between devices: none -> 11.9 us  [shift_rows(): return lax.all_to_all(moved, 'azi', 2, 1, tiled=True)]
    all_to_all x1 -> x2, starting transfers between devices: 6.83 us -> 14.9 us  [shift_rows(): full = lax.all_to_all(half, 'azi', 1, 2, tiled=True)]
    ppermute x4 -> x8, starting transfers between devices: 7.86 us -> 15.5 us  [extend(): lax.ppermute(cells[..., :width, :, :], 'rad', [(i + 1, i) for i in range(...]
    all_to_all x0 -> x2, starting transfers between devices: none -> 7.19 us  [shift_rows(): return lax.all_to_all(moved, 'azi', 2, 1, tiled=True)]
    ppermute x4 -> x8, starting transfers between devices: 0.76 us -> 6.9 us  [extend(): lax.ppermute(cells[..., cols - width:, :], 'azi', [(i, (i + 1) % sectors)...]
  transfers between devices with their start and end apart: 17 -> 36, of which waited for: 5 -> 9; matrix products, arithmetic and copies ran while one was open for 2% -> 10% of each run, Pallas kernels for 0% -> 0%
where the time goes in v5:
time: 202 us; the launch traced here: 200 us
  starting transfers between devices  122 us (60%)
  waiting for transfers between devices  45.5 us (23%)
  other arithmetic  17.7 us (9%)
  local copies, waits for them, and re-layouts  10.2 us (5%)
  between operations  4.44 us (2%)
    ppermute x8, starting transfers between devices, extend(): lax.ppermute(cells[..., rows - width:, :, :], 'rad', [(i, i + 1) for i in...  56.1 us
    ppermute x8, starting transfers between devices, extend(): lax.ppermute(cells[..., :width, :], 'azi', [((i + 1) % sectors, i) for i...  21.7 us
    ppermute x8, waiting for transfers between devices, extend(): lax.ppermute(cells[..., :width, :, :], 'rad', [(i + 1, i) for i in range(...  20.9 us
    ppermute x8, starting transfers between devices, extend(): lax.ppermute(cells[..., :width, :, :], 'rad', [(i + 1, i) for i in range(...  15.5 us
    all_to_all x2, starting transfers between devices, shift_rows(): full = lax.all_to_all(half, 'azi', 1, 2, tiled=True)  14.9 us
    all_to_all x2, waiting for transfers between devices, shift_rows(): full = lax.all_to_all(half, 'azi', 1, 2, tiled=True)  11.9 us
    all_to_all x2, waiting for transfers between devices, shift_rows(): return lax.all_to_all(moved, 'azi', 2, 1, tiled=True)  11.9 us
    all_to_all x2, starting transfers between devices, shift_rows(): return lax.all_to_all(moved, 'azi', 2, 1, tiled=True)  7.19 us
  transfers between devices with their start and end apart: 36, of which 9 were waited for; matrix products, arithmetic and copies ran while one was open for 10% of the time, Pallas kernels for 0%

profile of v5, /device:TPU:1, one launch (start us, length us, event | category | flops | bytes accessed | tf_op | source)
XLA Modules:
  0.0 200.2 jit_solution(1181467208800410658)
XLA Ops:
  1.3 2.2 %collective-permute-start.1 = (f32[3,32,2,128]{3,2,1,0:T(2,128)S(1)}, f32[3,32,2,128]{3,2,1,0:T(2,128)S(1)}, u32[]{:S(2)}, u32[]{:S(2)}) collective-permute-start(f32[3,32,2,128]{3,2,1,0:T(2,128)S(1)} %get-tuple-element.7), channel_id=1, source_target_pairs={{0,1},{1,2},{2,3},{3,4},{4,5},{5,6},{6,7},{7,8},{8,9},{9,10},{10,1... | collective-permute-start | bytes 294920 | tf_op jit(solution)/shard_map/ppermute | solution.py:40
  6.2 3.9 %collective-permute-start.18 = (f32[2,32,2,128]{3,2,1,0:T(2,128)S(1)}, f32[2,32,2,128]{3,2,1,0:T(2,128)S(1)}, u32[]{:S(2)}, u32[]{:S(2)}) collective-permute-start(f32[2,32,2,128]{3,2,1,0:T(2,128)S(1)} %get-tuple-element.12), channel_id=1, source_target_pairs={{1,0},{2,1},{3,2},{4,3},{5,4},{6,5},{7,6},{8,7},{9,8},{10,9},{11,1... | collective-permute-start | bytes 196616 | tf_op jit(solution)/shard_map/ppermute | solution.py:41
  10.8 5.4 %collective-permute-start.16 = (f32[2,2,16,128]{3,2,1,0:T(8,128)S(1)}, f32[2,2,16,128]{3,2,1,0:T(8,128)S(1)}, u32[]{:S(2)}, u32[]{:S(2)}) collective-permute-start(f32[2,2,16,128]{3,2,1,0:T(8,128)S(1)} %get-tuple-element.9), channel_id=1, source_target_pairs={{0,16},{16,32},{32,48},{48,64},{64,80},{80,96},{96,112},{112,128},... | collective-permute-start | bytes 98312 | tf_op jit(solution)/shard_map/ppermute | solution.py:42
  21.3 2.2 %collective-permute-done.19 = f32[2,2,16,128]{3,2,1,0:T(8,128)S(1)} collective-permute-done((f32[2,2,16,128]{3,2,1,0:T(8,128)S(1)}, f32[2,2,16,128]{3,2,1,0:T(8,128)S(1)}, u32[]{:S(2)}, u32[]{:S(2)}) %collective-permute-start.19) | collective-permute-done | bytes 32800 | tf_op jit(solution)/shard_map/ppermute | solution.py:43
  23.5 3.9 %collective-permute-start = (f32[3,2,16,128]{3,2,1,0:T(8,128)S(1)}, f32[3,2,16,128]{3,2,1,0:T(8,128)S(1)}, u32[]{:S(2)}, u32[]{:S(2)}) collective-permute-start(f32[3,2,16,128]{3,2,1,0:T(8,128)S(1)} %get-tuple-element.5), channel_id=1, source_target_pairs={{0,16},{16,32},{32,48},{48,64},{64,80},{80,96},{96,112},{112,128},... | collective-permute-start | bytes 147464 | tf_op jit(solution)/shard_map/ppermute | solution.py:42
  27.4 1.9 collective-permute-start.3
  30.9 3.6 %collective-permute-start.22 = (f32[2,32,2,128]{3,2,1,0:T(2,128)S(1)}, f32[2,32,2,128]{3,2,1,0:T(2,128)S(1)}, u32[]{:S(2)}, u32[]{:S(2)}) collective-permute-start(f32[2,32,2,128]{3,2,1,0:T(2,128)S(1)} %get-tuple-element.56), channel_id=1, source_target_pairs={{1,0},{2,1},{3,2},{4,3},{5,4},{6,5},{7,6},{8,7},{9,8},{10,9},{11,1... | collective-permute-start | bytes 196616 | tf_op jit(solution)/shard_map/ppermute | solution.py:41
  34.6 5.6 %collective-permute-start.20 = (f32[2,2,16,128]{3,2,1,0:T(8,128)S(1)}, f32[2,2,16,128]{3,2,1,0:T(8,128)S(1)}, u32[]{:S(2)}, u32[]{:S(2)}) collective-permute-start(f32[2,2,16,128]{3,2,1,0:T(8,128)S(1)} %get-tuple-element.53), channel_id=1, source_target_pairs={{0,16},{16,32},{32,48},{48,64},{64,80},{80,96},{96,112},{112,128},... | collective-permute-start | bytes 98312 | tf_op jit(solution)/shard_map/ppermute | solution.py:42
  42.3 2.1 %fusion.16 = f32[3,32,16,128]{3,2,1,0:T(8,128)S(1)} fusion(f32[3,32,16,128]{3,2,1,0:T(8,128)S(1)} %slice.558, f32[3,32,2,128]{3,2,1,0:T(2,128)S(1)} %collective-permute-done.2, f32[3,32,2,128]{3,2,1,0:T(2,128)S(1)} %collective-permute-done.1, f32[3,34,20,128]{3,2,1,0:T(8,128)S(1)} %get-tuple-element.20, f32[3,34,20,128]{3,2,1,0:T(8,128)S(1)} %get-tuple-element.19, ...), kind=kLoop, calls=%fused_computation.89 | loop fusion | flops 8650752 | bytes 5178112 | tf_op jit(solution)/shard_map/add | solution.py:50
  44.6 3.6 %collective-permute-start.6 = (f32[3,32,2,128]{3,2,1,0:T(2,128)S(1)}, f32[3,32,2,128]{3,2,1,0:T(2,128)S(1)}, u32[]{:S(2)}, u32[]{:S(2)}) collective-permute-start(f32[3,32,2,128]{3,2,1,0:T(2,128)S(1)} %get-tuple-element.34), channel_id=1, source_target_pairs={{1,0},{2,1},{3,2},{4,3},{5,4},{6,5},{7,6},{8,7},{9,8},{10,9},{11,1... | collective-permute-start | bytes 294920 | tf_op jit(solution)/shard_map/ppermute | solution.py:41
  50.5 5.8 %all-to-all-start.2 = ((f32[2,32,16,128]{3,2,0,1:T(8,128)}), f32[2,32,16,128]{3,2,0,1:T(8,128)S(1)}, u32[]{:S(2)}, u32[]{:S(2)}) async-start(f32[2,32,16,128]{3,2,0,1:T(8,128)} %copy.16), calls=%async_computation.2 | async-start | bytes 1048576 | tf_op jit(solution)/shard_map/all_to_all | solution.py:58
  56.3 6.0 %collective-permute-start.4 = (f32[3,2,16,128]{3,2,1,0:T(8,128)S(1)}, f32[3,2,16,128]{3,2,1,0:T(8,128)S(1)}, u32[]{:S(2)}, u32[]{:S(2)}) collective-permute-start(f32[3,2,16,128]{3,2,1,0:T(8,128)S(1)} %get-tuple-element.31), channel_id=1, source_target_pairs={{0,16},{16,32},{32,48},{48,64},{64,80},{80,96},{96,112},{112,128},... | collective-permute-start | bytes 147464 | tf_op jit(solution)/shard_map/ppermute | solution.py:42
  62.3 2.1 %collective-permute-start.7 = (f32[3,2,16,128]{3,2,1,0:T(8,128)S(1)}, f32[3,2,16,128]{3,2,1,0:T(8,128)S(1)}, u32[]{:S(2)}, u32[]{:S(2)}) collective-permute-start(f32[3,2,16,128]{3,2,1,0:T(8,128)S(1)} %get-tuple-element.32), channel_id=1, source_target_pairs={{16,0},{32,16},{48,32},{64,48},{80,64},{96,80},{112,96},{128,112},... | collective-permute-start | bytes 147464 | tf_op jit(solution)/shard_map/ppermute | solution.py:43
  64.4 5.1 %collective-permute-done.7 = f32[3,2,16,128]{3,2,1,0:T(8,128)S(1)} collective-permute-done((f32[3,2,16,128]{3,2,1,0:T(8,128)S(1)}, f32[3,2,16,128]{3,2,1,0:T(8,128)S(1)}, u32[]{:S(2)}, u32[]{:S(2)}) %collective-permute-start.7) | collective-permute-done | bytes 49184 | tf_op jit(solution)/shard_map/ppermute | solution.py:43
  69.8 2.1 %fusion.28 = f32[3,32,16,128]{3,2,1,0:T(8,128)S(1)} fusion(f32[3,32,16,128]{3,2,1,0:T(8,128)S(1)} %fusion.16, f32[3,32,2,128]{3,2,1,0:T(2,128)S(1)} %collective-permute-done.6, f32[3,32,2,128]{3,2,1,0:T(2,128)S(1)} %collective-permute-done.5, f32[3,34,20,128]{3,2,1,0:T(8,128)S(1)} %get-tuple-element.18, f32[3,34,20,128]{3,2,1,0:T(8,128)S(1)} %get-tuple-element.17, ...), kind=kLoop, calls=%fused_computation.101 | loop fusion | flops 9043968 | bytes 5964544 | tf_op jit(solution)/shard_map/mul | solution.py:51
  72.8 9.1 %all-to-all-start = ((f32[3,32,16,128]{3,2,0,1:T(8,128)}), f32[3,32,16,128]{3,2,0,1:T(8,128)S(1)}, u32[]{:S(2)}, u32[]{:S(2)}) async-start(f32[3,32,16,128]{3,2,0,1:T(8,128)} %copy.10), calls=%async_computation | async-start | bytes 1572864 | tf_op jit(solution)/shard_map/all_to_all | solution.py:58
  88.0 11.9 %all-to-all-done = f32[3,32,16,128]{3,2,0,1:T(8,128)S(1)} async-done(((f32[3,32,16,128]{3,2,0,1:T(8,128)}), f32[3,32,16,128]{3,2,0,1:T(8,128)S(1)}, u32[]{:S(2)}, u32[]{:S(2)}) %all-to-all-start) | async-done | bytes 786464 | tf_op jit(solution)/shard_map/all_to_all | solution.py:58
  99.9 3.6 %all-to-all-start.3 = ((f32[2,2,256,128]{3,1,0,2:T(2,128)}), f32[2,2,256,128]{3,1,0,2:T(2,128)S(1)}, u32[]{:S(2)}, u32[]{:S(2)}) async-start(f32[2,2,256,128]{3,1,0,2:T(2,128)} %copy.19), calls=%async_computation.3 | async-start | bytes 1048576 | tf_op jit(solution)/shard_map/all_to_all | solution.py:68
  105.4 11.9 %all-to-all-done.3 = f32[2,2,256,128]{3,1,0,2:T(2,128)S(1)} async-done(((f32[2,2,256,128]{3,1,0,2:T(2,128)}), f32[2,2,256,128]{3,1,0,2:T(2,128)S(1)}, u32[]{:S(2)}, u32[]{:S(2)}) %all-to-all-start.3) | async-done | bytes 524320 | tf_op jit(solution)/shard_map/all_to_all | solution.py:68
  117.3 3.6 %all-to-all-start.1 = ((f32[3,2,256,128]{3,1,0,2:T(2,128)}), f32[3,2,256,128]{3,1,0,2:T(2,128)S(1)}, u32[]{:S(2)}, u32[]{:S(2)}) async-start(f32[3,2,256,128]{3,1,0,2:T(2,128)} %copy.13), calls=%async_computation.1 | async-start | bytes 1572864 | tf_op jit(solution)/shard_map/all_to_all | solution.py:68
  122.4 2.3 %collective-permute-start.26 = (f32[2,32,2,128]{3,2,1,0:T(2,128)S(1)}, f32[2,32,2,128]{3,2,1,0:T(2,128)S(1)}, u32[]{:S(2)}, u32[]{:S(2)}) collective-permute-start(f32[2,32,2,128]{3,2,1,0:T(2,128)S(1)} %get-tuple-element.50), channel_id=1, source_target_pairs={{1,0},{2,1},{3,2},{4,3},{5,4},{6,5},{7,6},{8,7},{9,8},{10,9},{11,1... | collective-permute-start | bytes 196616 | tf_op jit(solution)/shard_map/ppermute | solution.py:41
  124.7 13.5 %collective-permute-start.24 = (f32[2,2,16,128]{3,2,1,0:T(8,128)S(1)}, f32[2,2,16,128]{3,2,1,0:T(8,128)S(1)}, u32[]{:S(2)}, u32[]{:S(2)}) collective-permute-start(f32[2,2,16,128]{3,2,1,0:T(8,128)S(1)} %get-tuple-element.47), channel_id=1, source_target_pairs={{0,16},{16,32},{32,48},{48,64},{64,80},{80,96},{96,112},{112,128},... | collective-permute-start | bytes 98312 | tf_op jit(solution)/shard_map/ppermute | solution.py:42
  140.2 5.0 %collective-permute-done.27 = f32[2,2,16,128]{3,2,1,0:T(8,128)S(1)} collective-permute-done((f32[2,2,16,128]{3,2,1,0:T(8,128)S(1)}, f32[2,2,16,128]{3,2,1,0:T(8,128)S(1)}, u32[]{:S(2)}, u32[]{:S(2)}) %collective-permute-start.27) | collective-permute-done | bytes 32800 | tf_op jit(solution)/shard_map/ppermute | solution.py:43
  146.7 3.6 %collective-permute-start.30 = (f32[2,32,2,128]{3,2,1,0:T(2,128)S(1)}, f32[2,32,2,128]{3,2,1,0:T(2,128)S(1)}, u32[]{:S(2)}, u32[]{:S(2)}) collective-permute-start(f32[2,32,2,128]{3,2,1,0:T(2,128)S(1)} %get-tuple-element.46), channel_id=1, source_target_pairs={{1,0},{2,1},{3,2},{4,3},{5,4},{6,5},{7,6},{8,7},{9,8},{10,9},{11,1... | collective-permute-start | bytes 196616 | tf_op jit(solution)/shard_map/ppermute | solution.py:41
  150.3 10.2 %collective-permute-start.28 = (f32[2,2,16,128]{3,2,1,0:T(8,128)S(1)}, f32[2,2,16,128]{3,2,1,0:T(8,128)S(1)}, u32[]{:S(2)}, u32[]{:S(2)}) collective-permute-start(f32[2,2,16,128]{3,2,1,0:T(8,128)S(1)} %get-tuple-element.43), channel_id=1, source_target_pairs={{0,16},{16,32},{32,48},{48,64},{64,80},{80,96},{96,112},{112,128},... | collective-permute-start | bytes 98312 | tf_op jit(solution)/shard_map/ppermute | solution.py:42
  164.3 4.8 %collective-permute-done.31 = f32[2,2,16,128]{3,2,1,0:T(8,128)S(1)} collective-permute-done((f32[2,2,16,128]{3,2,1,0:T(8,128)S(1)}, f32[2,2,16,128]{3,2,1,0:T(8,128)S(1)}, u32[]{:S(2)}, u32[]{:S(2)}) %collective-permute-start.31) | collective-permute-done | bytes 32800 | tf_op jit(solution)/shard_map/ppermute | solution.py:43
  171.0 5.4 %collective-permute-start.8 = (f32[3,2,16,128]{3,2,1,0:T(8,128)S(1)}, f32[3,2,16,128]{3,2,1,0:T(8,128)S(1)}, u32[]{:S(2)}, u32[]{:S(2)}) collective-permute-start(f32[3,2,16,128]{3,2,1,0:T(8,128)S(1)} %get-tuple-element.25), channel_id=1, source_target_pairs={{0,16},{16,32},{32,48},{48,64},{64,80},{80,96},{96,112},{112,128},... | collective-permute-start | bytes 147464 | tf_op jit(solution)/shard_map/ppermute | solution.py:42
  177.5 2.1 %fusion.39 = f32[3,32,16,128]{3,2,1,0:T(8,128)S(1)} fusion(f32[3,32,16,128]{3,2,1,0:T(8,128)S(1)} %bitcast.21, f32[3,32,2,128]{3,2,1,0:T(2,128)S(1)} %collective-permute-done.10, f32[3,32,2,128]{3,2,1,0:T(2,128)S(1)} %collective-permute-done.9, f32[3,34,20,128]{3,2,1,0:T(8,128)S(1)} %get-tuple-element.16, f32[3,34,20,128]{3,2,1,0:T(8,128)S(1)} %get-tuple-element.15, ...), kind=kLoop, calls=%fused_computation.112 | loop fusion | flops 8650752 | bytes 5178112 | tf_op jit(solution)/shard_map/add | solution.py:50
  179.8 3.6 %collective-permute-start.14 = (f32[3,32,2,128]{3,2,1,0:T(2,128)S(1)}, f32[3,32,2,128]{3,2,1,0:T(2,128)S(1)}, u32[]{:S(2)}, u32[]{:S(2)}) collective-permute-start(f32[3,32,2,128]{3,2,1,0:T(2,128)S(1)} %get-tuple-element.24), channel_id=1, source_target_pairs={{1,0},{2,1},{3,2},{4,3},{5,4},{6,5},{7,6},{8,7},{9,8},{10,9},{11,1... | collective-permute-start | bytes 294920 | tf_op jit(solution)/shard_map/ppermute | solution.py:41
  183.4 6.3 %collective-permute-start.12 = (f32[3,2,16,128]{3,2,1,0:T(8,128)S(1)}, f32[3,2,16,128]{3,2,1,0:T(8,128)S(1)}, u32[]{:S(2)}, u32[]{:S(2)}) collective-permute-start(f32[3,2,16,128]{3,2,1,0:T(8,128)S(1)} %get-tuple-element.21), channel_id=1, source_target_pairs={{0,16},{16,32},{32,48},{48,64},{64,80},{80,96},{96,112},{112,128},... | collective-permute-start | bytes 147464 | tf_op jit(solution)/shard_map/ppermute | solution.py:42
  192.9 3.7 %collective-permute-done.15 = f32[3,2,16,128]{3,2,1,0:T(8,128)S(1)} collective-permute-done((f32[3,2,16,128]{3,2,1,0:T(8,128)S(1)}, f32[3,2,16,128]{3,2,1,0:T(8,128)S(1)}, u32[]{:S(2)}, u32[]{:S(2)}) %collective-permute-start.15) | collective-permute-done | bytes 49184 | tf_op jit(solution)/shard_map/ppermute | solution.py:43
  196.9 2.2 %fusion.51 = f32[3,32,16,128]{3,2,1,0:T(8,128)S(1)} fusion(f32[3,32,16,128]{3,2,1,0:T(8,128)S(1)} %fusion.39, f32[3,32,2,128]{3,2,1,0:T(2,128)S(1)} %collective-permute-done.14, f32[3,32,2,128]{3,2,1,0:T(2,128)S(1)} %collective-permute-done.13, f32[3,34,20,128]{3,2,1,0:T(8,128)S(1)} %get-tuple-element.14, f32[3,34,20,128]{3,2,1,0:T(8,128)S(1)} %get-tuple-element.13, ...), kind=kLoop, calls=%fused_computation.124 | loop fusion | flops 9043968 | bytes 5964544 | tf_op jit(solution)/shard_map/mul | solution.py:51
  (106 shorter events, 37.9 us)
Async XLA Ops:
  1.3 38.8 %collective-permute-start.1 = (f32[3,32,2,128]{3,2,1,0:T(2,128)S(1)}, f32[3,32,2,128]{3,2,1,0:T(2,128)S(1)}, u32[]{:S(2)}, u32[]{:S(2)}) collective-permute-start(f32[3,32,2,128]{3,2,1,0:T(2,128)S(1)} %get-tuple-element.7), channel_id=1, source_target_pairs={{0,1},{1,2},{2,3},{3,4},{4,5},{5,6},{6,7},{7,8},{8,9},{9,10},{10,1... | collective-permute-start | bytes 294920 | tf_op jit(solution)/shard_map/ppermute | solution.py:40
  4.6 22.8 %collective-permute-start.17 = (f32[2,32,2,128]{3,2,1,0:T(2,128)S(1)}, f32[2,32,2,128]{3,2,1,0:T(2,128)S(1)}, u32[]{:S(2)}, u32[]{:S(2)}) collective-permute-start(f32[2,32,2,128]{3,2,1,0:T(2,128)S(1)} %get-tuple-element.11), channel_id=1, source_target_pairs={{0,1},{1,2},{2,3},{3,4},{4,5},{5,6},{6,7},{7,8},{8,9},{9,10},{10,1... | collective-permute-start | bytes 196616 | tf_op jit(solution)/shard_map/ppermute | solution.py:40
  6.2 23.1 %collective-permute-start.18 = (f32[2,32,2,128]{3,2,1,0:T(2,128)S(1)}, f32[2,32,2,128]{3,2,1,0:T(2,128)S(1)}, u32[]{:S(2)}, u32[]{:S(2)}) collective-permute-start(f32[2,32,2,128]{3,2,1,0:T(2,128)S(1)} %get-tuple-element.12), channel_id=1, source_target_pairs={{1,0},{2,1},{3,2},{4,3},{5,4},{6,5},{7,6},{8,7},{9,8},{10,9},{11,1... | collective-permute-start | bytes 196616 | tf_op jit(solution)/shard_map/ppermute | solution.py:41
  10.8 9.3 %collective-permute-start.16 = (f32[2,2,16,128]{3,2,1,0:T(8,128)S(1)}, f32[2,2,16,128]{3,2,1,0:T(8,128)S(1)}, u32[]{:S(2)}, u32[]{:S(2)}) collective-permute-start(f32[2,2,16,128]{3,2,1,0:T(8,128)S(1)} %get-tuple-element.9), channel_id=1, source_target_pairs={{0,16},{16,32},{32,48},{48,64},{64,80},{80,96},{96,112},{112,128},... | collective-permute-start | bytes 98312 | tf_op jit(solution)/shard_map/ppermute | solution.py:42
  16.2 7.3 %collective-permute-start.19 = (f32[2,2,16,128]{3,2,1,0:T(8,128)S(1)}, f32[2,2,16,128]{3,2,1,0:T(8,128)S(1)}, u32[]{:S(2)}, u32[]{:S(2)}) collective-permute-start(f32[2,2,16,128]{3,2,1,0:T(8,128)S(1)} %get-tuple-element.10), channel_id=1, source_target_pairs={{16,0},{32,16},{48,32},{64,48},{80,64},{96,80},{112,96},{128,112},... | collective-permute-start | bytes 98312 | tf_op jit(solution)/shard_map/ppermute | solution.py:43
  20.1 22.0 %collective-permute-start.2 = (f32[3,32,2,128]{3,2,1,0:T(2,128)S(1)}, f32[3,32,2,128]{3,2,1,0:T(2,128)S(1)}, u32[]{:S(2)}, u32[]{:S(2)}) collective-permute-start(f32[3,32,2,128]{3,2,1,0:T(2,128)S(1)} %get-tuple-element.8), channel_id=1, source_target_pairs={{1,0},{2,1},{3,2},{4,3},{5,4},{6,5},{7,6},{8,7},{9,8},{10,9},{11,1... | collective-permute-start | bytes 294920 | tf_op jit(solution)/shard_map/ppermute | solution.py:41
  23.5 7.4 %collective-permute-start = (f32[3,2,16,128]{3,2,1,0:T(8,128)S(1)}, f32[3,2,16,128]{3,2,1,0:T(8,128)S(1)}, u32[]{:S(2)}, u32[]{:S(2)}) collective-permute-start(f32[3,2,16,128]{3,2,1,0:T(8,128)S(1)} %get-tuple-element.5), channel_id=1, source_target_pairs={{0,16},{16,32},{32,48},{48,64},{64,80},{80,96},{96,112},{112,128},... | collective-permute-start | bytes 147464 | tf_op jit(solution)/shard_map/ppermute | solution.py:42
  30.8 17.4 %collective-permute-start.21 = (f32[2,32,2,128]{3,2,1,0:T(2,128)S(1)}, f32[2,32,2,128]{3,2,1,0:T(2,128)S(1)}, u32[]{:S(2)}, u32[]{:S(2)}) collective-permute-start(f32[2,32,2,128]{3,2,1,0:T(2,128)S(1)} %get-tuple-element.55), channel_id=1, source_target_pairs={{0,1},{1,2},{2,3},{3,4},{4,5},{5,6},{6,7},{7,8},{8,9},{9,10},{10,1... | collective-permute-start | bytes 196616 | tf_op jit(solution)/shard_map/ppermute | solution.py:40
  30.9 17.3 %collective-permute-start.22 = (f32[2,32,2,128]{3,2,1,0:T(2,128)S(1)}, f32[2,32,2,128]{3,2,1,0:T(2,128)S(1)}, u32[]{:S(2)}, u32[]{:S(2)}) collective-permute-start(f32[2,32,2,128]{3,2,1,0:T(2,128)S(1)} %get-tuple-element.56), channel_id=1, source_target_pairs={{1,0},{2,1},{3,2},{4,3},{5,4},{6,5},{7,6},{8,7},{9,8},{10,9},{11,1... | collective-permute-start | bytes 196616 | tf_op jit(solution)/shard_map/ppermute | solution.py:41
  34.6 10.0 %collective-permute-start.20 = (f32[2,2,16,128]{3,2,1,0:T(8,128)S(1)}, f32[2,2,16,128]{3,2,1,0:T(8,128)S(1)}, u32[]{:S(2)}, u32[]{:S(2)}) collective-permute-start(f32[2,2,16,128]{3,2,1,0:T(8,128)S(1)} %get-tuple-element.53), channel_id=1, source_target_pairs={{0,16},{16,32},{32,48},{48,64},{64,80},{80,96},{96,112},{112,128},... | collective-permute-start | bytes 98312 | tf_op jit(solution)/shard_map/ppermute | solution.py:42
  40.1 8.0 %collective-permute-start.23 = (f32[2,2,16,128]{3,2,1,0:T(8,128)S(1)}, f32[2,2,16,128]{3,2,1,0:T(8,128)S(1)}, u32[]{:S(2)}, u32[]{:S(2)}) collective-permute-start(f32[2,2,16,128]{3,2,1,0:T(8,128)S(1)} %get-tuple-element.54), channel_id=1, source_target_pairs={{16,0},{32,16},{48,32},{64,48},{80,64},{96,80},{112,96},{128,112},... | collective-permute-start | bytes 98312 | tf_op jit(solution)/shard_map/ppermute | solution.py:43
  44.5 25.0 %collective-permute-start.5 = (f32[3,32,2,128]{3,2,1,0:T(2,128)S(1)}, f32[3,32,2,128]{3,2,1,0:T(2,128)S(1)}, u32[]{:S(2)}, u32[]{:S(2)}) collective-permute-start(f32[3,32,2,128]{3,2,1,0:T(2,128)S(1)} %get-tuple-element.33), channel_id=1, source_target_pairs={{0,1},{1,2},{2,3},{3,4},{4,5},{5,6},{6,7},{7,8},{8,9},{9,10},{10,1... | collective-permute-start | bytes 294920 | tf_op jit(solution)/shard_map/ppermute | solution.py:40
  44.6 24.9 %collective-permute-start.6 = (f32[3,32,2,128]{3,2,1,0:T(2,128)S(1)}, f32[3,32,2,128]{3,2,1,0:T(2,128)S(1)}, u32[]{:S(2)}, u32[]{:S(2)}) collective-permute-start(f32[3,32,2,128]{3,2,1,0:T(2,128)S(1)} %get-tuple-element.34), channel_id=1, source_target_pairs={{1,0},{2,1},{3,2},{4,3},{5,4},{6,5},{7,6},{8,7},{9,8},{10,9},{11,1... | collective-permute-start | bytes 294920 | tf_op jit(solution)/shard_map/ppermute | solution.py:41
  50.5 22.3 %all-to-all-start.2 = ((f32[2,32,16,128]{3,2,0,1:T(8,128)}), f32[2,32,16,128]{3,2,0,1:T(8,128)S(1)}, u32[]{:S(2)}, u32[]{:S(2)}) async-start(f32[2,32,16,128]{3,2,0,1:T(8,128)} %copy.16), calls=%async_computation.2 | async-start | bytes 1048576 | tf_op jit(solution)/shard_map/all_to_all | solution.py:58
  56.3 8.1 %collective-permute-start.4 = (f32[3,2,16,128]{3,2,1,0:T(8,128)S(1)}, f32[3,2,16,128]{3,2,1,0:T(8,128)S(1)}, u32[]{:S(2)}, u32[]{:S(2)}) collective-permute-start(f32[3,2,16,128]{3,2,1,0:T(8,128)S(1)} %get-tuple-element.31), channel_id=1, source_target_pairs={{0,16},{16,32},{32,48},{48,64},{64,80},{80,96},{96,112},{112,128},... | collective-permute-start | bytes 147464 | tf_op jit(solution)/shard_map/ppermute | solution.py:42
  62.3 7.2 %collective-permute-start.7 = (f32[3,2,16,128]{3,2,1,0:T(8,128)S(1)}, f32[3,2,16,128]{3,2,1,0:T(8,128)S(1)}, u32[]{:S(2)}, u32[]{:S(2)}) collective-permute-start(f32[3,2,16,128]{3,2,1,0:T(8,128)S(1)} %get-tuple-element.32), channel_id=1, source_target_pairs={{16,0},{32,16},{48,32},{64,48},{80,64},{96,80},{112,96},{128,112},... | collective-permute-start | bytes 147464 | tf_op jit(solution)/shard_map/ppermute | solution.py:43
  72.8 27.0 %all-to-all-start = ((f32[3,32,16,128]{3,2,0,1:T(8,128)}), f32[3,32,16,128]{3,2,0,1:T(8,128)S(1)}, u32[]{:S(2)}, u32[]{:S(2)}) async-start(f32[3,32,16,128]{3,2,0,1:T(8,128)} %copy.10), calls=%async_computation | async-start | bytes 1572864 | tf_op jit(solution)/shard_map/all_to_all | solution.py:58
  99.9 17.4 %all-to-all-start.3 = ((f32[2,2,256,128]{3,1,0,2:T(2,128)}), f32[2,2,256,128]{3,1,0,2:T(2,128)S(1)}, u32[]{:S(2)}, u32[]{:S(2)}) async-start(f32[2,2,256,128]{3,1,0,2:T(2,128)} %copy.19), calls=%async_computation.3 | async-start | bytes 1048576 | tf_op jit(solution)/shard_map/all_to_all | solution.py:68
  117.3 45.2 %all-to-all-start.1 = ((f32[3,2,256,128]{3,1,0,2:T(2,128)}), f32[3,2,256,128]{3,1,0,2:T(2,128)S(1)}, u32[]{:S(2)}, u32[]{:S(2)}) async-start(f32[3,2,256,128]{3,1,0,2:T(2,128)} %copy.13), calls=%async_computation.1 | async-start | bytes 1572864 | tf_op jit(solution)/shard_map/all_to_all | solution.py:68
  121.1 24.1 %collective-permute-start.25 = (f32[2,32,2,128]{3,2,1,0:T(2,128)S(1)}, f32[2,32,2,128]{3,2,1,0:T(2,128)S(1)}, u32[]{:S(2)}, u32[]{:S(2)}) collective-permute-start(f32[2,32,2,128]{3,2,1,0:T(2,128)S(1)} %get-tuple-element.49), channel_id=1, source_target_pairs={{0,1},{1,2},{2,3},{3,4},{4,5},{5,6},{6,7},{7,8},{8,9},{9,10},{10,1... | collective-permute-start | bytes 196616 | tf_op jit(solution)/shard_map/ppermute | solution.py:40
  122.4 22.8 %collective-permute-start.26 = (f32[2,32,2,128]{3,2,1,0:T(2,128)S(1)}, f32[2,32,2,128]{3,2,1,0:T(2,128)S(1)}, u32[]{:S(2)}, u32[]{:S(2)}) collective-permute-start(f32[2,32,2,128]{3,2,1,0:T(2,128)S(1)} %get-tuple-element.50), channel_id=1, source_target_pairs={{1,0},{2,1},{3,2},{4,3},{5,4},{6,5},{7,6},{8,7},{9,8},{10,9},{11,1... | collective-permute-start | bytes 196616 | tf_op jit(solution)/shard_map/ppermute | solution.py:41
  124.7 15.4 %collective-permute-start.24 = (f32[2,2,16,128]{3,2,1,0:T(8,128)S(1)}, f32[2,2,16,128]{3,2,1,0:T(8,128)S(1)}, u32[]{:S(2)}, u32[]{:S(2)}) collective-permute-start(f32[2,2,16,128]{3,2,1,0:T(8,128)S(1)} %get-tuple-element.47), channel_id=1, source_target_pairs={{0,16},{16,32},{32,48},{48,64},{64,80},{80,96},{96,112},{112,128},... | collective-permute-start | bytes 98312 | tf_op jit(solution)/shard_map/ppermute | solution.py:42
  146.6 24.3 %collective-permute-start.29 = (f32[2,32,2,128]{3,2,1,0:T(2,128)S(1)}, f32[2,32,2,128]{3,2,1,0:T(2,128)S(1)}, u32[]{:S(2)}, u32[]{:S(2)}) collective-permute-start(f32[2,32,2,128]{3,2,1,0:T(2,128)S(1)} %get-tuple-element.45), channel_id=1, source_target_pairs={{0,1},{1,2},{2,3},{3,4},{4,5},{5,6},{6,7},{7,8},{8,9},{9,10},{10,1... | collective-permute-start | bytes 196616 | tf_op jit(solution)/shard_map/ppermute | solution.py:40
  146.7 29.6 %collective-permute-start.30 = (f32[2,32,2,128]{3,2,1,0:T(2,128)S(1)}, f32[2,32,2,128]{3,2,1,0:T(2,128)S(1)}, u32[]{:S(2)}, u32[]{:S(2)}) collective-permute-start(f32[2,32,2,128]{3,2,1,0:T(2,128)S(1)} %get-tuple-element.46), channel_id=1, source_target_pairs={{1,0},{2,1},{3,2},{4,3},{5,4},{6,5},{7,6},{8,7},{9,8},{10,9},{11,1... | collective-permute-start | bytes 196616 | tf_op jit(solution)/shard_map/ppermute | solution.py:41
  150.3 12.5 %collective-permute-start.28 = (f32[2,2,16,128]{3,2,1,0:T(8,128)S(1)}, f32[2,2,16,128]{3,2,1,0:T(8,128)S(1)}, u32[]{:S(2)}, u32[]{:S(2)}) collective-permute-start(f32[2,2,16,128]{3,2,1,0:T(8,128)S(1)} %get-tuple-element.43), channel_id=1, source_target_pairs={{0,16},{16,32},{32,48},{48,64},{64,80},{80,96},{96,112},{112,128},... | collective-permute-start | bytes 98312 | tf_op jit(solution)/shard_map/ppermute | solution.py:42
  160.5 8.5 %collective-permute-start.31 = (f32[2,2,16,128]{3,2,1,0:T(8,128)S(1)}, f32[2,2,16,128]{3,2,1,0:T(8,128)S(1)}, u32[]{:S(2)}, u32[]{:S(2)}) collective-permute-start(f32[2,2,16,128]{3,2,1,0:T(8,128)S(1)} %get-tuple-element.44), channel_id=1, source_target_pairs={{16,0},{32,16},{48,32},{64,48},{80,64},{96,80},{112,96},{128,112},... | collective-permute-start | bytes 98312 | tf_op jit(solution)/shard_map/ppermute | solution.py:43
  162.7 14.6 %collective-permute-start.10 = (f32[3,32,2,128]{3,2,1,0:T(2,128)S(1)}, f32[3,32,2,128]{3,2,1,0:T(2,128)S(1)}, u32[]{:S(2)}, u32[]{:S(2)}) collective-permute-start(f32[3,32,2,128]{3,2,1,0:T(2,128)S(1)} %get-tuple-element.28), channel_id=1, source_target_pairs={{1,0},{2,1},{3,2},{4,3},{5,4},{6,5},{7,6},{8,7},{9,8},{10,9},{11,1... | collective-permute-start | bytes 294920 | tf_op jit(solution)/shard_map/ppermute | solution.py:41
  162.8 14.5 %collective-permute-start.9 = (f32[3,32,2,128]{3,2,1,0:T(2,128)S(1)}, f32[3,32,2,128]{3,2,1,0:T(2,128)S(1)}, u32[]{:S(2)}, u32[]{:S(2)}) collective-permute-start(f32[3,32,2,128]{3,2,1,0:T(2,128)S(1)} %get-tuple-element.27), channel_id=1, source_target_pairs={{0,1},{1,2},{2,3},{3,4},{4,5},{5,6},{6,7},{7,8},{8,9},{9,10},{10,1... | collective-permute-start | bytes 294920 | tf_op jit(solution)/shard_map/ppermute | solution.py:40
  169.1 7.5 %collective-permute-start.11 = (f32[3,2,16,128]{3,2,1,0:T(8,128)S(1)}, f32[3,2,16,128]{3,2,1,0:T(8,128)S(1)}, u32[]{:S(2)}, u32[]{:S(2)}) collective-permute-start(f32[3,2,16,128]{3,2,1,0:T(8,128)S(1)} %get-tuple-element.26), channel_id=1, source_target_pairs={{16,0},{32,16},{48,32},{64,48},{80,64},{96,80},{112,96},{128,112},... | collective-permute-start | bytes 147464 | tf_op jit(solution)/shard_map/ppermute | solution.py:43
  179.7 16.9 %collective-permute-start.13 = (f32[3,32,2,128]{3,2,1,0:T(2,128)S(1)}, f32[3,32,2,128]{3,2,1,0:T(2,128)S(1)}, u32[]{:S(2)}, u32[]{:S(2)}) collective-permute-start(f32[3,32,2,128]{3,2,1,0:T(2,128)S(1)} %get-tuple-element.23), channel_id=1, source_target_pairs={{0,1},{1,2},{2,3},{3,4},{4,5},{5,6},{6,7},{7,8},{8,9},{9,10},{10,1... | collective-permute-start | bytes 294920 | tf_op jit(solution)/shard_map/ppermute | solution.py:40
  179.8 16.8 %collective-permute-start.14 = (f32[3,32,2,128]{3,2,1,0:T(2,128)S(1)}, f32[3,32,2,128]{3,2,1,0:T(2,128)S(1)}, u32[]{:S(2)}, u32[]{:S(2)}) collective-permute-start(f32[3,32,2,128]{3,2,1,0:T(2,128)S(1)} %get-tuple-element.24), channel_id=1, source_target_pairs={{1,0},{2,1},{3,2},{4,3},{5,4},{6,5},{7,6},{8,7},{9,8},{10,9},{11,1... | collective-permute-start | bytes 294920 | tf_op jit(solution)/shard_map/ppermute | solution.py:41
  183.4 9.5 %collective-permute-start.12 = (f32[3,2,16,128]{3,2,1,0:T(8,128)S(1)}, f32[3,2,16,128]{3,2,1,0:T(8,128)S(1)}, u32[]{:S(2)}, u32[]{:S(2)}) collective-permute-start(f32[3,2,16,128]{3,2,1,0:T(8,128)S(1)} %get-tuple-element.21), channel_id=1, source_target_pairs={{0,16},{16,32},{32,48},{48,64},{64,80},{80,96},{96,112},{112,128},... | collective-permute-start | bytes 147464 | tf_op jit(solution)/shard_map/ppermute | solution.py:42
  (8 other events, 97.4 us)

commit v6 on v4

--- a/solution.py
+++ b/solution.py
@@ -34,21 +34,32 @@
     )
 
 
-def extend(cells, width):
+def split_stencil(cells, kap, speed_r, speed_p, width=2):
     sectors, rings = lax.axis_size("azi"), lax.axis_size("rad")
     rows, cols = cells.shape[-3], cells.shape[-2]
     left = lax.ppermute(cells[..., cols - width :, :], "azi", [(i, (i + 1) % sectors) for i in range(sectors)])
     right = lax.ppermute(cells[..., :width, :], "azi", [((i + 1) % sectors, i) for i in range(sectors)])
     above = lax.ppermute(cells[..., rows - width :, :, :], "rad", [(i, i + 1) for i in range(rings - 1)])
     below = lax.ppermute(cells[..., :width, :, :], "rad", [(i + 1, i) for i in range(rings - 1)])
-    wide = jnp.concatenate([left, cells, right], axis=-2)
-    corners = [(0, 0)] * (cells.ndim - 2) + [(width, width), (0, 0)]
-    return jnp.concatenate([jnp.pad(above, corners), wide, jnp.pad(below, corners)], axis=-3)
+    middle = stencil(jnp.concatenate([above, cells, below], axis=1), kap[:, width : cols - width], speed_r, speed_p)
+    edge = 2 * width
+
+    def side(strip, near, far, pads):
+        wide = jnp.concatenate([strip, near] if pads[0] else [near, strip], axis=2)
+        corners = [(0, 0), (0, 0), pads, (0, 0)]
+        tall = jnp.concatenate([jnp.pad(far[0], corners), wide, jnp.pad(far[1], corners)], axis=1)
+        return tall
+
+    low = side(left, cells[:, :, :edge], (above[:, :, :edge], below[:, :, :edge]), (width, 0))
+    high = side(right, cells[:, :, cols - edge :], (above[:, :, cols - edge :], below[:, :, cols - edge :]), (0, width))
+    first = stencil(low, kap[:, :width], speed_r, speed_p)
+    last = stencil(high, kap[:, cols - width :], speed_r, speed_p)
+    return jnp.concatenate([first, middle, last], axis=2)
 
 
 def heun_sections(field, kappa, speed_r, speed_p):
-    first = field + stencil(extend(field, 2), kappa, speed_r, speed_p)
-    return 0.5 * (field + first + stencil(extend(first, 2), kappa, speed_r, speed_p))
+    first = field + split_stencil(field, kappa, speed_r, speed_p)
+    return 0.5 * (field + first + split_stencil(first, kappa, speed_r, speed_p))
 
 
 def shift_rows(half, shifts):

time: 169 us -> 165 us (0.976)
  starting transfers between devices: 56.1 us -> 49.3 us
  local copies, waits for them, and re-layouts: 6.44 us -> 10.1 us
  other arithmetic: 18.6 us -> 16 us
  waiting for transfers between devices: 45 us -> 47.1 us
    mul x2, other arithmetic: 8.39 us -> 1.25 us  [heun_sections(): return 0.5 * (field + first + split_stencil(first, kappa, speed_r, speed_p))]
    add x2 -> x14, other arithmetic: 7.34 us -> 13.6 us  [the longest x12 12.6 us: stencil(): -speed_r[:, :, None, None] * first_r - speed_p[:, :, None, None] * first_p]
    ppermute x16, starting transfers between devices: 49.2 us -> 43.6 us  [the longest x4 16.8 us: split_stencil(): lax.ppermute(cells[..., :width, :], 'azi', [((i + 1) % sectors, i) for i...]
    all_to_all x1, waiting for transfers between devices: 25.4 us -> 28.9 us  [shift_rows(): full = lax.all_to_all(half, 'azi', 1, 2, tiled=True)]
    unnamed x9 -> x12, local copies, waits for them, and re-layouts: 0.1 us -> 3.12 us
    mul x1 -> x5, local copies, waits for them, and re-layouts: 1.14 us -> 3.7 us  [the longest x2 3.62 us: heun_sections(): return 0.5 * (field + first + split_stencil(first, kappa, speed_r, speed_p))]
    slice x8 -> x24, local copies, waits for them, and re-layouts: 2.84 us -> 0.9 us  [the longest x8 0.45 us: tap(): return padded[:, 2 + a:2 + a + n_r, 2 + b:2 + b + n_p, :]]
  transfers between devices with their start and end apart: 17 -> 17, of which waited for: 5 -> 6; matrix products, arithmetic and copies ran while one was open for 2% -> 8% of each run, Pallas kernels for 0% -> 0%
where the time goes in v6:
time: 165 us; the launch traced here: 164 us
  starting transfers between devices  49.3 us (30%)
  waiting for transfers between devices  47.1 us (29%)
  blocking collectives  37.1 us (22%)
  other arithmetic  16 us (10%)
  local copies, waits for them, and re-layouts  10.1 us (6%)
  between operations  4.52 us (3%)
    all_to_all x1, blocking collectives, shift_rows(): return lax.all_to_all(moved, 'azi', 2, 1, tiled=True)  37.1 us
    all_to_all x1, waiting for transfers between devices, shift_rows(): full = lax.all_to_all(half, 'azi', 1, 2, tiled=True)  28.9 us
    ppermute x4, starting transfers between devices, split_stencil(): lax.ppermute(cells[..., :width, :], 'azi', [((i + 1) % sectors, i) for i...  16.8 us
    ppermute x4, waiting for transfers between devices, split_stencil(): lax.ppermute(cells[..., :width, :, :], 'rad', [(i + 1, i) for i in range(...  16.5 us
    ppermute x4, starting transfers between devices, split_stencil(): lax.ppermute(cells[..., rows - width:, :, :], 'rad', [(i, i + 1) for i in...  16.2 us
    add x12, other arithmetic, stencil(): -speed_r[:, :, None, None] * first_r - speed_p[:, :, None, None] * first_p  12.6 us
    ppermute x4, starting transfers between devices, split_stencil(): lax.ppermute(cells[..., :width, :, :], 'rad', [(i + 1, i) for i in range(...  8.17 us
    all_to_all x1, starting transfers between devices, shift_rows(): full = lax.all_to_all(half, 'azi', 1, 2, tiled=True)  5.73 us
  transfers between devices with their start and end apart: 17, of which 6 were waited for; matrix products, arithmetic and copies ran while one was open for 8% of the time, Pallas kernels for 0%

profile of v6, /device:TPU:1, one launch (start us, length us, event | category | flops | bytes accessed | tf_op | source)
XLA Modules:
  0.0 164.1 jit_solution(12375142759403873669)
XLA Ops:
  0.0 1.7 %constant_dynamic-update-slice_fusion.1 = (f32[5,34,16,128]{3,1,2,0:T(8,128)S(1)}, f32[5,32,16,128]{3,1,2,0:T(8,128)S(1)}) fusion(f32[5,32,16,128]{3,2,1,0:T(8,128)} %param.5), kind=kLoop, calls=%fused_computation.235 | loop fusion | bytes 3932160
  1.8 2.2 %collective-permute-start.1 = (f32[5,32,2,128]{3,1,2,0:T(8,128)S(1)}, f32[5,32,2,128]{3,1,2,0:T(8,128)S(1)}, u32[]{:S(2)}, u32[]{:S(2)}) collective-permute-start(f32[5,32,2,128]{3,1,2,0:T(8,128)S(1)} %get-tuple-element.34), channel_id=1, source_target_pairs={{0,1},{1,2},{2,3},{3,4},{4,5},{5,6},{6,7},{7,8},{8,9},{9,10},{10,1... | collective-permute-start | bytes 491528 | tf_op jit(solution)/shard_map/ppermute | solution.py:40
  4.0 5.4 %collective-permute-start.3 = (f32[5,32,2,128]{3,1,2,0:T(8,128)S(1)}, f32[5,32,2,128]{3,1,2,0:T(8,128)S(1)}, u32[]{:S(2)}, u32[]{:S(2)}) collective-permute-start(f32[5,32,2,128]{3,1,2,0:T(8,128)S(1)} %get-tuple-element.33), channel_id=1, source_target_pairs={{1,0},{2,1},{3,2},{4,3},{5,4},{6,5},{7,6},{8,7},{9,8},{10,9},{11,1... | collective-permute-start | bytes 491528 | tf_op jit(solution)/shard_map/ppermute | solution.py:41
  9.5 5.4 %collective-permute-start = (f32[5,2,16,128]{3,1,2,0:T(2,128)S(1)}, f32[5,2,16,128]{3,1,2,0:T(2,128)S(1)}, u32[]{:S(2)}, u32[]{:S(2)}) collective-permute-start(f32[5,2,16,128]{3,1,2,0:T(2,128)S(1)} %get-tuple-element.31), channel_id=1, source_target_pairs={{0,16},{16,32},{32,48},{48,64},{64,80},{80,96},{96,112},{112,128},... | collective-permute-start | bytes 245768 | tf_op jit(solution)/shard_map/ppermute | solution.py:42
  14.8 1.9 %collective-permute-start.2 = (f32[5,2,16,128]{3,1,2,0:T(2,128)S(1)}, f32[5,2,16,128]{3,1,2,0:T(2,128)S(1)}, u32[]{:S(2)}, u32[]{:S(2)}) collective-permute-start(f32[5,2,16,128]{3,1,2,0:T(2,128)S(1)} %get-tuple-element.32), channel_id=1, source_target_pairs={{16,0},{32,16},{48,32},{64,48},{80,64},{96,80},{112,96},{128,112},... | collective-permute-start | bytes 245768 | tf_op jit(solution)/shard_map/ppermute | solution.py:43
  17.2 4.9 %collective-permute-done.2 = f32[5,2,16,128]{3,1,2,0:T(2,128)S(1)} collective-permute-done((f32[5,2,16,128]{3,1,2,0:T(2,128)S(1)}, f32[5,2,16,128]{3,1,2,0:T(2,128)S(1)}, u32[]{:S(2)}, u32[]{:S(2)}) %collective-permute-start.2) | collective-permute-done | bytes 81952 | tf_op jit(solution)/shard_map/ppermute | solution.py:43
  22.1 2.0 %fusion.15 = f32[5,32,12,128]{3,1,2,0:T(8,128)S(1)} fusion(f32[5,32,12,128]{3,1,2,0:T(8,128)S(1)} %slice.946, f32[5,32,16,128]{3,1,2,0:T(8,128)S(1)} %get-tuple-element.30, f32[5,34,16,128]{3,1,2,0:T(8,128)S(1)} %constant_dynamic-update-slice_fusion, f32[5,2,16,128]{3,1,2,0:T(2,128)S(1)} %collective-permute-done, f32[32,12,128]{2,0,1:T(8,128)S(1)} %copy.29, ...), kind=kLoop, calls=%fused_computation.52 | loop fusion | flops 10076160 | bytes 9461760 | tf_op jit(solution)/shard_map/add | solution.py:31
  25.2 0.9 copy-done
  26.8 1.9 %collective-permute-start.4 = (f32[5,2,16,128]{3,1,2,0:T(2,128)S(1)}, f32[5,2,16,128]{3,1,2,0:T(2,128)S(1)}, u32[]{:S(2)}, u32[]{:S(2)}) collective-permute-start(f32[5,2,16,128]{3,1,2,0:T(2,128)S(1)} %get-tuple-element.23), channel_id=1, source_target_pairs={{0,16},{16,32},{32,48},{48,64},{64,80},{80,96},{96,112},{112,128},... | collective-permute-start | bytes 245768 | tf_op jit(solution)/shard_map/ppermute | solution.py:42
  28.9 2.4 %collective-permute-start.6 = (f32[5,2,16,128]{3,1,2,0:T(2,128)S(1)}, f32[5,2,16,128]{3,1,2,0:T(2,128)S(1)}, u32[]{:S(2)}, u32[]{:S(2)}) collective-permute-start(f32[5,2,16,128]{3,1,2,0:T(2,128)S(1)} %get-tuple-element.24), channel_id=1, source_target_pairs={{16,0},{32,16},{48,32},{64,48},{80,64},{96,80},{112,96},{128,112},... | collective-permute-start | bytes 245768 | tf_op jit(solution)/shard_map/ppermute | solution.py:43
  31.3 3.9 %collective-permute-start.7 = (f32[5,32,2,128]{3,1,2,0:T(8,128)S(1)}, f32[5,32,2,128]{3,1,2,0:T(8,128)S(1)}, u32[]{:S(2)}, u32[]{:S(2)}) collective-permute-start(f32[5,32,2,128]{3,1,2,0:T(8,128)S(1)} %get-tuple-element.25), channel_id=1, source_target_pairs={{1,0},{2,1},{3,2},{4,3},{5,4},{6,5},{7,6},{8,7},{9,8},{10,9},{11,1... | collective-permute-start | bytes 491528 | tf_op jit(solution)/shard_map/ppermute | solution.py:41
  35.2 4.7 %collective-permute-done.6 = f32[5,2,16,128]{3,1,2,0:T(2,128)S(1)} collective-permute-done((f32[5,2,16,128]{3,1,2,0:T(2,128)S(1)}, f32[5,2,16,128]{3,1,2,0:T(2,128)S(1)}, u32[]{:S(2)}, u32[]{:S(2)}) %collective-permute-start.6) | collective-permute-done | bytes 81952 | tf_op jit(solution)/shard_map/ppermute | solution.py:43
  39.9 2.7 %fusion.25 = f32[5,32,12,128]{3,1,2,0:T(8,128)S(1)} fusion(f32[5,32,12,128]{3,1,2,0:T(8,128)S(1)} %slice.977, f32[5,32,16,128]{3,1,2,0:T(8,128)S(1)} %maximum_add_fusion, f32[5,2,16,128]{3,1,2,0:T(2,128)S(1)} %collective-permute-done.6, f32[5,2,16,128]{3,1,2,0:T(2,128)S(1)} %collective-permute-done.4, f32[32,12,128]{2,0,1:T(8,128)S(1)} %copy.29, ...), kind=kLoop, calls=%fused_computation.62 | loop fusion | flops 10567680 | bytes 7577600 | tf_op jit(solution)/shard_map/add | solution.py:31
  44.3 1.8 %copy.36 = f32[5,32,16,128]{3,2,0,1:T(8,128)} copy(f32[5,32,16,128]{3,1,2,0:T(8,128)S(1)} %fusion) | data formatting | bytes 2621440 | tf_op jit(solution)/shard_map/mul | solution.py:62
  46.1 5.7 %all-to-all-start = ((f32[5,32,16,128]{3,2,0,1:T(8,128)}), f32[5,32,16,128]{3,2,0,1:T(8,128)S(1)}, u32[]{:S(2)}, u32[]{:S(2)}) async-start(f32[5,32,16,128]{3,2,0,1:T(8,128)} %copy.36), calls=%async_computation | async-start | bytes 2621440 | tf_op jit(solution)/shard_map/all_to_all | solution.py:69
  51.9 0.6 fusion.149
  56.5 28.9 %all-to-all-done = f32[5,32,16,128]{3,2,0,1:T(8,128)S(1)} async-done(((f32[5,32,16,128]{3,2,0,1:T(8,128)}), f32[5,32,16,128]{3,2,0,1:T(8,128)S(1)}, u32[]{:S(2)}, u32[]{:S(2)}) %all-to-all-start) | async-done | bytes 1310752 | tf_op jit(solution)/shard_map/all_to_all | solution.py:69
  86.1 1.0 copy.39
  87.2 37.1 %all_to_all.36 = f32[5,2,256,128]{3,1,0,2:T(2,128)S(1)} all-to-all(f32[5,2,256,128]{3,1,0,2:T(2,128)S(1)} %copy.39), channel_id=1, replica_groups=mesh['rad'=16,'azi'=16] {'azi'}, dimensions={2} | all-to-all | bytes 2621440 | tf_op jit(solution)/shard_map/all_to_all | solution.py:79
  125.0 4.3 %collective-permute-start.8 = (f32[5,2,16,128]{3,1,2,0:T(2,128)S(1)}, f32[5,2,16,128]{3,1,2,0:T(2,128)S(1)}, u32[]{:S(2)}, u32[]{:S(2)}) collective-permute-start(f32[5,2,16,128]{3,1,2,0:T(2,128)S(1)} %get-tuple-element.15), channel_id=1, source_target_pairs={{0,16},{16,32},{32,48},{48,64},{64,80},{80,96},{96,112},{112,128},... | collective-permute-start | bytes 245768 | tf_op jit(solution)/shard_map/ppermute | solution.py:42
  129.6 1.9 %collective-permute-start.10 = (f32[5,2,16,128]{3,1,2,0:T(2,128)S(1)}, f32[5,2,16,128]{3,1,2,0:T(2,128)S(1)}, u32[]{:S(2)}, u32[]{:S(2)}) collective-permute-start(f32[5,2,16,128]{3,1,2,0:T(2,128)S(1)} %get-tuple-element.16), channel_id=1, source_target_pairs={{16,0},{32,16},{48,32},{64,48},{80,64},{96,80},{112,96},{128,112},... | collective-permute-start | bytes 245768 | tf_op jit(solution)/shard_map/ppermute | solution.py:43
  131.5 3.6 %collective-permute-start.11 = (f32[5,32,2,128]{3,1,2,0:T(8,128)S(1)}, f32[5,32,2,128]{3,1,2,0:T(8,128)S(1)}, u32[]{:S(2)}, u32[]{:S(2)}) collective-permute-start(f32[5,32,2,128]{3,1,2,0:T(8,128)S(1)} %get-tuple-element.17), channel_id=1, source_target_pairs={{1,0},{2,1},{3,2},{4,3},{5,4},{6,5},{7,6},{8,7},{9,8},{10,9},{11,1... | collective-permute-start | bytes 491528 | tf_op jit(solution)/shard_map/ppermute | solution.py:41
  135.2 1.9 %collective-permute-done.10 = f32[5,2,16,128]{3,1,2,0:T(2,128)S(1)} collective-permute-done((f32[5,2,16,128]{3,1,2,0:T(2,128)S(1)}, f32[5,2,16,128]{3,1,2,0:T(2,128)S(1)}, u32[]{:S(2)}, u32[]{:S(2)}) %collective-permute-start.10) | collective-permute-done | bytes 81952 | tf_op jit(solution)/shard_map/ppermute | solution.py:43
  137.1 2.0 %fusion.35 = f32[5,32,12,128]{3,1,2,0:T(8,128)S(1)} fusion(f32[5,32,12,128]{3,1,2,0:T(8,128)S(1)} %slice.1010, f32[5,32,16,128]{3,1,2,0:T(8,128)S(1)} %get-tuple-element.14, f32[5,34,16,128]{3,1,2,0:T(8,128)S(1)} %constant_dynamic-update-slice_fusion.2, f32[5,2,16,128]{3,1,2,0:T(2,128)S(1)} %collective-permute-done.8, f32[32,12,128]{2,0,1:T(8,128)S(1)} %copy.29, ...), kind=kLoop, calls=%fused_computation.72 | loop fusion | flops 10076160 | bytes 9461760 | tf_op jit(solution)/shard_map/add | solution.py:31
  139.6 1.6 collective-permute-done.11
  142.3 4.6 %collective-permute-start.12 = (f32[5,2,16,128]{3,1,2,0:T(2,128)S(1)}, f32[5,2,16,128]{3,1,2,0:T(2,128)S(1)}, u32[]{:S(2)}, u32[]{:S(2)}) collective-permute-start(f32[5,2,16,128]{3,1,2,0:T(2,128)S(1)} %get-tuple-element.7), channel_id=1, source_target_pairs={{0,16},{16,32},{32,48},{48,64},{64,80},{80,96},{96,112},{112,128},... | collective-permute-start | bytes 245768 | tf_op jit(solution)/shard_map/ppermute | solution.py:42
  147.1 1.9 %collective-permute-start.14 = (f32[5,2,16,128]{3,1,2,0:T(2,128)S(1)}, f32[5,2,16,128]{3,1,2,0:T(2,128)S(1)}, u32[]{:S(2)}, u32[]{:S(2)}) collective-permute-start(f32[5,2,16,128]{3,1,2,0:T(2,128)S(1)} %get-tuple-element.8), channel_id=1, source_target_pairs={{16,0},{32,16},{48,32},{64,48},{80,64},{96,80},{112,96},{128,112},... | collective-permute-start | bytes 245768 | tf_op jit(solution)/shard_map/ppermute | solution.py:43
  149.1 3.8 %collective-permute-start.15 = (f32[5,32,2,128]{3,1,2,0:T(8,128)S(1)}, f32[5,32,2,128]{3,1,2,0:T(8,128)S(1)}, u32[]{:S(2)}, u32[]{:S(2)}) collective-permute-start(f32[5,32,2,128]{3,1,2,0:T(8,128)S(1)} %get-tuple-element.9), channel_id=1, source_target_pairs={{1,0},{2,1},{3,2},{4,3},{5,4},{6,5},{7,6},{8,7},{9,8},{10,9},{11,1... | collective-permute-start | bytes 491528 | tf_op jit(solution)/shard_map/ppermute | solution.py:41
  152.9 5.0 %collective-permute-done.14 = f32[5,2,16,128]{3,1,2,0:T(2,128)S(1)} collective-permute-done((f32[5,2,16,128]{3,1,2,0:T(2,128)S(1)}, f32[5,2,16,128]{3,1,2,0:T(2,128)S(1)}, u32[]{:S(2)}, u32[]{:S(2)}) %collective-permute-start.14) | collective-permute-done | bytes 81952 | tf_op jit(solution)/shard_map/ppermute | solution.py:43
  157.9 2.7 %fusion.45 = f32[5,32,12,128]{3,1,2,0:T(8,128)S(1)} fusion(f32[5,32,12,128]{3,1,2,0:T(8,128)S(1)} %slice.1041, f32[5,32,16,128]{3,1,2,0:T(8,128)S(1)} %maximum_add_fusion.2, f32[5,2,16,128]{3,1,2,0:T(2,128)S(1)} %collective-permute-done.14, f32[5,2,16,128]{3,1,2,0:T(2,128)S(1)} %collective-permute-done.12, f32[32,12,128]{2,0,1:T(8,128)S(1)} %copy.29, ...), kind=kLoop, calls=%fused_computation.82 | loop fusion | flops 10567680 | bytes 7577600 | tf_op jit(solution)/shard_map/add | solution.py:31
  161.6 0.6 fusion.1
  162.3 1.8 %copy.61 = f32[5,32,16,128]{3,2,1,0:T(8,128)} copy(f32[5,32,16,128]{3,1,2,0:T(8,128)S(1)} %fusion.1) | data formatting | bytes 2621440 | tf_op jit(solution)/shard_map/mul | solution.py:62
  (82 shorter events, 8.2 us)
Async XLA Ops:
  1.7 15.1 %copy-start.1 = (f32[32,16,128]{2,1,0:T(8,128)S(1)}, f32[32,16,128]{2,1,0:T(8,128)}, u32[]{:S(2)}) copy-start(f32[32,16,128]{2,1,0:T(8,128)} %param.6) | copy-start | bytes 786436
  1.8 15.1 %copy-start.2 = (f32[5,32]{1,0:T(8,128)S(1)}, f32[5,32]{1,0:T(8,128)}, u32[]{:S(2)}) copy-start(f32[5,32]{1,0:T(8,128)} %param.7) | copy-start | bytes 1924
  1.8 15.1 %copy-start.3 = (f32[5,32]{1,0:T(8,128)S(1)}, f32[5,32]{1,0:T(8,128)}, u32[]{:S(2)}) copy-start(f32[5,32]{1,0:T(8,128)} %param.8) | copy-start | bytes 1924
  1.8 22.4 %collective-permute-start.1 = (f32[5,32,2,128]{3,1,2,0:T(8,128)S(1)}, f32[5,32,2,128]{3,1,2,0:T(8,128)S(1)}, u32[]{:S(2)}, u32[]{:S(2)}) collective-permute-start(f32[5,32,2,128]{3,1,2,0:T(8,128)S(1)} %get-tuple-element.34), channel_id=1, source_target_pairs={{0,1},{1,2},{2,3},{3,4},{4,5},{5,6},{6,7},{7,8},{8,9},{9,10},{10,1... | collective-permute-start | bytes 491528 | tf_op jit(solution)/shard_map/ppermute | solution.py:40
  4.0 20.2 %collective-permute-start.3 = (f32[5,32,2,128]{3,1,2,0:T(8,128)S(1)}, f32[5,32,2,128]{3,1,2,0:T(8,128)S(1)}, u32[]{:S(2)}, u32[]{:S(2)}) collective-permute-start(f32[5,32,2,128]{3,1,2,0:T(8,128)S(1)} %get-tuple-element.33), channel_id=1, source_target_pairs={{1,0},{2,1},{3,2},{4,3},{5,4},{6,5},{7,6},{8,7},{9,8},{10,9},{11,1... | collective-permute-start | bytes 491528 | tf_op jit(solution)/shard_map/ppermute | solution.py:41
  9.5 7.7 %collective-permute-start = (f32[5,2,16,128]{3,1,2,0:T(2,128)S(1)}, f32[5,2,16,128]{3,1,2,0:T(2,128)S(1)}, u32[]{:S(2)}, u32[]{:S(2)}) collective-permute-start(f32[5,2,16,128]{3,1,2,0:T(2,128)S(1)} %get-tuple-element.31), channel_id=1, source_target_pairs={{0,16},{16,32},{32,48},{48,64},{64,80},{80,96},{96,112},{112,128},... | collective-permute-start | bytes 245768 | tf_op jit(solution)/shard_map/ppermute | solution.py:42
  14.8 7.3 %collective-permute-start.2 = (f32[5,2,16,128]{3,1,2,0:T(2,128)S(1)}, f32[5,2,16,128]{3,1,2,0:T(2,128)S(1)}, u32[]{:S(2)}, u32[]{:S(2)}) collective-permute-start(f32[5,2,16,128]{3,1,2,0:T(2,128)S(1)} %get-tuple-element.32), channel_id=1, source_target_pairs={{16,0},{32,16},{48,32},{64,48},{80,64},{96,80},{112,96},{128,112},... | collective-permute-start | bytes 245768 | tf_op jit(solution)/shard_map/ppermute | solution.py:43
  24.8 1.3 copy-start
  26.8 8.5 %collective-permute-start.4 = (f32[5,2,16,128]{3,1,2,0:T(2,128)S(1)}, f32[5,2,16,128]{3,1,2,0:T(2,128)S(1)}, u32[]{:S(2)}, u32[]{:S(2)}) collective-permute-start(f32[5,2,16,128]{3,1,2,0:T(2,128)S(1)} %get-tuple-element.23), channel_id=1, source_target_pairs={{0,16},{16,32},{32,48},{48,64},{64,80},{80,96},{96,112},{112,128},... | collective-permute-start | bytes 245768 | tf_op jit(solution)/shard_map/ppermute | solution.py:42
  28.8 13.9 %collective-permute-start.5 = (f32[5,32,2,128]{3,1,2,0:T(8,128)S(1)}, f32[5,32,2,128]{3,1,2,0:T(8,128)S(1)}, u32[]{:S(2)}, u32[]{:S(2)}) collective-permute-start(f32[5,32,2,128]{3,1,2,0:T(8,128)S(1)} %get-tuple-element.26), channel_id=1, source_target_pairs={{0,1},{1,2},{2,3},{3,4},{4,5},{5,6},{6,7},{7,8},{8,9},{9,10},{10,1... | collective-permute-start | bytes 491528 | tf_op jit(solution)/shard_map/ppermute | solution.py:40
  28.9 11.0 %collective-permute-start.6 = (f32[5,2,16,128]{3,1,2,0:T(2,128)S(1)}, f32[5,2,16,128]{3,1,2,0:T(2,128)S(1)}, u32[]{:S(2)}, u32[]{:S(2)}) collective-permute-start(f32[5,2,16,128]{3,1,2,0:T(2,128)S(1)} %get-tuple-element.24), channel_id=1, source_target_pairs={{16,0},{32,16},{48,32},{64,48},{80,64},{96,80},{112,96},{128,112},... | collective-permute-start | bytes 245768 | tf_op jit(solution)/shard_map/ppermute | solution.py:43
  31.3 11.8 %collective-permute-start.7 = (f32[5,32,2,128]{3,1,2,0:T(8,128)S(1)}, f32[5,32,2,128]{3,1,2,0:T(8,128)S(1)}, u32[]{:S(2)}, u32[]{:S(2)}) collective-permute-start(f32[5,32,2,128]{3,1,2,0:T(8,128)S(1)} %get-tuple-element.25), channel_id=1, source_target_pairs={{1,0},{2,1},{3,2},{4,3},{5,4},{6,5},{7,6},{8,7},{9,8},{10,9},{11,1... | collective-permute-start | bytes 491528 | tf_op jit(solution)/shard_map/ppermute | solution.py:41
  46.1 5.7 %copy-start.4 = (s32[32]{0:T(128)S(1)}, s32[32]{0:T(128)}, u32[]{:S(2)}) copy-start(s32[32]{0:T(128)} %param.9) | copy-start | bytes 388
  46.1 39.3 %all-to-all-start = ((f32[5,32,16,128]{3,2,0,1:T(8,128)}), f32[5,32,16,128]{3,2,0,1:T(8,128)S(1)}, u32[]{:S(2)}, u32[]{:S(2)}) async-start(f32[5,32,16,128]{3,2,0,1:T(8,128)} %copy.36), calls=%async_computation | async-start | bytes 2621440 | tf_op jit(solution)/shard_map/all_to_all | solution.py:69
  125.0 10.1 %collective-permute-start.8 = (f32[5,2,16,128]{3,1,2,0:T(2,128)S(1)}, f32[5,2,16,128]{3,1,2,0:T(2,128)S(1)}, u32[]{:S(2)}, u32[]{:S(2)}) collective-permute-start(f32[5,2,16,128]{3,1,2,0:T(2,128)S(1)} %get-tuple-element.15), channel_id=1, source_target_pairs={{0,16},{16,32},{32,48},{48,64},{64,80},{80,96},{96,112},{112,128},... | collective-permute-start | bytes 245768 | tf_op jit(solution)/shard_map/ppermute | solution.py:42
  129.5 9.6 %collective-permute-start.9 = (f32[5,32,2,128]{3,1,2,0:T(8,128)S(1)}, f32[5,32,2,128]{3,1,2,0:T(8,128)S(1)}, u32[]{:S(2)}, u32[]{:S(2)}) collective-permute-start(f32[5,32,2,128]{3,1,2,0:T(8,128)S(1)} %get-tuple-element.18), channel_id=1, source_target_pairs={{0,1},{1,2},{2,3},{3,4},{4,5},{5,6},{6,7},{7,8},{8,9},{9,10},{10,1... | collective-permute-start | bytes 491528 | tf_op jit(solution)/shard_map/ppermute | solution.py:40
  129.6 7.4 %collective-permute-start.10 = (f32[5,2,16,128]{3,1,2,0:T(2,128)S(1)}, f32[5,2,16,128]{3,1,2,0:T(2,128)S(1)}, u32[]{:S(2)}, u32[]{:S(2)}) collective-permute-start(f32[5,2,16,128]{3,1,2,0:T(2,128)S(1)} %get-tuple-element.16), channel_id=1, source_target_pairs={{16,0},{32,16},{48,32},{64,48},{80,64},{96,80},{112,96},{128,112},... | collective-permute-start | bytes 245768 | tf_op jit(solution)/shard_map/ppermute | solution.py:43
  131.5 9.7 %collective-permute-start.11 = (f32[5,32,2,128]{3,1,2,0:T(8,128)S(1)}, f32[5,32,2,128]{3,1,2,0:T(8,128)S(1)}, u32[]{:S(2)}, u32[]{:S(2)}) collective-permute-start(f32[5,32,2,128]{3,1,2,0:T(8,128)S(1)} %get-tuple-element.17), channel_id=1, source_target_pairs={{1,0},{2,1},{3,2},{4,3},{5,4},{6,5},{7,6},{8,7},{9,8},{10,9},{11,1... | collective-permute-start | bytes 491528 | tf_op jit(solution)/shard_map/ppermute | solution.py:41
  142.3 10.6 %collective-permute-start.12 = (f32[5,2,16,128]{3,1,2,0:T(2,128)S(1)}, f32[5,2,16,128]{3,1,2,0:T(2,128)S(1)}, u32[]{:S(2)}, u32[]{:S(2)}) collective-permute-start(f32[5,2,16,128]{3,1,2,0:T(2,128)S(1)} %get-tuple-element.7), channel_id=1, source_target_pairs={{0,16},{16,32},{32,48},{48,64},{64,80},{80,96},{96,112},{112,128},... | collective-permute-start | bytes 245768 | tf_op jit(solution)/shard_map/ppermute | solution.py:42
  147.0 13.6 %collective-permute-start.13 = (f32[5,32,2,128]{3,1,2,0:T(8,128)S(1)}, f32[5,32,2,128]{3,1,2,0:T(8,128)S(1)}, u32[]{:S(2)}, u32[]{:S(2)}) collective-permute-start(f32[5,32,2,128]{3,1,2,0:T(8,128)S(1)} %get-tuple-element.10), channel_id=1, source_target_pairs={{0,1},{1,2},{2,3},{3,4},{4,5},{5,6},{6,7},{7,8},{8,9},{9,10},{10,1... | collective-permute-start | bytes 491528 | tf_op jit(solution)/shard_map/ppermute | solution.py:40
  147.1 10.8 %collective-permute-start.14 = (f32[5,2,16,128]{3,1,2,0:T(2,128)S(1)}, f32[5,2,16,128]{3,1,2,0:T(2,128)S(1)}, u32[]{:S(2)}, u32[]{:S(2)}) collective-permute-start(f32[5,2,16,128]{3,1,2,0:T(2,128)S(1)} %get-tuple-element.8), channel_id=1, source_target_pairs={{16,0},{32,16},{48,32},{64,48},{80,64},{96,80},{112,96},{128,112},... | collective-permute-start | bytes 245768 | tf_op jit(solution)/shard_map/ppermute | solution.py:43
  149.1 12.1 %collective-permute-start.15 = (f32[5,32,2,128]{3,1,2,0:T(8,128)S(1)}, f32[5,32,2,128]{3,1,2,0:T(8,128)S(1)}, u32[]{:S(2)}, u32[]{:S(2)}) collective-permute-start(f32[5,32,2,128]{3,1,2,0:T(8,128)S(1)} %get-tuple-element.9), channel_id=1, source_target_pairs={{1,0},{2,1},{3,2},{4,3},{5,4},{6,5},{7,6},{8,7},{9,8},{10,9},{11,1... | collective-permute-start | bytes 491528 | tf_op jit(solution)/shard_map/ppermute | solution.py:41

commit v7 on v6

--- a/solution.py
+++ b/solution.py
@@ -2,6 +2,7 @@
 import jax.numpy as jnp
 from jax import lax
 from jax.sharding import PartitionSpec as P
+from jax.experimental.layout import Layout, with_layout_constraint
 
 
 def stencil(padded, kap, speed_r, speed_p):
@@ -80,9 +81,9 @@
 
 
 def shards(fields, kappa, radial_speed, azimuth_speed, shifts):
-    half = heun_sections(fields, kappa, radial_speed, azimuth_speed)
+    half = with_layout_constraint(heun_sections(fields, kappa, radial_speed, azimuth_speed), Layout((1, 0, 2, 3)))
     moved = shift_rows(half, shifts)
-    return heun_sections(moved, kappa, radial_speed, azimuth_speed)
+    return with_layout_constraint(heun_sections(moved, kappa, radial_speed, azimuth_speed), Layout((0, 1, 2, 3)))
 
 
 def solution(mesh):

time: 165 us -> 174 us (1.055); the launches traced: 164 us -> 170 us
  other arithmetic: 16 us -> 29.8 us
  waiting for transfers between devices: 47.1 us -> 41.4 us
  local copies, waits for them, and re-layouts: 10.1 us -> 7.69 us
    add x12, other arithmetic: 12.6 us -> 25.5 us  [stencil(): -speed_r[:, :, None, None] * first_r - speed_p[:, :, None, None] * first_p]
    unnamed x12 -> x11, local copies, waits for them, and re-layouts: 3.12 us -> 0.03 us
    mul x2 -> x1, local copies, waits for them, and re-layouts: 3.62 us -> 1.14 us  [heun_sections(): return 0.5 * (field + first + split_stencil(first, kappa, speed_r, speed_p))]
    ppermute x4, waiting for transfers between devices: 16.5 us -> 14.3 us  [split_stencil(): lax.ppermute(cells[..., :width, :, :], 'rad', [(i + 1, i) for i in range(...]
    slice x8 -> x12, local copies, waits for them, and re-layouts: 0.45 us -> 2.36 us  [tap(): return padded[:, 2 + a:2 + a + n_r, 2 + b:2 + b + n_p, :]]
    all_to_all x1, waiting for transfers between devices: 28.9 us -> 27.1 us  [shift_rows(): full = lax.all_to_all(half, 'azi', 1, 2, tiled=True)]
  transfers between devices with their start and end apart: 17 -> 17, of which waited for: 6 -> 5; matrix products, arithmetic and copies ran while one was open for 8% -> 13% of each run, Pallas kernels for 0% -> 0%
where the time goes in v7:
time: 174 us; the launch traced here: 170 us
  starting transfers between devices  50.4 us (29%)
  waiting for transfers between devices  41.4 us (24%)
  blocking collectives  36.6 us (21%)
  other arithmetic  29.8 us (17%)
  local copies, waits for them, and re-layouts  7.69 us (4%)
  between operations  4.64 us (3%)
    all_to_all x1, blocking collectives, shift_rows(): return lax.all_to_all(moved, 'azi', 2, 1, tiled=True)  36.6 us
    all_to_all x1, waiting for transfers between devices, shift_rows(): full = lax.all_to_all(half, 'azi', 1, 2, tiled=True)  27.1 us
    add x12, other arithmetic, stencil(): -speed_r[:, :, None, None] * first_r - speed_p[:, :, None, None] * first_p  25.5 us
    ppermute x4, starting transfers between devices, split_stencil(): lax.ppermute(cells[..., rows - width:, :, :], 'rad', [(i, i + 1) for i in...  17 us
    ppermute x4, starting transfers between devices, split_stencil(): lax.ppermute(cells[..., :width, :], 'azi', [((i + 1) % sectors, i) for i...  15.9 us
    ppermute x4, waiting for transfers between devices, split_stencil(): lax.ppermute(cells[..., :width, :, :], 'rad', [(i + 1, i) for i in range(...  14.3 us
    ppermute x4, starting transfers between devices, split_stencil(): lax.ppermute(cells[..., :width, :, :], 'rad', [(i + 1, i) for i in range(...  8.92 us
    all_to_all x1, starting transfers between devices, shift_rows(): full = lax.all_to_all(half, 'azi', 1, 2, tiled=True)  5.95 us
  transfers between devices with their start and end apart: 17, of which 5 were waited for; matrix products, arithmetic and copies ran while one was open for 13% of the time, Pallas kernels for 0%

profile of v7, /device:TPU:1, one launch (start us, length us, event | category | flops | bytes accessed | tf_op | source)
XLA Modules:
  0.0 170.4 jit_solution(4854588079132472556)
XLA Ops:
  0.0 1.5 fusion.124
  1.5 2.2 %collective-permute-start.1 = (f32[5,32,2,128]{3,1,2,0:T(8,128)S(1)}, f32[5,32,2,128]{3,1,2,0:T(8,128)S(1)}, u32[]{:S(2)}, u32[]{:S(2)}) collective-permute-start(f32[5,32,2,128]{3,1,2,0:T(8,128)S(1)} %copy.47), channel_id=1, source_target_pairs={{0,1},{1,2},{2,3},{3,4},{4,5},{5,6},{6,7},{7,8},{8,9},{9,10},{10,1... | collective-permute-start | bytes 491528 | tf_op jit(solution)/shard_map/ppermute | solution.py:41
  3.8 5.4 %collective-permute-start.3 = (f32[5,32,2,128]{3,1,2,0:T(8,128)S(1)}, f32[5,32,2,128]{3,1,2,0:T(8,128)S(1)}, u32[]{:S(2)}, u32[]{:S(2)}) collective-permute-start(f32[5,32,2,128]{3,1,2,0:T(8,128)S(1)} %copy.55), channel_id=1, source_target_pairs={{1,0},{2,1},{3,2},{4,3},{5,4},{6,5},{7,6},{8,7},{9,8},{10,9},{11,1... | collective-permute-start | bytes 491528 | tf_op jit(solution)/shard_map/ppermute | solution.py:42
  9.2 5.4 %collective-permute-start = (f32[5,2,16,128]{3,2,1,0:T(8,128)S(1)}, f32[5,2,16,128]{3,2,1,0:T(8,128)S(1)}, u32[]{:S(2)}, u32[]{:S(2)}) collective-permute-start(f32[5,2,16,128]{3,2,1,0:T(8,128)S(1)} %get-tuple-element.29), channel_id=1, source_target_pairs={{0,16},{16,32},{32,48},{48,64},{64,80},{80,96},{96,112},{112,128},... | collective-permute-start | bytes 245768 | tf_op jit(solution)/shard_map/ppermute | solution.py:43
  14.6 1.9 %collective-permute-start.2 = (f32[5,2,16,128]{3,2,1,0:T(8,128)S(1)}, f32[5,2,16,128]{3,2,1,0:T(8,128)S(1)}, u32[]{:S(2)}, u32[]{:S(2)}) collective-permute-start(f32[5,2,16,128]{3,2,1,0:T(8,128)S(1)} %get-tuple-element.30), channel_id=1, source_target_pairs={{16,0},{32,16},{48,32},{64,48},{80,64},{96,80},{112,96},{128,112},... | collective-permute-start | bytes 245768 | tf_op jit(solution)/shard_map/ppermute | solution.py:44
  17.1 4.7 %collective-permute-done.2 = f32[5,2,16,128]{3,2,1,0:T(8,128)S(1)} collective-permute-done((f32[5,2,16,128]{3,2,1,0:T(8,128)S(1)}, f32[5,2,16,128]{3,2,1,0:T(8,128)S(1)}, u32[]{:S(2)}, u32[]{:S(2)}) %collective-permute-start.2) | collective-permute-done | bytes 81952 | tf_op jit(solution)/shard_map/ppermute | solution.py:44
  21.8 3.2 %fusion.13 = f32[5,32,12,128]{3,2,1,0:T(8,128)S(1)} fusion(f32[5,32,12,128]{3,2,1,0:T(8,128)S(1)} %slice.766, f32[5,32,16,128]{3,2,1,0:T(8,128)S(1)} %copy-done, f32[5,34,16,128]{3,2,1,0:T(8,128)S(1)} %constant_dynamic-update-slice_fusion.2, f32[5,34,16,128]{3,2,1,0:T(8,128)S(1)} %get-tuple-element.27, f32[32,12,128]{2,1,0:T(8,128)S(1)} %slice_multiply_fusion, ...), kind=kLoop, calls=%fused_computation.43 | loop fusion | flops 9584640 | bytes 10028288 | tf_op jit(solution)/shard_map/add | solution.py:32
  25.7 1.4 multiply_add_fusion.7
  27.2 1.4 multiply_add_fusion.6
  29.1 1.9 %collective-permute-start.4 = (f32[5,2,16,128]{3,2,1,0:T(8,128)S(1)}, f32[5,2,16,128]{3,2,1,0:T(8,128)S(1)}, u32[]{:S(2)}, u32[]{:S(2)}) collective-permute-start(f32[5,2,16,128]{3,2,1,0:T(8,128)S(1)} %get-tuple-element.21), channel_id=1, source_target_pairs={{0,16},{16,32},{32,48},{48,64},{64,80},{80,96},{96,112},{112,128},... | collective-permute-start | bytes 245768 | tf_op jit(solution)/shard_map/ppermute | solution.py:43
  31.4 2.4 %collective-permute-start.6 = (f32[5,2,16,128]{3,2,1,0:T(8,128)S(1)}, f32[5,2,16,128]{3,2,1,0:T(8,128)S(1)}, u32[]{:S(2)}, u32[]{:S(2)}) collective-permute-start(f32[5,2,16,128]{3,2,1,0:T(8,128)S(1)} %get-tuple-element.22), channel_id=1, source_target_pairs={{16,0},{32,16},{48,32},{64,48},{80,64},{96,80},{112,96},{128,112},... | collective-permute-start | bytes 245768 | tf_op jit(solution)/shard_map/ppermute | solution.py:44
  33.8 3.9 %collective-permute-start.7 = (f32[5,32,2,128]{3,1,2,0:T(8,128)S(1)}, f32[5,32,2,128]{3,1,2,0:T(8,128)S(1)}, u32[]{:S(2)}, u32[]{:S(2)}) collective-permute-start(f32[5,32,2,128]{3,1,2,0:T(8,128)S(1)} %copy.71), channel_id=1, source_target_pairs={{1,0},{2,1},{3,2},{4,3},{5,4},{6,5},{7,6},{8,7},{9,8},{10,9},{11,1... | collective-permute-start | bytes 491528 | tf_op jit(solution)/shard_map/ppermute | solution.py:42
  37.8 4.7 %collective-permute-done.6 = f32[5,2,16,128]{3,2,1,0:T(8,128)S(1)} collective-permute-done((f32[5,2,16,128]{3,2,1,0:T(8,128)S(1)}, f32[5,2,16,128]{3,2,1,0:T(8,128)S(1)}, u32[]{:S(2)}, u32[]{:S(2)}) %collective-permute-start.6) | collective-permute-done | bytes 81952 | tf_op jit(solution)/shard_map/ppermute | solution.py:44
  42.4 3.6 %fusion.23 = f32[5,32,12,128]{3,2,1,0:T(8,128)S(1)} fusion(f32[5,32,12,128]{3,2,1,0:T(8,128)S(1)} %slice.962, f32[5,32,16,128]{3,2,1,0:T(8,128)S(1)} %maximum_add_fusion, f32[5,2,16,128]{3,2,1,0:T(8,128)S(1)} %collective-permute-done.6, f32[5,2,16,128]{3,2,1,0:T(8,128)S(1)} %collective-permute-done.4, f32[32,12,128]{2,1,0:T(8,128)S(1)} %slice_multiply_fusion, ...), kind=kLoop, calls=%fused_computation.53 | loop fusion | flops 10567680 | bytes 9281536 | tf_op jit(solution)/shard_map/add | solution.py:32
  46.3 1.4 multiply_add_fusion.5
  48.1 1.4 multiply_add_fusion.4
  51.1 6.0 %all-to-all-start = ((f32[5,32,16,128]{3,2,0,1:T(8,128)}), f32[5,32,16,128]{3,2,0,1:T(8,128)S(1)}, u32[]{:S(2)}, u32[]{:S(2)}) async-start(f32[5,32,16,128]{3,2,0,1:T(8,128)} %copy.79), calls=%async_computation | async-start | bytes 2621440 | tf_op jit(solution)/shard_map/all_to_all | solution.py:70
  61.7 27.1 %all-to-all-done = f32[5,32,16,128]{3,2,0,1:T(8,128)S(1)} async-done(((f32[5,32,16,128]{3,2,0,1:T(8,128)}), f32[5,32,16,128]{3,2,0,1:T(8,128)S(1)}, u32[]{:S(2)}, u32[]{:S(2)}) %all-to-all-start) | async-done | bytes 1310752 | tf_op jit(solution)/shard_map/all_to_all | solution.py:70
  90.5 36.6 %all_to_all.36 = f32[5,2,256,128]{3,1,0,2:T(2,128)S(1)} all-to-all(f32[5,2,256,128]{3,1,0,2:T(2,128)S(1)} %copy.81), channel_id=1, replica_groups=mesh['rad'=16,'azi'=16] {'azi'}, dimensions={2} | all-to-all | bytes 2621440 | tf_op jit(solution)/shard_map/all_to_all | solution.py:80
  127.5 6.8 %collective-permute-start.8 = (f32[5,2,16,128]{3,2,1,0:T(8,128)S(1)}, f32[5,2,16,128]{3,2,1,0:T(8,128)S(1)}, u32[]{:S(2)}, u32[]{:S(2)}) collective-permute-start(f32[5,2,16,128]{3,2,1,0:T(8,128)S(1)} %get-tuple-element.13), channel_id=1, source_target_pairs={{0,16},{16,32},{32,48},{48,64},{64,80},{80,96},{96,112},{112,128},... | collective-permute-start | bytes 245768 | tf_op jit(solution)/shard_map/ppermute | solution.py:43
  134.6 1.9 %collective-permute-start.10 = (f32[5,2,16,128]{3,2,1,0:T(8,128)S(1)}, f32[5,2,16,128]{3,2,1,0:T(8,128)S(1)}, u32[]{:S(2)}, u32[]{:S(2)}) collective-permute-start(f32[5,2,16,128]{3,2,1,0:T(8,128)S(1)} %get-tuple-element.14), channel_id=1, source_target_pairs={{16,0},{32,16},{48,32},{64,48},{80,64},{96,80},{112,96},{128,112},... | collective-permute-start | bytes 245768 | tf_op jit(solution)/shard_map/ppermute | solution.py:44
  136.5 3.6 %collective-permute-start.11 = (f32[5,32,2,128]{3,1,2,0:T(8,128)S(1)}, f32[5,32,2,128]{3,1,2,0:T(8,128)S(1)}, u32[]{:S(2)}, u32[]{:S(2)}) collective-permute-start(f32[5,32,2,128]{3,1,2,0:T(8,128)S(1)} %copy.92), channel_id=1, source_target_pairs={{1,0},{2,1},{3,2},{4,3},{5,4},{6,5},{7,6},{8,7},{9,8},{10,9},{11,1... | collective-permute-start | bytes 491528 | tf_op jit(solution)/shard_map/ppermute | solution.py:42
  140.2 3.1 %collective-permute-done.10 = f32[5,2,16,128]{3,2,1,0:T(8,128)S(1)} collective-permute-done((f32[5,2,16,128]{3,2,1,0:T(8,128)S(1)}, f32[5,2,16,128]{3,2,1,0:T(8,128)S(1)}, u32[]{:S(2)}, u32[]{:S(2)}) %collective-permute-start.10) | collective-permute-done | bytes 81952 | tf_op jit(solution)/shard_map/ppermute | solution.py:44
  143.3 3.6 %fusion.33 = f32[5,32,12,128]{3,2,1,0:T(8,128)S(1)} fusion(f32[5,32,12,128]{3,2,1,0:T(8,128)S(1)} %slice.995, f32[5,32,16,128]{3,2,1,0:T(8,128)S(1)} %bitcast.14, f32[5,2,16,128]{3,2,1,0:T(8,128)S(1)} %collective-permute-done.10, f32[5,2,16,128]{3,2,1,0:T(8,128)S(1)} %collective-permute-done.8, f32[32,12,128]{2,1,0:T(8,128)S(1)} %slice_multiply_fusion, ...), kind=kLoop, calls=%fused_computation.63 | loop fusion | flops 10567680 | bytes 9281536 | tf_op jit(solution)/shard_map/add | solution.py:32
  148.9 1.4 multiply_add_fusion.2
  150.8 3.0 %collective-permute-start.12 = (f32[5,2,16,128]{3,2,1,0:T(8,128)S(1)}, f32[5,2,16,128]{3,2,1,0:T(8,128)S(1)}, u32[]{:S(2)}, u32[]{:S(2)}) collective-permute-start(f32[5,2,16,128]{3,2,1,0:T(8,128)S(1)} %get-tuple-element.7), channel_id=1, source_target_pairs={{0,16},{16,32},{32,48},{48,64},{64,80},{80,96},{96,112},{112,128},... | collective-permute-start | bytes 245768 | tf_op jit(solution)/shard_map/ppermute | solution.py:43
  154.3 2.7 %collective-permute-start.14 = (f32[5,2,16,128]{3,2,1,0:T(8,128)S(1)}, f32[5,2,16,128]{3,2,1,0:T(8,128)S(1)}, u32[]{:S(2)}, u32[]{:S(2)}) collective-permute-start(f32[5,2,16,128]{3,2,1,0:T(8,128)S(1)} %get-tuple-element.8), channel_id=1, source_target_pairs={{16,0},{32,16},{48,32},{64,48},{80,64},{96,80},{112,96},{128,112},... | collective-permute-start | bytes 245768 | tf_op jit(solution)/shard_map/ppermute | solution.py:44
  157.0 3.0 %collective-permute-start.15 = (f32[5,32,2,128]{3,1,2,0:T(8,128)S(1)}, f32[5,32,2,128]{3,1,2,0:T(8,128)S(1)}, u32[]{:S(2)}, u32[]{:S(2)}) collective-permute-start(f32[5,32,2,128]{3,1,2,0:T(8,128)S(1)} %copy.108), channel_id=1, source_target_pairs={{1,0},{2,1},{3,2},{4,3},{5,4},{6,5},{7,6},{8,7},{9,8},{10,9},{11,1... | collective-permute-start | bytes 491528 | tf_op jit(solution)/shard_map/ppermute | solution.py:42
  160.0 1.8 %collective-permute-done.14 = f32[5,2,16,128]{3,2,1,0:T(8,128)S(1)} collective-permute-done((f32[5,2,16,128]{3,2,1,0:T(8,128)S(1)}, f32[5,2,16,128]{3,2,1,0:T(8,128)S(1)}, u32[]{:S(2)}, u32[]{:S(2)}) %collective-permute-start.14) | collective-permute-done | bytes 81952 | tf_op jit(solution)/shard_map/ppermute | solution.py:44
  161.8 3.6 %fusion.43 = f32[5,32,12,128]{3,2,1,0:T(8,128)S(1)} fusion(f32[5,32,12,128]{3,2,1,0:T(8,128)S(1)} %slice.1026, f32[5,32,16,128]{3,2,1,0:T(8,128)S(1)} %maximum_add_fusion.2, f32[5,2,16,128]{3,2,1,0:T(8,128)S(1)} %collective-permute-done.14, f32[5,2,16,128]{3,2,1,0:T(8,128)S(1)} %collective-permute-done.12, f32[32,12,128]{2,1,0:T(8,128)S(1)} %slice_multiply_fusion, ...), kind=kLoop, calls=%fused_computation.73 | loop fusion | flops 10567680 | bytes 9281536 | tf_op jit(solution)/shard_map/add | solution.py:32
  167.5 1.4 multiply_add_fusion
  169.0 1.5 fusion.47
  (93 shorter events, 12.2 us)
Async XLA Ops:
  0.0 9.2 %copy-start = (f32[5,32,16,128]{3,2,1,0:T(8,128)S(1)}, f32[5,32,16,128]{3,2,1,0:T(8,128)}, u32[]{:S(2)}) copy-start(f32[5,32,16,128]{3,2,1,0:T(8,128)} %param.5) | copy-start | bytes 3932164
  1.5 15.1 %copy-start.1 = (f32[32,16,128]{2,1,0:T(8,128)S(1)}, f32[32,16,128]{2,1,0:T(8,128)}, u32[]{:S(2)}) copy-start(f32[32,16,128]{2,1,0:T(8,128)} %param.6) | copy-start | bytes 786436
  1.5 23.6 %collective-permute-start.1 = (f32[5,32,2,128]{3,1,2,0:T(8,128)S(1)}, f32[5,32,2,128]{3,1,2,0:T(8,128)S(1)}, u32[]{:S(2)}, u32[]{:S(2)}) collective-permute-start(f32[5,32,2,128]{3,1,2,0:T(8,128)S(1)} %copy.47), channel_id=1, source_target_pairs={{0,1},{1,2},{2,3},{3,4},{4,5},{5,6},{6,7},{7,8},{8,9},{9,10},{10,1... | collective-permute-start | bytes 491528 | tf_op jit(solution)/shard_map/ppermute | solution.py:41
  3.7 13.0 %copy-start.2 = (f32[5,32]{1,0:T(8,128)S(1)}, f32[5,32]{1,0:T(8,128)}, u32[]{:S(2)}) copy-start(f32[5,32]{1,0:T(8,128)} %param.7) | copy-start | bytes 1924
  3.7 13.0 %copy-start.3 = (f32[5,32]{1,0:T(8,128)S(1)}, f32[5,32]{1,0:T(8,128)}, u32[]{:S(2)}) copy-start(f32[5,32]{1,0:T(8,128)} %param.8) | copy-start | bytes 1924
  3.8 21.5 %collective-permute-start.3 = (f32[5,32,2,128]{3,1,2,0:T(8,128)S(1)}, f32[5,32,2,128]{3,1,2,0:T(8,128)S(1)}, u32[]{:S(2)}, u32[]{:S(2)}) collective-permute-start(f32[5,32,2,128]{3,1,2,0:T(8,128)S(1)} %copy.55), channel_id=1, source_target_pairs={{1,0},{2,1},{3,2},{4,3},{5,4},{6,5},{7,6},{8,7},{9,8},{10,9},{11,1... | collective-permute-start | bytes 491528 | tf_op jit(solution)/shard_map/ppermute | solution.py:42
  9.2 7.7 %collective-permute-start = (f32[5,2,16,128]{3,2,1,0:T(8,128)S(1)}, f32[5,2,16,128]{3,2,1,0:T(8,128)S(1)}, u32[]{:S(2)}, u32[]{:S(2)}) collective-permute-start(f32[5,2,16,128]{3,2,1,0:T(8,128)S(1)} %get-tuple-element.29), channel_id=1, source_target_pairs={{0,16},{16,32},{32,48},{48,64},{64,80},{80,96},{96,112},{112,128},... | collective-permute-start | bytes 245768 | tf_op jit(solution)/shard_map/ppermute | solution.py:43
  14.6 7.3 %collective-permute-start.2 = (f32[5,2,16,128]{3,2,1,0:T(8,128)S(1)}, f32[5,2,16,128]{3,2,1,0:T(8,128)S(1)}, u32[]{:S(2)}, u32[]{:S(2)}) collective-permute-start(f32[5,2,16,128]{3,2,1,0:T(8,128)S(1)} %get-tuple-element.30), channel_id=1, source_target_pairs={{16,0},{32,16},{48,32},{64,48},{80,64},{96,80},{112,96},{128,112},... | collective-permute-start | bytes 245768 | tf_op jit(solution)/shard_map/ppermute | solution.py:44
  29.1 8.6 %collective-permute-start.4 = (f32[5,2,16,128]{3,2,1,0:T(8,128)S(1)}, f32[5,2,16,128]{3,2,1,0:T(8,128)S(1)}, u32[]{:S(2)}, u32[]{:S(2)}) collective-permute-start(f32[5,2,16,128]{3,2,1,0:T(8,128)S(1)} %get-tuple-element.21), channel_id=1, source_target_pairs={{0,16},{16,32},{32,48},{48,64},{64,80},{80,96},{96,112},{112,128},... | collective-permute-start | bytes 245768 | tf_op jit(solution)/shard_map/ppermute | solution.py:43
  31.3 14.7 %collective-permute-start.5 = (f32[5,32,2,128]{3,1,2,0:T(8,128)S(1)}, f32[5,32,2,128]{3,1,2,0:T(8,128)S(1)}, u32[]{:S(2)}, u32[]{:S(2)}) collective-permute-start(f32[5,32,2,128]{3,1,2,0:T(8,128)S(1)} %copy.63), channel_id=1, source_target_pairs={{0,1},{1,2},{2,3},{3,4},{4,5},{5,6},{6,7},{7,8},{8,9},{9,10},{10,1... | collective-permute-start | bytes 491528 | tf_op jit(solution)/shard_map/ppermute | solution.py:41
  31.4 11.0 %collective-permute-start.6 = (f32[5,2,16,128]{3,2,1,0:T(8,128)S(1)}, f32[5,2,16,128]{3,2,1,0:T(8,128)S(1)}, u32[]{:S(2)}, u32[]{:S(2)}) collective-permute-start(f32[5,2,16,128]{3,2,1,0:T(8,128)S(1)} %get-tuple-element.22), channel_id=1, source_target_pairs={{16,0},{32,16},{48,32},{64,48},{80,64},{96,80},{112,96},{128,112},... | collective-permute-start | bytes 245768 | tf_op jit(solution)/shard_map/ppermute | solution.py:44
  33.8 13.9 %collective-permute-start.7 = (f32[5,32,2,128]{3,1,2,0:T(8,128)S(1)}, f32[5,32,2,128]{3,1,2,0:T(8,128)S(1)}, u32[]{:S(2)}, u32[]{:S(2)}) collective-permute-start(f32[5,32,2,128]{3,1,2,0:T(8,128)S(1)} %copy.71), channel_id=1, source_target_pairs={{1,0},{2,1},{3,2},{4,3},{5,4},{6,5},{7,6},{8,7},{9,8},{10,9},{11,1... | collective-permute-start | bytes 491528 | tf_op jit(solution)/shard_map/ppermute | solution.py:42
  51.1 6.0 %copy-start.4 = (s32[32]{0:T(128)S(1)}, s32[32]{0:T(128)}, u32[]{:S(2)}) copy-start(s32[32]{0:T(128)} %param.9) | copy-start | bytes 388
  51.1 37.6 %all-to-all-start = ((f32[5,32,16,128]{3,2,0,1:T(8,128)}), f32[5,32,16,128]{3,2,0,1:T(8,128)S(1)}, u32[]{:S(2)}, u32[]{:S(2)}) async-start(f32[5,32,16,128]{3,2,0,1:T(8,128)} %copy.79), calls=%async_computation | async-start | bytes 2621440 | tf_op jit(solution)/shard_map/all_to_all | solution.py:70
  127.5 12.7 %collective-permute-start.8 = (f32[5,2,16,128]{3,2,1,0:T(8,128)S(1)}, f32[5,2,16,128]{3,2,1,0:T(8,128)S(1)}, u32[]{:S(2)}, u32[]{:S(2)}) collective-permute-start(f32[5,2,16,128]{3,2,1,0:T(8,128)S(1)} %get-tuple-element.13), channel_id=1, source_target_pairs={{0,16},{16,32},{32,48},{48,64},{64,80},{80,96},{96,112},{112,128},... | collective-permute-start | bytes 245768 | tf_op jit(solution)/shard_map/ppermute | solution.py:43
  134.5 12.3 %collective-permute-start.9 = (f32[5,32,2,128]{3,1,2,0:T(8,128)S(1)}, f32[5,32,2,128]{3,1,2,0:T(8,128)S(1)}, u32[]{:S(2)}, u32[]{:S(2)}) collective-permute-start(f32[5,32,2,128]{3,1,2,0:T(8,128)S(1)} %copy.84), channel_id=1, source_target_pairs={{0,1},{1,2},{2,3},{3,4},{4,5},{5,6},{6,7},{7,8},{8,9},{9,10},{10,1... | collective-permute-start | bytes 491528 | tf_op jit(solution)/shard_map/ppermute | solution.py:41
  134.6 8.7 %collective-permute-start.10 = (f32[5,2,16,128]{3,2,1,0:T(8,128)S(1)}, f32[5,2,16,128]{3,2,1,0:T(8,128)S(1)}, u32[]{:S(2)}, u32[]{:S(2)}) collective-permute-start(f32[5,2,16,128]{3,2,1,0:T(8,128)S(1)} %get-tuple-element.14), channel_id=1, source_target_pairs={{16,0},{32,16},{48,32},{64,48},{80,64},{96,80},{112,96},{128,112},... | collective-permute-start | bytes 245768 | tf_op jit(solution)/shard_map/ppermute | solution.py:44
  136.5 12.1 %collective-permute-start.11 = (f32[5,32,2,128]{3,1,2,0:T(8,128)S(1)}, f32[5,32,2,128]{3,1,2,0:T(8,128)S(1)}, u32[]{:S(2)}, u32[]{:S(2)}) collective-permute-start(f32[5,32,2,128]{3,1,2,0:T(8,128)S(1)} %copy.92), channel_id=1, source_target_pairs={{1,0},{2,1},{3,2},{4,3},{5,4},{6,5},{7,6},{8,7},{9,8},{10,9},{11,1... | collective-permute-start | bytes 491528 | tf_op jit(solution)/shard_map/ppermute | solution.py:42
  150.8 9.2 %collective-permute-start.12 = (f32[5,2,16,128]{3,2,1,0:T(8,128)S(1)}, f32[5,2,16,128]{3,2,1,0:T(8,128)S(1)}, u32[]{:S(2)}, u32[]{:S(2)}) collective-permute-start(f32[5,2,16,128]{3,2,1,0:T(8,128)S(1)} %get-tuple-element.7), channel_id=1, source_target_pairs={{0,16},{16,32},{32,48},{48,64},{64,80},{80,96},{96,112},{112,128},... | collective-permute-start | bytes 245768 | tf_op jit(solution)/shard_map/ppermute | solution.py:43
  154.1 11.3 %collective-permute-start.13 = (f32[5,32,2,128]{3,1,2,0:T(8,128)S(1)}, f32[5,32,2,128]{3,1,2,0:T(8,128)S(1)}, u32[]{:S(2)}, u32[]{:S(2)}) collective-permute-start(f32[5,32,2,128]{3,1,2,0:T(8,128)S(1)} %copy.100), channel_id=1, source_target_pairs={{0,1},{1,2},{2,3},{3,4},{4,5},{5,6},{6,7},{7,8},{8,9},{9,10},{10,1... | collective-permute-start | bytes 491528 | tf_op jit(solution)/shard_map/ppermute | solution.py:41
  154.3 7.5 %collective-permute-start.14 = (f32[5,2,16,128]{3,2,1,0:T(8,128)S(1)}, f32[5,2,16,128]{3,2,1,0:T(8,128)S(1)}, u32[]{:S(2)}, u32[]{:S(2)}) collective-permute-start(f32[5,2,16,128]{3,2,1,0:T(8,128)S(1)} %get-tuple-element.8), channel_id=1, source_target_pairs={{16,0},{32,16},{48,32},{64,48},{80,64},{96,80},{112,96},{128,112},... | collective-permute-start | bytes 245768 | tf_op jit(solution)/shard_map/ppermute | solution.py:44
  157.0 10.2 %collective-permute-start.15 = (f32[5,32,2,128]{3,1,2,0:T(8,128)S(1)}, f32[5,32,2,128]{3,1,2,0:T(8,128)S(1)}, u32[]{:S(2)}, u32[]{:S(2)}) collective-permute-start(f32[5,32,2,128]{3,1,2,0:T(8,128)S(1)} %copy.108), channel_id=1, source_target_pairs={{1,0},{2,1},{3,2},{4,3},{5,4},{6,5},{7,6},{8,7},{9,8},{10,9},{11,1... | collective-permute-start | bytes 491528 | tf_op jit(solution)/shard_map/ppermute | solution.py:42

commit v8 on v4

--- a/solution.py
+++ b/solution.py
@@ -34,21 +34,59 @@
     )
 
 
-def extend(cells, width):
-    sectors, rings = lax.axis_size("azi"), lax.axis_size("rad")
-    rows, cols = cells.shape[-3], cells.shape[-2]
-    left = lax.ppermute(cells[..., cols - width :, :], "azi", [(i, (i + 1) % sectors) for i in range(sectors)])
-    right = lax.ppermute(cells[..., :width, :], "azi", [((i + 1) % sectors, i) for i in range(sectors)])
-    above = lax.ppermute(cells[..., rows - width :, :, :], "rad", [(i, i + 1) for i in range(rings - 1)])
-    below = lax.ppermute(cells[..., :width, :, :], "rad", [(i + 1, i) for i in range(rings - 1)])
-    wide = jnp.concatenate([left, cells, right], axis=-2)
-    corners = [(0, 0)] * (cells.ndim - 2) + [(width, width), (0, 0)]
-    return jnp.concatenate([jnp.pad(above, corners), wide, jnp.pad(below, corners)], axis=-3)
+def shifted(cells, axis, by, closed):
+    peers = lax.axis_size(axis)
+    ends = peers if closed else peers - 1
+    if by > 0:
+        return lax.ppermute(cells, axis, [(i, (i + 1) % peers) for i in range(ends)])
+    return lax.ppermute(cells, axis, [((i + 1) % peers, i) for i in range(ends)])
 
 
-def heun_sections(field, kappa, speed_r, speed_p):
-    first = field + stencil(extend(field, 2), kappa, speed_r, speed_p)
-    return 0.5 * (field + first + stencil(extend(first, 2), kappa, speed_r, speed_p))
+def fringe(strip, cols):
+    return jnp.pad(strip, [(0, 0), (0, 0), (cols, cols), (0, 0)])
+
+
+def heun_sections(field, kap_wide, speed_r, speed_p, kap_strips=None):
+    fcount, rows, cols = field.shape[0], field.shape[1], field.shape[2]
+    sides = (field[:, :, cols - 4 :], field[:, :, :4])
+    if kap_strips is not None:
+        sides = tuple(jnp.concatenate([s, k[None]], axis=0) for s, k in zip(sides, kap_strips))
+    left = shifted(sides[0], "azi", 1, True)
+    right = shifted(sides[1], "azi", -1, True)
+    above = shifted(field[:, rows - 2 :], "rad", 1, False)
+    below = shifted(field[:, :2], "rad", -1, False)
+    if kap_strips is not None:
+        kap_wide = jnp.concatenate([left[fcount, :, 2:], kap_wide, right[fcount, :, :2]], axis=1)
+        left, right = left[:fcount], right[:fcount]
+    wide = jnp.concatenate([left, field, right], axis=2)
+    grown = jnp.concatenate([fringe(above, 4), wide, fringe(below, 4)], axis=1)
+    first = wide[:, :, 2:-2] + stencil(grown, kap_wide, speed_r, speed_p)
+
+    def corners(part):
+        return jnp.concatenate([part[:, :, 2:4], part[:, :, cols + 4 : cols + 6]], axis=2)
+
+    up = jnp.concatenate([first[:, rows - 2 :, 2 : cols + 2], corners(wide[:, rows - 2 :])], axis=2)
+    down = jnp.concatenate([first[:, :2, 2 : cols + 2], corners(wide[:, :2])], axis=2)
+    top = shifted(up, "rad", 1, False)
+    bottom = shifted(down, "rad", -1, False)
+
+    fixes = []
+    for side_rows, halo, outer in ((slice(0, 2), top, True), (slice(rows - 2, rows), bottom, False)):
+        for lo, cstart in ((cols, 0), (cols + 2, cols + 2)):
+            near = grown[:, 2:6] if outer else grown[:, rows - 2 : rows + 2]
+            near = near[:, :, cstart : cstart + 6]
+            block = jnp.zeros((fcount, 2, 6, field.shape[3]), field.dtype)
+            block = block.at[:, :, 2:4].set(halo[:, :, lo : lo + 2])
+            tile = jnp.concatenate([block, near] if outer else [near, block], axis=1)
+            out_rows = slice(0, 2) if outer else slice(rows - 2, rows)
+            kap = kap_wide[out_rows, cstart : cstart + 2]
+            base = wide[:, out_rows, cstart + 2 : cstart + 4]
+            fixes.append((out_rows, cstart, base + stencil(tile, kap, speed_r[:, out_rows], speed_p[:, out_rows])))
+    for out_rows, cstart, value in fixes:
+        first = first.at[:, out_rows, cstart : cstart + 2].set(value)
+    tall = jnp.concatenate([fringe(top[:, :, :cols], 2), first, fringe(bottom[:, :, :cols], 2)], axis=1)
+    inner = stencil(tall, kap_wide[:, 2:-2], speed_r, speed_p)
+    return 0.5 * (field + first[:, :, 2:-2] + inner), kap_wide
 
 
 def shift_rows(half, shifts):
@@ -69,9 +107,11 @@
 
 
 def shards(fields, kappa, radial_speed, azimuth_speed, shifts):
-    half = heun_sections(fields, kappa, radial_speed, azimuth_speed)
+    cols = kappa.shape[1]
+    strips = (kappa[:, cols - 4 :], kappa[:, :4])
+    half, kap_wide = heun_sections(fields, kappa, radial_speed, azimuth_speed, strips)
     moved = shift_rows(half, shifts)
-    return heun_sections(moved, kappa, radial_speed, azimuth_speed)
+    return heun_sections(moved, kap_wide, radial_speed, azimuth_speed)[0]
 
 
 def solution(mesh):

time: 169 us -> 189 us (1.12)
  the two profiles are of different devices: /device:TPU:1 before, /device:TPU:36 now
where the time goes in v8:
time: 189 us; the launch traced here: 188 us
  starting transfers between devices  45.8 us (24%)
  waiting for transfers between devices  45.8 us (24%)
  blocking collectives  39 us (21%)
  other arithmetic  34.4 us (18%)
  local copies, waits for them, and re-layouts  18.8 us (10%)
  between operations  4.6 us (2%)
    all_to_all x1, blocking collectives, shift_rows(): return lax.all_to_all(moved, 'azi', 2, 1, tiled=True)  39 us
    all_to_all x1, waiting for transfers between devices, shift_rows(): full = lax.all_to_all(half, 'azi', 1, 2, tiled=True)  24.8 us
    ppermute x6, starting transfers between devices, shifted(): lax.ppermute(cells, axis, [((i + 1) % peers, i) for i in range(ends)])  24.4 us
    ppermute x6, waiting for transfers between devices, shifted(): lax.ppermute(cells, axis, [(i, (i + 1) % peers) for i in range(ends)])  18 us
    ppermute x6, starting transfers between devices, shifted(): lax.ppermute(cells, axis, [(i, (i + 1) % peers) for i in range(ends)])  11.4 us
    all_to_all x1, starting transfers between devices, shift_rows(): full = lax.all_to_all(half, 'azi', 1, 2, tiled=True)  9.99 us
    add x2, other arithmetic, heun_sections(): first = wide[:, :, 2:-2] + stencil(grown, kap_wide, speed_r, speed_p)  9.46 us
    mul x2, other arithmetic, heun_sections(): return (0.5 * (field + first[:, :, 2:-2] + inner), kap_wide)  7.37 us
  transfers between devices with their start and end apart: 13, of which 6 were waited for; matrix products, arithmetic and copies ran while one was open for 9% of the time, Pallas kernels for 0%

profile of v8, /device:TPU:36, one launch (start us, length us, event | category | flops | bytes accessed | tf_op | source)
XLA Modules:
  0.0 188.3 jit_solution(3052171018723328858)
XLA Ops:
  0.0 1.5 fusion.156
  2.7 1.7 collective-permute-start
  4.4 1.4 collective-permute-start.1
  5.9 1.9 %collective-permute-start.2 = (f32[5,2,16,128]{3,2,1,0:T(8,128)S(1)}, f32[5,2,16,128]{3,2,1,0:T(8,128)S(1)}, u32[]{:S(2)}, u32[]{:S(2)}) collective-permute-start(f32[5,2,16,128]{3,2,1,0:T(8,128)S(1)} %get-tuple-element.227), channel_id=1, source_target_pairs={{0,16},{16,32},{32,48},{48,64},{64,80},{80,96},{96,112},{112,128},... | collective-permute-start | bytes 245768 | tf_op jit(solution)/shard_map/ppermute | solution.py:41
  7.8 6.0 %collective-permute-start.3 = (f32[5,2,16,128]{3,2,1,0:T(8,128)S(1)}, f32[5,2,16,128]{3,2,1,0:T(8,128)S(1)}, u32[]{:S(2)}, u32[]{:S(2)}) collective-permute-start(f32[5,2,16,128]{3,2,1,0:T(8,128)S(1)} %get-tuple-element.228), channel_id=1, source_target_pairs={{16,0},{32,16},{48,32},{64,48},{80,64},{96,80},{112,96},{128,112},... | collective-permute-start | bytes 245768 | tf_op jit(solution)/shard_map/ppermute | solution.py:42
  15.4 7.4 %collective-permute-done = f32[6,32,4,128]{3,2,1,0:T(4,128)S(1)} collective-permute-done((f32[6,32,4,128]{3,2,1,0:T(4,128)S(1)}, f32[6,32,4,128]{3,2,1,0:T(4,128)S(1)}, u32[]{:S(2)}, u32[]{:S(2)}) %collective-permute-start) | collective-permute-done | bytes 393248 | tf_op jit(solution)/shard_map/ppermute | solution.py:41
  25.3 4.7 %fusion.8 = f32[5,32,20,128]{3,2,1,0:T(8,128)S(1)} fusion(f32[5,32,20,128]{3,2,1,0:T(8,128)S(1)} %slice.1592, f32[5,32,4,128]{3,2,1,0:T(4,128)S(1)} %slice.1591, f32[5,32,16,128]{3,2,1,0:T(8,128)S(1)} %copy-done, f32[5,32,24,128]{3,2,1,0:T(8,128)S(1)} %pad_maximum_fusion.4, f32[5,32,4,128]{3,2,1,0:T(4,128)S(1)} %slice.1590, ...), kind=kLoop, calls=%fused_computation.74 | loop fusion | flops 17203200 | bytes 15402240 | tf_op jit(solution)/shard_map/add | solution.py:63
  30.7 3.1 %collective-permute-start.4 = (f32[5,2,20,128]{3,2,1,0:T(8,128)S(1)}, f32[5,2,20,128]{3,2,1,0:T(8,128)S(1)}, u32[]{:S(2)}, u32[]{:S(2)}) collective-permute-start(f32[5,2,20,128]{3,2,1,0:T(8,128)S(1)} %pad_maximum_fusion.9), channel_id=1, source_target_pairs={{0,16},{16,32},{32,48},{48,64},{64,80},{80,96},{96,112},{112,128},... | collective-permute-start | bytes 307208 | tf_op jit(solution)/shard_map/ppermute | solution.py:41
  34.5 4.9 %collective-permute-start.5 = (f32[5,2,20,128]{3,2,1,0:T(8,128)}, f32[5,2,20,128]{3,2,1,0:T(8,128)}, u32[]{:S(2)}, u32[]{:S(2)}) collective-permute-start(f32[5,2,20,128]{3,2,1,0:T(8,128)} %pad_maximum_fusion.10), channel_id=1, source_target_pairs={{16,0},{32,16},{48,32},{64,48},{80,64},{96,80},{112,96},{128,112},... | collective-permute-start | bytes 307208 | tf_op jit(solution)/shard_map/ppermute | solution.py:42
  41.9 2.8 %fusion.144 = f32[5,2,2,128]{3,2,1,0:T(2,128)} fusion(f32[5,2,2,128]{3,2,1,0:T(2,128)S(1)} %get-tuple-element.235, f32[5,32,20,128]{3,2,1,0:T(8,128)S(1)} %fusion.146, s32[]{:T(128)} %bitcast.6, s32[]{:T(128)} %bitcast.7, f32[5,2,2,128]{3,2,1,0:T(2,128)S(1)} %get-tuple-element.251, f32[6,32,4,128]{3,2,1,0:T(4,128)S(1)} %collective-permute-done.1, ...), kind=kLoop, calls=%fused_computation.287 | loop fusion | flops 117760 | bytes 1822729 | tf_op jit(solution)/shard_map/select.19
  44.6 2.2 %scatter.59 = f32[5,32,20,128]{3,2,1,0:T(8,128)S(1)} dynamic-update-slice(f32[5,32,20,128]{3,2,1,0:T(8,128)S(1)} %fusion.146, f32[5,2,2,128]{3,2,1,0:T(2,128)} %fusion.144, s32[]{:T(128)} %constant.468.clone.1, s32[]{:T(128)} %bitcast.6, s32[]{:T(128)} %bitcast.7, s32[]{:T(128)} %constant.468.clone.1) | dynamic-update-slice | bytes 20484 | tf_op jit(solution)/shard_map/scatter | solution.py:86
  47.7 1.1 fusion.142
  48.9 1.1 fusion.140
  51.7 3.4 %fusion.35 = f32[5,32,16,128]{3,2,1,0:T(8,128)S(1)} fusion(f32[5,32,16,128]{3,2,1,0:T(8,128)S(1)} %slice.1647, f32[5,32,20,128]{3,2,1,0:T(8,128)S(1)} %fusion.140, f32[5,34,20,128]{3,2,1,0:T(8,128)S(1)} %get-tuple-element.204, f32[5,34,20,128]{3,2,1,0:T(8,128)S(1)} %get-tuple-element.203, f32[5,32,16,128]{3,2,1,0:T(8,128)S(1)} %copy-done, ...), kind=kLoop, calls=%fused_computation.105 | loop fusion | flops 13762560 | bytes 14681344 | tf_op jit(solution)/shard_map/mul | solution.py:89
  55.2 1.1 copy.8
  56.3 10.0 %all-to-all-start = ((f32[5,32,16,128]{3,2,0,1:T(8,128)}), f32[5,32,16,128]{3,2,0,1:T(8,128)S(1)}, u32[]{:S(2)}, u32[]{:S(2)}) async-start(f32[5,32,16,128]{3,2,0,1:T(8,128)} %copy.8), calls=%async_computation | async-start | bytes 2621440 | tf_op jit(solution)/shard_map/all_to_all | solution.py:96
  70.9 24.8 %all-to-all-done = f32[5,32,16,128]{3,2,0,1:T(8,128)S(1)} async-done(((f32[5,32,16,128]{3,2,0,1:T(8,128)}), f32[5,32,16,128]{3,2,0,1:T(8,128)S(1)}, u32[]{:S(2)}, u32[]{:S(2)}) %all-to-all-start) | async-done | bytes 1310752 | tf_op jit(solution)/shard_map/all_to_all | solution.py:96
  97.4 39.0 %all_to_all.36 = f32[5,2,256,128]{3,1,0,2:T(2,128)S(1)} all-to-all(f32[5,2,256,128]{3,1,0,2:T(2,128)S(1)} %copy.11), channel_id=1, replica_groups=mesh['rad'=16,'azi'=16] {'azi'}, dimensions={2} | all-to-all | bytes 2621440 | tf_op jit(solution)/shard_map/all_to_all | solution.py:106
  137.6 2.1 %collective-permute-start.7 = (f32[5,32,4,128]{3,2,1,0:T(4,128)S(1)}, f32[5,32,4,128]{3,2,1,0:T(4,128)S(1)}, u32[]{:S(2)}, u32[]{:S(2)}) collective-permute-start(f32[5,32,4,128]{3,2,1,0:T(4,128)S(1)} %get-tuple-element.222), channel_id=1, source_target_pairs={{1,0},{2,1},{3,2},{4,3},{5,4},{6,5},{7,6},{8,7},{9,8},{10,9},{11,1... | collective-permute-start | bytes 983048 | tf_op jit(solution)/shard_map/ppermute | solution.py:42
  139.7 1.9 %collective-permute-start.8 = (f32[5,2,16,128]{3,2,1,0:T(8,128)S(1)}, f32[5,2,16,128]{3,2,1,0:T(8,128)S(1)}, u32[]{:S(2)}, u32[]{:S(2)}) collective-permute-start(f32[5,2,16,128]{3,2,1,0:T(8,128)S(1)} %get-tuple-element.219), channel_id=1, source_target_pairs={{0,16},{16,32},{32,48},{48,64},{64,80},{80,96},{96,112},{112,128},... | collective-permute-start | bytes 245768 | tf_op jit(solution)/shard_map/ppermute | solution.py:41
  141.7 6.2 %collective-permute-start.9 = (f32[5,2,16,128]{3,2,1,0:T(8,128)S(1)}, f32[5,2,16,128]{3,2,1,0:T(8,128)S(1)}, u32[]{:S(2)}, u32[]{:S(2)}) collective-permute-start(f32[5,2,16,128]{3,2,1,0:T(8,128)S(1)} %get-tuple-element.220), channel_id=1, source_target_pairs={{16,0},{32,16},{48,32},{64,48},{80,64},{96,80},{112,96},{128,112},... | collective-permute-start | bytes 245768 | tf_op jit(solution)/shard_map/ppermute | solution.py:42
  147.9 4.6 %collective-permute-done.6 = f32[5,32,4,128]{3,2,1,0:T(4,128)S(1)} collective-permute-done((f32[5,32,4,128]{3,2,1,0:T(4,128)S(1)}, f32[5,32,4,128]{3,2,1,0:T(4,128)S(1)}, u32[]{:S(2)}, u32[]{:S(2)}) %collective-permute-start.6) | collective-permute-done | bytes 327712 | tf_op jit(solution)/shard_map/ppermute | solution.py:41
  152.5 2.0 %collective-permute-done.7 = f32[5,32,4,128]{3,2,1,0:T(4,128)S(1)} collective-permute-done((f32[5,32,4,128]{3,2,1,0:T(4,128)S(1)}, f32[5,32,4,128]{3,2,1,0:T(4,128)S(1)}, u32[]{:S(2)}, u32[]{:S(2)}) %collective-permute-start.7) | collective-permute-done | bytes 327712 | tf_op jit(solution)/shard_map/ppermute | solution.py:42
  156.0 4.7 %fusion.19 = f32[5,32,20,128]{3,2,1,0:T(8,128)S(1)} fusion(f32[5,32,20,128]{3,2,1,0:T(8,128)S(1)} %slice.1662, f32[5,32,4,128]{3,2,1,0:T(4,128)S(1)} %collective-permute-done.7, f32[5,32,16,128]{3,2,1,0:T(8,128)S(1)} %bitcast.32, f32[5,32,24,128]{3,2,1,0:T(8,128)S(1)} %pad_maximum_fusion.5, f32[5,32,4,128]{3,2,1,0:T(4,128)S(1)} %collective-permute-done.6, ...), kind=kLoop, calls=%fused_computation.85 | loop fusion | flops 17203200 | bytes 15402240 | tf_op jit(solution)/shard_map/add | solution.py:63
  161.5 3.7 %collective-permute-start.11 = (f32[5,2,20,128]{3,2,1,0:T(8,128)}, f32[5,2,20,128]{3,2,1,0:T(8,128)}, u32[]{:S(2)}, u32[]{:S(2)}) collective-permute-start(f32[5,2,20,128]{3,2,1,0:T(8,128)} %pad_maximum_fusion.12), channel_id=1, source_target_pairs={{16,0},{32,16},{48,32},{64,48},{80,64},{96,80},{112,96},{128,112},... | collective-permute-start | bytes 307208 | tf_op jit(solution)/shard_map/ppermute | solution.py:42
  165.3 1.9 %collective-permute-start.10 = (f32[5,2,20,128]{3,2,1,0:T(8,128)S(1)}, f32[5,2,20,128]{3,2,1,0:T(8,128)S(1)}, u32[]{:S(2)}, u32[]{:S(2)}) collective-permute-start(f32[5,2,20,128]{3,2,1,0:T(8,128)S(1)} %pad_maximum_fusion.11), channel_id=1, source_target_pairs={{0,16},{16,32},{32,48},{48,64},{64,80},{80,96},{96,112},{112,128},... | collective-permute-start | bytes 307208 | tf_op jit(solution)/shard_map/ppermute | solution.py:41
  167.9 6.0 %collective-permute-done.10 = f32[5,2,20,128]{3,2,1,0:T(8,128)S(1)} collective-permute-done((f32[5,2,20,128]{3,2,1,0:T(8,128)S(1)}, f32[5,2,20,128]{3,2,1,0:T(8,128)S(1)}, u32[]{:S(2)}, u32[]{:S(2)}) %collective-permute-start.10) | collective-permute-done | bytes 102432 | tf_op jit(solution)/shard_map/ppermute | solution.py:41
  174.5 2.7 %fusion.136 = f32[5,2,2,128]{3,2,1,0:T(2,128)} fusion(f32[5,2,2,128]{3,2,1,0:T(2,128)S(1)} %get-tuple-element.239, f32[5,32,20,128]{3,2,1,0:T(8,128)S(1)} %fusion.138, s32[]{:T(128)} %bitcast.6, s32[]{:T(128)} %bitcast.7, f32[5,2,2,128]{3,2,1,0:T(2,128)S(1)} %get-tuple-element.247, f32[5,32,4,128]{3,2,1,0:T(4,128)S(1)} %collective-permute-done.7, ...), kind=kLoop, calls=%fused_computation.275 | loop fusion | flops 117760 | bytes 1822729 | tf_op jit(solution)/shard_map/select.27
  177.3 2.2 %scatter.71 = f32[5,32,20,128]{3,2,1,0:T(8,128)S(1)} dynamic-update-slice(f32[5,32,20,128]{3,2,1,0:T(8,128)S(1)} %fusion.138, f32[5,2,2,128]{3,2,1,0:T(2,128)} %fusion.136, s32[]{:T(128)} %constant.468.clone.1, s32[]{:T(128)} %bitcast.6, s32[]{:T(128)} %bitcast.7, s32[]{:T(128)} %constant.468.clone.1) | dynamic-update-slice | bytes 20484 | tf_op jit(solution)/shard_map/scatter | solution.py:86
  180.4 1.2 fusion.134
  181.6 1.0 fusion.132
  184.4 3.9 %fusion.47 = f32[5,32,16,128]{3,2,1,0:T(8,128)} fusion(f32[5,32,16,128]{3,2,1,0:T(8,128)S(1)} %slice.1717, f32[5,32,20,128]{3,2,1,0:T(8,128)S(1)} %fusion.132, f32[5,34,20,128]{3,2,1,0:T(8,128)S(1)} %get-tuple-element.198, f32[5,34,20,128]{3,2,1,0:T(8,128)S(1)} %get-tuple-element.197, f32[5,32,16,128]{3,2,1,0:T(8,128)S(1)} %bitcast.38, ...), kind=kLoop, calls=%fused_computation.117 | loop fusion | flops 13762560 | bytes 14681344 | tf_op jit(solution)/shard_map/mul | solution.py:89
  (140 shorter events, 21.3 us)
Async XLA Ops:
  0.0 14.6 %copy-start.32 = (s32[4]{0:T(128)S(1)}, s32[4]{0:T(128)}, u32[]{:S(2)}) copy-start(s32[4]{0:T(128)} %constant.471.clone.1) | copy-start | bytes 52
  0.0 5.8 %copy-start = (f32[5,32,16,128]{3,2,1,0:T(8,128)S(1)}, f32[5,32,16,128]{3,2,1,0:T(8,128)}, u32[]{:S(2)}) copy-start(f32[5,32,16,128]{3,2,1,0:T(8,128)} %param.37) | copy-start | bytes 3932164
  0.0 15.4 %copy-start.9 = (f32[32,16,128]{2,1,0:T(8,128)S(1)}, f32[32,16,128]{2,1,0:T(8,128)}, u32[]{:S(2)}) copy-start(f32[32,16,128]{2,1,0:T(8,128)} %param.38) | copy-start | bytes 786436
  0.0 13.8 %copy-start.26 = (f32[5,32]{1,0:T(8,128)S(1)}, f32[5,32]{1,0:T(8,128)}, u32[]{:S(2)}) copy-start(f32[5,32]{1,0:T(8,128)} %param.39) | copy-start | bytes 1924
  0.0 13.8 %copy-start.27 = (f32[5,32]{1,0:T(8,128)S(1)}, f32[5,32]{1,0:T(8,128)}, u32[]{:S(2)}) copy-start(f32[5,32]{1,0:T(8,128)} %param.40) | copy-start | bytes 1924
  2.7 20.2 %collective-permute-start = (f32[6,32,4,128]{3,2,1,0:T(4,128)S(1)}, f32[6,32,4,128]{3,2,1,0:T(4,128)S(1)}, u32[]{:S(2)}, u32[]{:S(2)}) collective-permute-start(f32[6,32,4,128]{3,2,1,0:T(4,128)S(1)} %pad_maximum_fusion.7), channel_id=1, source_target_pairs={{0,1},{1,2},{2,3},{3,4},{4,5},{5,6},{6,7},{7,8},{8,9},{9,10},{10,1... | collective-permute-start | bytes 1179656 | tf_op jit(solution)/shard_map/ppermute | solution.py:41
  4.4 19.5 %collective-permute-start.1 = (f32[6,32,4,128]{3,2,1,0:T(4,128)S(1)}, f32[6,32,4,128]{3,2,1,0:T(4,128)S(1)}, u32[]{:S(2)}, u32[]{:S(2)}) collective-permute-start(f32[6,32,4,128]{3,2,1,0:T(4,128)S(1)} %pad_maximum_fusion.8), channel_id=1, source_target_pairs={{1,0},{2,1},{3,2},{4,3},{5,4},{6,5},{7,6},{8,7},{9,8},{10,9},{11,1... | collective-permute-start | bytes 1179656 | tf_op jit(solution)/shard_map/ppermute | solution.py:42
  5.9 18.7 %collective-permute-start.2 = (f32[5,2,16,128]{3,2,1,0:T(8,128)S(1)}, f32[5,2,16,128]{3,2,1,0:T(8,128)S(1)}, u32[]{:S(2)}, u32[]{:S(2)}) collective-permute-start(f32[5,2,16,128]{3,2,1,0:T(8,128)S(1)} %get-tuple-element.227), channel_id=1, source_target_pairs={{0,16},{16,32},{32,48},{48,64},{64,80},{80,96},{96,112},{112,128},... | collective-permute-start | bytes 245768 | tf_op jit(solution)/shard_map/ppermute | solution.py:41
  7.8 16.8 %collective-permute-start.3 = (f32[5,2,16,128]{3,2,1,0:T(8,128)S(1)}, f32[5,2,16,128]{3,2,1,0:T(8,128)S(1)}, u32[]{:S(2)}, u32[]{:S(2)}) collective-permute-start(f32[5,2,16,128]{3,2,1,0:T(8,128)S(1)} %get-tuple-element.228), channel_id=1, source_target_pairs={{16,0},{32,16},{48,32},{64,48},{80,64},{96,80},{112,96},{128,112},... | collective-permute-start | bytes 245768 | tf_op jit(solution)/shard_map/ppermute | solution.py:42
  13.9 11.1 %copy-start.14 = (f32[5,32]{1,0:T(8,128)}, f32[5,32]{1,0:T(8,128)S(1)}, u32[]{:S(2)}) copy-start(f32[5,32]{1,0:T(8,128)S(1)} %get-tuple-element.261) | copy-start | bytes 1924
  13.9 11.1 %copy-start.18 = (f32[5,32]{1,0:T(8,128)}, f32[5,32]{1,0:T(8,128)S(1)}, u32[]{:S(2)}) copy-start(f32[5,32]{1,0:T(8,128)S(1)} %get-tuple-element.262) | copy-start | bytes 1924
  22.9 18.4 %copy-start.10 = (f32[6,32,4,128]{3,2,1,0:T(4,128)}, f32[6,32,4,128]{3,2,1,0:T(4,128)S(1)}, u32[]{:S(2)}) copy-start(f32[6,32,4,128]{3,2,1,0:T(4,128)S(1)} %collective-permute-done) | copy-start | bytes 1179652
  22.9 18.4 %copy-start.3 = (f32[5,32,4,128]{3,2,1,0:T(4,128)}, f32[5,32,4,128]{3,2,1,0:T(4,128)S(1)}, u32[]{:S(2)}) copy-start(f32[5,32,4,128]{3,2,1,0:T(4,128)S(1)} %slice.1590) | copy-start | bytes 983044
  23.9 17.6 %copy-start.11 = (f32[6,32,4,128]{3,2,1,0:T(4,128)}, f32[6,32,4,128]{3,2,1,0:T(4,128)S(1)}, u32[]{:S(2)}) copy-start(f32[6,32,4,128]{3,2,1,0:T(4,128)S(1)} %collective-permute-done.1) | copy-start | bytes 1179652
  23.9 17.5 %copy-start.1 = (f32[5,32,4,128]{3,2,1,0:T(4,128)}, f32[5,32,4,128]{3,2,1,0:T(4,128)S(1)}, u32[]{:S(2)}) copy-start(f32[5,32,4,128]{3,2,1,0:T(4,128)S(1)} %slice.1591) | copy-start | bytes 983044
  30.7 10.5 %collective-permute-start.4 = (f32[5,2,20,128]{3,2,1,0:T(8,128)S(1)}, f32[5,2,20,128]{3,2,1,0:T(8,128)S(1)}, u32[]{:S(2)}, u32[]{:S(2)}) collective-permute-start(f32[5,2,20,128]{3,2,1,0:T(8,128)S(1)} %pad_maximum_fusion.9), channel_id=1, source_target_pairs={{0,16},{16,32},{32,48},{48,64},{64,80},{80,96},{96,112},{112,128},... | collective-permute-start | bytes 307208 | tf_op jit(solution)/shard_map/ppermute | solution.py:41
  34.5 12.4 %collective-permute-start.5 = (f32[5,2,20,128]{3,2,1,0:T(8,128)}, f32[5,2,20,128]{3,2,1,0:T(8,128)}, u32[]{:S(2)}, u32[]{:S(2)}) collective-permute-start(f32[5,2,20,128]{3,2,1,0:T(8,128)} %pad_maximum_fusion.10), channel_id=1, source_target_pairs={{16,0},{32,16},{48,32},{64,48},{80,64},{96,80},{112,96},{128,112},... | collective-permute-start | bytes 307208 | tf_op jit(solution)/shard_map/ppermute | solution.py:42
  48.9 2.2 %slice-start = ((f32[5,2,20,128]{3,2,1,0:T(8,128)}), f32[5,2,16,128]{3,2,1,0:T(8,128)S(1)}, s32[]{:S(2)}) async-start(f32[5,2,20,128]{3,2,1,0:T(8,128)} %copy-done.12), calls=%async_computation.2 | async-start | bytes 163840 | tf_op jit(solution)/shard_map/slice | solution.py:87
  56.3 10.0 %copy-start.33 = (s32[32]{0:T(128)S(1)}, s32[32]{0:T(128)}, u32[]{:S(2)}) copy-start(s32[32]{0:T(128)} %param.41) | copy-start | bytes 388
  56.3 39.3 %all-to-all-start = ((f32[5,32,16,128]{3,2,0,1:T(8,128)}), f32[5,32,16,128]{3,2,0,1:T(8,128)S(1)}, u32[]{:S(2)}, u32[]{:S(2)}) async-start(f32[5,32,16,128]{3,2,0,1:T(8,128)} %copy.8), calls=%async_computation | async-start | bytes 2621440 | tf_op jit(solution)/shard_map/all_to_all | solution.py:96
  136.7 15.8 %collective-permute-start.6 = (f32[5,32,4,128]{3,2,1,0:T(4,128)S(1)}, f32[5,32,4,128]{3,2,1,0:T(4,128)S(1)}, u32[]{:S(2)}, u32[]{:S(2)}) collective-permute-start(f32[5,32,4,128]{3,2,1,0:T(4,128)S(1)} %get-tuple-element.221), channel_id=1, source_target_pairs={{0,1},{1,2},{2,3},{3,4},{4,5},{5,6},{6,7},{7,8},{8,9},{9,10},{10,1... | collective-permute-start | bytes 983048 | tf_op jit(solution)/shard_map/ppermute | solution.py:41
  137.6 16.9 %collective-permute-start.7 = (f32[5,32,4,128]{3,2,1,0:T(4,128)S(1)}, f32[5,32,4,128]{3,2,1,0:T(4,128)S(1)}, u32[]{:S(2)}, u32[]{:S(2)}) collective-permute-start(f32[5,32,4,128]{3,2,1,0:T(4,128)S(1)} %get-tuple-element.222), channel_id=1, source_target_pairs={{1,0},{2,1},{3,2},{4,3},{5,4},{6,5},{7,6},{8,7},{9,8},{10,9},{11,1... | collective-permute-start | bytes 983048 | tf_op jit(solution)/shard_map/ppermute | solution.py:42
  139.7 15.3 %collective-permute-start.8 = (f32[5,2,16,128]{3,2,1,0:T(8,128)S(1)}, f32[5,2,16,128]{3,2,1,0:T(8,128)S(1)}, u32[]{:S(2)}, u32[]{:S(2)}) collective-permute-start(f32[5,2,16,128]{3,2,1,0:T(8,128)S(1)} %get-tuple-element.219), channel_id=1, source_target_pairs={{0,16},{16,32},{32,48},{48,64},{64,80},{80,96},{96,112},{112,128},... | collective-permute-start | bytes 245768 | tf_op jit(solution)/shard_map/ppermute | solution.py:41
  141.7 13.4 %collective-permute-start.9 = (f32[5,2,16,128]{3,2,1,0:T(8,128)S(1)}, f32[5,2,16,128]{3,2,1,0:T(8,128)S(1)}, u32[]{:S(2)}, u32[]{:S(2)}) collective-permute-start(f32[5,2,16,128]{3,2,1,0:T(8,128)S(1)} %get-tuple-element.220), channel_id=1, source_target_pairs={{16,0},{32,16},{48,32},{64,48},{80,64},{96,80},{112,96},{128,112},... | collective-permute-start | bytes 245768 | tf_op jit(solution)/shard_map/ppermute | solution.py:42
  152.5 21.4 %copy-start.4 = (f32[5,32,4,128]{3,2,1,0:T(4,128)}, f32[5,32,4,128]{3,2,1,0:T(4,128)S(1)}, u32[]{:S(2)}) copy-start(f32[5,32,4,128]{3,2,1,0:T(4,128)S(1)} %collective-permute-done.6) | copy-start | bytes 983044
  154.5 19.6 %copy-start.5 = (f32[5,32,4,128]{3,2,1,0:T(4,128)}, f32[5,32,4,128]{3,2,1,0:T(4,128)S(1)}, u32[]{:S(2)}) copy-start(f32[5,32,4,128]{3,2,1,0:T(4,128)S(1)} %collective-permute-done.7) | copy-start | bytes 983044
  160.8 13.2 %copy-start.31 = (f32[2,2,128]{2,1,0:T(2,128)S(1)}, f32[2,2,128]{2,1,0:T(2,128)}, u32[]{:S(2)}) copy-start(f32[2,2,128]{2,1,0:T(2,128)} %copy-done.30) | copy-start | bytes 6148
  160.8 4.4 %copy-start.23 = (f32[5,2,2,128]{3,2,1,0:T(2,128)}, f32[5,2,2,128]{3,2,1,0:T(2,128)S(1)}, u32[]{:S(2)}) copy-start(f32[5,2,2,128]{3,2,1,0:T(2,128)S(1)} %get-tuple-element.240) | copy-start | bytes 30724
  160.8 4.4 %copy-start.25 = (f32[5,2,2,128]{3,2,1,0:T(2,128)}, f32[5,2,2,128]{3,2,1,0:T(2,128)S(1)}, u32[]{:S(2)}) copy-start(f32[5,2,2,128]{3,2,1,0:T(2,128)S(1)} %get-tuple-element.241) | copy-start | bytes 30724
  161.5 18.0 %collective-permute-start.11 = (f32[5,2,20,128]{3,2,1,0:T(8,128)}, f32[5,2,20,128]{3,2,1,0:T(8,128)}, u32[]{:S(2)}, u32[]{:S(2)}) collective-permute-start(f32[5,2,20,128]{3,2,1,0:T(8,128)} %pad_maximum_fusion.12), channel_id=1, source_target_pairs={{16,0},{32,16},{48,32},{64,48},{80,64},{96,80},{112,96},{128,112},... | collective-permute-start | bytes 307208 | tf_op jit(solution)/shard_map/ppermute | solution.py:42
  165.3 9.3 %copy-start.29 = (f32[2,2,128]{2,1,0:T(2,128)S(1)}, f32[2,2,128]{2,1,0:T(2,128)}, u32[]{:S(2)}) copy-start(f32[2,2,128]{2,1,0:T(2,128)} %copy-done.28) | copy-start | bytes 6148
  165.3 8.6 %collective-permute-start.10 = (f32[5,2,20,128]{3,2,1,0:T(8,128)S(1)}, f32[5,2,20,128]{3,2,1,0:T(8,128)S(1)}, u32[]{:S(2)}, u32[]{:S(2)}) collective-permute-start(f32[5,2,20,128]{3,2,1,0:T(8,128)S(1)} %pad_maximum_fusion.11), channel_id=1, source_target_pairs={{0,16},{16,32},{32,48},{48,64},{64,80},{80,96},{96,112},{112,128},... | collective-permute-start | bytes 307208 | tf_op jit(solution)/shard_map/ppermute | solution.py:41
  (17 other events, 17.6 us)

commit v9 on v8

--- a/solution.py
+++ b/solution.py
@@ -70,20 +70,28 @@
     top = shifted(up, "rad", 1, False)
     bottom = shifted(down, "rad", -1, False)
 
-    fixes = []
-    for side_rows, halo, outer in ((slice(0, 2), top, True), (slice(rows - 2, rows), bottom, False)):
+    tiles, kaps, rates, turns, bases = [], [], [], [], []
+    for halo, outer in ((top, True), (bottom, False)):
+        out_rows = slice(0, 2) if outer else slice(rows - 2, rows)
         for lo, cstart in ((cols, 0), (cols + 2, cols + 2)):
             near = grown[:, 2:6] if outer else grown[:, rows - 2 : rows + 2]
             near = near[:, :, cstart : cstart + 6]
-            block = jnp.zeros((fcount, 2, 6, field.shape[3]), field.dtype)
-            block = block.at[:, :, 2:4].set(halo[:, :, lo : lo + 2])
-            tile = jnp.concatenate([block, near] if outer else [near, block], axis=1)
-            out_rows = slice(0, 2) if outer else slice(rows - 2, rows)
-            kap = kap_wide[out_rows, cstart : cstart + 2]
-            base = wide[:, out_rows, cstart + 2 : cstart + 4]
-            fixes.append((out_rows, cstart, base + stencil(tile, kap, speed_r[:, out_rows], speed_p[:, out_rows])))
-    for out_rows, cstart, value in fixes:
-        first = first.at[:, out_rows, cstart : cstart + 2].set(value)
+            block = jnp.pad(halo[:, :, lo : lo + 2], [(0, 0), (0, 0), (2, 2), (0, 0)])
+            tiles.append(jnp.concatenate([block, near] if outer else [near, block], axis=1))
+            kaps.append(kap_wide[out_rows, cstart : cstart + 2])
+            rates.append(speed_r[:, out_rows])
+            turns.append(speed_p[:, out_rows])
+            bases.append(wide[:, out_rows, cstart + 2 : cstart + 4])
+    fixed = jnp.stack(bases) + jax.vmap(stencil)(jnp.stack(tiles), jnp.stack(kaps), jnp.stack(rates), jnp.stack(turns))
+    gap = jnp.zeros((fcount, 2, cols, field.shape[3]), field.dtype)
+    bands = [jnp.concatenate([fixed[2 * k], gap, fixed[2 * k + 1]], axis=2) for k in (0, 1)]
+    middle = jnp.zeros((fcount, rows - 4, cols + 4, field.shape[3]), field.dtype)
+    patches = jnp.concatenate([bands[0], middle, bands[1]], axis=1)
+    row_at = lax.broadcasted_iota(jnp.int32, (rows, cols + 4), 0)
+    col_at = lax.broadcasted_iota(jnp.int32, (rows, cols + 4), 1)
+    edge_rows = (row_at < 2) | (row_at >= rows - 2)
+    edge_cols = (col_at < 2) | (col_at >= cols + 2)
+    first = jnp.where((edge_rows & edge_cols)[None, :, :, None], patches, first)
     tall = jnp.concatenate([fringe(top[:, :, :cols], 2), first, fringe(bottom[:, :, :cols], 2)], axis=1)
     inner = stencil(tall, kap_wide[:, 2:-2], speed_r, speed_p)
     return 0.5 * (field + first[:, :, 2:-2] + inner), kap_wide

time: 189 us -> 175 us (0.926)
  the two profiles are of different devices: /device:TPU:36 before, /device:TPU:1 now
where the time goes in v9:
time: 175 us; the launch traced here: 172 us
  starting transfers between devices  50.8 us (29%)
  waiting for transfers between devices  47.3 us (27%)
  blocking collectives  37.5 us (21%)
  other arithmetic  22.2 us (13%)
  local copies, waits for them, and re-layouts  10.1 us (6%)
  between operations  4.49 us (3%)
    all_to_all x1, blocking collectives, shift_rows(): return lax.all_to_all(moved, 'azi', 2, 1, tiled=True)  37.5 us
    all_to_all x1, waiting for transfers between devices, shift_rows(): full = lax.all_to_all(half, 'azi', 1, 2, tiled=True)  25.4 us
    ppermute x6, starting transfers between devices, shifted(): lax.ppermute(cells, axis, [(i, (i + 1) % peers) for i in range(ends)])  25 us
    ppermute x6, waiting for transfers between devices, shifted(): lax.ppermute(cells, axis, [((i + 1) % peers, i) for i in range(ends)])  20.3 us
    ppermute x6, starting transfers between devices, shifted(): lax.ppermute(cells, axis, [((i + 1) % peers, i) for i in range(ends)])  16.8 us
    add x2, other arithmetic, heun_sections(): first = wide[:, :, 2:-2] + stencil(grown, kap_wide, speed_r, speed_p)  9.51 us
    all_to_all x1, starting transfers between devices, shift_rows(): full = lax.all_to_all(half, 'azi', 1, 2, tiled=True)  9.02 us
    mul x2, other arithmetic, heun_sections(): return (0.5 * (field + first[:, :, 2:-2] + inner), kap_wide)  7.4 us
  transfers between devices with their start and end apart: 13, of which 8 were waited for; matrix products, arithmetic and copies ran while one was open for 3% of the time, Pallas kernels for 0%

profile of v9, /device:TPU:1, one launch (start us, length us, event | category | flops | bytes accessed | tf_op | source)
XLA Modules:
  0.0 172.4 jit_solution(18143880569061830161)
XLA Ops:
  0.0 1.5 fusion.99
  1.5 1.0 slice_bitcast_fusion.1
  2.7 2.2 %collective-permute-start = (f32[6,32,4,128]{3,2,1,0:T(4,128)S(1)}, f32[6,32,4,128]{3,2,1,0:T(4,128)S(1)}, u32[]{:S(2)}, u32[]{:S(2)}) collective-permute-start(f32[6,32,4,128]{3,2,1,0:T(4,128)S(1)} %pad_maximum_fusion.11), channel_id=1, source_target_pairs={{0,1},{1,2},{2,3},{3,4},{4,5},{5,6},{6,7},{7,8},{8,9},{9,10},{10,1... | collective-permute-start | bytes 1179656 | tf_op jit(solution)/shard_map/ppermute | solution.py:41
  5.0 5.4 %collective-permute-start.1 = (f32[6,32,4,128]{3,2,1,0:T(4,128)S(1)}, f32[6,32,4,128]{3,2,1,0:T(4,128)S(1)}, u32[]{:S(2)}, u32[]{:S(2)}) collective-permute-start(f32[6,32,4,128]{3,2,1,0:T(4,128)S(1)} %pad_maximum_fusion.12), channel_id=1, source_target_pairs={{1,0},{2,1},{3,2},{4,3},{5,4},{6,5},{7,6},{8,7},{9,8},{10,9},{11,1... | collective-permute-start | bytes 1179656 | tf_op jit(solution)/shard_map/ppermute | solution.py:42
  11.0 5.4 %collective-permute-start.2 = (f32[5,2,16,128]{3,2,1,0:T(8,128)}, f32[5,2,16,128]{3,2,1,0:T(8,128)}, u32[]{:S(2)}, u32[]{:S(2)}) collective-permute-start(f32[5,2,16,128]{3,2,1,0:T(8,128)} %get-tuple-element.35), channel_id=1, source_target_pairs={{0,16},{16,32},{32,48},{48,64},{64,80},{80,96},{96,112},{112,128},... | collective-permute-start | bytes 245768 | tf_op jit(solution)/shard_map/ppermute | solution.py:41
  16.4 1.9 %collective-permute-start.3 = (f32[5,2,16,128]{3,2,1,0:T(8,128)S(1)}, f32[5,2,16,128]{3,2,1,0:T(8,128)}, u32[]{:S(2)}, u32[]{:S(2)}) collective-permute-start(f32[5,2,16,128]{3,2,1,0:T(8,128)S(1)} %get-tuple-element.36), channel_id=1, source_target_pairs={{16,0},{32,16},{48,32},{64,48},{80,64},{96,80},{112,96},{128,112},... | collective-permute-start | bytes 245768 | tf_op jit(solution)/shard_map/ppermute | solution.py:42
  19.3 1.6 collective-permute-done
  20.9 3.0 %collective-permute-done.1 = f32[6,32,4,128]{3,2,1,0:T(4,128)S(1)} collective-permute-done((f32[6,32,4,128]{3,2,1,0:T(4,128)S(1)}, f32[6,32,4,128]{3,2,1,0:T(4,128)S(1)}, u32[]{:S(2)}, u32[]{:S(2)}) %collective-permute-start.1) | collective-permute-done | bytes 393248 | tf_op jit(solution)/shard_map/ppermute | solution.py:42
  24.9 1.4 collective-permute-done.3
  26.3 1.3 select_maximum_fusion.7
  27.6 4.8 %fusion.18 = f32[5,32,20,128]{3,2,1,0:T(8,128)S(1)} fusion(f32[5,32,20,128]{3,2,1,0:T(8,128)S(1)} %slice.726, f32[5,32,4,128]{3,2,1,0:T(4,128)S(1)} %slice.725, f32[5,32,16,128]{3,2,1,0:T(8,128)S(1)} %copy-done, f32[5,32,24,128]{3,2,1,0:T(8,128)S(1)} %pad_maximum_fusion.8, f32[5,32,4,128]{3,2,1,0:T(4,128)S(1)} %slice.724, ...), kind=kLoop, calls=%fused_computation.72 | loop fusion | flops 17203200 | bytes 15402240 | tf_op jit(solution)/shard_map/add | solution.py:63
  32.4 0.8 fusion.103
  33.2 4.5 %collective-permute-start.4 = (f32[5,2,20,128]{3,2,1,0:T(8,128)S(1)}, f32[5,2,20,128]{3,2,1,0:T(8,128)S(1)}, u32[]{:S(2)}, u32[]{:S(2)}) collective-permute-start(f32[5,2,20,128]{3,2,1,0:T(8,128)S(1)} %pad_maximum_fusion.13), channel_id=1, source_target_pairs={{0,16},{16,32},{32,48},{48,64},{64,80},{80,96},{96,112},{112,128},... | collective-permute-start | bytes 307208 | tf_op jit(solution)/shard_map/ppermute | solution.py:41
  37.7 1.9 %collective-permute-start.5 = (f32[5,2,20,128]{3,2,1,0:T(8,128)S(1)}, f32[5,2,20,128]{3,2,1,0:T(8,128)S(1)}, u32[]{:S(2)}, u32[]{:S(2)}) collective-permute-start(f32[5,2,20,128]{3,2,1,0:T(8,128)S(1)} %pad_maximum_fusion.14), channel_id=1, source_target_pairs={{16,0},{32,16},{48,32},{64,48},{80,64},{96,80},{112,96},{128,112},... | collective-permute-start | bytes 307208 | tf_op jit(solution)/shard_map/ppermute | solution.py:42
  39.6 0.7 fusion.101
  40.4 5.0 %collective-permute-done.5 = f32[5,2,20,128]{3,2,1,0:T(8,128)S(1)} collective-permute-done((f32[5,2,20,128]{3,2,1,0:T(8,128)S(1)}, f32[5,2,20,128]{3,2,1,0:T(8,128)S(1)}, u32[]{:S(2)}, u32[]{:S(2)}) %collective-permute-start.5) | collective-permute-done | bytes 102432 | tf_op jit(solution)/shard_map/ppermute | solution.py:42
  46.6 3.5 %fusion.45 = f32[5,32,16,128]{3,2,1,0:T(8,128)S(1)} fusion(f32[5,32,16,128]{3,2,1,0:T(8,128)S(1)} %slice.757, f32[5,32,20,128]{3,2,1,0:T(8,128)S(1)} %fusion.3, f32[5,34,20,128]{3,2,1,0:T(8,128)S(1)} %get-tuple-element.12, f32[5,34,20,128]{3,2,1,0:T(8,128)S(1)} %get-tuple-element.11, f32[5,32,16,128]{3,2,1,0:T(8,128)S(1)} %copy-done, ...), kind=kLoop, calls=%fused_computation.103 | loop fusion | flops 13762560 | bytes 14681344 | tf_op jit(solution)/shard_map/mul | solution.py:97
  50.0 1.1 copy.52
  51.2 9.0 %all-to-all-start = ((f32[5,32,16,128]{3,2,0,1:T(8,128)}), f32[5,32,16,128]{3,2,0,1:T(8,128)S(1)}, u32[]{:S(2)}, u32[]{:S(2)}) async-start(f32[5,32,16,128]{3,2,0,1:T(8,128)} %copy.52), calls=%async_computation | async-start | bytes 2621440 | tf_op jit(solution)/shard_map/all_to_all | solution.py:104
  60.3 0.6 fusion.110
  64.8 25.4 %all-to-all-done = f32[5,32,16,128]{3,2,0,1:T(8,128)S(1)} async-done(((f32[5,32,16,128]{3,2,0,1:T(8,128)}), f32[5,32,16,128]{3,2,0,1:T(8,128)S(1)}, u32[]{:S(2)}, u32[]{:S(2)}) %all-to-all-start) | async-done | bytes 1310752 | tf_op jit(solution)/shard_map/all_to_all | solution.py:104
  90.9 1.0 copy.55
  91.9 37.5 %all_to_all.36 = f32[5,2,256,128]{3,1,0,2:T(2,128)S(1)} all-to-all(f32[5,2,256,128]{3,1,0,2:T(2,128)S(1)} %copy.55), channel_id=1, replica_groups=mesh['rad'=16,'azi'=16] {'azi'}, dimensions={2} | all-to-all | bytes 2621440 | tf_op jit(solution)/shard_map/all_to_all | solution.py:114
  129.9 3.6 %collective-permute-start.7 = (f32[5,32,4,128]{3,2,1,0:T(4,128)S(1)}, f32[5,32,4,128]{3,2,1,0:T(4,128)S(1)}, u32[]{:S(2)}, u32[]{:S(2)}) collective-permute-start(f32[5,32,4,128]{3,2,1,0:T(4,128)S(1)} %get-tuple-element.30), channel_id=1, source_target_pairs={{1,0},{2,1},{3,2},{4,3},{5,4},{6,5},{7,6},{8,7},{9,8},{10,9},{11,1... | collective-permute-start | bytes 983048 | tf_op jit(solution)/shard_map/ppermute | solution.py:42
  133.5 8.8 %collective-permute-start.8 = (f32[5,2,16,128]{3,2,1,0:T(8,128)S(1)}, f32[5,2,16,128]{3,2,1,0:T(8,128)S(1)}, u32[]{:S(2)}, u32[]{:S(2)}) collective-permute-start(f32[5,2,16,128]{3,2,1,0:T(8,128)S(1)} %get-tuple-element.27), channel_id=1, source_target_pairs={{0,16},{16,32},{32,48},{48,64},{64,80},{80,96},{96,112},{112,128},... | collective-permute-start | bytes 245768 | tf_op jit(solution)/shard_map/ppermute | solution.py:41
  142.3 2.1 %collective-permute-start.9 = (f32[5,2,16,128]{3,2,1,0:T(8,128)S(1)}, f32[5,2,16,128]{3,2,1,0:T(8,128)S(1)}, u32[]{:S(2)}, u32[]{:S(2)}) collective-permute-start(f32[5,2,16,128]{3,2,1,0:T(8,128)S(1)} %get-tuple-element.28), channel_id=1, source_target_pairs={{16,0},{32,16},{48,32},{64,48},{80,64},{96,80},{112,96},{128,112},... | collective-permute-start | bytes 245768 | tf_op jit(solution)/shard_map/ppermute | solution.py:42
  145.3 4.9 %collective-permute-done.9 = f32[5,2,16,128]{3,2,1,0:T(8,128)S(1)} collective-permute-done((f32[5,2,16,128]{3,2,1,0:T(8,128)S(1)}, f32[5,2,16,128]{3,2,1,0:T(8,128)S(1)}, u32[]{:S(2)}, u32[]{:S(2)}) %collective-permute-start.9) | collective-permute-done | bytes 81952 | tf_op jit(solution)/shard_map/ppermute | solution.py:42
  150.6 4.8 %fusion.29 = f32[5,32,20,128]{3,2,1,0:T(8,128)S(1)} fusion(f32[5,32,20,128]{3,2,1,0:T(8,128)S(1)} %slice.776, f32[5,32,4,128]{3,2,1,0:T(4,128)S(1)} %collective-permute-done.7, f32[5,32,16,128]{3,2,1,0:T(8,128)S(1)} %bitcast.78, f32[5,32,24,128]{3,2,1,0:T(8,128)S(1)} %pad_maximum_fusion.9, f32[5,32,4,128]{3,2,1,0:T(4,128)S(1)} %collective-permute-done.6, ...), kind=kLoop, calls=%fused_computation.83 | loop fusion | flops 17203200 | bytes 15402240 | tf_op jit(solution)/shard_map/add | solution.py:63
  155.5 4.0 %collective-permute-start.10 = (f32[5,2,20,128]{3,2,1,0:T(8,128)S(1)}, f32[5,2,20,128]{3,2,1,0:T(8,128)S(1)}, u32[]{:S(2)}, u32[]{:S(2)}) collective-permute-start(f32[5,2,20,128]{3,2,1,0:T(8,128)S(1)} %pad_maximum_fusion.15), channel_id=1, source_target_pairs={{0,16},{16,32},{32,48},{48,64},{64,80},{80,96},{96,112},{112,128},... | collective-permute-start | bytes 307208 | tf_op jit(solution)/shard_map/ppermute | solution.py:41
  159.6 1.9 %collective-permute-start.11 = (f32[5,2,20,128]{3,2,1,0:T(8,128)S(1)}, f32[5,2,20,128]{3,2,1,0:T(8,128)S(1)}, u32[]{:S(2)}, u32[]{:S(2)}) collective-permute-start(f32[5,2,20,128]{3,2,1,0:T(8,128)S(1)} %pad_maximum_fusion.16), channel_id=1, source_target_pairs={{16,0},{32,16},{48,32},{64,48},{80,64},{96,80},{112,96},{128,112},... | collective-permute-start | bytes 307208 | tf_op jit(solution)/shard_map/ppermute | solution.py:42
  161.6 5.6 %collective-permute-done.11 = f32[5,2,20,128]{3,2,1,0:T(8,128)S(1)} collective-permute-done((f32[5,2,20,128]{3,2,1,0:T(8,128)S(1)}, f32[5,2,20,128]{3,2,1,0:T(8,128)S(1)}, u32[]{:S(2)}, u32[]{:S(2)}) %collective-permute-start.11) | collective-permute-done | bytes 102432 | tf_op jit(solution)/shard_map/ppermute | solution.py:42
  168.5 3.9 %fusion.57 = f32[5,32,16,128]{3,2,1,0:T(8,128)} fusion(f32[5,32,16,128]{3,2,1,0:T(8,128)S(1)} %slice.803, f32[5,32,20,128]{3,2,1,0:T(8,128)S(1)} %fusion.7, f32[5,34,20,128]{3,2,1,0:T(8,128)S(1)} %get-tuple-element.6, f32[5,34,20,128]{3,2,1,0:T(8,128)S(1)} %get-tuple-element.5, f32[5,32,16,128]{3,2,1,0:T(8,128)S(1)} %bitcast.80, ...), kind=kLoop, calls=%fused_computation.115 | loop fusion | flops 13762560 | bytes 14681344 | tf_op jit(solution)/shard_map/mul | solution.py:97
  (101 shorter events, 7.8 us)
Async XLA Ops:
  0.0 10.3 %copy-start = (f32[5,32,16,128]{3,2,1,0:T(8,128)S(1)}, f32[5,32,16,128]{3,2,1,0:T(8,128)}, u32[]{:S(2)}) copy-start(f32[5,32,16,128]{3,2,1,0:T(8,128)} %param.5) | copy-start | bytes 3932164
  0.0 19.2 %copy-start.1 = (f32[32,16,128]{2,1,0:T(8,128)S(1)}, f32[32,16,128]{2,1,0:T(8,128)}, u32[]{:S(2)}) copy-start(f32[32,16,128]{2,1,0:T(8,128)} %param.6) | copy-start | bytes 786436
  0.0 18.3 %copy-start.3 = (f32[5,32]{1,0:T(8,128)S(1)}, f32[5,32]{1,0:T(8,128)}, u32[]{:S(2)}) copy-start(f32[5,32]{1,0:T(8,128)} %param.7) | copy-start | bytes 1924
  0.0 18.4 %copy-start.4 = (f32[5,32]{1,0:T(8,128)S(1)}, f32[5,32]{1,0:T(8,128)}, u32[]{:S(2)}) copy-start(f32[5,32]{1,0:T(8,128)} %param.8) | copy-start | bytes 1924
  2.7 18.2 %collective-permute-start = (f32[6,32,4,128]{3,2,1,0:T(4,128)S(1)}, f32[6,32,4,128]{3,2,1,0:T(4,128)S(1)}, u32[]{:S(2)}, u32[]{:S(2)}) collective-permute-start(f32[6,32,4,128]{3,2,1,0:T(4,128)S(1)} %pad_maximum_fusion.11), channel_id=1, source_target_pairs={{0,1},{1,2},{2,3},{3,4},{4,5},{5,6},{6,7},{7,8},{8,9},{9,10},{10,1... | collective-permute-start | bytes 1179656 | tf_op jit(solution)/shard_map/ppermute | solution.py:41
  5.0 19.0 %collective-permute-start.1 = (f32[6,32,4,128]{3,2,1,0:T(4,128)S(1)}, f32[6,32,4,128]{3,2,1,0:T(4,128)S(1)}, u32[]{:S(2)}, u32[]{:S(2)}) collective-permute-start(f32[6,32,4,128]{3,2,1,0:T(4,128)S(1)} %pad_maximum_fusion.12), channel_id=1, source_target_pairs={{1,0},{2,1},{3,2},{4,3},{5,4},{6,5},{7,6},{8,7},{9,8},{10,9},{11,1... | collective-permute-start | bytes 1179656 | tf_op jit(solution)/shard_map/ppermute | solution.py:42
  11.0 13.9 %collective-permute-start.2 = (f32[5,2,16,128]{3,2,1,0:T(8,128)}, f32[5,2,16,128]{3,2,1,0:T(8,128)}, u32[]{:S(2)}, u32[]{:S(2)}) collective-permute-start(f32[5,2,16,128]{3,2,1,0:T(8,128)} %get-tuple-element.35), channel_id=1, source_target_pairs={{0,16},{16,32},{32,48},{48,64},{64,80},{80,96},{96,112},{112,128},... | collective-permute-start | bytes 245768 | tf_op jit(solution)/shard_map/ppermute | solution.py:41
  16.4 9.9 %collective-permute-start.3 = (f32[5,2,16,128]{3,2,1,0:T(8,128)S(1)}, f32[5,2,16,128]{3,2,1,0:T(8,128)}, u32[]{:S(2)}, u32[]{:S(2)}) collective-permute-start(f32[5,2,16,128]{3,2,1,0:T(8,128)S(1)} %get-tuple-element.36), channel_id=1, source_target_pairs={{16,0},{32,16},{48,32},{64,48},{80,64},{96,80},{112,96},{128,112},... | collective-permute-start | bytes 245768 | tf_op jit(solution)/shard_map/ppermute | solution.py:42
  23.9 0.7 copy-start.2
  33.2 7.2 %collective-permute-start.4 = (f32[5,2,20,128]{3,2,1,0:T(8,128)S(1)}, f32[5,2,20,128]{3,2,1,0:T(8,128)S(1)}, u32[]{:S(2)}, u32[]{:S(2)}) collective-permute-start(f32[5,2,20,128]{3,2,1,0:T(8,128)S(1)} %pad_maximum_fusion.13), channel_id=1, source_target_pairs={{0,16},{16,32},{32,48},{48,64},{64,80},{80,96},{96,112},{112,128},... | collective-permute-start | bytes 307208 | tf_op jit(solution)/shard_map/ppermute | solution.py:41
  37.7 7.7 %collective-permute-start.5 = (f32[5,2,20,128]{3,2,1,0:T(8,128)S(1)}, f32[5,2,20,128]{3,2,1,0:T(8,128)S(1)}, u32[]{:S(2)}, u32[]{:S(2)}) collective-permute-start(f32[5,2,20,128]{3,2,1,0:T(8,128)S(1)} %pad_maximum_fusion.14), channel_id=1, source_target_pairs={{16,0},{32,16},{48,32},{64,48},{80,64},{96,80},{112,96},{128,112},... | collective-permute-start | bytes 307208 | tf_op jit(solution)/shard_map/ppermute | solution.py:42
  51.2 9.0 %copy-start.5 = (s32[32]{0:T(128)S(1)}, s32[32]{0:T(128)}, u32[]{:S(2)}) copy-start(s32[32]{0:T(128)} %param.9) | copy-start | bytes 388
  51.2 39.0 %all-to-all-start = ((f32[5,32,16,128]{3,2,0,1:T(8,128)}), f32[5,32,16,128]{3,2,0,1:T(8,128)S(1)}, u32[]{:S(2)}, u32[]{:S(2)}) async-start(f32[5,32,16,128]{3,2,0,1:T(8,128)} %copy.52), calls=%async_computation | async-start | bytes 2621440 | tf_op jit(solution)/shard_map/all_to_all | solution.py:104
  129.8 14.6 %collective-permute-start.6 = (f32[5,32,4,128]{3,2,1,0:T(4,128)S(1)}, f32[5,32,4,128]{3,2,1,0:T(4,128)S(1)}, u32[]{:S(2)}, u32[]{:S(2)}) collective-permute-start(f32[5,32,4,128]{3,2,1,0:T(4,128)S(1)} %get-tuple-element.29), channel_id=1, source_target_pairs={{0,1},{1,2},{2,3},{3,4},{4,5},{5,6},{6,7},{7,8},{8,9},{9,10},{10,1... | collective-permute-start | bytes 983048 | tf_op jit(solution)/shard_map/ppermute | solution.py:41
  129.9 14.9 %collective-permute-start.7 = (f32[5,32,4,128]{3,2,1,0:T(4,128)S(1)}, f32[5,32,4,128]{3,2,1,0:T(4,128)S(1)}, u32[]{:S(2)}, u32[]{:S(2)}) collective-permute-start(f32[5,32,4,128]{3,2,1,0:T(4,128)S(1)} %get-tuple-element.30), channel_id=1, source_target_pairs={{1,0},{2,1},{3,2},{4,3},{5,4},{6,5},{7,6},{8,7},{9,8},{10,9},{11,1... | collective-permute-start | bytes 983048 | tf_op jit(solution)/shard_map/ppermute | solution.py:42
  133.5 11.8 %collective-permute-start.8 = (f32[5,2,16,128]{3,2,1,0:T(8,128)S(1)}, f32[5,2,16,128]{3,2,1,0:T(8,128)S(1)}, u32[]{:S(2)}, u32[]{:S(2)}) collective-permute-start(f32[5,2,16,128]{3,2,1,0:T(8,128)S(1)} %get-tuple-element.27), channel_id=1, source_target_pairs={{0,16},{16,32},{32,48},{48,64},{64,80},{80,96},{96,112},{112,128},... | collective-permute-start | bytes 245768 | tf_op jit(solution)/shard_map/ppermute | solution.py:41
  142.3 8.0 %collective-permute-start.9 = (f32[5,2,16,128]{3,2,1,0:T(8,128)S(1)}, f32[5,2,16,128]{3,2,1,0:T(8,128)S(1)}, u32[]{:S(2)}, u32[]{:S(2)}) collective-permute-start(f32[5,2,16,128]{3,2,1,0:T(8,128)S(1)} %get-tuple-element.28), channel_id=1, source_target_pairs={{16,0},{32,16},{48,32},{64,48},{80,64},{96,80},{112,96},{128,112},... | collective-permute-start | bytes 245768 | tf_op jit(solution)/shard_map/ppermute | solution.py:42
  155.5 6.1 %collective-permute-start.10 = (f32[5,2,20,128]{3,2,1,0:T(8,128)S(1)}, f32[5,2,20,128]{3,2,1,0:T(8,128)S(1)}, u32[]{:S(2)}, u32[]{:S(2)}) collective-permute-start(f32[5,2,20,128]{3,2,1,0:T(8,128)S(1)} %pad_maximum_fusion.15), channel_id=1, source_target_pairs={{0,16},{16,32},{32,48},{48,64},{64,80},{80,96},{96,112},{112,128},... | collective-permute-start | bytes 307208 | tf_op jit(solution)/shard_map/ppermute | solution.py:41
  159.6 7.7 %collective-permute-start.11 = (f32[5,2,20,128]{3,2,1,0:T(8,128)S(1)}, f32[5,2,20,128]{3,2,1,0:T(8,128)S(1)}, u32[]{:S(2)}, u32[]{:S(2)}) collective-permute-start(f32[5,2,20,128]{3,2,1,0:T(8,128)S(1)} %pad_maximum_fusion.16), channel_id=1, source_target_pairs={{16,0},{32,16},{48,32},{64,48},{80,64},{96,80},{112,96},{128,112},... | collective-permute-start | bytes 307208 | tf_op jit(solution)/shard_map/ppermute | solution.py:42

commit v10 on v6

--- a/solution.py
+++ b/solution.py
@@ -62,9 +62,9 @@
     return 0.5 * (field + first + split_stencil(first, kappa, speed_r, speed_p))
 
 
-def shift_rows(half, shifts):
+def shift_rows(half, shifts, width=2):
     peers = lax.axis_size("azi")
-    rows = half.shape[1]
+    fcount, rows, cols, height = half.shape
     per = rows // peers
     full = lax.all_to_all(half, "azi", 1, 2, tiled=True)
     length = full.shape[2]
@@ -76,13 +76,24 @@
         start = (length - mine[row] % length) % length
         rolled.append(lax.dynamic_slice_in_dim(doubled[:, row], start, length, axis=1))
     moved = jnp.stack(rolled, axis=1)
-    return lax.all_to_all(moved, "azi", 2, 1, tiled=True)
+    ring = jnp.concatenate([moved[:, :, length - width :], moved, moved[:, :, :width]], axis=2)
+    windows = jnp.stack([ring[:, :, k * cols : k * cols + cols + 2 * width] for k in range(peers)])
+    back = lax.all_to_all(windows, "azi", 0, 0)
+    return jnp.moveaxis(back, 0, 1).reshape(fcount, rows, cols + 2 * width, height)
 
 
 def shards(fields, kappa, radial_speed, azimuth_speed, shifts):
     half = heun_sections(fields, kappa, radial_speed, azimuth_speed)
-    moved = shift_rows(half, shifts)
-    return heun_sections(moved, kappa, radial_speed, azimuth_speed)
+    wide = shift_rows(half, shifts)
+    moved = wide[:, :, 2:-2]
+    rows = moved.shape[1]
+    above = lax.ppermute(moved[:, rows - 2 :], "rad", [(i, i + 1) for i in range(lax.axis_size("rad") - 1)])
+    below = lax.ppermute(moved[:, :2], "rad", [(i + 1, i) for i in range(lax.axis_size("rad") - 1)])
+    corners = [(0, 0), (0, 0), (2, 2), (0, 0)]
+    padded = jnp.concatenate([jnp.pad(above, corners), wide, jnp.pad(below, corners)], axis=1)
+    first = moved + stencil(padded, kappa, radial_speed, azimuth_speed)
+    inner = split_stencil(first, kappa, radial_speed, azimuth_speed)
+    return 0.5 * (moved + first + inner)
 
 
 def solution(mesh):

time: 165 us -> 170 us (1.030)
  blocking collectives: 37.1 us -> 47.5 us
  starting transfers between devices: 49.3 us -> 43.7 us
    all_to_all x1, blocking collectives: 37.1 us -> 47.5 us  [shift_rows(): back = lax.all_to_all(windows, 'azi', 0, 0)]
    ppermute x4 -> x3, starting transfers between devices: 16.8 us -> 7.59 us  [split_stencil(): lax.ppermute(cells[..., :width, :], 'azi', [((i + 1) % sectors, i) for i...]
    ppermute x0 -> x2, starting transfers between devices: none -> 9.12 us  [the longest x1 7.2 us: shards(): lax.ppermute(moved[:, rows - 2:], 'rad', [(i, i + 1) for i in range(lax.a...]
    ppermute x0 -> x2, waiting for transfers between devices: none -> 5.05 us  [the longest x1 5.05 us: shards(): lax.ppermute(moved[:, :2], 'rad', [(i + 1, i) for i in range(lax.axis_siz...]
    all_to_all x1, waiting for transfers between devices: 28.9 us -> 26.1 us  [shift_rows(): full = lax.all_to_all(half, 'azi', 1, 2, tiled=True)]
    add x12 -> x9, other arithmetic: 12.6 us -> 9.8 us  [stencil(): -speed_r[:, :, None, None] * first_r - speed_p[:, :, None, None] * first_p]
    add x0 -> x1, other arithmetic: none -> 2.34 us  [shards(): first = moved + stencil(padded, kappa, radial_speed, azimuth_speed)]
    ppermute x4 -> x3, starting transfers between devices: 8.17 us -> 6.25 us  [split_stencil(): lax.ppermute(cells[..., :width, :, :], 'rad', [(i + 1, i) for i in range(...]
  transfers between devices with their start and end apart: 17 -> 15, of which waited for: 6 -> 7; matrix products, arithmetic and copies ran while one was open for 8% -> 6% of each run, Pallas kernels for 0% -> 0%
where the time goes in v10:
time: 170 us; the launch traced here: 169 us
  waiting for transfers between devices  48.2 us (28%)
  blocking collectives  47.5 us (28%)
  starting transfers between devices  43.7 us (26%)
  other arithmetic  15.3 us (9%)
  local copies, waits for them, and re-layouts  10.1 us (6%)
  between operations  4.28 us (3%)
    all_to_all x1, blocking collectives, shift_rows(): back = lax.all_to_all(windows, 'azi', 0, 0)  47.5 us
    all_to_all x1, waiting for transfers between devices, shift_rows(): full = lax.all_to_all(half, 'azi', 1, 2, tiled=True)  26.1 us
    ppermute x3, waiting for transfers between devices, split_stencil(): lax.ppermute(cells[..., :width, :, :], 'rad', [(i + 1, i) for i in range(...  16 us
    ppermute x3, starting transfers between devices, split_stencil(): lax.ppermute(cells[..., rows - width:, :, :], 'rad', [(i, i + 1) for i in...  15.3 us
    add x9, other arithmetic, stencil(): -speed_r[:, :, None, None] * first_r - speed_p[:, :, None, None] * first_p  9.8 us
    ppermute x3, starting transfers between devices, split_stencil(): lax.ppermute(cells[..., :width, :], 'azi', [((i + 1) % sectors, i) for i...  7.59 us
    ppermute x1, starting transfers between devices, shards(): lax.ppermute(moved[:, rows - 2:], 'rad', [(i, i + 1) for i in range(lax.a...  7.2 us
    ppermute x3, starting transfers between devices, split_stencil(): lax.ppermute(cells[..., :width, :, :], 'rad', [(i + 1, i) for i in range(...  6.25 us
  transfers between devices with their start and end apart: 15, of which 7 were waited for; matrix products, arithmetic and copies ran while one was open for 6% of the time, Pallas kernels for 0%

profile of v10, /device:TPU:1, one launch (start us, length us, event | category | flops | bytes accessed | tf_op | source)
XLA Modules:
  0.0 169.2 jit_solution(10882702166370395515)
XLA Ops:
  0.0 1.8 %constant_dynamic-update-slice_fusion.1 = (f32[5,34,16,128]{3,1,2,0:T(8,128)S(1)}, f32[5,32,16,128]{3,1,2,0:T(8,128)S(1)}) fusion(f32[5,32,16,128]{3,2,1,0:T(8,128)} %param.5), kind=kLoop, calls=%fused_computation.282 | loop fusion | bytes 3932160
  1.9 6.2 %collective-permute-start = (f32[5,2,16,128]{3,1,2,0:T(2,128)S(1)}, f32[5,2,16,128]{3,1,2,0:T(2,128)S(1)}, u32[]{:S(2)}, u32[]{:S(2)}) collective-permute-start(f32[5,2,16,128]{3,1,2,0:T(2,128)S(1)} %get-tuple-element.27), channel_id=1, source_target_pairs={{0,16},{16,32},{32,48},{48,64},{64,80},{80,96},{96,112},{112,128},... | collective-permute-start | bytes 245768 | tf_op jit(solution)/shard_map/ppermute | solution.py:42
  8.1 1.9 %collective-permute-start.2 = (f32[5,2,16,128]{3,1,2,0:T(2,128)S(1)}, f32[5,2,16,128]{3,1,2,0:T(2,128)S(1)}, u32[]{:S(2)}, u32[]{:S(2)}) collective-permute-start(f32[5,2,16,128]{3,1,2,0:T(2,128)S(1)} %get-tuple-element.28), channel_id=1, source_target_pairs={{16,0},{32,16},{48,32},{64,48},{80,64},{96,80},{112,96},{128,112},... | collective-permute-start | bytes 245768 | tf_op jit(solution)/shard_map/ppermute | solution.py:43
  10.1 5.8 %collective-permute-start.3 = (f32[5,32,2,128]{3,1,2,0:T(8,128)S(1)}, f32[5,32,2,128]{3,1,2,0:T(8,128)S(1)}, u32[]{:S(2)}, u32[]{:S(2)}) collective-permute-start(f32[5,32,2,128]{3,1,2,0:T(8,128)S(1)} %get-tuple-element.29), channel_id=1, source_target_pairs={{1,0},{2,1},{3,2},{4,3},{5,4},{6,5},{7,6},{8,7},{9,8},{10,9},{11,1... | collective-permute-start | bytes 491528 | tf_op jit(solution)/shard_map/ppermute | solution.py:41
  16.2 2.9 %collective-permute-done.2 = f32[5,2,16,128]{3,1,2,0:T(2,128)S(1)} collective-permute-done((f32[5,2,16,128]{3,1,2,0:T(2,128)S(1)}, f32[5,2,16,128]{3,1,2,0:T(2,128)S(1)}, u32[]{:S(2)}, u32[]{:S(2)}) %collective-permute-start.2) | collective-permute-done | bytes 81952 | tf_op jit(solution)/shard_map/ppermute | solution.py:43
  19.2 2.0 %fusion.27 = f32[5,32,12,128]{3,1,2,0:T(8,128)S(1)} fusion(f32[5,32,12,128]{3,1,2,0:T(8,128)S(1)} %slice.870, f32[5,32,16,128]{3,1,2,0:T(8,128)S(1)} %get-tuple-element.26, f32[5,34,16,128]{3,1,2,0:T(8,128)S(1)} %constant_dynamic-update-slice_fusion, f32[5,2,16,128]{3,1,2,0:T(2,128)S(1)} %collective-permute-done, f32[32,12,128]{2,0,1:T(8,128)S(1)} %copy_multiply_fusion, ...), kind=kLoop, calls=%fused_computation.93 | loop fusion | flops 10076160 | bytes 9461760 | tf_op jit(solution)/shard_map/add | solution.py:31
  21.3 0.8 collective-permute-done.1
  23.1 0.9 copy-done
  24.0 0.5 maximum_add_fusion
  24.6 7.2 %collective-permute-start.4 = (f32[5,2,16,128]{3,1,2,0:T(2,128)S(1)}, f32[5,2,16,128]{3,1,2,0:T(2,128)S(1)}, u32[]{:S(2)}, u32[]{:S(2)}) collective-permute-start(f32[5,2,16,128]{3,1,2,0:T(2,128)S(1)} %get-tuple-element.19), channel_id=1, source_target_pairs={{0,16},{16,32},{32,48},{48,64},{64,80},{80,96},{96,112},{112,128},... | collective-permute-start | bytes 245768 | tf_op jit(solution)/shard_map/ppermute | solution.py:42
  32.0 1.9 %collective-permute-start.6 = (f32[5,2,16,128]{3,1,2,0:T(2,128)S(1)}, f32[5,2,16,128]{3,1,2,0:T(2,128)S(1)}, u32[]{:S(2)}, u32[]{:S(2)}) collective-permute-start(f32[5,2,16,128]{3,1,2,0:T(2,128)S(1)} %get-tuple-element.20), channel_id=1, source_target_pairs={{16,0},{32,16},{48,32},{64,48},{80,64},{96,80},{112,96},{128,112},... | collective-permute-start | bytes 245768 | tf_op jit(solution)/shard_map/ppermute | solution.py:43
  33.9 1.7 %collective-permute-start.7 = (f32[5,32,2,128]{3,1,2,0:T(8,128)S(1)}, f32[5,32,2,128]{3,1,2,0:T(8,128)S(1)}, u32[]{:S(2)}, u32[]{:S(2)}) collective-permute-start(f32[5,32,2,128]{3,1,2,0:T(8,128)S(1)} %get-tuple-element.21), channel_id=1, source_target_pairs={{1,0},{2,1},{3,2},{4,3},{5,4},{6,5},{7,6},{8,7},{9,8},{10,9},{11,1... | collective-permute-start | bytes 491528 | tf_op jit(solution)/shard_map/ppermute | solution.py:41
  35.8 5.5 %collective-permute-done.6 = f32[5,2,16,128]{3,1,2,0:T(2,128)S(1)} collective-permute-done((f32[5,2,16,128]{3,1,2,0:T(2,128)S(1)}, f32[5,2,16,128]{3,1,2,0:T(2,128)S(1)}, u32[]{:S(2)}, u32[]{:S(2)}) %collective-permute-start.6) | collective-permute-done | bytes 81952 | tf_op jit(solution)/shard_map/ppermute | solution.py:43
  41.4 2.7 %fusion.37 = f32[5,32,12,128]{3,1,2,0:T(8,128)S(1)} fusion(f32[5,32,12,128]{3,1,2,0:T(8,128)S(1)} %slice.901, f32[5,32,16,128]{3,1,2,0:T(8,128)S(1)} %maximum_add_fusion, f32[5,2,16,128]{3,1,2,0:T(2,128)S(1)} %collective-permute-done.6, f32[5,2,16,128]{3,1,2,0:T(2,128)S(1)} %collective-permute-done.4, f32[32,12,128]{2,0,1:T(8,128)S(1)} %copy_multiply_fusion, ...), kind=kLoop, calls=%fused_computation.103 | loop fusion | flops 10567680 | bytes 7577600 | tf_op jit(solution)/shard_map/add | solution.py:31
  45.1 0.6 fusion.11
  45.7 1.8 %copy.83 = f32[5,32,16,128]{3,2,0,1:T(8,128)} copy(f32[5,32,16,128]{3,1,2,0:T(8,128)S(1)} %fusion.11) | data formatting | bytes 2621440 | tf_op jit(solution)/shard_map/mul | solution.py:62
  47.5 4.0 %all-to-all-start = ((f32[5,32,16,128]{3,2,0,1:T(8,128)}), f32[5,32,16,128]{3,2,0,1:T(8,128)S(1)}, u32[]{:S(2)}, u32[]{:S(2)}) async-start(f32[5,32,16,128]{3,2,0,1:T(8,128)} %copy.83), calls=%async_computation | async-start | bytes 2621440 | tf_op jit(solution)/shard_map/all_to_all | solution.py:69
  51.7 0.6 fusion.176
  55.9 26.1 %all-to-all-done = f32[5,32,16,128]{3,2,0,1:T(8,128)S(1)} async-done(((f32[5,32,16,128]{3,2,0,1:T(8,128)}), f32[5,32,16,128]{3,2,0,1:T(8,128)S(1)}, u32[]{:S(2)}, u32[]{:S(2)}) %all-to-all-start) | async-done | bytes 1310752 | tf_op jit(solution)/shard_map/all_to_all | solution.py:69
  83.0 0.8 copy.86
  83.8 47.5 %all_to_all.23 = f32[16,5,2,20,128]{4,2,3,1,0:T(2,128)S(1)} all-to-all(f32[16,5,2,20,128]{4,2,3,1,0:T(2,128)S(1)} %copy.86), channel_id=1, replica_groups=mesh['rad'=16,'azi'=16] {'azi'}, dimensions={0} | all-to-all | bytes 3276800 | tf_op jit(solution)/shard_map/all_to_all | solution.py:81
  131.3 0.9 copy.87
  132.3 7.2 %collective-permute-start.8 = (f32[5,2,16,128]{3,1,2,0:T(2,128)S(1)}, f32[5,2,16,128]{3,1,2,0:T(2,128)S(1)}, u32[]{:S(2)}, u32[]{:S(2)}) collective-permute-start(f32[5,2,16,128]{3,1,2,0:T(2,128)S(1)} %get-tuple-element.7), channel_id=1, source_target_pairs={{0,16},{16,32},{32,48},{48,64},{64,80},{80,96},{96,112},{112,128},... | collective-permute-start | bytes 245768 | tf_op jit(solution)/shard_map/ppermute | solution.py:90
  139.5 1.9 %collective-permute-start.9 = (f32[5,2,16,128]{3,1,2,0:T(2,128)S(1)}, f32[5,2,16,128]{3,1,2,0:T(2,128)S(1)}, u32[]{:S(2)}, u32[]{:S(2)}) collective-permute-start(f32[5,2,16,128]{3,1,2,0:T(2,128)S(1)} %get-tuple-element.8), channel_id=1, source_target_pairs={{16,0},{32,16},{48,32},{64,48},{80,64},{96,80},{112,96},{128,112},... | collective-permute-start | bytes 245768 | tf_op jit(solution)/shard_map/ppermute | solution.py:91
  141.7 5.0 %collective-permute-done.9 = f32[5,2,16,128]{3,1,2,0:T(2,128)S(1)} collective-permute-done((f32[5,2,16,128]{3,1,2,0:T(2,128)S(1)}, f32[5,2,16,128]{3,1,2,0:T(2,128)S(1)}, u32[]{:S(2)}, u32[]{:S(2)}) %collective-permute-start.9) | collective-permute-done | bytes 81952 | tf_op jit(solution)/shard_map/ppermute | solution.py:91
  147.2 2.3 %fusion.8 = f32[5,32,16,128]{3,1,2,0:T(8,128)S(1)} fusion(f32[5,32,16,128]{3,1,2,0:T(8,128)S(1)} %slice.941, f32[5,32,20,128]{3,1,2,0:T(8,128)S(1)} %bitcast.75, f32[5,34,20,128]{3,1,2,0:T(8,128)S(1)} %get-tuple-element.6, f32[5,34,20,128]{3,1,2,0:T(8,128)S(1)} %get-tuple-element.5, f32[32,16,128]{2,0,1:T(8,128)S(1)} %copy.88, ...), kind=kLoop, calls=%fused_computation.68 | loop fusion | flops 13107200 | bytes 13370624 | tf_op jit(solution)/shard_map/add | solution.py:94
  149.6 1.9 %collective-permute-start.10 = (f32[5,2,16,128]{3,1,2,0:T(2,128)S(1)}, f32[5,2,16,128]{3,1,2,0:T(2,128)S(1)}, u32[]{:S(2)}, u32[]{:S(2)}) collective-permute-start(f32[5,2,16,128]{3,1,2,0:T(2,128)S(1)} %get-tuple-element.11), channel_id=1, source_target_pairs={{0,16},{16,32},{32,48},{48,64},{64,80},{80,96},{96,112},{112,128},... | collective-permute-start | bytes 245768 | tf_op jit(solution)/shard_map/ppermute | solution.py:42
  151.7 2.4 %collective-permute-start.12 = (f32[5,2,16,128]{3,1,2,0:T(2,128)S(1)}, f32[5,2,16,128]{3,1,2,0:T(2,128)S(1)}, u32[]{:S(2)}, u32[]{:S(2)}) collective-permute-start(f32[5,2,16,128]{3,1,2,0:T(2,128)S(1)} %get-tuple-element.12), channel_id=1, source_target_pairs={{16,0},{32,16},{48,32},{64,48},{80,64},{96,80},{112,96},{128,112},... | collective-permute-start | bytes 245768 | tf_op jit(solution)/shard_map/ppermute | solution.py:43
  154.2 1.5 collective-permute-start.11
  155.6 7.6 %collective-permute-done.12 = f32[5,2,16,128]{3,1,2,0:T(2,128)S(1)} collective-permute-done((f32[5,2,16,128]{3,1,2,0:T(2,128)S(1)}, f32[5,2,16,128]{3,1,2,0:T(2,128)S(1)}, u32[]{:S(2)}, u32[]{:S(2)}) %collective-permute-start.12) | collective-permute-done | bytes 81952 | tf_op jit(solution)/shard_map/ppermute | solution.py:43
  163.2 2.7 %fusion.47 = f32[5,32,12,128]{3,1,2,0:T(8,128)S(1)} fusion(f32[5,32,12,128]{3,1,2,0:T(8,128)S(1)} %slice.973, f32[5,32,16,128]{3,1,2,0:T(8,128)S(1)} %fusion.8, f32[5,2,16,128]{3,1,2,0:T(2,128)S(1)} %collective-permute-done.12, f32[5,2,16,128]{3,1,2,0:T(2,128)S(1)} %collective-permute-done.10, f32[32,12,128]{2,0,1:T(8,128)S(1)} %copy_multiply_fusion, ...), kind=kLoop, calls=%fused_computation.113 | loop fusion | flops 10567680 | bytes 7577600 | tf_op jit(solution)/shard_map/add | solution.py:31
  167.4 1.8 %copy.89 = f32[5,32,16,128]{3,2,1,0:T(8,128)} copy(f32[5,32,16,128]{3,1,2,0:T(8,128)S(1)} %fusion.12) | data formatting | bytes 2621440 | tf_op jit(solution)/shard_map/mul | solution.py:96
  (83 shorter events, 6.1 us)
Async XLA Ops:
  0.0 15.8 %copy-start.1 = (f32[32,16,128]{2,1,0:T(8,128)S(1)}, f32[32,16,128]{2,1,0:T(8,128)}, u32[]{:S(2)}) copy-start(f32[32,16,128]{2,1,0:T(8,128)} %param.6) | copy-start | bytes 786436
  1.9 14.3 %collective-permute-start = (f32[5,2,16,128]{3,1,2,0:T(2,128)S(1)}, f32[5,2,16,128]{3,1,2,0:T(2,128)S(1)}, u32[]{:S(2)}, u32[]{:S(2)}) collective-permute-start(f32[5,2,16,128]{3,1,2,0:T(2,128)S(1)} %get-tuple-element.27), channel_id=1, source_target_pairs={{0,16},{16,32},{32,48},{48,64},{64,80},{80,96},{96,112},{112,128},... | collective-permute-start | bytes 245768 | tf_op jit(solution)/shard_map/ppermute | solution.py:42
  8.1 11.1 %collective-permute-start.2 = (f32[5,2,16,128]{3,1,2,0:T(2,128)S(1)}, f32[5,2,16,128]{3,1,2,0:T(2,128)S(1)}, u32[]{:S(2)}, u32[]{:S(2)}) collective-permute-start(f32[5,2,16,128]{3,1,2,0:T(2,128)S(1)} %get-tuple-element.28), channel_id=1, source_target_pairs={{16,0},{32,16},{48,32},{64,48},{80,64},{96,80},{112,96},{128,112},... | collective-permute-start | bytes 245768 | tf_op jit(solution)/shard_map/ppermute | solution.py:43
  10.0 6.0 %copy-start.2 = (f32[5,32]{1,0:T(8,128)S(1)}, f32[5,32]{1,0:T(8,128)}, u32[]{:S(2)}) copy-start(f32[5,32]{1,0:T(8,128)} %param.7) | copy-start | bytes 1924
  10.0 6.0 %copy-start.3 = (f32[5,32]{1,0:T(8,128)S(1)}, f32[5,32]{1,0:T(8,128)}, u32[]{:S(2)}) copy-start(f32[5,32]{1,0:T(8,128)} %param.8) | copy-start | bytes 1924
  10.1 11.2 %collective-permute-start.3 = (f32[5,32,2,128]{3,1,2,0:T(8,128)S(1)}, f32[5,32,2,128]{3,1,2,0:T(8,128)S(1)}, u32[]{:S(2)}, u32[]{:S(2)}) collective-permute-start(f32[5,32,2,128]{3,1,2,0:T(8,128)S(1)} %get-tuple-element.29), channel_id=1, source_target_pairs={{1,0},{2,1},{3,2},{4,3},{5,4},{6,5},{7,6},{8,7},{9,8},{10,9},{11,1... | collective-permute-start | bytes 491528 | tf_op jit(solution)/shard_map/ppermute | solution.py:41
  15.8 6.3 %collective-permute-start.1 = (f32[5,32,2,128]{3,1,2,0:T(8,128)S(1)}, f32[5,32,2,128]{3,1,2,0:T(8,128)S(1)}, u32[]{:S(2)}, u32[]{:S(2)}) collective-permute-start(f32[5,32,2,128]{3,1,2,0:T(8,128)S(1)} %get-tuple-element.30), channel_id=1, source_target_pairs={{0,1},{1,2},{2,3},{3,4},{4,5},{5,6},{6,7},{7,8},{8,9},{9,10},{10,1... | collective-permute-start | bytes 491528 | tf_op jit(solution)/shard_map/ppermute | solution.py:40
  22.7 1.3 copy-start
  24.6 11.2 %collective-permute-start.4 = (f32[5,2,16,128]{3,1,2,0:T(2,128)S(1)}, f32[5,2,16,128]{3,1,2,0:T(2,128)S(1)}, u32[]{:S(2)}, u32[]{:S(2)}) collective-permute-start(f32[5,2,16,128]{3,1,2,0:T(2,128)S(1)} %get-tuple-element.19), channel_id=1, source_target_pairs={{0,16},{16,32},{32,48},{48,64},{64,80},{80,96},{96,112},{112,128},... | collective-permute-start | bytes 245768 | tf_op jit(solution)/shard_map/ppermute | solution.py:42
  32.0 9.4 %collective-permute-start.6 = (f32[5,2,16,128]{3,1,2,0:T(2,128)S(1)}, f32[5,2,16,128]{3,1,2,0:T(2,128)S(1)}, u32[]{:S(2)}, u32[]{:S(2)}) collective-permute-start(f32[5,2,16,128]{3,1,2,0:T(2,128)S(1)} %get-tuple-element.20), channel_id=1, source_target_pairs={{16,0},{32,16},{48,32},{64,48},{80,64},{96,80},{112,96},{128,112},... | collective-permute-start | bytes 245768 | tf_op jit(solution)/shard_map/ppermute | solution.py:43
  33.9 10.7 %collective-permute-start.7 = (f32[5,32,2,128]{3,1,2,0:T(8,128)S(1)}, f32[5,32,2,128]{3,1,2,0:T(8,128)S(1)}, u32[]{:S(2)}, u32[]{:S(2)}) collective-permute-start(f32[5,32,2,128]{3,1,2,0:T(8,128)S(1)} %get-tuple-element.21), channel_id=1, source_target_pairs={{1,0},{2,1},{3,2},{4,3},{5,4},{6,5},{7,6},{8,7},{9,8},{10,9},{11,1... | collective-permute-start | bytes 491528 | tf_op jit(solution)/shard_map/ppermute | solution.py:41
  35.6 8.5 %collective-permute-start.5 = (f32[5,32,2,128]{3,1,2,0:T(8,128)S(1)}, f32[5,32,2,128]{3,1,2,0:T(8,128)S(1)}, u32[]{:S(2)}, u32[]{:S(2)}) collective-permute-start(f32[5,32,2,128]{3,1,2,0:T(8,128)S(1)} %get-tuple-element.22), channel_id=1, source_target_pairs={{0,1},{1,2},{2,3},{3,4},{4,5},{5,6},{6,7},{7,8},{8,9},{9,10},{10,1... | collective-permute-start | bytes 491528 | tf_op jit(solution)/shard_map/ppermute | solution.py:40
  47.5 4.0 %copy-start.4 = (s32[32]{0:T(128)S(1)}, s32[32]{0:T(128)}, u32[]{:S(2)}) copy-start(s32[32]{0:T(128)} %param.9) | copy-start | bytes 388
  47.5 34.4 %all-to-all-start = ((f32[5,32,16,128]{3,2,0,1:T(8,128)}), f32[5,32,16,128]{3,2,0,1:T(8,128)S(1)}, u32[]{:S(2)}, u32[]{:S(2)}) async-start(f32[5,32,16,128]{3,2,0,1:T(8,128)} %copy.83), calls=%async_computation | async-start | bytes 2621440 | tf_op jit(solution)/shard_map/all_to_all | solution.py:69
  132.3 9.4 %collective-permute-start.8 = (f32[5,2,16,128]{3,1,2,0:T(2,128)S(1)}, f32[5,2,16,128]{3,1,2,0:T(2,128)S(1)}, u32[]{:S(2)}, u32[]{:S(2)}) collective-permute-start(f32[5,2,16,128]{3,1,2,0:T(2,128)S(1)} %get-tuple-element.7), channel_id=1, source_target_pairs={{0,16},{16,32},{32,48},{48,64},{64,80},{80,96},{96,112},{112,128},... | collective-permute-start | bytes 245768 | tf_op jit(solution)/shard_map/ppermute | solution.py:90
  139.5 7.3 %collective-permute-start.9 = (f32[5,2,16,128]{3,1,2,0:T(2,128)S(1)}, f32[5,2,16,128]{3,1,2,0:T(2,128)S(1)}, u32[]{:S(2)}, u32[]{:S(2)}) collective-permute-start(f32[5,2,16,128]{3,1,2,0:T(2,128)S(1)} %get-tuple-element.8), channel_id=1, source_target_pairs={{16,0},{32,16},{48,32},{64,48},{80,64},{96,80},{112,96},{128,112},... | collective-permute-start | bytes 245768 | tf_op jit(solution)/shard_map/ppermute | solution.py:91
  149.6 6.0 %collective-permute-start.10 = (f32[5,2,16,128]{3,1,2,0:T(2,128)S(1)}, f32[5,2,16,128]{3,1,2,0:T(2,128)S(1)}, u32[]{:S(2)}, u32[]{:S(2)}) collective-permute-start(f32[5,2,16,128]{3,1,2,0:T(2,128)S(1)} %get-tuple-element.11), channel_id=1, source_target_pairs={{0,16},{16,32},{32,48},{48,64},{64,80},{80,96},{96,112},{112,128},... | collective-permute-start | bytes 245768 | tf_op jit(solution)/shard_map/ppermute | solution.py:42
  151.7 11.5 %collective-permute-start.12 = (f32[5,2,16,128]{3,1,2,0:T(2,128)S(1)}, f32[5,2,16,128]{3,1,2,0:T(2,128)S(1)}, u32[]{:S(2)}, u32[]{:S(2)}) collective-permute-start(f32[5,2,16,128]{3,1,2,0:T(2,128)S(1)} %get-tuple-element.12), channel_id=1, source_target_pairs={{16,0},{32,16},{48,32},{64,48},{80,64},{96,80},{112,96},{128,112},... | collective-permute-start | bytes 245768 | tf_op jit(solution)/shard_map/ppermute | solution.py:43
  154.1 12.3 %collective-permute-start.13 = (f32[5,32,2,128]{3,1,2,0:T(8,128)S(1)}, f32[5,32,2,128]{3,1,2,0:T(8,128)S(1)}, u32[]{:S(2)}, u32[]{:S(2)}) collective-permute-start(f32[5,32,2,128]{3,1,2,0:T(8,128)S(1)} %get-tuple-element.13), channel_id=1, source_target_pairs={{1,0},{2,1},{3,2},{4,3},{5,4},{6,5},{7,6},{8,7},{9,8},{10,9},{11,1... | collective-permute-start | bytes 491528 | tf_op jit(solution)/shard_map/ppermute | solution.py:41
  154.2 11.8 %collective-permute-start.11 = (f32[5,32,2,128]{3,1,2,0:T(8,128)S(1)}, f32[5,32,2,128]{3,1,2,0:T(8,128)S(1)}, u32[]{:S(2)}, u32[]{:S(2)}) collective-permute-start(f32[5,32,2,128]{3,1,2,0:T(8,128)S(1)} %get-tuple-element.14), channel_id=1, source_target_pairs={{0,1},{1,2},{2,3},{3,4},{4,5},{5,6},{6,7},{7,8},{8,9},{9,10},{10,1... | collective-permute-start | bytes 491528 | tf_op jit(solution)/shard_map/ppermute | solution.py:40

commit v11 on v6

--- a/solution.py
+++ b/solution.py
@@ -34,14 +34,24 @@
     )
 
 
-def split_stencil(cells, kap, speed_r, speed_p, width=2):
+def split_stencil(cells, kap, speed_r, speed_p, width=2, core=False):
     sectors, rings = lax.axis_size("azi"), lax.axis_size("rad")
     rows, cols = cells.shape[-3], cells.shape[-2]
     left = lax.ppermute(cells[..., cols - width :, :], "azi", [(i, (i + 1) % sectors) for i in range(sectors)])
     right = lax.ppermute(cells[..., :width, :], "azi", [((i + 1) % sectors, i) for i in range(sectors)])
     above = lax.ppermute(cells[..., rows - width :, :, :], "rad", [(i, i + 1) for i in range(rings - 1)])
     below = lax.ppermute(cells[..., :width, :, :], "rad", [(i + 1, i) for i in range(rings - 1)])
-    middle = stencil(jnp.concatenate([above, cells, below], axis=1), kap[:, width : cols - width], speed_r, speed_p)
+    tall = jnp.concatenate([above, cells, below], axis=1)
+    inner = kap[:, width : cols - width]
+    if core:
+        parts = [
+            stencil(tall[:, : 3 * width], inner[:width], speed_r[:, :width], speed_p[:, :width]),
+            stencil(cells, inner[width : rows - width], speed_r[:, width : rows - width], speed_p[:, width : rows - width]),
+            stencil(tall[:, rows - width :], inner[rows - width :], speed_r[:, rows - width :], speed_p[:, rows - width :]),
+        ]
+        middle = jnp.concatenate(parts, axis=1)
+    else:
+        middle = stencil(tall, inner, speed_r, speed_p)
     edge = 2 * width
 
     def side(strip, near, far, pads):
@@ -57,8 +67,8 @@
     return jnp.concatenate([first, middle, last], axis=2)
 
 
-def heun_sections(field, kappa, speed_r, speed_p):
-    first = field + split_stencil(field, kappa, speed_r, speed_p)
+def heun_sections(field, kappa, speed_r, speed_p, core=False):
+    first = field + split_stencil(field, kappa, speed_r, speed_p, core=core)
     return 0.5 * (field + first + split_stencil(first, kappa, speed_r, speed_p))
 
 
@@ -80,7 +90,7 @@
 
 
 def shards(fields, kappa, radial_speed, azimuth_speed, shifts):
-    half = heun_sections(fields, kappa, radial_speed, azimuth_speed)
+    half = heun_sections(fields, kappa, radial_speed, azimuth_speed, core=True)
     moved = shift_rows(half, shifts)
     return heun_sections(moved, kappa, radial_speed, azimuth_speed)
 

time: 165 us -> 164 us (level)
  waiting for transfers between devices: 47.1 us -> 41 us
  starting transfers between devices: 49.3 us -> 54 us
    ppermute x4, starting transfers between devices: 16.2 us -> 21.2 us  [split_stencil(): lax.ppermute(cells[..., rows - width:, :, :], 'rad', [(i, i + 1) for i in...]
    ppermute x4, waiting for transfers between devices: 16.5 us -> 12.8 us  [split_stencil(): lax.ppermute(cells[..., :width, :, :], 'rad', [(i + 1, i) for i in range(...]
    add x12 -> x14, other arithmetic: 12.6 us -> 13.5 us  [stencil(): -speed_r[:, :, None, None] * first_r - speed_p[:, :, None, None] * first_p]
  transfers between devices with their start and end apart: 17 -> 17, of which waited for: 6 -> 5; matrix products, arithmetic and copies ran while one was open for 8% -> 8% of each run, Pallas kernels for 0% -> 0%
where the time goes in v11:
time: 164 us
  starting transfers between devices  54 us (33%)
  waiting for transfers between devices  41 us (25%)
  blocking collectives  36.2 us (22%)
  other arithmetic  17.3 us (11%)
  local copies, waits for them, and re-layouts  10.6 us (6%)
  between operations  4.67 us (3%)
    all_to_all x1, blocking collectives, shift_rows(): return lax.all_to_all(moved, 'azi', 2, 1, tiled=True)  36.2 us
    all_to_all x1, waiting for transfers between devices, shift_rows(): full = lax.all_to_all(half, 'azi', 1, 2, tiled=True)  28.2 us
    ppermute x4, starting transfers between devices, split_stencil(): lax.ppermute(cells[..., rows - width:, :, :], 'rad', [(i, i + 1) for i in...  21.2 us
    ppermute x4, starting transfers between devices, split_stencil(): lax.ppermute(cells[..., :width, :], 'azi', [((i + 1) % sectors, i) for i...  16.4 us
    add x14, other arithmetic, stencil(): -speed_r[:, :, None, None] * first_r - speed_p[:, :, None, None] * first_p  13.5 us
    ppermute x4, waiting for transfers between devices, split_stencil(): lax.ppermute(cells[..., :width, :, :], 'rad', [(i + 1, i) for i in range(...  12.8 us
    ppermute x4, starting transfers between devices, split_stencil(): lax.ppermute(cells[..., :width, :, :], 'rad', [(i + 1, i) for i in range(...  7.68 us
    all_to_all x1, starting transfers between devices, shift_rows(): full = lax.all_to_all(half, 'azi', 1, 2, tiled=True)  6.02 us
  transfers between devices with their start and end apart: 17, of which 5 were waited for; matrix products, arithmetic and copies ran while one was open for 8% of the time, Pallas kernels for 0%

profile of v11, /device:TPU:1, one launch (start us, length us, event | category | flops | bytes accessed | tf_op | source)
XLA Modules:
  0.0 163.8 jit_solution(1917964680300439179)
XLA Ops:
  0.0 1.7 %copy.55 = f32[5,32,16,128]{3,1,2,0:T(8,128)S(1)} copy(f32[5,32,16,128]{3,2,1,0:T(8,128)} %param.5) | data formatting | bytes 2621440 | tf_op args[0]
  1.8 2.2 %collective-permute-start.1 = (f32[5,32,2,128]{3,1,2,0:T(8,128)S(1)}, f32[5,32,2,128]{3,1,2,0:T(8,128)S(1)}, u32[]{:S(2)}, u32[]{:S(2)}) collective-permute-start(f32[5,32,2,128]{3,1,2,0:T(8,128)S(1)} %get-tuple-element.34), channel_id=1, source_target_pairs={{0,1},{1,2},{2,3},{3,4},{4,5},{5,6},{6,7},{7,8},{8,9},{9,10},{10,1... | collective-permute-start | bytes 491528 | tf_op jit(solution)/shard_map/ppermute | solution.py:40
  4.0 5.4 %collective-permute-start.3 = (f32[5,32,2,128]{3,1,2,0:T(8,128)S(1)}, f32[5,32,2,128]{3,1,2,0:T(8,128)S(1)}, u32[]{:S(2)}, u32[]{:S(2)}) collective-permute-start(f32[5,32,2,128]{3,1,2,0:T(8,128)S(1)} %get-tuple-element.33), channel_id=1, source_target_pairs={{1,0},{2,1},{3,2},{4,3},{5,4},{6,5},{7,6},{8,7},{9,8},{10,9},{11,1... | collective-permute-start | bytes 491528 | tf_op jit(solution)/shard_map/ppermute | solution.py:41
  9.4 5.4 %collective-permute-start = (f32[5,2,16,128]{3,1,2,0:T(2,128)S(1)}, f32[5,2,16,128]{3,1,2,0:T(2,128)S(1)}, u32[]{:S(2)}, u32[]{:S(2)}) collective-permute-start(f32[5,2,16,128]{3,1,2,0:T(2,128)S(1)} %get-tuple-element.31), channel_id=1, source_target_pairs={{0,16},{16,32},{32,48},{48,64},{64,80},{80,96},{96,112},{112,128},... | collective-permute-start | bytes 245768 | tf_op jit(solution)/shard_map/ppermute | solution.py:42
  14.8 1.9 %collective-permute-start.2 = (f32[5,2,16,128]{3,1,2,0:T(2,128)S(1)}, f32[5,2,16,128]{3,1,2,0:T(2,128)S(1)}, u32[]{:S(2)}, u32[]{:S(2)}) collective-permute-start(f32[5,2,16,128]{3,1,2,0:T(2,128)S(1)} %get-tuple-element.32), channel_id=1, source_target_pairs={{16,0},{32,16},{48,32},{64,48},{80,64},{96,80},{112,96},{128,112},... | collective-permute-start | bytes 245768 | tf_op jit(solution)/shard_map/ppermute | solution.py:43
  17.8 2.0 %fusion.14 = f32[5,28,12,128]{3,1,2,0:T(8,128)S(1)} fusion(f32[5,28,12,128]{3,1,2,0:T(8,128)S(1)} %slice.1147, f32[5,32,16,128]{3,1,2,0:T(8,128)S(1)} %copy.55, f32[28,12,128]{2,0,1:T(8,128)S(1)} %copy.40, f32[5,28]{1,0:T(8,128)S(1)} %get-tuple-element.83, f32[5,28]{1,0:T(8,128)S(1)} %get-tuple-element.84), kind=kLoop, calls=%fused_computation.49 | loop fusion | flops 8386560 | bytes 8774752 | tf_op jit(solution)/shard_map/add | solution.py:31
  20.5 1.6 collective-permute-done.2
  23.6 0.9 copy-done
  25.3 3.6 %collective-permute-start.4 = (f32[5,2,16,128]{3,1,2,0:T(2,128)S(1)}, f32[5,2,16,128]{3,1,2,0:T(2,128)S(1)}, u32[]{:S(2)}, u32[]{:S(2)}) collective-permute-start(f32[5,2,16,128]{3,1,2,0:T(2,128)S(1)} %get-tuple-element.23), channel_id=1, source_target_pairs={{0,16},{16,32},{32,48},{48,64},{64,80},{80,96},{96,112},{112,128},... | collective-permute-start | bytes 245768 | tf_op jit(solution)/shard_map/ppermute | solution.py:42
  29.1 1.9 %collective-permute-start.6 = (f32[5,2,16,128]{3,1,2,0:T(2,128)S(1)}, f32[5,2,16,128]{3,1,2,0:T(2,128)S(1)}, u32[]{:S(2)}, u32[]{:S(2)}) collective-permute-start(f32[5,2,16,128]{3,1,2,0:T(2,128)S(1)} %get-tuple-element.24), channel_id=1, source_target_pairs={{16,0},{32,16},{48,32},{64,48},{80,64},{96,80},{112,96},{128,112},... | collective-permute-start | bytes 245768 | tf_op jit(solution)/shard_map/ppermute | solution.py:43
  31.0 3.8 %collective-permute-start.7 = (f32[5,32,2,128]{3,1,2,0:T(8,128)S(1)}, f32[5,32,2,128]{3,1,2,0:T(8,128)S(1)}, u32[]{:S(2)}, u32[]{:S(2)}) collective-permute-start(f32[5,32,2,128]{3,1,2,0:T(8,128)S(1)} %get-tuple-element.25), channel_id=1, source_target_pairs={{1,0},{2,1},{3,2},{4,3},{5,4},{6,5},{7,6},{8,7},{9,8},{10,9},{11,1... | collective-permute-start | bytes 491528 | tf_op jit(solution)/shard_map/ppermute | solution.py:41
  34.8 4.3 %collective-permute-done.6 = f32[5,2,16,128]{3,1,2,0:T(2,128)S(1)} collective-permute-done((f32[5,2,16,128]{3,1,2,0:T(2,128)S(1)}, f32[5,2,16,128]{3,1,2,0:T(2,128)S(1)}, u32[]{:S(2)}, u32[]{:S(2)}) %collective-permute-start.6) | collective-permute-done | bytes 81952 | tf_op jit(solution)/shard_map/ppermute | solution.py:43
  39.1 2.7 %fusion.24 = f32[5,32,12,128]{3,1,2,0:T(8,128)S(1)} fusion(f32[5,32,12,128]{3,1,2,0:T(8,128)S(1)} %slice.1186, f32[5,32,16,128]{3,1,2,0:T(8,128)S(1)} %maximum_add_fusion, f32[5,2,16,128]{3,1,2,0:T(2,128)S(1)} %collective-permute-done.6, f32[5,2,16,128]{3,1,2,0:T(2,128)S(1)} %collective-permute-done.4, f32[32,12,128]{2,0,1:T(8,128)S(1)} %copy.56, ...), kind=kLoop, calls=%fused_computation.59 | loop fusion | flops 10567680 | bytes 7577600 | tf_op jit(solution)/shard_map/add | solution.py:31
  42.8 0.6 fusion
  43.5 1.8 %copy.57 = f32[5,32,16,128]{3,2,0,1:T(8,128)} copy(f32[5,32,16,128]{3,1,2,0:T(8,128)S(1)} %fusion) | data formatting | bytes 2621440 | tf_op jit(solution)/shard_map/mul | solution.py:72
  45.3 6.0 %all-to-all-start = ((f32[5,32,16,128]{3,2,0,1:T(8,128)}), f32[5,32,16,128]{3,2,0,1:T(8,128)S(1)}, u32[]{:S(2)}, u32[]{:S(2)}) async-start(f32[5,32,16,128]{3,2,0,1:T(8,128)} %copy.57), calls=%async_computation | async-start | bytes 2621440 | tf_op jit(solution)/shard_map/all_to_all | solution.py:79
  51.4 0.6 fusion.164
  56.1 28.2 %all-to-all-done = f32[5,32,16,128]{3,2,0,1:T(8,128)S(1)} async-done(((f32[5,32,16,128]{3,2,0,1:T(8,128)}), f32[5,32,16,128]{3,2,0,1:T(8,128)S(1)}, u32[]{:S(2)}, u32[]{:S(2)}) %all-to-all-start) | async-done | bytes 1310752 | tf_op jit(solution)/shard_map/all_to_all | solution.py:79
  84.9 1.0 copy.60
  86.0 36.2 %all_to_all.36 = f32[5,2,256,128]{3,1,0,2:T(2,128)S(1)} all-to-all(f32[5,2,256,128]{3,1,0,2:T(2,128)S(1)} %copy.60), channel_id=1, replica_groups=mesh['rad'=16,'azi'=16] {'azi'}, dimensions={2} | all-to-all | bytes 2621440 | tf_op jit(solution)/shard_map/all_to_all | solution.py:89
  123.0 6.5 %collective-permute-start.8 = (f32[5,2,16,128]{3,1,2,0:T(2,128)S(1)}, f32[5,2,16,128]{3,1,2,0:T(2,128)S(1)}, u32[]{:S(2)}, u32[]{:S(2)}) collective-permute-start(f32[5,2,16,128]{3,1,2,0:T(2,128)S(1)} %get-tuple-element.15), channel_id=1, source_target_pairs={{0,16},{16,32},{32,48},{48,64},{64,80},{80,96},{96,112},{112,128},... | collective-permute-start | bytes 245768 | tf_op jit(solution)/shard_map/ppermute | solution.py:42
  129.7 1.9 %collective-permute-start.10 = (f32[5,2,16,128]{3,1,2,0:T(2,128)S(1)}, f32[5,2,16,128]{3,1,2,0:T(2,128)S(1)}, u32[]{:S(2)}, u32[]{:S(2)}) collective-permute-start(f32[5,2,16,128]{3,1,2,0:T(2,128)S(1)} %get-tuple-element.16), channel_id=1, source_target_pairs={{16,0},{32,16},{48,32},{64,48},{80,64},{96,80},{112,96},{128,112},... | collective-permute-start | bytes 245768 | tf_op jit(solution)/shard_map/ppermute | solution.py:43
  131.7 3.6 %collective-permute-start.11 = (f32[5,32,2,128]{3,1,2,0:T(8,128)S(1)}, f32[5,32,2,128]{3,1,2,0:T(8,128)S(1)}, u32[]{:S(2)}, u32[]{:S(2)}) collective-permute-start(f32[5,32,2,128]{3,1,2,0:T(8,128)S(1)} %get-tuple-element.17), channel_id=1, source_target_pairs={{1,0},{2,1},{3,2},{4,3},{5,4},{6,5},{7,6},{8,7},{9,8},{10,9},{11,1... | collective-permute-start | bytes 491528 | tf_op jit(solution)/shard_map/ppermute | solution.py:41
  135.3 1.7 %collective-permute-done.10 = f32[5,2,16,128]{3,1,2,0:T(2,128)S(1)} collective-permute-done((f32[5,2,16,128]{3,1,2,0:T(2,128)S(1)}, f32[5,2,16,128]{3,1,2,0:T(2,128)S(1)}, u32[]{:S(2)}, u32[]{:S(2)}) %collective-permute-start.10) | collective-permute-done | bytes 81952 | tf_op jit(solution)/shard_map/ppermute | solution.py:43
  137.0 2.0 %fusion.34 = f32[5,32,12,128]{3,1,2,0:T(8,128)S(1)} fusion(f32[5,32,12,128]{3,1,2,0:T(8,128)S(1)} %slice.1219, f32[5,32,16,128]{3,1,2,0:T(8,128)S(1)} %get-tuple-element.14, f32[5,34,16,128]{3,1,2,0:T(8,128)S(1)} %constant_dynamic-update-slice_fusion, f32[5,2,16,128]{3,1,2,0:T(2,128)S(1)} %collective-permute-done.8, f32[32,12,128]{2,0,1:T(8,128)S(1)} %copy.56, ...), kind=kLoop, calls=%fused_computation.69 | loop fusion | flops 10076160 | bytes 9461760 | tf_op jit(solution)/shard_map/add | solution.py:31
  140.7 5.7 %collective-permute-start.12 = (f32[5,2,16,128]{3,1,2,0:T(2,128)S(1)}, f32[5,2,16,128]{3,1,2,0:T(2,128)S(1)}, u32[]{:S(2)}, u32[]{:S(2)}) collective-permute-start(f32[5,2,16,128]{3,1,2,0:T(2,128)S(1)} %get-tuple-element.7), channel_id=1, source_target_pairs={{0,16},{16,32},{32,48},{48,64},{64,80},{80,96},{96,112},{112,128},... | collective-permute-start | bytes 245768 | tf_op jit(solution)/shard_map/ppermute | solution.py:42
  146.9 1.9 %collective-permute-start.14 = (f32[5,2,16,128]{3,1,2,0:T(2,128)S(1)}, f32[5,2,16,128]{3,1,2,0:T(2,128)S(1)}, u32[]{:S(2)}, u32[]{:S(2)}) collective-permute-start(f32[5,2,16,128]{3,1,2,0:T(2,128)S(1)} %get-tuple-element.8), channel_id=1, source_target_pairs={{16,0},{32,16},{48,32},{64,48},{80,64},{96,80},{112,96},{128,112},... | collective-permute-start | bytes 245768 | tf_op jit(solution)/shard_map/ppermute | solution.py:43
  148.8 3.6 %collective-permute-start.15 = (f32[5,32,2,128]{3,1,2,0:T(8,128)S(1)}, f32[5,32,2,128]{3,1,2,0:T(8,128)S(1)}, u32[]{:S(2)}, u32[]{:S(2)}) collective-permute-start(f32[5,32,2,128]{3,1,2,0:T(8,128)S(1)} %get-tuple-element.9), channel_id=1, source_target_pairs={{1,0},{2,1},{3,2},{4,3},{5,4},{6,5},{7,6},{8,7},{9,8},{10,9},{11,1... | collective-permute-start | bytes 491528 | tf_op jit(solution)/shard_map/ppermute | solution.py:41
  152.4 5.2 %collective-permute-done.14 = f32[5,2,16,128]{3,1,2,0:T(2,128)S(1)} collective-permute-done((f32[5,2,16,128]{3,1,2,0:T(2,128)S(1)}, f32[5,2,16,128]{3,1,2,0:T(2,128)S(1)}, u32[]{:S(2)}, u32[]{:S(2)}) %collective-permute-start.14) | collective-permute-done | bytes 81952 | tf_op jit(solution)/shard_map/ppermute | solution.py:43
  157.7 2.7 %fusion.44 = f32[5,32,12,128]{3,1,2,0:T(8,128)S(1)} fusion(f32[5,32,12,128]{3,1,2,0:T(8,128)S(1)} %slice.1250, f32[5,32,16,128]{3,1,2,0:T(8,128)S(1)} %maximum_add_fusion.2, f32[5,2,16,128]{3,1,2,0:T(2,128)S(1)} %collective-permute-done.14, f32[5,2,16,128]{3,1,2,0:T(2,128)S(1)} %collective-permute-done.12, f32[32,12,128]{2,0,1:T(8,128)S(1)} %copy.56, ...), kind=kLoop, calls=%fused_computation.79 | loop fusion | flops 10567680 | bytes 7577600 | tf_op jit(solution)/shard_map/add | solution.py:31
  161.4 0.6 fusion.1
  162.0 1.8 %copy.82 = f32[5,32,16,128]{3,2,1,0:T(8,128)} copy(f32[5,32,16,128]{3,1,2,0:T(8,128)S(1)} %fusion.1) | data formatting | bytes 2621440 | tf_op jit(solution)/shard_map/mul | solution.py:72
  (91 shorter events, 9.8 us)
Async XLA Ops:
  1.7 15.1 %copy-start.1 = (f32[32,16,128]{2,1,0:T(8,128)S(1)}, f32[32,16,128]{2,1,0:T(8,128)}, u32[]{:S(2)}) copy-start(f32[32,16,128]{2,1,0:T(8,128)} %param.6) | copy-start | bytes 786436
  1.8 20.8 %collective-permute-start.1 = (f32[5,32,2,128]{3,1,2,0:T(8,128)S(1)}, f32[5,32,2,128]{3,1,2,0:T(8,128)S(1)}, u32[]{:S(2)}, u32[]{:S(2)}) collective-permute-start(f32[5,32,2,128]{3,1,2,0:T(8,128)S(1)} %get-tuple-element.34), channel_id=1, source_target_pairs={{0,1},{1,2},{2,3},{3,4},{4,5},{5,6},{6,7},{7,8},{8,9},{9,10},{10,1... | collective-permute-start | bytes 491528 | tf_op jit(solution)/shard_map/ppermute | solution.py:40
  4.0 18.6 %collective-permute-start.3 = (f32[5,32,2,128]{3,1,2,0:T(8,128)S(1)}, f32[5,32,2,128]{3,1,2,0:T(8,128)S(1)}, u32[]{:S(2)}, u32[]{:S(2)}) collective-permute-start(f32[5,32,2,128]{3,1,2,0:T(8,128)S(1)} %get-tuple-element.33), channel_id=1, source_target_pairs={{1,0},{2,1},{3,2},{4,3},{5,4},{6,5},{7,6},{8,7},{9,8},{10,9},{11,1... | collective-permute-start | bytes 491528 | tf_op jit(solution)/shard_map/ppermute | solution.py:41
  9.4 10.5 %collective-permute-start = (f32[5,2,16,128]{3,1,2,0:T(2,128)S(1)}, f32[5,2,16,128]{3,1,2,0:T(2,128)S(1)}, u32[]{:S(2)}, u32[]{:S(2)}) collective-permute-start(f32[5,2,16,128]{3,1,2,0:T(2,128)S(1)} %get-tuple-element.31), channel_id=1, source_target_pairs={{0,16},{16,32},{32,48},{48,64},{64,80},{80,96},{96,112},{112,128},... | collective-permute-start | bytes 245768 | tf_op jit(solution)/shard_map/ppermute | solution.py:42
  14.8 7.3 %collective-permute-start.2 = (f32[5,2,16,128]{3,1,2,0:T(2,128)S(1)}, f32[5,2,16,128]{3,1,2,0:T(2,128)S(1)}, u32[]{:S(2)}, u32[]{:S(2)}) collective-permute-start(f32[5,2,16,128]{3,1,2,0:T(2,128)S(1)} %get-tuple-element.32), channel_id=1, source_target_pairs={{16,0},{32,16},{48,32},{64,48},{80,64},{96,80},{112,96},{128,112},... | collective-permute-start | bytes 245768 | tf_op jit(solution)/shard_map/ppermute | solution.py:43
  16.8 0.7 copy-start.2
  16.8 0.7 copy-start.3
  23.2 1.3 copy-start
  25.3 9.5 %collective-permute-start.4 = (f32[5,2,16,128]{3,1,2,0:T(2,128)S(1)}, f32[5,2,16,128]{3,1,2,0:T(2,128)S(1)}, u32[]{:S(2)}, u32[]{:S(2)}) collective-permute-start(f32[5,2,16,128]{3,1,2,0:T(2,128)S(1)} %get-tuple-element.23), channel_id=1, source_target_pairs={{0,16},{16,32},{32,48},{48,64},{64,80},{80,96},{96,112},{112,128},... | collective-permute-start | bytes 245768 | tf_op jit(solution)/shard_map/ppermute | solution.py:42
  29.0 12.9 %collective-permute-start.5 = (f32[5,32,2,128]{3,1,2,0:T(8,128)S(1)}, f32[5,32,2,128]{3,1,2,0:T(8,128)S(1)}, u32[]{:S(2)}, u32[]{:S(2)}) collective-permute-start(f32[5,32,2,128]{3,1,2,0:T(8,128)S(1)} %get-tuple-element.26), channel_id=1, source_target_pairs={{0,1},{1,2},{2,3},{3,4},{4,5},{5,6},{6,7},{7,8},{8,9},{9,10},{10,1... | collective-permute-start | bytes 491528 | tf_op jit(solution)/shard_map/ppermute | solution.py:40
  29.1 10.0 %collective-permute-start.6 = (f32[5,2,16,128]{3,1,2,0:T(2,128)S(1)}, f32[5,2,16,128]{3,1,2,0:T(2,128)S(1)}, u32[]{:S(2)}, u32[]{:S(2)}) collective-permute-start(f32[5,2,16,128]{3,1,2,0:T(2,128)S(1)} %get-tuple-element.24), channel_id=1, source_target_pairs={{16,0},{32,16},{48,32},{64,48},{80,64},{96,80},{112,96},{128,112},... | collective-permute-start | bytes 245768 | tf_op jit(solution)/shard_map/ppermute | solution.py:43
  31.0 11.3 %collective-permute-start.7 = (f32[5,32,2,128]{3,1,2,0:T(8,128)S(1)}, f32[5,32,2,128]{3,1,2,0:T(8,128)S(1)}, u32[]{:S(2)}, u32[]{:S(2)}) collective-permute-start(f32[5,32,2,128]{3,1,2,0:T(8,128)S(1)} %get-tuple-element.25), channel_id=1, source_target_pairs={{1,0},{2,1},{3,2},{4,3},{5,4},{6,5},{7,6},{8,7},{9,8},{10,9},{11,1... | collective-permute-start | bytes 491528 | tf_op jit(solution)/shard_map/ppermute | solution.py:41
  45.3 6.0 %copy-start.4 = (s32[32]{0:T(128)S(1)}, s32[32]{0:T(128)}, u32[]{:S(2)}) copy-start(s32[32]{0:T(128)} %param.9) | copy-start | bytes 388
  45.3 38.9 %all-to-all-start = ((f32[5,32,16,128]{3,2,0,1:T(8,128)}), f32[5,32,16,128]{3,2,0,1:T(8,128)S(1)}, u32[]{:S(2)}, u32[]{:S(2)}) async-start(f32[5,32,16,128]{3,2,0,1:T(8,128)} %copy.57), calls=%async_computation | async-start | bytes 2621440 | tf_op jit(solution)/shard_map/all_to_all | solution.py:79
  123.0 12.3 %collective-permute-start.8 = (f32[5,2,16,128]{3,1,2,0:T(2,128)S(1)}, f32[5,2,16,128]{3,1,2,0:T(2,128)S(1)}, u32[]{:S(2)}, u32[]{:S(2)}) collective-permute-start(f32[5,2,16,128]{3,1,2,0:T(2,128)S(1)} %get-tuple-element.15), channel_id=1, source_target_pairs={{0,16},{16,32},{32,48},{48,64},{64,80},{80,96},{96,112},{112,128},... | collective-permute-start | bytes 245768 | tf_op jit(solution)/shard_map/ppermute | solution.py:42
  129.6 9.5 %collective-permute-start.9 = (f32[5,32,2,128]{3,1,2,0:T(8,128)S(1)}, f32[5,32,2,128]{3,1,2,0:T(8,128)S(1)}, u32[]{:S(2)}, u32[]{:S(2)}) collective-permute-start(f32[5,32,2,128]{3,1,2,0:T(8,128)S(1)} %get-tuple-element.18), channel_id=1, source_target_pairs={{0,1},{1,2},{2,3},{3,4},{4,5},{5,6},{6,7},{7,8},{8,9},{9,10},{10,1... | collective-permute-start | bytes 491528 | tf_op jit(solution)/shard_map/ppermute | solution.py:40
  129.7 7.3 %collective-permute-start.10 = (f32[5,2,16,128]{3,1,2,0:T(2,128)S(1)}, f32[5,2,16,128]{3,1,2,0:T(2,128)S(1)}, u32[]{:S(2)}, u32[]{:S(2)}) collective-permute-start(f32[5,2,16,128]{3,1,2,0:T(2,128)S(1)} %get-tuple-element.16), channel_id=1, source_target_pairs={{16,0},{32,16},{48,32},{64,48},{80,64},{96,80},{112,96},{128,112},... | collective-permute-start | bytes 245768 | tf_op jit(solution)/shard_map/ppermute | solution.py:43
  131.7 7.9 %collective-permute-start.11 = (f32[5,32,2,128]{3,1,2,0:T(8,128)S(1)}, f32[5,32,2,128]{3,1,2,0:T(8,128)S(1)}, u32[]{:S(2)}, u32[]{:S(2)}) collective-permute-start(f32[5,32,2,128]{3,1,2,0:T(8,128)S(1)} %get-tuple-element.17), channel_id=1, source_target_pairs={{1,0},{2,1},{3,2},{4,3},{5,4},{6,5},{7,6},{8,7},{9,8},{10,9},{11,1... | collective-permute-start | bytes 491528 | tf_op jit(solution)/shard_map/ppermute | solution.py:41
  140.7 11.7 %collective-permute-start.12 = (f32[5,2,16,128]{3,1,2,0:T(2,128)S(1)}, f32[5,2,16,128]{3,1,2,0:T(2,128)S(1)}, u32[]{:S(2)}, u32[]{:S(2)}) collective-permute-start(f32[5,2,16,128]{3,1,2,0:T(2,128)S(1)} %get-tuple-element.7), channel_id=1, source_target_pairs={{0,16},{16,32},{32,48},{48,64},{64,80},{80,96},{96,112},{112,128},... | collective-permute-start | bytes 245768 | tf_op jit(solution)/shard_map/ppermute | solution.py:42
  146.6 13.8 %collective-permute-start.13 = (f32[5,32,2,128]{3,1,2,0:T(8,128)S(1)}, f32[5,32,2,128]{3,1,2,0:T(8,128)S(1)}, u32[]{:S(2)}, u32[]{:S(2)}) collective-permute-start(f32[5,32,2,128]{3,1,2,0:T(8,128)S(1)} %get-tuple-element.10), channel_id=1, source_target_pairs={{0,1},{1,2},{2,3},{3,4},{4,5},{5,6},{6,7},{7,8},{8,9},{9,10},{10,1... | collective-permute-start | bytes 491528 | tf_op jit(solution)/shard_map/ppermute | solution.py:40
  146.9 10.8 %collective-permute-start.14 = (f32[5,2,16,128]{3,1,2,0:T(2,128)S(1)}, f32[5,2,16,128]{3,1,2,0:T(2,128)S(1)}, u32[]{:S(2)}, u32[]{:S(2)}) collective-permute-start(f32[5,2,16,128]{3,1,2,0:T(2,128)S(1)} %get-tuple-element.8), channel_id=1, source_target_pairs={{16,0},{32,16},{48,32},{64,48},{80,64},{96,80},{112,96},{128,112},... | collective-permute-start | bytes 245768 | tf_op jit(solution)/shard_map/ppermute | solution.py:43
  148.8 12.1 %collective-permute-start.15 = (f32[5,32,2,128]{3,1,2,0:T(8,128)S(1)}, f32[5,32,2,128]{3,1,2,0:T(8,128)S(1)}, u32[]{:S(2)}, u32[]{:S(2)}) collective-permute-start(f32[5,32,2,128]{3,1,2,0:T(8,128)S(1)} %get-tuple-element.9), channel_id=1, source_target_pairs={{1,0},{2,1},{3,2},{4,3},{5,4},{6,5},{7,6},{8,7},{9,8},{10,9},{11,1... | collective-permute-start | bytes 491528 | tf_op jit(solution)/shard_map/ppermute | solution.py:41

commit v12 on v11

--- a/solution.py
+++ b/solution.py
@@ -34,7 +34,7 @@
     )
 
 
-def split_stencil(cells, kap, speed_r, speed_p, width=2, core=False):
+def split_stencil(cells, kap, speed_r, speed_p, width=2):
     sectors, rings = lax.axis_size("azi"), lax.axis_size("rad")
     rows, cols = cells.shape[-3], cells.shape[-2]
     left = lax.ppermute(cells[..., cols - width :, :], "azi", [(i, (i + 1) % sectors) for i in range(sectors)])
@@ -43,7 +43,7 @@
     below = lax.ppermute(cells[..., :width, :, :], "rad", [(i + 1, i) for i in range(rings - 1)])
     tall = jnp.concatenate([above, cells, below], axis=1)
     inner = kap[:, width : cols - width]
-    if core:
+    if rows > 4 * width:
         parts = [
             stencil(tall[:, : 3 * width], inner[:width], speed_r[:, :width], speed_p[:, :width]),
             stencil(cells, inner[width : rows - width], speed_r[:, width : rows - width], speed_p[:, width : rows - width]),
@@ -67,8 +67,8 @@
     return jnp.concatenate([first, middle, last], axis=2)
 
 
-def heun_sections(field, kappa, speed_r, speed_p, core=False):
-    first = field + split_stencil(field, kappa, speed_r, speed_p, core=core)
+def heun_sections(field, kappa, speed_r, speed_p):
+    first = field + split_stencil(field, kappa, speed_r, speed_p)
     return 0.5 * (field + first + split_stencil(first, kappa, speed_r, speed_p))
 
 
@@ -90,7 +90,7 @@
 
 
 def shards(fields, kappa, radial_speed, azimuth_speed, shifts):
-    half = heun_sections(fields, kappa, radial_speed, azimuth_speed, core=True)
+    half = heun_sections(fields, kappa, radial_speed, azimuth_speed)
     moved = shift_rows(half, shifts)
     return heun_sections(moved, kappa, radial_speed, azimuth_speed)
 

time: 164 us -> 167 us (1.018); the launches traced: 164 us -> 164 us
  waiting for transfers between devices: 41 us -> 36.9 us
  blocking collectives: 36.2 us -> 39.7 us
  other arithmetic: 17.3 us -> 19 us
    ppermute x4, waiting for transfers between devices: 12.8 us -> 4.65 us  [split_stencil(): lax.ppermute(cells[..., :width, :, :], 'rad', [(i + 1, i) for i in range(...]
    ppermute x4, waiting for transfers between devices: 0.01 us -> 3.85 us  [split_stencil(): lax.ppermute(cells[..., cols - width:, :], 'azi', [(i, (i + 1) % sectors)...]
    all_to_all x1, blocking collectives: 36.2 us -> 39.7 us  [shift_rows(): return lax.all_to_all(moved, 'azi', 2, 1, tiled=True)]
    ppermute x4, waiting for transfers between devices: 0.01 us -> 1.76 us  [split_stencil(): lax.ppermute(cells[..., :width, :], 'azi', [((i + 1) % sectors, i) for i...]
    add x14 -> x20, other arithmetic: 13.5 us -> 15 us  [stencil(): -speed_r[:, :, None, None] * first_r - speed_p[:, :, None, None] * first_p]
    unnamed x12 -> x11, local copies, waits for them, and re-layouts: 3.6 us -> 3.16 us
  transfers between devices with their start and end apart: 17 -> 17, of which waited for: 5 -> 7; matrix products, arithmetic and copies ran while one was open for 8% -> 9% of each run, Pallas kernels for 0% -> 0%
where the time goes in v12:
time: 167 us; the launch traced here: 164 us
  starting transfers between devices  54 us (32%)
  blocking collectives  39.7 us (24%)
  waiting for transfers between devices  36.9 us (22%)
  other arithmetic  19 us (11%)
  local copies, waits for them, and re-layouts  10.7 us (6%)
  between operations  4.05 us (2%)
    all_to_all x1, blocking collectives, shift_rows(): return lax.all_to_all(moved, 'azi', 2, 1, tiled=True)  39.7 us
    all_to_all x1, waiting for transfers between devices, shift_rows(): full = lax.all_to_all(half, 'azi', 1, 2, tiled=True)  26.7 us
    ppermute x4, starting transfers between devices, split_stencil(): lax.ppermute(cells[..., rows - width:, :, :], 'rad', [(i, i + 1) for i in...  21.2 us
    ppermute x4, starting transfers between devices, split_stencil(): lax.ppermute(cells[..., :width, :], 'azi', [((i + 1) % sectors, i) for i...  16.1 us
    add x20, other arithmetic, stencil(): -speed_r[:, :, None, None] * first_r - speed_p[:, :, None, None] * first_p  15 us
    ppermute x4, starting transfers between devices, split_stencil(): lax.ppermute(cells[..., :width, :, :], 'rad', [(i + 1, i) for i in range(...  7.68 us
    all_to_all x1, starting transfers between devices, shift_rows(): full = lax.all_to_all(half, 'azi', 1, 2, tiled=True)  6.63 us
    ppermute x4, waiting for transfers between devices, split_stencil(): lax.ppermute(cells[..., :width, :, :], 'rad', [(i + 1, i) for i in range(...  4.65 us
  transfers between devices with their start and end apart: 17, of which 7 were waited for; matrix products, arithmetic and copies ran while one was open for 9% of the time, Pallas kernels for 0%

profile of v12, /device:TPU:1, one launch (start us, length us, event | category | flops | bytes accessed | tf_op | source)
XLA Modules:
  0.0 164.3 jit_solution(2389620417834806602)
XLA Ops:
  0.0 1.7 %copy.55 = f32[5,32,16,128]{3,1,2,0:T(8,128)S(1)} copy(f32[5,32,16,128]{3,2,1,0:T(8,128)} %param.5) | data formatting | bytes 2621440 | tf_op args[0]
  1.8 2.2 %collective-permute-start.1 = (f32[5,32,2,128]{3,1,2,0:T(8,128)S(1)}, f32[5,32,2,128]{3,1,2,0:T(8,128)S(1)}, u32[]{:S(2)}, u32[]{:S(2)}) collective-permute-start(f32[5,32,2,128]{3,1,2,0:T(8,128)S(1)} %get-tuple-element.38), channel_id=1, source_target_pairs={{0,1},{1,2},{2,3},{3,4},{4,5},{5,6},{6,7},{7,8},{8,9},{9,10},{10,1... | collective-permute-start | bytes 491528 | tf_op jit(solution)/shard_map/ppermute | solution.py:40
  4.0 5.4 %collective-permute-start.3 = (f32[5,32,2,128]{3,1,2,0:T(8,128)S(1)}, f32[5,32,2,128]{3,1,2,0:T(8,128)S(1)}, u32[]{:S(2)}, u32[]{:S(2)}) collective-permute-start(f32[5,32,2,128]{3,1,2,0:T(8,128)S(1)} %get-tuple-element.37), channel_id=1, source_target_pairs={{1,0},{2,1},{3,2},{4,3},{5,4},{6,5},{7,6},{8,7},{9,8},{10,9},{11,1... | collective-permute-start | bytes 491528 | tf_op jit(solution)/shard_map/ppermute | solution.py:41
  9.4 5.4 %collective-permute-start = (f32[5,2,16,128]{3,1,2,0:T(2,128)S(1)}, f32[5,2,16,128]{3,1,2,0:T(2,128)S(1)}, u32[]{:S(2)}, u32[]{:S(2)}) collective-permute-start(f32[5,2,16,128]{3,1,2,0:T(2,128)S(1)} %get-tuple-element.35), channel_id=1, source_target_pairs={{0,16},{16,32},{32,48},{48,64},{64,80},{80,96},{96,112},{112,128},... | collective-permute-start | bytes 245768 | tf_op jit(solution)/shard_map/ppermute | solution.py:42
  14.8 1.9 %collective-permute-start.2 = (f32[5,2,16,128]{3,1,2,0:T(2,128)S(1)}, f32[5,2,16,128]{3,1,2,0:T(2,128)S(1)}, u32[]{:S(2)}, u32[]{:S(2)}) collective-permute-start(f32[5,2,16,128]{3,1,2,0:T(2,128)S(1)} %get-tuple-element.36), channel_id=1, source_target_pairs={{16,0},{32,16},{48,32},{64,48},{80,64},{96,80},{112,96},{128,112},... | collective-permute-start | bytes 245768 | tf_op jit(solution)/shard_map/ppermute | solution.py:43
  17.7 2.0 %fusion.9 = f32[5,28,12,128]{3,1,2,0:T(8,128)S(1)} fusion(f32[5,28,12,128]{3,1,2,0:T(8,128)S(1)} %slice.1633, f32[5,32,16,128]{3,1,2,0:T(8,128)S(1)} %copy.55, f32[28,12,128]{2,0,1:T(8,128)S(1)} %copy.40, f32[5,28]{1,0:T(8,128)S(1)} %get-tuple-element.87, f32[5,28]{1,0:T(8,128)S(1)} %get-tuple-element.88), kind=kLoop, calls=%fused_computation.34 | loop fusion | flops 8386560 | bytes 8774752 | tf_op jit(solution)/shard_map/add | solution.py:31
  20.4 1.7 %collective-permute-done.2 = f32[5,2,16,128]{3,1,2,0:T(2,128)S(1)} collective-permute-done((f32[5,2,16,128]{3,1,2,0:T(2,128)S(1)}, f32[5,2,16,128]{3,1,2,0:T(2,128)S(1)}, u32[]{:S(2)}, u32[]{:S(2)}) %collective-permute-start.2) | collective-permute-done | bytes 81952 | tf_op jit(solution)/shard_map/ppermute | solution.py:43
  23.6 0.9 copy-done
  25.4 3.5 %collective-permute-start.4 = (f32[5,2,16,128]{3,1,2,0:T(2,128)S(1)}, f32[5,2,16,128]{3,1,2,0:T(2,128)S(1)}, u32[]{:S(2)}, u32[]{:S(2)}) collective-permute-start(f32[5,2,16,128]{3,1,2,0:T(2,128)S(1)} %get-tuple-element.27), channel_id=1, source_target_pairs={{0,16},{16,32},{32,48},{48,64},{64,80},{80,96},{96,112},{112,128},... | collective-permute-start | bytes 245768 | tf_op jit(solution)/shard_map/ppermute | solution.py:42
  28.9 1.9 %collective-permute-start.6 = (f32[5,2,16,128]{3,1,2,0:T(2,128)S(1)}, f32[5,2,16,128]{3,1,2,0:T(2,128)S(1)}, u32[]{:S(2)}, u32[]{:S(2)}) collective-permute-start(f32[5,2,16,128]{3,1,2,0:T(2,128)S(1)} %get-tuple-element.28), channel_id=1, source_target_pairs={{16,0},{32,16},{48,32},{64,48},{80,64},{96,80},{112,96},{128,112},... | collective-permute-start | bytes 245768 | tf_op jit(solution)/shard_map/ppermute | solution.py:43
  30.8 2.0 %fusion.19 = f32[5,28,12,128]{3,1,2,0:T(8,128)S(1)} fusion(f32[5,28,12,128]{3,1,2,0:T(8,128)S(1)} %slice.1680, f32[5,32,16,128]{3,1,2,0:T(8,128)S(1)} %maximum_add_fusion, f32[28,12,128]{2,0,1:T(8,128)S(1)} %copy.40, f32[5,28]{1,0:T(8,128)S(1)} %get-tuple-element.87, f32[5,28]{1,0:T(8,128)S(1)} %get-tuple-element.88), kind=kLoop, calls=%fused_computation.44 | loop fusion | flops 8386560 | bytes 8774752 | tf_op jit(solution)/shard_map/add | solution.py:31
  32.9 3.6 %collective-permute-start.7 = (f32[5,32,2,128]{3,1,2,0:T(8,128)S(1)}, f32[5,32,2,128]{3,1,2,0:T(8,128)S(1)}, u32[]{:S(2)}, u32[]{:S(2)}) collective-permute-start(f32[5,32,2,128]{3,1,2,0:T(8,128)S(1)} %get-tuple-element.29), channel_id=1, source_target_pairs={{1,0},{2,1},{3,2},{4,3},{5,4},{6,5},{7,6},{8,7},{9,8},{10,9},{11,1... | collective-permute-start | bytes 491528 | tf_op jit(solution)/shard_map/ppermute | solution.py:41
  37.0 2.9 %collective-permute-done.6 = f32[5,2,16,128]{3,1,2,0:T(2,128)S(1)} collective-permute-done((f32[5,2,16,128]{3,1,2,0:T(2,128)S(1)}, f32[5,2,16,128]{3,1,2,0:T(2,128)S(1)}, u32[]{:S(2)}, u32[]{:S(2)}) %collective-permute-start.6) | collective-permute-done | bytes 81952 | tf_op jit(solution)/shard_map/ppermute | solution.py:43
  41.9 0.7 fusion
  42.6 1.8 %copy.56 = f32[5,32,16,128]{3,2,0,1:T(8,128)} copy(f32[5,32,16,128]{3,1,2,0:T(8,128)S(1)} %fusion) | data formatting | bytes 2621440 | tf_op jit(solution)/shard_map/mul | solution.py:72
  44.4 6.6 %all-to-all-start = ((f32[5,32,16,128]{3,2,0,1:T(8,128)}), f32[5,32,16,128]{3,2,0,1:T(8,128)S(1)}, u32[]{:S(2)}, u32[]{:S(2)}) async-start(f32[5,32,16,128]{3,2,0,1:T(8,128)} %copy.56), calls=%async_computation | async-start | bytes 2621440 | tf_op jit(solution)/shard_map/all_to_all | solution.py:79
  55.1 26.7 %all-to-all-done = f32[5,32,16,128]{3,2,0,1:T(8,128)S(1)} async-done(((f32[5,32,16,128]{3,2,0,1:T(8,128)}), f32[5,32,16,128]{3,2,0,1:T(8,128)S(1)}, u32[]{:S(2)}, u32[]{:S(2)}) %all-to-all-start) | async-done | bytes 1310752 | tf_op jit(solution)/shard_map/all_to_all | solution.py:79
  82.5 1.0 copy.59
  83.5 39.7 %all_to_all.36 = f32[5,2,256,128]{3,1,0,2:T(2,128)S(1)} all-to-all(f32[5,2,256,128]{3,1,0,2:T(2,128)S(1)} %copy.59), channel_id=1, replica_groups=mesh['rad'=16,'azi'=16] {'azi'}, dimensions={2} | all-to-all | bytes 2621440 | tf_op jit(solution)/shard_map/all_to_all | solution.py:89
  124.1 5.6 %collective-permute-start.8 = (f32[5,2,16,128]{3,1,2,0:T(2,128)S(1)}, f32[5,2,16,128]{3,1,2,0:T(2,128)S(1)}, u32[]{:S(2)}, u32[]{:S(2)}) collective-permute-start(f32[5,2,16,128]{3,1,2,0:T(2,128)S(1)} %get-tuple-element.17), channel_id=1, source_target_pairs={{0,16},{16,32},{32,48},{48,64},{64,80},{80,96},{96,112},{112,128},... | collective-permute-start | bytes 245768 | tf_op jit(solution)/shard_map/ppermute | solution.py:42
  129.7 1.9 %collective-permute-start.10 = (f32[5,2,16,128]{3,1,2,0:T(2,128)S(1)}, f32[5,2,16,128]{3,1,2,0:T(2,128)S(1)}, u32[]{:S(2)}, u32[]{:S(2)}) collective-permute-start(f32[5,2,16,128]{3,1,2,0:T(2,128)S(1)} %get-tuple-element.18), channel_id=1, source_target_pairs={{16,0},{32,16},{48,32},{64,48},{80,64},{96,80},{112,96},{128,112},... | collective-permute-start | bytes 245768 | tf_op jit(solution)/shard_map/ppermute | solution.py:43
  131.7 2.0 %fusion.29 = f32[5,28,12,128]{3,1,2,0:T(8,128)S(1)} fusion(f32[5,28,12,128]{3,1,2,0:T(8,128)S(1)} %slice.1729, f32[5,32,16,128]{3,1,2,0:T(8,128)S(1)} %copy.98, f32[28,12,128]{2,0,1:T(8,128)S(1)} %copy.40, f32[5,28]{1,0:T(8,128)S(1)} %get-tuple-element.87, f32[5,28]{1,0:T(8,128)S(1)} %get-tuple-element.88), kind=kLoop, calls=%fused_computation.54 | loop fusion | flops 8386560 | bytes 8774752 | tf_op jit(solution)/shard_map/add | solution.py:31
  133.8 3.6 %collective-permute-start.11 = (f32[5,32,2,128]{3,1,2,0:T(8,128)S(1)}, f32[5,32,2,128]{3,1,2,0:T(8,128)S(1)}, u32[]{:S(2)}, u32[]{:S(2)}) collective-permute-start(f32[5,32,2,128]{3,1,2,0:T(8,128)S(1)} %get-tuple-element.19), channel_id=1, source_target_pairs={{1,0},{2,1},{3,2},{4,3},{5,4},{6,5},{7,6},{8,7},{9,8},{10,9},{11,1... | collective-permute-start | bytes 491528 | tf_op jit(solution)/shard_map/ppermute | solution.py:41
  138.4 2.1 %collective-permute-done.9 = f32[5,32,2,128]{3,1,2,0:T(8,128)S(1)} collective-permute-done((f32[5,32,2,128]{3,1,2,0:T(8,128)S(1)}, f32[5,32,2,128]{3,1,2,0:T(8,128)S(1)}, u32[]{:S(2)}, u32[]{:S(2)}) %collective-permute-start.9) | collective-permute-done | bytes 163872 | tf_op jit(solution)/shard_map/ppermute | solution.py:40
  141.0 1.3 collective-permute-done.11
  143.6 6.7 %collective-permute-start.12 = (f32[5,2,16,128]{3,1,2,0:T(2,128)S(1)}, f32[5,2,16,128]{3,1,2,0:T(2,128)S(1)}, u32[]{:S(2)}, u32[]{:S(2)}) collective-permute-start(f32[5,2,16,128]{3,1,2,0:T(2,128)S(1)} %get-tuple-element.9), channel_id=1, source_target_pairs={{0,16},{16,32},{32,48},{48,64},{64,80},{80,96},{96,112},{112,128},... | collective-permute-start | bytes 245768 | tf_op jit(solution)/shard_map/ppermute | solution.py:42
  150.4 1.9 %collective-permute-start.14 = (f32[5,2,16,128]{3,1,2,0:T(2,128)S(1)}, f32[5,2,16,128]{3,1,2,0:T(2,128)S(1)}, u32[]{:S(2)}, u32[]{:S(2)}) collective-permute-start(f32[5,2,16,128]{3,1,2,0:T(2,128)S(1)} %get-tuple-element.10), channel_id=1, source_target_pairs={{16,0},{32,16},{48,32},{64,48},{80,64},{96,80},{112,96},{128,112},... | collective-permute-start | bytes 245768 | tf_op jit(solution)/shard_map/ppermute | solution.py:43
  152.3 2.0 %fusion.39 = f32[5,28,12,128]{3,1,2,0:T(8,128)S(1)} fusion(f32[5,28,12,128]{3,1,2,0:T(8,128)S(1)} %slice.1776, f32[5,32,16,128]{3,1,2,0:T(8,128)S(1)} %maximum_add_fusion.2, f32[28,12,128]{2,0,1:T(8,128)S(1)} %copy.40, f32[5,28]{1,0:T(8,128)S(1)} %get-tuple-element.87, f32[5,28]{1,0:T(8,128)S(1)} %get-tuple-element.88), kind=kLoop, calls=%fused_computation.64 | loop fusion | flops 8386560 | bytes 8774752 | tf_op jit(solution)/shard_map/add | solution.py:31
  154.4 3.6 %collective-permute-start.15 = (f32[5,32,2,128]{3,1,2,0:T(8,128)S(1)}, f32[5,32,2,128]{3,1,2,0:T(8,128)S(1)}, u32[]{:S(2)}, u32[]{:S(2)}) collective-permute-start(f32[5,32,2,128]{3,1,2,0:T(8,128)S(1)} %get-tuple-element.11), channel_id=1, source_target_pairs={{1,0},{2,1},{3,2},{4,3},{5,4},{6,5},{7,6},{8,7},{9,8},{10,9},{11,1... | collective-permute-start | bytes 491528 | tf_op jit(solution)/shard_map/ppermute | solution.py:41
  159.1 1.7 %collective-permute-done.13 = f32[5,32,2,128]{3,1,2,0:T(8,128)S(1)} collective-permute-done((f32[5,32,2,128]{3,1,2,0:T(8,128)S(1)}, f32[5,32,2,128]{3,1,2,0:T(8,128)S(1)}, u32[]{:S(2)}, u32[]{:S(2)}) %collective-permute-start.13) | collective-permute-done | bytes 163872 | tf_op jit(solution)/shard_map/ppermute | solution.py:40
  161.8 0.7 fusion.1
  162.5 1.8 %copy.99 = f32[5,32,16,128]{3,2,1,0:T(8,128)} copy(f32[5,32,16,128]{3,1,2,0:T(8,128)S(1)} %fusion.1) | data formatting | bytes 2621440 | tf_op jit(solution)/shard_map/mul | solution.py:72
  (97 shorter events, 13.8 us)
Async XLA Ops:
  1.7 15.1 %copy-start.1 = (f32[32,16,128]{2,1,0:T(8,128)S(1)}, f32[32,16,128]{2,1,0:T(8,128)}, u32[]{:S(2)}) copy-start(f32[32,16,128]{2,1,0:T(8,128)} %param.6) | copy-start | bytes 786436
  1.8 20.8 %collective-permute-start.1 = (f32[5,32,2,128]{3,1,2,0:T(8,128)S(1)}, f32[5,32,2,128]{3,1,2,0:T(8,128)S(1)}, u32[]{:S(2)}, u32[]{:S(2)}) collective-permute-start(f32[5,32,2,128]{3,1,2,0:T(8,128)S(1)} %get-tuple-element.38), channel_id=1, source_target_pairs={{0,1},{1,2},{2,3},{3,4},{4,5},{5,6},{6,7},{7,8},{8,9},{9,10},{10,1... | collective-permute-start | bytes 491528 | tf_op jit(solution)/shard_map/ppermute | solution.py:40
  4.0 18.6 %collective-permute-start.3 = (f32[5,32,2,128]{3,1,2,0:T(8,128)S(1)}, f32[5,32,2,128]{3,1,2,0:T(8,128)S(1)}, u32[]{:S(2)}, u32[]{:S(2)}) collective-permute-start(f32[5,32,2,128]{3,1,2,0:T(8,128)S(1)} %get-tuple-element.37), channel_id=1, source_target_pairs={{1,0},{2,1},{3,2},{4,3},{5,4},{6,5},{7,6},{8,7},{9,8},{10,9},{11,1... | collective-permute-start | bytes 491528 | tf_op jit(solution)/shard_map/ppermute | solution.py:41
  9.4 10.4 %collective-permute-start = (f32[5,2,16,128]{3,1,2,0:T(2,128)S(1)}, f32[5,2,16,128]{3,1,2,0:T(2,128)S(1)}, u32[]{:S(2)}, u32[]{:S(2)}) collective-permute-start(f32[5,2,16,128]{3,1,2,0:T(2,128)S(1)} %get-tuple-element.35), channel_id=1, source_target_pairs={{0,16},{16,32},{32,48},{48,64},{64,80},{80,96},{96,112},{112,128},... | collective-permute-start | bytes 245768 | tf_op jit(solution)/shard_map/ppermute | solution.py:42
  14.8 7.3 %collective-permute-start.2 = (f32[5,2,16,128]{3,1,2,0:T(2,128)S(1)}, f32[5,2,16,128]{3,1,2,0:T(2,128)S(1)}, u32[]{:S(2)}, u32[]{:S(2)}) collective-permute-start(f32[5,2,16,128]{3,1,2,0:T(2,128)S(1)} %get-tuple-element.36), channel_id=1, source_target_pairs={{16,0},{32,16},{48,32},{64,48},{80,64},{96,80},{112,96},{128,112},... | collective-permute-start | bytes 245768 | tf_op jit(solution)/shard_map/ppermute | solution.py:43
  16.8 0.7 copy-start.2
  16.8 0.7 copy-start.3
  23.2 1.3 copy-start
  25.4 11.1 %collective-permute-start.4 = (f32[5,2,16,128]{3,1,2,0:T(2,128)S(1)}, f32[5,2,16,128]{3,1,2,0:T(2,128)S(1)}, u32[]{:S(2)}, u32[]{:S(2)}) collective-permute-start(f32[5,2,16,128]{3,1,2,0:T(2,128)S(1)} %get-tuple-element.27), channel_id=1, source_target_pairs={{0,16},{16,32},{32,48},{48,64},{64,80},{80,96},{96,112},{112,128},... | collective-permute-start | bytes 245768 | tf_op jit(solution)/shard_map/ppermute | solution.py:42
  28.9 11.1 %collective-permute-start.6 = (f32[5,2,16,128]{3,1,2,0:T(2,128)S(1)}, f32[5,2,16,128]{3,1,2,0:T(2,128)S(1)}, u32[]{:S(2)}, u32[]{:S(2)}) collective-permute-start(f32[5,2,16,128]{3,1,2,0:T(2,128)S(1)} %get-tuple-element.28), channel_id=1, source_target_pairs={{16,0},{32,16},{48,32},{64,48},{80,64},{96,80},{112,96},{128,112},... | collective-permute-start | bytes 245768 | tf_op jit(solution)/shard_map/ppermute | solution.py:43
  32.9 7.7 %collective-permute-start.5 = (f32[5,32,2,128]{3,1,2,0:T(8,128)S(1)}, f32[5,32,2,128]{3,1,2,0:T(8,128)S(1)}, u32[]{:S(2)}, u32[]{:S(2)}) collective-permute-start(f32[5,32,2,128]{3,1,2,0:T(8,128)S(1)} %get-tuple-element.30), channel_id=1, source_target_pairs={{0,1},{1,2},{2,3},{3,4},{4,5},{5,6},{6,7},{7,8},{8,9},{9,10},{10,1... | collective-permute-start | bytes 491528 | tf_op jit(solution)/shard_map/ppermute | solution.py:40
  32.9 8.5 %collective-permute-start.7 = (f32[5,32,2,128]{3,1,2,0:T(8,128)S(1)}, f32[5,32,2,128]{3,1,2,0:T(8,128)S(1)}, u32[]{:S(2)}, u32[]{:S(2)}) collective-permute-start(f32[5,32,2,128]{3,1,2,0:T(8,128)S(1)} %get-tuple-element.29), channel_id=1, source_target_pairs={{1,0},{2,1},{3,2},{4,3},{5,4},{6,5},{7,6},{8,7},{9,8},{10,9},{11,1... | collective-permute-start | bytes 491528 | tf_op jit(solution)/shard_map/ppermute | solution.py:41
  44.4 6.6 %copy-start.4 = (s32[32]{0:T(128)S(1)}, s32[32]{0:T(128)}, u32[]{:S(2)}) copy-start(s32[32]{0:T(128)} %param.9) | copy-start | bytes 388
  44.4 37.3 %all-to-all-start = ((f32[5,32,16,128]{3,2,0,1:T(8,128)}), f32[5,32,16,128]{3,2,0,1:T(8,128)S(1)}, u32[]{:S(2)}, u32[]{:S(2)}) async-start(f32[5,32,16,128]{3,2,0,1:T(8,128)} %copy.56), calls=%async_computation | async-start | bytes 2621440 | tf_op jit(solution)/shard_map/all_to_all | solution.py:79
  124.1 13.3 %collective-permute-start.8 = (f32[5,2,16,128]{3,1,2,0:T(2,128)S(1)}, f32[5,2,16,128]{3,1,2,0:T(2,128)S(1)}, u32[]{:S(2)}, u32[]{:S(2)}) collective-permute-start(f32[5,2,16,128]{3,1,2,0:T(2,128)S(1)} %get-tuple-element.17), channel_id=1, source_target_pairs={{0,16},{16,32},{32,48},{48,64},{64,80},{80,96},{96,112},{112,128},... | collective-permute-start | bytes 245768 | tf_op jit(solution)/shard_map/ppermute | solution.py:42
  129.7 8.2 %collective-permute-start.10 = (f32[5,2,16,128]{3,1,2,0:T(2,128)S(1)}, f32[5,2,16,128]{3,1,2,0:T(2,128)S(1)}, u32[]{:S(2)}, u32[]{:S(2)}) collective-permute-start(f32[5,2,16,128]{3,1,2,0:T(2,128)S(1)} %get-tuple-element.18), channel_id=1, source_target_pairs={{16,0},{32,16},{48,32},{64,48},{80,64},{96,80},{112,96},{128,112},... | collective-permute-start | bytes 245768 | tf_op jit(solution)/shard_map/ppermute | solution.py:43
  133.7 6.8 %collective-permute-start.9 = (f32[5,32,2,128]{3,1,2,0:T(8,128)S(1)}, f32[5,32,2,128]{3,1,2,0:T(8,128)S(1)}, u32[]{:S(2)}, u32[]{:S(2)}) collective-permute-start(f32[5,32,2,128]{3,1,2,0:T(8,128)S(1)} %get-tuple-element.20), channel_id=1, source_target_pairs={{0,1},{1,2},{2,3},{3,4},{4,5},{5,6},{6,7},{7,8},{8,9},{9,10},{10,1... | collective-permute-start | bytes 491528 | tf_op jit(solution)/shard_map/ppermute | solution.py:40
  133.8 8.5 %collective-permute-start.11 = (f32[5,32,2,128]{3,1,2,0:T(8,128)S(1)}, f32[5,32,2,128]{3,1,2,0:T(8,128)S(1)}, u32[]{:S(2)}, u32[]{:S(2)}) collective-permute-start(f32[5,32,2,128]{3,1,2,0:T(8,128)S(1)} %get-tuple-element.19), channel_id=1, source_target_pairs={{1,0},{2,1},{3,2},{4,3},{5,4},{6,5},{7,6},{8,7},{9,8},{10,9},{11,1... | collective-permute-start | bytes 491528 | tf_op jit(solution)/shard_map/ppermute | solution.py:41
  143.6 14.4 %collective-permute-start.12 = (f32[5,2,16,128]{3,1,2,0:T(2,128)S(1)}, f32[5,2,16,128]{3,1,2,0:T(2,128)S(1)}, u32[]{:S(2)}, u32[]{:S(2)}) collective-permute-start(f32[5,2,16,128]{3,1,2,0:T(2,128)S(1)} %get-tuple-element.9), channel_id=1, source_target_pairs={{0,16},{16,32},{32,48},{48,64},{64,80},{80,96},{96,112},{112,128},... | collective-permute-start | bytes 245768 | tf_op jit(solution)/shard_map/ppermute | solution.py:42
  150.4 8.2 %collective-permute-start.14 = (f32[5,2,16,128]{3,1,2,0:T(2,128)S(1)}, f32[5,2,16,128]{3,1,2,0:T(2,128)S(1)}, u32[]{:S(2)}, u32[]{:S(2)}) collective-permute-start(f32[5,2,16,128]{3,1,2,0:T(2,128)S(1)} %get-tuple-element.10), channel_id=1, source_target_pairs={{16,0},{32,16},{48,32},{64,48},{80,64},{96,80},{112,96},{128,112},... | collective-permute-start | bytes 245768 | tf_op jit(solution)/shard_map/ppermute | solution.py:43
  154.3 6.5 %collective-permute-start.13 = (f32[5,32,2,128]{3,1,2,0:T(8,128)S(1)}, f32[5,32,2,128]{3,1,2,0:T(8,128)S(1)}, u32[]{:S(2)}, u32[]{:S(2)}) collective-permute-start(f32[5,32,2,128]{3,1,2,0:T(8,128)S(1)} %get-tuple-element.12), channel_id=1, source_target_pairs={{0,1},{1,2},{2,3},{3,4},{4,5},{5,6},{6,7},{7,8},{8,9},{9,10},{10,1... | collective-permute-start | bytes 491528 | tf_op jit(solution)/shard_map/ppermute | solution.py:40
  154.4 6.9 %collective-permute-start.15 = (f32[5,32,2,128]{3,1,2,0:T(8,128)S(1)}, f32[5,32,2,128]{3,1,2,0:T(8,128)S(1)}, u32[]{:S(2)}, u32[]{:S(2)}) collective-permute-start(f32[5,32,2,128]{3,1,2,0:T(8,128)S(1)} %get-tuple-element.11), channel_id=1, source_target_pairs={{1,0},{2,1},{3,2},{4,3},{5,4},{6,5},{7,6},{8,7},{9,8},{10,9},{11,1... | collective-permute-start | bytes 491528 | tf_op jit(solution)/shard_map/ppermute | solution.py:41

commit v13 on v11

--- a/solution.py
+++ b/solution.py
@@ -34,13 +34,14 @@
     )
 
 
-def split_stencil(cells, kap, speed_r, speed_p, width=2, core=False):
+def split_stencil(cells, kap, speed_r, speed_p, width=2, core=False, source=None):
     sectors, rings = lax.axis_size("azi"), lax.axis_size("rad")
     rows, cols = cells.shape[-3], cells.shape[-2]
-    left = lax.ppermute(cells[..., cols - width :, :], "azi", [(i, (i + 1) % sectors) for i in range(sectors)])
-    right = lax.ppermute(cells[..., :width, :], "azi", [((i + 1) % sectors, i) for i in range(sectors)])
-    above = lax.ppermute(cells[..., rows - width :, :, :], "rad", [(i, i + 1) for i in range(rings - 1)])
-    below = lax.ppermute(cells[..., :width, :, :], "rad", [(i + 1, i) for i in range(rings - 1)])
+    sent = cells if source is None else source
+    left = lax.ppermute(sent[..., cols - width :, :], "azi", [(i, (i + 1) % sectors) for i in range(sectors)])
+    right = lax.ppermute(sent[..., :width, :], "azi", [((i + 1) % sectors, i) for i in range(sectors)])
+    above = lax.ppermute(sent[..., rows - width :, :, :], "rad", [(i, i + 1) for i in range(rings - 1)])
+    below = lax.ppermute(sent[..., :width, :, :], "rad", [(i + 1, i) for i in range(rings - 1)])
     tall = jnp.concatenate([above, cells, below], axis=1)
     inner = kap[:, width : cols - width]
     if core:
@@ -68,7 +69,8 @@
 
 
 def heun_sections(field, kappa, speed_r, speed_p, core=False):
-    first = field + split_stencil(field, kappa, speed_r, speed_p, core=core)
+    source = lax.optimization_barrier(field) if core else None
+    first = field + split_stencil(field, kappa, speed_r, speed_p, core=core, source=source)
     return 0.5 * (field + first + split_stencil(first, kappa, speed_r, speed_p))
 
 

time: 164 us -> 166 us (1.012)
  the two profiles are of different devices: /device:TPU:1 before, /device:TPU:3 now
where the time goes in v13:
time: 166 us
  starting transfers between devices  52.2 us (31%)
  waiting for transfers between devices  42.4 us (26%)
  blocking collectives  37.5 us (23%)
  other arithmetic  17.2 us (10%)
  local copies, waits for them, and re-layouts  12.1 us (7%)
  between operations  4.38 us (3%)
    all_to_all x1, blocking collectives, shift_rows(): return lax.all_to_all(moved, 'azi', 2, 1, tiled=True)  37.5 us
    all_to_all x1, waiting for transfers between devices, shift_rows(): full = lax.all_to_all(half, 'azi', 1, 2, tiled=True)  29.1 us
    ppermute x4, starting transfers between devices, split_stencil(): lax.ppermute(sent[..., rows - width:, :, :], 'rad', [(i, i + 1) for i in...  21.8 us
    ppermute x4, starting transfers between devices, split_stencil(): lax.ppermute(sent[..., :width, :], 'azi', [((i + 1) % sectors, i) for i i...  16.4 us
    add x14, other arithmetic, stencil(): -speed_r[:, :, None, None] * first_r - speed_p[:, :, None, None] * first_p  13.5 us
    ppermute x4, waiting for transfers between devices, split_stencil(): lax.ppermute(sent[..., :width, :, :], 'rad', [(i + 1, i) for i in range(r...  13.3 us
    ppermute x4, starting transfers between devices, split_stencil(): lax.ppermute(sent[..., :width, :, :], 'rad', [(i + 1, i) for i in range(r...  7.68 us
    all_to_all x1, starting transfers between devices, shift_rows(): full = lax.all_to_all(half, 'azi', 1, 2, tiled=True)  5.32 us
  transfers between devices with their start and end apart: 17, of which 4 were waited for; matrix products, arithmetic and copies ran while one was open for 9% of the time, Pallas kernels for 0%

profile of v13, /device:TPU:3, one launch (start us, length us, event | category | flops | bytes accessed | tf_op | source)
XLA Modules:
  0.0 165.9 jit_solution(14570277144311683638)
XLA Ops:
  0.0 1.0 fusion.155
  1.1 5.4 %collective-permute-start = (f32[5,2,16,128]{3,1,2,0:T(2,128)S(1)}, f32[5,2,16,128]{3,1,2,0:T(2,128)S(1)}, u32[]{:S(2)}, u32[]{:S(2)}) collective-permute-start(f32[5,2,16,128]{3,1,2,0:T(2,128)S(1)} %copy.86), channel_id=1, source_target_pairs={{0,16},{16,32},{32,48},{48,64},{64,80},{80,96},{96,112},{112,128},... | collective-permute-start | bytes 245768 | tf_op jit(solution)/shard_map/ppermute | solution.py:43
  6.5 1.9 %collective-permute-start.2 = (f32[5,2,16,128]{3,1,2,0:T(2,128)S(1)}, f32[5,2,16,128]{3,1,2,0:T(2,128)S(1)}, u32[]{:S(2)}, u32[]{:S(2)}) collective-permute-start(f32[5,2,16,128]{3,1,2,0:T(2,128)S(1)} %copy.88), channel_id=1, source_target_pairs={{16,0},{32,16},{48,32},{64,48},{80,64},{96,80},{112,96},{128,112},... | collective-permute-start | bytes 245768 | tf_op jit(solution)/shard_map/ppermute | solution.py:44
  8.5 1.4 fusion.154
  10.4 5.4 %collective-permute-start.3 = (f32[5,32,2,128]{3,1,2,0:T(8,128)S(1)}, f32[5,32,2,128]{3,1,2,0:T(8,128)S(1)}, u32[]{:S(2)}, u32[]{:S(2)}) collective-permute-start(f32[5,32,2,128]{3,1,2,0:T(8,128)S(1)} %copy.89), channel_id=1, source_target_pairs={{1,0},{2,1},{3,2},{4,3},{5,4},{6,5},{7,6},{8,7},{9,8},{10,9},{11,1... | collective-permute-start | bytes 491528 | tf_op jit(solution)/shard_map/ppermute | solution.py:42
  17.4 2.0 %fusion.14 = f32[5,28,12,128]{3,1,2,0:T(8,128)S(1)} fusion(f32[5,28,12,128]{3,1,2,0:T(8,128)S(1)} %slice.1153, f32[5,32,16,128]{3,1,2,0:T(8,128)S(1)} %copy.57, f32[28,12,128]{2,0,1:T(8,128)S(1)} %copy.40, f32[5,28]{1,0:T(8,128)S(1)} %get-tuple-element.83, f32[5,28]{1,0:T(8,128)S(1)} %get-tuple-element.84), kind=kLoop, calls=%fused_computation.49 | loop fusion | flops 8386560 | bytes 8774752 | tf_op jit(solution)/shard_map/add | solution.py:31
  20.8 1.2 copy-done.1
  22.8 0.6 maximum_add_fusion
  23.5 6.0 %collective-permute-start.4 = (f32[5,2,16,128]{3,1,2,0:T(2,128)S(1)}, f32[5,2,16,128]{3,1,2,0:T(2,128)S(1)}, u32[]{:S(2)}, u32[]{:S(2)}) collective-permute-start(f32[5,2,16,128]{3,1,2,0:T(2,128)S(1)} %get-tuple-element.23), channel_id=1, source_target_pairs={{0,16},{16,32},{32,48},{48,64},{64,80},{80,96},{96,112},{112,128},... | collective-permute-start | bytes 245768 | tf_op jit(solution)/shard_map/ppermute | solution.py:43
  29.8 1.9 %collective-permute-start.6 = (f32[5,2,16,128]{3,1,2,0:T(2,128)S(1)}, f32[5,2,16,128]{3,1,2,0:T(2,128)S(1)}, u32[]{:S(2)}, u32[]{:S(2)}) collective-permute-start(f32[5,2,16,128]{3,1,2,0:T(2,128)S(1)} %get-tuple-element.24), channel_id=1, source_target_pairs={{16,0},{32,16},{48,32},{64,48},{80,64},{96,80},{112,96},{128,112},... | collective-permute-start | bytes 245768 | tf_op jit(solution)/shard_map/ppermute | solution.py:44
  31.7 3.8 %collective-permute-start.7 = (f32[5,32,2,128]{3,1,2,0:T(8,128)S(1)}, f32[5,32,2,128]{3,1,2,0:T(8,128)S(1)}, u32[]{:S(2)}, u32[]{:S(2)}) collective-permute-start(f32[5,32,2,128]{3,1,2,0:T(8,128)S(1)} %get-tuple-element.25), channel_id=1, source_target_pairs={{1,0},{2,1},{3,2},{4,3},{5,4},{6,5},{7,6},{8,7},{9,8},{10,9},{11,1... | collective-permute-start | bytes 491528 | tf_op jit(solution)/shard_map/ppermute | solution.py:42
  35.5 4.6 %collective-permute-done.6 = f32[5,2,16,128]{3,1,2,0:T(2,128)S(1)} collective-permute-done((f32[5,2,16,128]{3,1,2,0:T(2,128)S(1)}, f32[5,2,16,128]{3,1,2,0:T(2,128)S(1)}, u32[]{:S(2)}, u32[]{:S(2)}) %collective-permute-start.6) | collective-permute-done | bytes 81952 | tf_op jit(solution)/shard_map/ppermute | solution.py:44
  40.2 2.7 %fusion.24 = f32[5,32,12,128]{3,1,2,0:T(8,128)S(1)} fusion(f32[5,32,12,128]{3,1,2,0:T(8,128)S(1)} %slice.1194, f32[5,32,16,128]{3,1,2,0:T(8,128)S(1)} %maximum_add_fusion, f32[5,2,16,128]{3,1,2,0:T(2,128)S(1)} %collective-permute-done.6, f32[5,2,16,128]{3,1,2,0:T(2,128)S(1)} %collective-permute-done.4, f32[32,12,128]{2,0,1:T(8,128)S(1)} %copy.58, ...), kind=kLoop, calls=%fused_computation.59 | loop fusion | flops 10567680 | bytes 7577600 | tf_op jit(solution)/shard_map/add | solution.py:31
  43.9 0.6 fusion
  44.5 1.8 %copy.59 = f32[5,32,16,128]{3,2,0,1:T(8,128)} copy(f32[5,32,16,128]{3,1,2,0:T(8,128)S(1)} %fusion) | data formatting | bytes 2621440 | tf_op jit(solution)/shard_map/mul | solution.py:74
  46.3 5.3 %all-to-all-start = ((f32[5,32,16,128]{3,2,0,1:T(8,128)}), f32[5,32,16,128]{3,2,0,1:T(8,128)S(1)}, u32[]{:S(2)}, u32[]{:S(2)}) async-start(f32[5,32,16,128]{3,2,0,1:T(8,128)} %copy.59), calls=%async_computation | async-start | bytes 2621440 | tf_op jit(solution)/shard_map/all_to_all | solution.py:81
  51.8 0.6 fusion.164
  56.0 29.1 %all-to-all-done = f32[5,32,16,128]{3,2,0,1:T(8,128)S(1)} async-done(((f32[5,32,16,128]{3,2,0,1:T(8,128)}), f32[5,32,16,128]{3,2,0,1:T(8,128)S(1)}, u32[]{:S(2)}, u32[]{:S(2)}) %all-to-all-start) | async-done | bytes 1310752 | tf_op jit(solution)/shard_map/all_to_all | solution.py:81
  85.8 1.0 copy.62
  86.8 37.5 %all_to_all.36 = f32[5,2,256,128]{3,1,0,2:T(2,128)S(1)} all-to-all(f32[5,2,256,128]{3,1,0,2:T(2,128)S(1)} %copy.62), channel_id=1, replica_groups=mesh['rad'=16,'azi'=16] {'azi'}, dimensions={2} | all-to-all | bytes 2621440 | tf_op jit(solution)/shard_map/all_to_all | solution.py:91
  125.1 6.6 %collective-permute-start.8 = (f32[5,2,16,128]{3,1,2,0:T(2,128)S(1)}, f32[5,2,16,128]{3,1,2,0:T(2,128)S(1)}, u32[]{:S(2)}, u32[]{:S(2)}) collective-permute-start(f32[5,2,16,128]{3,1,2,0:T(2,128)S(1)} %get-tuple-element.15), channel_id=1, source_target_pairs={{0,16},{16,32},{32,48},{48,64},{64,80},{80,96},{96,112},{112,128},... | collective-permute-start | bytes 245768 | tf_op jit(solution)/shard_map/ppermute | solution.py:43
  131.9 1.9 %collective-permute-start.10 = (f32[5,2,16,128]{3,1,2,0:T(2,128)S(1)}, f32[5,2,16,128]{3,1,2,0:T(2,128)S(1)}, u32[]{:S(2)}, u32[]{:S(2)}) collective-permute-start(f32[5,2,16,128]{3,1,2,0:T(2,128)S(1)} %get-tuple-element.16), channel_id=1, source_target_pairs={{16,0},{32,16},{48,32},{64,48},{80,64},{96,80},{112,96},{128,112},... | collective-permute-start | bytes 245768 | tf_op jit(solution)/shard_map/ppermute | solution.py:44
  133.9 3.6 %collective-permute-start.11 = (f32[5,32,2,128]{3,1,2,0:T(8,128)S(1)}, f32[5,32,2,128]{3,1,2,0:T(8,128)S(1)}, u32[]{:S(2)}, u32[]{:S(2)}) collective-permute-start(f32[5,32,2,128]{3,1,2,0:T(8,128)S(1)} %get-tuple-element.17), channel_id=1, source_target_pairs={{1,0},{2,1},{3,2},{4,3},{5,4},{6,5},{7,6},{8,7},{9,8},{10,9},{11,1... | collective-permute-start | bytes 491528 | tf_op jit(solution)/shard_map/ppermute | solution.py:42
  137.5 3.5 %collective-permute-done.10 = f32[5,2,16,128]{3,1,2,0:T(2,128)S(1)} collective-permute-done((f32[5,2,16,128]{3,1,2,0:T(2,128)S(1)}, f32[5,2,16,128]{3,1,2,0:T(2,128)S(1)}, u32[]{:S(2)}, u32[]{:S(2)}) %collective-permute-start.10) | collective-permute-done | bytes 81952 | tf_op jit(solution)/shard_map/ppermute | solution.py:44
  141.0 2.0 %fusion.34 = f32[5,32,12,128]{3,1,2,0:T(8,128)S(1)} fusion(f32[5,32,12,128]{3,1,2,0:T(8,128)S(1)} %slice.1227, f32[5,32,16,128]{3,1,2,0:T(8,128)S(1)} %get-tuple-element.14, f32[5,34,16,128]{3,1,2,0:T(8,128)S(1)} %constant_dynamic-update-slice_fusion, f32[5,2,16,128]{3,1,2,0:T(2,128)S(1)} %collective-permute-done.8, f32[32,12,128]{2,0,1:T(8,128)S(1)} %copy.58, ...), kind=kLoop, calls=%fused_computation.69 | loop fusion | flops 10076160 | bytes 9461760 | tf_op jit(solution)/shard_map/add | solution.py:31
  144.6 3.9 %collective-permute-start.12 = (f32[5,2,16,128]{3,1,2,0:T(2,128)S(1)}, f32[5,2,16,128]{3,1,2,0:T(2,128)S(1)}, u32[]{:S(2)}, u32[]{:S(2)}) collective-permute-start(f32[5,2,16,128]{3,1,2,0:T(2,128)S(1)} %get-tuple-element.7), channel_id=1, source_target_pairs={{0,16},{16,32},{32,48},{48,64},{64,80},{80,96},{96,112},{112,128},... | collective-permute-start | bytes 245768 | tf_op jit(solution)/shard_map/ppermute | solution.py:43
  148.9 1.9 %collective-permute-start.14 = (f32[5,2,16,128]{3,1,2,0:T(2,128)S(1)}, f32[5,2,16,128]{3,1,2,0:T(2,128)S(1)}, u32[]{:S(2)}, u32[]{:S(2)}) collective-permute-start(f32[5,2,16,128]{3,1,2,0:T(2,128)S(1)} %get-tuple-element.8), channel_id=1, source_target_pairs={{16,0},{32,16},{48,32},{64,48},{80,64},{96,80},{112,96},{128,112},... | collective-permute-start | bytes 245768 | tf_op jit(solution)/shard_map/ppermute | solution.py:44
  150.9 3.6 %collective-permute-start.15 = (f32[5,32,2,128]{3,1,2,0:T(8,128)S(1)}, f32[5,32,2,128]{3,1,2,0:T(8,128)S(1)}, u32[]{:S(2)}, u32[]{:S(2)}) collective-permute-start(f32[5,32,2,128]{3,1,2,0:T(8,128)S(1)} %get-tuple-element.9), channel_id=1, source_target_pairs={{1,0},{2,1},{3,2},{4,3},{5,4},{6,5},{7,6},{8,7},{9,8},{10,9},{11,1... | collective-permute-start | bytes 491528 | tf_op jit(solution)/shard_map/ppermute | solution.py:42
  154.5 5.2 %collective-permute-done.14 = f32[5,2,16,128]{3,1,2,0:T(2,128)S(1)} collective-permute-done((f32[5,2,16,128]{3,1,2,0:T(2,128)S(1)}, f32[5,2,16,128]{3,1,2,0:T(2,128)S(1)}, u32[]{:S(2)}, u32[]{:S(2)}) %collective-permute-start.14) | collective-permute-done | bytes 81952 | tf_op jit(solution)/shard_map/ppermute | solution.py:44
  159.7 2.7 %fusion.44 = f32[5,32,12,128]{3,1,2,0:T(8,128)S(1)} fusion(f32[5,32,12,128]{3,1,2,0:T(8,128)S(1)} %slice.1258, f32[5,32,16,128]{3,1,2,0:T(8,128)S(1)} %maximum_add_fusion.2, f32[5,2,16,128]{3,1,2,0:T(2,128)S(1)} %collective-permute-done.14, f32[5,2,16,128]{3,1,2,0:T(2,128)S(1)} %collective-permute-done.12, f32[32,12,128]{2,0,1:T(8,128)S(1)} %copy.58, ...), kind=kLoop, calls=%fused_computation.79 | loop fusion | flops 10567680 | bytes 7577600 | tf_op jit(solution)/shard_map/add | solution.py:31
  163.4 0.6 fusion.1
  164.1 1.8 %copy.84 = f32[5,32,16,128]{3,2,1,0:T(8,128)} copy(f32[5,32,16,128]{3,1,2,0:T(8,128)S(1)} %fusion.1) | data formatting | bytes 2621440 | tf_op jit(solution)/shard_map/mul | solution.py:74
  (102 shorter events, 10.1 us)
Async XLA Ops:
  0.0 15.8 %copy-start.2 = (f32[5,32,16,128]{3,2,1,0:T(8,128)S(1)}, f32[5,32,16,128]{3,2,1,0:T(8,128)}, u32[]{:S(2)}) copy-start(f32[5,32,16,128]{3,2,1,0:T(8,128)} %param.5) | copy-start | bytes 3932164
  1.1 18.4 %collective-permute-start = (f32[5,2,16,128]{3,1,2,0:T(2,128)S(1)}, f32[5,2,16,128]{3,1,2,0:T(2,128)S(1)}, u32[]{:S(2)}, u32[]{:S(2)}) collective-permute-start(f32[5,2,16,128]{3,1,2,0:T(2,128)S(1)} %copy.86), channel_id=1, source_target_pairs={{0,16},{16,32},{32,48},{48,64},{64,80},{80,96},{96,112},{112,128},... | collective-permute-start | bytes 245768 | tf_op jit(solution)/shard_map/ppermute | solution.py:43
  6.5 13.5 %collective-permute-start.2 = (f32[5,2,16,128]{3,1,2,0:T(2,128)S(1)}, f32[5,2,16,128]{3,1,2,0:T(2,128)S(1)}, u32[]{:S(2)}, u32[]{:S(2)}) collective-permute-start(f32[5,2,16,128]{3,1,2,0:T(2,128)S(1)} %copy.88), channel_id=1, source_target_pairs={{16,0},{32,16},{48,32},{64,48},{80,64},{96,80},{112,96},{128,112},... | collective-permute-start | bytes 245768 | tf_op jit(solution)/shard_map/ppermute | solution.py:44
  9.9 10.7 %collective-permute-start.1 = (f32[5,32,2,128]{3,1,2,0:T(8,128)S(1)}, f32[5,32,2,128]{3,1,2,0:T(8,128)S(1)}, u32[]{:S(2)}, u32[]{:S(2)}) collective-permute-start(f32[5,32,2,128]{3,1,2,0:T(8,128)S(1)} %copy.87), channel_id=1, source_target_pairs={{0,1},{1,2},{2,3},{3,4},{4,5},{5,6},{6,7},{7,8},{8,9},{9,10},{10,1... | collective-permute-start | bytes 491528 | tf_op jit(solution)/shard_map/ppermute | solution.py:41
  10.4 5.8 %copy-start.3 = (f32[32,16,128]{2,1,0:T(8,128)S(1)}, f32[32,16,128]{2,1,0:T(8,128)}, u32[]{:S(2)}) copy-start(f32[32,16,128]{2,1,0:T(8,128)} %param.6) | copy-start | bytes 786436
  10.4 10.3 %collective-permute-start.3 = (f32[5,32,2,128]{3,1,2,0:T(8,128)S(1)}, f32[5,32,2,128]{3,1,2,0:T(8,128)S(1)}, u32[]{:S(2)}, u32[]{:S(2)}) collective-permute-start(f32[5,32,2,128]{3,1,2,0:T(8,128)S(1)} %copy.89), channel_id=1, source_target_pairs={{1,0},{2,1},{3,2},{4,3},{5,4},{6,5},{7,6},{8,7},{9,8},{10,9},{11,1... | collective-permute-start | bytes 491528 | tf_op jit(solution)/shard_map/ppermute | solution.py:42
  16.2 3.9 %copy-start = (f32[5,32,16,128]{3,1,2,0:T(8,128)}, f32[5,32,16,128]{3,1,2,0:T(8,128)S(1)}, u32[]{:S(2)}) copy-start(f32[5,32,16,128]{3,1,2,0:T(8,128)S(1)} %copy.57) | copy-start | bytes 3932164
  16.3 0.7 copy-start.4
  16.3 0.8 copy-start.5
  20.7 1.3 copy-start.1
  20.7 1.3 slice-start
  23.5 12.0 %collective-permute-start.4 = (f32[5,2,16,128]{3,1,2,0:T(2,128)S(1)}, f32[5,2,16,128]{3,1,2,0:T(2,128)S(1)}, u32[]{:S(2)}, u32[]{:S(2)}) collective-permute-start(f32[5,2,16,128]{3,1,2,0:T(2,128)S(1)} %get-tuple-element.23), channel_id=1, source_target_pairs={{0,16},{16,32},{32,48},{48,64},{64,80},{80,96},{96,112},{112,128},... | collective-permute-start | bytes 245768 | tf_op jit(solution)/shard_map/ppermute | solution.py:43
  29.7 13.2 %collective-permute-start.5 = (f32[5,32,2,128]{3,1,2,0:T(8,128)S(1)}, f32[5,32,2,128]{3,1,2,0:T(8,128)S(1)}, u32[]{:S(2)}, u32[]{:S(2)}) collective-permute-start(f32[5,32,2,128]{3,1,2,0:T(8,128)S(1)} %get-tuple-element.26), channel_id=1, source_target_pairs={{0,1},{1,2},{2,3},{3,4},{4,5},{5,6},{6,7},{7,8},{8,9},{9,10},{10,1... | collective-permute-start | bytes 491528 | tf_op jit(solution)/shard_map/ppermute | solution.py:41
  29.8 10.4 %collective-permute-start.6 = (f32[5,2,16,128]{3,1,2,0:T(2,128)S(1)}, f32[5,2,16,128]{3,1,2,0:T(2,128)S(1)}, u32[]{:S(2)}, u32[]{:S(2)}) collective-permute-start(f32[5,2,16,128]{3,1,2,0:T(2,128)S(1)} %get-tuple-element.24), channel_id=1, source_target_pairs={{16,0},{32,16},{48,32},{64,48},{80,64},{96,80},{112,96},{128,112},... | collective-permute-start | bytes 245768 | tf_op jit(solution)/shard_map/ppermute | solution.py:44
  31.7 11.7 %collective-permute-start.7 = (f32[5,32,2,128]{3,1,2,0:T(8,128)S(1)}, f32[5,32,2,128]{3,1,2,0:T(8,128)S(1)}, u32[]{:S(2)}, u32[]{:S(2)}) collective-permute-start(f32[5,32,2,128]{3,1,2,0:T(8,128)S(1)} %get-tuple-element.25), channel_id=1, source_target_pairs={{1,0},{2,1},{3,2},{4,3},{5,4},{6,5},{7,6},{8,7},{9,8},{10,9},{11,1... | collective-permute-start | bytes 491528 | tf_op jit(solution)/shard_map/ppermute | solution.py:42
  46.3 5.3 %copy-start.6 = (s32[32]{0:T(128)S(1)}, s32[32]{0:T(128)}, u32[]{:S(2)}) copy-start(s32[32]{0:T(128)} %param.9) | copy-start | bytes 388
  46.3 38.7 %all-to-all-start = ((f32[5,32,16,128]{3,2,0,1:T(8,128)}), f32[5,32,16,128]{3,2,0,1:T(8,128)S(1)}, u32[]{:S(2)}, u32[]{:S(2)}) async-start(f32[5,32,16,128]{3,2,0,1:T(8,128)} %copy.59), calls=%async_computation | async-start | bytes 2621440 | tf_op jit(solution)/shard_map/all_to_all | solution.py:81
  125.1 12.3 %collective-permute-start.8 = (f32[5,2,16,128]{3,1,2,0:T(2,128)S(1)}, f32[5,2,16,128]{3,1,2,0:T(2,128)S(1)}, u32[]{:S(2)}, u32[]{:S(2)}) collective-permute-start(f32[5,2,16,128]{3,1,2,0:T(2,128)S(1)} %get-tuple-element.15), channel_id=1, source_target_pairs={{0,16},{16,32},{32,48},{48,64},{64,80},{80,96},{96,112},{112,128},... | collective-permute-start | bytes 245768 | tf_op jit(solution)/shard_map/ppermute | solution.py:43
  131.8 11.2 %collective-permute-start.9 = (f32[5,32,2,128]{3,1,2,0:T(8,128)S(1)}, f32[5,32,2,128]{3,1,2,0:T(8,128)S(1)}, u32[]{:S(2)}, u32[]{:S(2)}) collective-permute-start(f32[5,32,2,128]{3,1,2,0:T(8,128)S(1)} %get-tuple-element.18), channel_id=1, source_target_pairs={{0,1},{1,2},{2,3},{3,4},{4,5},{5,6},{6,7},{7,8},{8,9},{9,10},{10,1... | collective-permute-start | bytes 491528 | tf_op jit(solution)/shard_map/ppermute | solution.py:41
  131.9 9.0 %collective-permute-start.10 = (f32[5,2,16,128]{3,1,2,0:T(2,128)S(1)}, f32[5,2,16,128]{3,1,2,0:T(2,128)S(1)}, u32[]{:S(2)}, u32[]{:S(2)}) collective-permute-start(f32[5,2,16,128]{3,1,2,0:T(2,128)S(1)} %get-tuple-element.16), channel_id=1, source_target_pairs={{16,0},{32,16},{48,32},{64,48},{80,64},{96,80},{112,96},{128,112},... | collective-permute-start | bytes 245768 | tf_op jit(solution)/shard_map/ppermute | solution.py:44
  133.9 9.7 %collective-permute-start.11 = (f32[5,32,2,128]{3,1,2,0:T(8,128)S(1)}, f32[5,32,2,128]{3,1,2,0:T(8,128)S(1)}, u32[]{:S(2)}, u32[]{:S(2)}) collective-permute-start(f32[5,32,2,128]{3,1,2,0:T(8,128)S(1)} %get-tuple-element.17), channel_id=1, source_target_pairs={{1,0},{2,1},{3,2},{4,3},{5,4},{6,5},{7,6},{8,7},{9,8},{10,9},{11,1... | collective-permute-start | bytes 491528 | tf_op jit(solution)/shard_map/ppermute | solution.py:42
  144.6 9.9 %collective-permute-start.12 = (f32[5,2,16,128]{3,1,2,0:T(2,128)S(1)}, f32[5,2,16,128]{3,1,2,0:T(2,128)S(1)}, u32[]{:S(2)}, u32[]{:S(2)}) collective-permute-start(f32[5,2,16,128]{3,1,2,0:T(2,128)S(1)} %get-tuple-element.7), channel_id=1, source_target_pairs={{0,16},{16,32},{32,48},{48,64},{64,80},{80,96},{96,112},{112,128},... | collective-permute-start | bytes 245768 | tf_op jit(solution)/shard_map/ppermute | solution.py:43
  148.6 13.8 %collective-permute-start.13 = (f32[5,32,2,128]{3,1,2,0:T(8,128)S(1)}, f32[5,32,2,128]{3,1,2,0:T(8,128)S(1)}, u32[]{:S(2)}, u32[]{:S(2)}) collective-permute-start(f32[5,32,2,128]{3,1,2,0:T(8,128)S(1)} %get-tuple-element.10), channel_id=1, source_target_pairs={{0,1},{1,2},{2,3},{3,4},{4,5},{5,6},{6,7},{7,8},{8,9},{9,10},{10,1... | collective-permute-start | bytes 491528 | tf_op jit(solution)/shard_map/ppermute | solution.py:41
  148.9 10.8 %collective-permute-start.14 = (f32[5,2,16,128]{3,1,2,0:T(2,128)S(1)}, f32[5,2,16,128]{3,1,2,0:T(2,128)S(1)}, u32[]{:S(2)}, u32[]{:S(2)}) collective-permute-start(f32[5,2,16,128]{3,1,2,0:T(2,128)S(1)} %get-tuple-element.8), channel_id=1, source_target_pairs={{16,0},{32,16},{48,32},{64,48},{80,64},{96,80},{112,96},{128,112},... | collective-permute-start | bytes 245768 | tf_op jit(solution)/shard_map/ppermute | solution.py:44
  150.9 12.1 %collective-permute-start.15 = (f32[5,32,2,128]{3,1,2,0:T(8,128)S(1)}, f32[5,32,2,128]{3,1,2,0:T(8,128)S(1)}, u32[]{:S(2)}, u32[]{:S(2)}) collective-permute-start(f32[5,32,2,128]{3,1,2,0:T(8,128)S(1)} %get-tuple-element.9), channel_id=1, source_target_pairs={{1,0},{2,1},{3,2},{4,3},{5,4},{6,5},{7,6},{8,7},{9,8},{10,9},{11,1... | collective-permute-start | bytes 491528 | tf_op jit(solution)/shard_map/ppermute | solution.py:42

commit v14 on v11

--- a/solution.py
+++ b/solution.py
@@ -64,12 +64,14 @@
     high = side(right, cells[:, :, cols - edge :], (above[:, :, cols - edge :], below[:, :, cols - edge :]), (0, width))
     first = stencil(low, kap[:, :width], speed_r, speed_p)
     last = stencil(high, kap[:, cols - width :], speed_r, speed_p)
-    return jnp.concatenate([first, middle, last], axis=2)
+    start = jnp.minimum(lax.axis_index("rad"), 0) + width
+    return jnp.concatenate([first, middle, last], axis=2), lax.dynamic_slice_in_dim(tall, start, rows, axis=1)
 
 
 def heun_sections(field, kappa, speed_r, speed_p, core=False):
-    first = field + split_stencil(field, kappa, speed_r, speed_p, core=core)
-    return 0.5 * (field + first + split_stencil(first, kappa, speed_r, speed_p))
+    change, held = split_stencil(field, kappa, speed_r, speed_p, core=core)
+    first = held + change
+    return 0.5 * (held + first + split_stencil(first, kappa, speed_r, speed_p)[0])
 
 
 def shift_rows(half, shifts):

time: 164 us -> 176 us (1.073)
  other arithmetic: 17.3 us -> 25.2 us
  waiting for transfers between devices: 41 us -> 34.5 us
  starting transfers between devices: 54 us -> 60 us
  local copies, waits for them, and re-layouts: 10.6 us -> 13.6 us
    ppermute x4, starting transfers between devices: 21.2 us -> 27.3 us  [split_stencil(): lax.ppermute(cells[..., rows - width:, :, :], 'rad', [(i, i + 1) for i in...]
    add x14, other arithmetic: 13.5 us -> 18.2 us  [stencil(): -speed_r[:, :, None, None] * first_r - speed_p[:, :, None, None] * first_p]
    ppermute x4, waiting for transfers between devices: 12.8 us -> 9.17 us  [split_stencil(): lax.ppermute(cells[..., :width, :, :], 'rad', [(i + 1, i) for i in range(...]
    all_to_all x1, waiting for transfers between devices: 28.2 us -> 25.2 us  [shift_rows(): full = lax.all_to_all(half, 'azi', 1, 2, tiled=True)]
    all_to_all x1, starting transfers between devices: 6.02 us -> 7.85 us  [shift_rows(): full = lax.all_to_all(half, 'azi', 1, 2, tiled=True)]
    ppermute x4, starting transfers between devices: 2.67 us -> 0.87 us  [split_stencil(): lax.ppermute(cells[..., cols - width:, :], 'azi', [(i, (i + 1) % sectors)...]
    unnamed x12 -> x20, local copies, waits for them, and re-layouts: 3.6 us -> 2.68 us
  transfers between devices with their start and end apart: 17 -> 17, of which waited for: 5 -> 4; matrix products, arithmetic and copies ran while one was open for 8% -> 11% of each run, Pallas kernels for 0% -> 0%
where the time goes in v14:
time: 176 us; the launch traced here: 175 us
  starting transfers between devices  60 us (34%)
  blocking collectives  37.6 us (21%)
  waiting for transfers between devices  34.5 us (20%)
  other arithmetic  25.2 us (14%)
  local copies, waits for them, and re-layouts  13.6 us (8%)
  between operations  4.31 us (2%)
    all_to_all x1, blocking collectives, shift_rows(): return lax.all_to_all(moved, 'azi', 2, 1, tiled=True)  37.6 us
    ppermute x4, starting transfers between devices, split_stencil(): lax.ppermute(cells[..., rows - width:, :, :], 'rad', [(i, i + 1) for i in...  27.3 us
    all_to_all x1, waiting for transfers between devices, shift_rows(): full = lax.all_to_all(half, 'azi', 1, 2, tiled=True)  25.2 us
    add x14, other arithmetic, stencil(): -speed_r[:, :, None, None] * first_r - speed_p[:, :, None, None] * first_p  18.2 us
    ppermute x4, starting transfers between devices, split_stencil(): lax.ppermute(cells[..., :width, :], 'azi', [((i + 1) % sectors, i) for i...  16.4 us
    ppermute x4, waiting for transfers between devices, split_stencil(): lax.ppermute(cells[..., :width, :, :], 'rad', [(i + 1, i) for i in range(...  9.17 us
    all_to_all x1, starting transfers between devices, shift_rows(): full = lax.all_to_all(half, 'azi', 1, 2, tiled=True)  7.85 us
    ppermute x4, starting transfers between devices, split_stencil(): lax.ppermute(cells[..., :width, :, :], 'rad', [(i + 1, i) for i in range(...  7.68 us
  transfers between devices with their start and end apart: 17, of which 4 were waited for; matrix products, arithmetic and copies ran while one was open for 11% of the time, Pallas kernels for 0%

profile of v14, /device:TPU:1, one launch (start us, length us, event | category | flops | bytes accessed | tf_op | source)
XLA Modules:
  0.0 175.1 jit_solution(16627120039500412469)
XLA Ops:
  0.0 1.7 copy.14
  2.5 6.2 %collective-permute-start = (f32[5,2,16,128]{3,1,2,0:T(2,128)}, f32[5,2,16,128]{3,1,2,0:T(2,128)S(1)}, u32[]{:S(2)}, u32[]{:S(2)}) collective-permute-start(f32[5,2,16,128]{3,1,2,0:T(2,128)} %get-tuple-element.35), channel_id=1, source_target_pairs={{0,16},{16,32},{32,48},{48,64},{64,80},{80,96},{96,112},{112,128},... | collective-permute-start | bytes 245768 | tf_op jit(solution)/shard_map/ppermute | solution.py:42
  8.7 1.9 %collective-permute-start.1 = (f32[5,2,16,128]{3,1,2,0:T(2,128)}, f32[5,2,16,128]{3,1,2,0:T(2,128)}, u32[]{:S(2)}, u32[]{:S(2)}) collective-permute-start(f32[5,2,16,128]{3,1,2,0:T(2,128)} %get-tuple-element.36), channel_id=1, source_target_pairs={{16,0},{32,16},{48,32},{64,48},{80,64},{96,80},{112,96},{128,112},... | collective-permute-start | bytes 245768 | tf_op jit(solution)/shard_map/ppermute | solution.py:43
  11.7 5.3 %collective-permute-start.3 = (f32[5,32,2,128]{3,1,2,0:T(8,128)}, f32[5,32,2,128]{3,1,2,0:T(8,128)}, u32[]{:S(2)}, u32[]{:S(2)}) collective-permute-start(f32[5,32,2,128]{3,1,2,0:T(8,128)} %get-tuple-element.37), channel_id=1, source_target_pairs={{1,0},{2,1},{3,2},{4,3},{5,4},{6,5},{7,6},{8,7},{9,8},{10,9},{11,1... | collective-permute-start | bytes 491528 | tf_op jit(solution)/shard_map/ppermute | solution.py:41
  18.7 2.0 %fusion.18 = f32[5,28,12,128]{3,1,2,0:T(8,128)S(1)} fusion(f32[5,28,12,128]{3,1,2,0:T(8,128)S(1)} %slice.1147, f32[5,32,16,128]{3,1,2,0:T(8,128)S(1)} %copy.14, f32[28,12,128]{2,0,1:T(8,128)S(1)} %copy.41, f32[5,28]{1,0:T(8,128)S(1)} %get-tuple-element.87, f32[5,28]{1,0:T(8,128)S(1)} %get-tuple-element.88), kind=kLoop, calls=%fused_computation.59 | loop fusion | flops 8386560 | bytes 8774752 | tf_op jit(solution)/shard_map/add | solution.py:31
  23.3 1.5 multiply_add_fusion.1
  24.9 1.4 multiply_add_fusion
  27.1 1.4 select_maximum_fusion.13
  28.4 1.7 fusion.59
  30.2 1.8 %fusion.69 = f32[5,32,2,128]{3,1,2,0:T(8,128)S(1)} fusion(f32[5,32,2,128]{3,1,2,0:T(8,128)} %get-tuple-element.38, f32[5,32,2,128]{3,1,2,0:T(8,128)} %collective-permute-done.3, f32[5,32,4,128]{3,1,2,0:T(8,128)S(1)} %get-tuple-element.32, f32[5,32,16,128]{3,1,2,0:T(8,128)S(1)} %copy.14, f32[5,34,6,128]{3,1,2,0:T(8,128)S(1)} %get-tuple-element.54, ...), kind=kLoop, calls=%fused_computation.168 | loop fusion | flops 1638400 | bytes 1836288 | tf_op jit(solution)/shard_map/add | solution.py:31
  31.9 1.6 maximum_add_fusion
  33.6 6.0 %collective-permute-start.4 = (f32[5,2,16,128]{3,1,2,0:T(2,128)S(1)}, f32[5,2,16,128]{3,1,2,0:T(2,128)S(1)}, u32[]{:S(2)}, u32[]{:S(2)}) collective-permute-start(f32[5,2,16,128]{3,1,2,0:T(2,128)S(1)} %get-tuple-element.27), channel_id=1, source_target_pairs={{0,16},{16,32},{32,48},{48,64},{64,80},{80,96},{96,112},{112,128},... | collective-permute-start | bytes 245768 | tf_op jit(solution)/shard_map/ppermute | solution.py:42
  39.9 1.9 %collective-permute-start.6 = (f32[5,2,16,128]{3,1,2,0:T(2,128)S(1)}, f32[5,2,16,128]{3,1,2,0:T(2,128)S(1)}, u32[]{:S(2)}, u32[]{:S(2)}) collective-permute-start(f32[5,2,16,128]{3,1,2,0:T(2,128)S(1)} %get-tuple-element.28), channel_id=1, source_target_pairs={{16,0},{32,16},{48,32},{64,48},{80,64},{96,80},{112,96},{128,112},... | collective-permute-start | bytes 245768 | tf_op jit(solution)/shard_map/ppermute | solution.py:43
  41.8 3.8 %collective-permute-start.7 = (f32[5,32,2,128]{3,1,2,0:T(8,128)S(1)}, f32[5,32,2,128]{3,1,2,0:T(8,128)S(1)}, u32[]{:S(2)}, u32[]{:S(2)}) collective-permute-start(f32[5,32,2,128]{3,1,2,0:T(8,128)S(1)} %get-tuple-element.29), channel_id=1, source_target_pairs={{1,0},{2,1},{3,2},{4,3},{5,4},{6,5},{7,6},{8,7},{9,8},{10,9},{11,1... | collective-permute-start | bytes 491528 | tf_op jit(solution)/shard_map/ppermute | solution.py:41
  45.7 2.0 %collective-permute-done.6 = f32[5,2,16,128]{3,1,2,0:T(2,128)S(1)} collective-permute-done((f32[5,2,16,128]{3,1,2,0:T(2,128)S(1)}, f32[5,2,16,128]{3,1,2,0:T(2,128)S(1)}, u32[]{:S(2)}, u32[]{:S(2)}) %collective-permute-start.6) | collective-permute-done | bytes 81952 | tf_op jit(solution)/shard_map/ppermute | solution.py:43
  47.6 2.7 %fusion.28 = f32[5,32,12,128]{3,1,2,0:T(8,128)S(1)} fusion(f32[5,32,12,128]{3,1,2,0:T(8,128)S(1)} %slice.1186, f32[5,32,16,128]{3,1,2,0:T(8,128)S(1)} %get-tuple-element.7, f32[5,2,16,128]{3,1,2,0:T(2,128)S(1)} %collective-permute-done.6, f32[5,2,16,128]{3,1,2,0:T(2,128)S(1)} %collective-permute-done.4, f32[32,12,128]{2,0,1:T(8,128)S(1)} %copy.55, ...), kind=kLoop, calls=%fused_computation.69 | loop fusion | flops 10567680 | bytes 7577600 | tf_op jit(solution)/shard_map/add | solution.py:31
  51.8 1.8 %copy.56 = f32[5,32,16,128]{3,2,0,1:T(8,128)} copy(f32[5,32,16,128]{3,1,2,0:T(8,128)S(1)} %fusion.4) | data formatting | bytes 2621440 | tf_op jit(solution)/shard_map/mul | solution.py:74
  53.6 7.8 %all-to-all-start = ((f32[5,32,16,128]{3,2,0,1:T(8,128)}), f32[5,32,16,128]{3,2,0,1:T(8,128)S(1)}, u32[]{:S(2)}, u32[]{:S(2)}) async-start(f32[5,32,16,128]{3,2,0,1:T(8,128)} %copy.56), calls=%async_computation | async-start | bytes 2621440 | tf_op jit(solution)/shard_map/all_to_all | solution.py:81
  65.8 25.2 %all-to-all-done = f32[5,32,16,128]{3,2,0,1:T(8,128)S(1)} async-done(((f32[5,32,16,128]{3,2,0,1:T(8,128)}), f32[5,32,16,128]{3,2,0,1:T(8,128)S(1)}, u32[]{:S(2)}, u32[]{:S(2)}) %all-to-all-start) | async-done | bytes 1310752 | tf_op jit(solution)/shard_map/all_to_all | solution.py:81
  91.8 1.0 copy.59
  92.8 37.6 %all_to_all.36 = f32[5,2,256,128]{3,1,0,2:T(2,128)S(1)} all-to-all(f32[5,2,256,128]{3,1,0,2:T(2,128)S(1)} %copy.59), channel_id=1, replica_groups=mesh['rad'=16,'azi'=16] {'azi'}, dimensions={2} | all-to-all | bytes 2621440 | tf_op jit(solution)/shard_map/all_to_all | solution.py:91
  131.2 8.9 %collective-permute-start.8 = (f32[5,2,16,128]{3,1,2,0:T(2,128)S(1)}, f32[5,2,16,128]{3,1,2,0:T(2,128)S(1)}, u32[]{:S(2)}, u32[]{:S(2)}) collective-permute-start(f32[5,2,16,128]{3,1,2,0:T(2,128)S(1)} %get-tuple-element.19), channel_id=1, source_target_pairs={{0,16},{16,32},{32,48},{48,64},{64,80},{80,96},{96,112},{112,128},... | collective-permute-start | bytes 245768 | tf_op jit(solution)/shard_map/ppermute | solution.py:42
  140.3 1.9 %collective-permute-start.9 = (f32[5,2,16,128]{3,1,2,0:T(2,128)S(1)}, f32[5,2,16,128]{3,1,2,0:T(2,128)S(1)}, u32[]{:S(2)}, u32[]{:S(2)}) collective-permute-start(f32[5,2,16,128]{3,1,2,0:T(2,128)S(1)} %get-tuple-element.20), channel_id=1, source_target_pairs={{16,0},{32,16},{48,32},{64,48},{80,64},{96,80},{112,96},{128,112},... | collective-permute-start | bytes 245768 | tf_op jit(solution)/shard_map/ppermute | solution.py:43
  142.2 3.6 %collective-permute-start.11 = (f32[5,32,2,128]{3,1,2,0:T(8,128)S(1)}, f32[5,32,2,128]{3,1,2,0:T(8,128)S(1)}, u32[]{:S(2)}, u32[]{:S(2)}) collective-permute-start(f32[5,32,2,128]{3,1,2,0:T(8,128)S(1)} %get-tuple-element.21), channel_id=1, source_target_pairs={{1,0},{2,1},{3,2},{4,3},{5,4},{6,5},{7,6},{8,7},{9,8},{10,9},{11,1... | collective-permute-start | bytes 491528 | tf_op jit(solution)/shard_map/ppermute | solution.py:41
  145.9 2.0 %collective-permute-done.9 = f32[5,2,16,128]{3,1,2,0:T(2,128)S(1)} collective-permute-done((f32[5,2,16,128]{3,1,2,0:T(2,128)S(1)}, f32[5,2,16,128]{3,1,2,0:T(2,128)S(1)}, u32[]{:S(2)}, u32[]{:S(2)}) %collective-permute-start.9) | collective-permute-done | bytes 81952 | tf_op jit(solution)/shard_map/ppermute | solution.py:43
  147.9 2.0 %fusion.38 = f32[5,32,12,128]{3,1,2,0:T(8,128)S(1)} fusion(f32[5,32,12,128]{3,1,2,0:T(8,128)S(1)} %slice.1219, f32[5,32,16,128]{3,1,2,0:T(8,128)S(1)} %get-tuple-element.18, f32[5,34,16,128]{3,1,2,0:T(8,128)S(1)} %constant_dynamic-update-slice_fusion, f32[5,2,16,128]{3,1,2,0:T(2,128)S(1)} %collective-permute-done.8, f32[32,12,128]{2,0,1:T(8,128)S(1)} %copy.55, ...), kind=kLoop, calls=%fused_computation.79 | loop fusion | flops 10076160 | bytes 9461760 | tf_op jit(solution)/shard_map/add | solution.py:31
  151.7 6.2 %collective-permute-start.12 = (f32[5,2,16,128]{3,1,2,0:T(2,128)S(1)}, f32[5,2,16,128]{3,1,2,0:T(2,128)S(1)}, u32[]{:S(2)}, u32[]{:S(2)}) collective-permute-start(f32[5,2,16,128]{3,1,2,0:T(2,128)S(1)} %get-tuple-element.11), channel_id=1, source_target_pairs={{0,16},{16,32},{32,48},{48,64},{64,80},{80,96},{96,112},{112,128},... | collective-permute-start | bytes 245768 | tf_op jit(solution)/shard_map/ppermute | solution.py:42
  158.3 1.9 %collective-permute-start.14 = (f32[5,2,16,128]{3,1,2,0:T(2,128)S(1)}, f32[5,2,16,128]{3,1,2,0:T(2,128)S(1)}, u32[]{:S(2)}, u32[]{:S(2)}) collective-permute-start(f32[5,2,16,128]{3,1,2,0:T(2,128)S(1)} %get-tuple-element.12), channel_id=1, source_target_pairs={{16,0},{32,16},{48,32},{64,48},{80,64},{96,80},{112,96},{128,112},... | collective-permute-start | bytes 245768 | tf_op jit(solution)/shard_map/ppermute | solution.py:43
  160.2 3.6 %collective-permute-start.15 = (f32[5,32,2,128]{3,1,2,0:T(8,128)S(1)}, f32[5,32,2,128]{3,1,2,0:T(8,128)S(1)}, u32[]{:S(2)}, u32[]{:S(2)}) collective-permute-start(f32[5,32,2,128]{3,1,2,0:T(8,128)S(1)} %get-tuple-element.13), channel_id=1, source_target_pairs={{1,0},{2,1},{3,2},{4,3},{5,4},{6,5},{7,6},{8,7},{9,8},{10,9},{11,1... | collective-permute-start | bytes 491528 | tf_op jit(solution)/shard_map/ppermute | solution.py:41
  163.9 5.2 %collective-permute-done.14 = f32[5,2,16,128]{3,1,2,0:T(2,128)S(1)} collective-permute-done((f32[5,2,16,128]{3,1,2,0:T(2,128)S(1)}, f32[5,2,16,128]{3,1,2,0:T(2,128)S(1)}, u32[]{:S(2)}, u32[]{:S(2)}) %collective-permute-start.14) | collective-permute-done | bytes 81952 | tf_op jit(solution)/shard_map/ppermute | solution.py:43
  169.1 2.7 %fusion.48 = f32[5,32,12,128]{3,1,2,0:T(8,128)S(1)} fusion(f32[5,32,12,128]{3,1,2,0:T(8,128)S(1)} %slice.1250, f32[5,32,16,128]{3,1,2,0:T(8,128)S(1)} %get-tuple-element.5, f32[5,2,16,128]{3,1,2,0:T(2,128)S(1)} %collective-permute-done.14, f32[5,2,16,128]{3,1,2,0:T(2,128)S(1)} %collective-permute-done.12, f32[32,12,128]{2,0,1:T(8,128)S(1)} %copy.55, ...), kind=kLoop, calls=%fused_computation.89 | loop fusion | flops 10567680 | bytes 7577600 | tf_op jit(solution)/shard_map/add | solution.py:31
  173.3 1.8 %copy.80 = f32[5,32,16,128]{3,2,1,0:T(8,128)} copy(f32[5,32,16,128]{3,1,2,0:T(8,128)S(1)} %fusion.5) | data formatting | bytes 2621440 | tf_op jit(solution)/shard_map/mul | solution.py:74
  (99 shorter events, 14.4 us)
Async XLA Ops:
  1.7 15.4 %copy-start = (f32[32,16,128]{2,1,0:T(8,128)S(1)}, f32[32,16,128]{2,1,0:T(8,128)}, u32[]{:S(2)}) copy-start(f32[32,16,128]{2,1,0:T(8,128)} %param.6) | copy-start | bytes 786436
  2.5 20.8 %collective-permute-start = (f32[5,2,16,128]{3,1,2,0:T(2,128)}, f32[5,2,16,128]{3,1,2,0:T(2,128)S(1)}, u32[]{:S(2)}, u32[]{:S(2)}) collective-permute-start(f32[5,2,16,128]{3,1,2,0:T(2,128)} %get-tuple-element.35), channel_id=1, source_target_pairs={{0,16},{16,32},{32,48},{48,64},{64,80},{80,96},{96,112},{112,128},... | collective-permute-start | bytes 245768 | tf_op jit(solution)/shard_map/ppermute | solution.py:42
  8.7 16.1 %collective-permute-start.1 = (f32[5,2,16,128]{3,1,2,0:T(2,128)}, f32[5,2,16,128]{3,1,2,0:T(2,128)}, u32[]{:S(2)}, u32[]{:S(2)}) collective-permute-start(f32[5,2,16,128]{3,1,2,0:T(2,128)} %get-tuple-element.36), channel_id=1, source_target_pairs={{16,0},{32,16},{48,32},{64,48},{80,64},{96,80},{112,96},{128,112},... | collective-permute-start | bytes 245768 | tf_op jit(solution)/shard_map/ppermute | solution.py:43
  11.3 15.7 %collective-permute-start.2 = (f32[5,32,2,128]{3,1,2,0:T(8,128)}, f32[5,32,2,128]{3,1,2,0:T(8,128)}, u32[]{:S(2)}, u32[]{:S(2)}) collective-permute-start(f32[5,32,2,128]{3,1,2,0:T(8,128)} %get-tuple-element.38), channel_id=1, source_target_pairs={{0,1},{1,2},{2,3},{3,4},{4,5},{5,6},{6,7},{7,8},{8,9},{9,10},{10,1... | collective-permute-start | bytes 491528 | tf_op jit(solution)/shard_map/ppermute | solution.py:40
  11.7 15.3 %collective-permute-start.3 = (f32[5,32,2,128]{3,1,2,0:T(8,128)}, f32[5,32,2,128]{3,1,2,0:T(8,128)}, u32[]{:S(2)}, u32[]{:S(2)}) collective-permute-start(f32[5,32,2,128]{3,1,2,0:T(8,128)} %get-tuple-element.37), channel_id=1, source_target_pairs={{1,0},{2,1},{3,2},{4,3},{5,4},{6,5},{7,6},{8,7},{9,8},{10,9},{11,1... | collective-permute-start | bytes 491528 | tf_op jit(solution)/shard_map/ppermute | solution.py:41
  17.1 0.7 copy-start.3
  17.1 0.7 copy-start.4
  23.2 1.6 copy-start.5
  23.2 1.6 copy-start.6
  23.2 1.6 copy-start.7
  27.0 1.4 copy-start.1
  27.0 1.4 copy-start.2
  33.6 12.0 %collective-permute-start.4 = (f32[5,2,16,128]{3,1,2,0:T(2,128)S(1)}, f32[5,2,16,128]{3,1,2,0:T(2,128)S(1)}, u32[]{:S(2)}, u32[]{:S(2)}) collective-permute-start(f32[5,2,16,128]{3,1,2,0:T(2,128)S(1)} %get-tuple-element.27), channel_id=1, source_target_pairs={{0,16},{16,32},{32,48},{48,64},{64,80},{80,96},{96,112},{112,128},... | collective-permute-start | bytes 245768 | tf_op jit(solution)/shard_map/ppermute | solution.py:42
  39.8 10.6 %collective-permute-start.5 = (f32[5,32,2,128]{3,1,2,0:T(8,128)S(1)}, f32[5,32,2,128]{3,1,2,0:T(8,128)S(1)}, u32[]{:S(2)}, u32[]{:S(2)}) collective-permute-start(f32[5,32,2,128]{3,1,2,0:T(8,128)S(1)} %get-tuple-element.30), channel_id=1, source_target_pairs={{0,1},{1,2},{2,3},{3,4},{4,5},{5,6},{6,7},{7,8},{8,9},{9,10},{10,1... | collective-permute-start | bytes 491528 | tf_op jit(solution)/shard_map/ppermute | solution.py:40
  39.9 7.7 %collective-permute-start.6 = (f32[5,2,16,128]{3,1,2,0:T(2,128)S(1)}, f32[5,2,16,128]{3,1,2,0:T(2,128)S(1)}, u32[]{:S(2)}, u32[]{:S(2)}) collective-permute-start(f32[5,2,16,128]{3,1,2,0:T(2,128)S(1)} %get-tuple-element.28), channel_id=1, source_target_pairs={{16,0},{32,16},{48,32},{64,48},{80,64},{96,80},{112,96},{128,112},... | collective-permute-start | bytes 245768 | tf_op jit(solution)/shard_map/ppermute | solution.py:43
  41.8 9.0 %collective-permute-start.7 = (f32[5,32,2,128]{3,1,2,0:T(8,128)S(1)}, f32[5,32,2,128]{3,1,2,0:T(8,128)S(1)}, u32[]{:S(2)}, u32[]{:S(2)}) collective-permute-start(f32[5,32,2,128]{3,1,2,0:T(8,128)S(1)} %get-tuple-element.29), channel_id=1, source_target_pairs={{1,0},{2,1},{3,2},{4,3},{5,4},{6,5},{7,6},{8,7},{9,8},{10,9},{11,1... | collective-permute-start | bytes 491528 | tf_op jit(solution)/shard_map/ppermute | solution.py:41
  53.6 7.9 %copy-start.8 = (s32[32]{0:T(128)S(1)}, s32[32]{0:T(128)}, u32[]{:S(2)}) copy-start(s32[32]{0:T(128)} %param.9) | copy-start | bytes 388
  53.6 37.4 %all-to-all-start = ((f32[5,32,16,128]{3,2,0,1:T(8,128)}), f32[5,32,16,128]{3,2,0,1:T(8,128)S(1)}, u32[]{:S(2)}, u32[]{:S(2)}) async-start(f32[5,32,16,128]{3,2,0,1:T(8,128)} %copy.56), calls=%async_computation | async-start | bytes 2621440 | tf_op jit(solution)/shard_map/all_to_all | solution.py:81
  131.2 14.7 %collective-permute-start.8 = (f32[5,2,16,128]{3,1,2,0:T(2,128)S(1)}, f32[5,2,16,128]{3,1,2,0:T(2,128)S(1)}, u32[]{:S(2)}, u32[]{:S(2)}) collective-permute-start(f32[5,2,16,128]{3,1,2,0:T(2,128)S(1)} %get-tuple-element.19), channel_id=1, source_target_pairs={{0,16},{16,32},{32,48},{48,64},{64,80},{80,96},{96,112},{112,128},... | collective-permute-start | bytes 245768 | tf_op jit(solution)/shard_map/ppermute | solution.py:42
  140.2 9.8 %collective-permute-start.10 = (f32[5,32,2,128]{3,1,2,0:T(8,128)S(1)}, f32[5,32,2,128]{3,1,2,0:T(8,128)S(1)}, u32[]{:S(2)}, u32[]{:S(2)}) collective-permute-start(f32[5,32,2,128]{3,1,2,0:T(8,128)S(1)} %get-tuple-element.22), channel_id=1, source_target_pairs={{0,1},{1,2},{2,3},{3,4},{4,5},{5,6},{6,7},{7,8},{8,9},{9,10},{10,1... | collective-permute-start | bytes 491528 | tf_op jit(solution)/shard_map/ppermute | solution.py:40
  140.3 7.6 %collective-permute-start.9 = (f32[5,2,16,128]{3,1,2,0:T(2,128)S(1)}, f32[5,2,16,128]{3,1,2,0:T(2,128)S(1)}, u32[]{:S(2)}, u32[]{:S(2)}) collective-permute-start(f32[5,2,16,128]{3,1,2,0:T(2,128)S(1)} %get-tuple-element.20), channel_id=1, source_target_pairs={{16,0},{32,16},{48,32},{64,48},{80,64},{96,80},{112,96},{128,112},... | collective-permute-start | bytes 245768 | tf_op jit(solution)/shard_map/ppermute | solution.py:43
  142.2 8.2 %collective-permute-start.11 = (f32[5,32,2,128]{3,1,2,0:T(8,128)S(1)}, f32[5,32,2,128]{3,1,2,0:T(8,128)S(1)}, u32[]{:S(2)}, u32[]{:S(2)}) collective-permute-start(f32[5,32,2,128]{3,1,2,0:T(8,128)S(1)} %get-tuple-element.21), channel_id=1, source_target_pairs={{1,0},{2,1},{3,2},{4,3},{5,4},{6,5},{7,6},{8,7},{9,8},{10,9},{11,1... | collective-permute-start | bytes 491528 | tf_op jit(solution)/shard_map/ppermute | solution.py:41
  151.7 12.2 %collective-permute-start.12 = (f32[5,2,16,128]{3,1,2,0:T(2,128)S(1)}, f32[5,2,16,128]{3,1,2,0:T(2,128)S(1)}, u32[]{:S(2)}, u32[]{:S(2)}) collective-permute-start(f32[5,2,16,128]{3,1,2,0:T(2,128)S(1)} %get-tuple-element.11), channel_id=1, source_target_pairs={{0,16},{16,32},{32,48},{48,64},{64,80},{80,96},{96,112},{112,128},... | collective-permute-start | bytes 245768 | tf_op jit(solution)/shard_map/ppermute | solution.py:42
  158.0 13.9 %collective-permute-start.13 = (f32[5,32,2,128]{3,1,2,0:T(8,128)S(1)}, f32[5,32,2,128]{3,1,2,0:T(8,128)S(1)}, u32[]{:S(2)}, u32[]{:S(2)}) collective-permute-start(f32[5,32,2,128]{3,1,2,0:T(8,128)S(1)} %get-tuple-element.14), channel_id=1, source_target_pairs={{0,1},{1,2},{2,3},{3,4},{4,5},{5,6},{6,7},{7,8},{8,9},{9,10},{10,1... | collective-permute-start | bytes 491528 | tf_op jit(solution)/shard_map/ppermute | solution.py:40
  158.3 10.8 %collective-permute-start.14 = (f32[5,2,16,128]{3,1,2,0:T(2,128)S(1)}, f32[5,2,16,128]{3,1,2,0:T(2,128)S(1)}, u32[]{:S(2)}, u32[]{:S(2)}) collective-permute-start(f32[5,2,16,128]{3,1,2,0:T(2,128)S(1)} %get-tuple-element.12), channel_id=1, source_target_pairs={{16,0},{32,16},{48,32},{64,48},{80,64},{96,80},{112,96},{128,112},... | collective-permute-start | bytes 245768 | tf_op jit(solution)/shard_map/ppermute | solution.py:43
  160.2 12.1 %collective-permute-start.15 = (f32[5,32,2,128]{3,1,2,0:T(8,128)S(1)}, f32[5,32,2,128]{3,1,2,0:T(8,128)S(1)}, u32[]{:S(2)}, u32[]{:S(2)}) collective-permute-start(f32[5,32,2,128]{3,1,2,0:T(8,128)S(1)} %get-tuple-element.13), channel_id=1, source_target_pairs={{1,0},{2,1},{3,2},{4,3},{5,4},{6,5},{7,6},{8,7},{9,8},{10,9},{11,1... | collective-permute-start | bytes 491528 | tf_op jit(solution)/shard_map/ppermute | solution.py:41
